TPU v7x, 32 devices: a whole 2x2x4 slice. The times are simulated.
32 devices in a mesh: grp: 2 (over x), pt: 16 (over z, y, core).
Axes of the slice: x: 2, y: 2, z: 4, core: 2. Of those that a mesh axis runs over, the one named last changes fastest.
Arguments:
- left_factor: float32 [16, 128, 2048], P('grp', 'pt'), may hold values from 0 to 7340032, as said below
- right_factor: float32 [128, 128, 2048], P('grp', 'pt'), may hold values from 0 to 7340032, as said below
Outputs:
- product: float32 [16, 128, 4096], P('grp', 'pt')
Inputs may be any that keep to these rules, and one draw needn't show every extreme that they name: `left_factor`: every entry is a whole number, a residue modulo 7340033. `right_factor`: every entry is a whole number, a residue modulo 7340033.
All inputs are finite; a program needn't handle non-finite values.
Results may differ from a plain program's by a relative error of at most 0.0003.
Values sent between devices are 32-bit elements; how exact they have to be, the bound alone decides.
No kernel may reach another device: no remote copies, remote signals or barrier semaphores. Data moves between devices by JAX's collectives and lax.ppermute only.
A program may use at most 192 MiB of HBM per device.

v0:
```python
import jax
import jax.numpy as jnp
import numpy as np
from jax import lax
from jax.sharding import PartitionSpec as P

FIRST = 32
SECOND = 128


modulus = 7340033


def root_powers(length_all):
    for generator in range(2, 64):
        candidate = pow(generator, (modulus - 1) // length_all, modulus)
        if pow(candidate, length_all // 2, modulus) == modulus - 1:
            break
    powers = [1]
    for counter in range(length_all - 1):
        powers.append(powers[-1] * candidate % modulus)
    return np.array(powers, dtype=np.int64)


def power_table(powers, exponents):
    return powers[exponents % powers.shape[0]]


def dft_tables():
    length_all = FIRST * SECOND
    powers = root_powers(length_all)
    half_first = np.arange(FIRST // 2)
    range_first = np.arange(FIRST)
    range_second = np.arange(SECOND)
    first_table = power_table(powers, SECOND * np.outer(half_first, range_first))
    twist_table = power_table(powers, np.outer(range_first, range_second))
    second_table = power_table(powers, FIRST * np.outer(range_second, range_second))
    back_first_table = power_table(powers, -FIRST * np.outer(range_second, range_second))
    back_twist_table = power_table(powers, -np.outer(range_second, range_first))
    scale_inv = pow(length_all, modulus - 2, modulus)
    back_second_table = (
        power_table(powers, -SECOND * np.outer(range_first, range_first)) * scale_inv % modulus
    )
    return (
        first_table,
        twist_table,
        second_table,
        back_first_table,
        back_twist_table,
        back_second_table,
    )


def stacked_table(table_np):
    pieces = [table_np // 256**limb_level % 256 for limb_level in range(3)]
    stacked = np.zeros((5, 3) + table_np.shape, dtype=np.float32)
    for total_level in range(5):
        for limb_level in range(3):
            partner = total_level - limb_level
            if 0 <= partner < 3:
                stacked[total_level, limb_level] = pieces[partner]
    return stacked


def limb_split(values):
    return [values % 256, values // 256 % 256, values // 65536]


def fold_sums(level_sums):
    result = level_sums[4] % modulus
    for limb_level in (3, 2, 1, 0):
        result = (result * 256 + level_sums[limb_level]) % modulus
    return result


def times_table(values, table_np):
    left_limbs = limb_split(values)
    right_limbs = limb_split(jnp.asarray(table_np.astype(np.int32)))
    level_sums = []
    for total_level in range(5):
        running = jnp.zeros_like(values)
        for limb_level in range(3):
            partner = total_level - limb_level
            if 0 <= partner < 3:
                running = running + left_limbs[limb_level] * right_limbs[partner]
        level_sums.append(running)
    return fold_sums(level_sums)


def limb_stack(values):
    return jnp.stack([piece.astype(jnp.bfloat16) for piece in limb_split(values)])


def contract(form, values, table_np):
    planes = jnp.einsum(
        form,
        limb_stack(values),
        jnp.asarray(stacked_table(table_np), jnp.bfloat16),
        preferred_element_type=jnp.float32,
    )
    return fold_sums([planes[limb_level].astype(jnp.int32) for limb_level in range(5)])


def forward(rows_in, tables):
    first_table, twist_table, second_table = (tables[0], tables[1], tables[2])
    entries = rows_in.shape[0]
    current = rows_in.reshape(entries, FIRST // 2, SECOND)
    current = contract("leab,slac->secb", current, first_table)
    current = times_table(current, twist_table)
    current = contract("lecb,slbd->sdce", current, second_table)
    return current.reshape(FIRST * SECOND, entries)


def inverse(point_values, tables):
    back_first_table, back_twist_table, back_second_table = (tables[3], tables[4], tables[5])
    entries = point_values.shape[1]
    current = point_values.reshape(SECOND, FIRST, entries)
    current = contract("ldce,sldb->sebc", current, back_first_table)
    current = times_table(current, back_twist_table)
    current = contract("lebc,slca->seab", current, back_second_table)
    return current.reshape(entries, FIRST * SECOND)


def multiply_points(left_points, right_points):
    planes = jnp.einsum(
        "xpik,ypjk->xypij",
        limb_stack(left_points),
        limb_stack(right_points),
        preferred_element_type=jnp.float32,
    )
    level_sums = []
    for total_level in range(5):
        running = jnp.zeros(planes.shape[2:], jnp.int32)
        for limb_level in range(3):
            partner = total_level - limb_level
            if 0 <= partner < 3:
                running = running + planes[limb_level, partner].astype(jnp.int32)
        level_sums.append(running)
    return fold_sums(level_sums)


def body(left_factor, right_factor):
    tables = dft_tables()
    length_all = FIRST * SECOND
    left_rows = left_factor.shape[0]
    inner_cols = left_factor.shape[1]
    right_rows = right_factor.shape[0]
    left_eval = forward(left_factor.astype(jnp.int32).reshape(-1, left_factor.shape[2]), tables)
    right_eval = forward(right_factor.astype(jnp.int32).reshape(-1, right_factor.shape[2]), tables)
    left_send = left_eval.astype(jnp.float32).reshape(length_all, left_rows, inner_cols)
    right_send = right_eval.astype(jnp.float32).reshape(length_all, right_rows, inner_cols)
    left_owned, right_owned = (
        lax.all_to_all(left_send, "pt", split_axis=0, concat_axis=2, tiled=True),
        lax.all_to_all(right_send, "pt", split_axis=0, concat_axis=2, tiled=True),
    )
    right_whole = lax.all_gather(right_owned, "grp", axis=1, tiled=True)
    product_points = multiply_points(left_owned.astype(jnp.int32), right_whole.astype(jnp.int32))
    returned = lax.all_to_all(
        product_points.astype(jnp.float32), "pt", split_axis=2, concat_axis=0, tiled=True
    )
    point_rows = returned.reshape(length_all, -1)
    coefficients = inverse(point_rows.astype(jnp.int32), tables)
    return (coefficients.astype(jnp.float32) / modulus).reshape(left_rows, inner_cols, length_all)


def solution(mesh):
    return jax.shard_map(
        body,
        mesh=mesh,
        in_specs=(P("grp", "pt", None), P("grp", "pt", None)),
        out_specs=P("grp", "pt", None),
        check_vma=False,
    )
```

profile of v0, /device:TPU:1, one launch (start us, length us, event | category | flops | bytes accessed | tf_op | source)
XLA Modules:
  0.0 1053.8 jit_solution(5138153870478670075)
XLA Ops:
  10.1 8.4 fusion.73
  18.5 17.4 %convolution_bitcast_fusion = f32[5,512,32,128]{3,2,0,1:T(8,128)} fusion(bf16[5,3,16,32,1]{3,2,1,0,4:T(8,128)(2,1)S(1)} %copy-done.5, bf16[1,512,16,128]{3,2,0,1:T(8,128)(2,1)S(1)} %get-tuple-element.29, bf16[1,512,16,128]{3,2,0,1:T(8,128)(2,1)} %get-tuple-element.30, bf16[1,512,16,128]{3,2,0,1:T(8,128)(2,1)S(1)} %get-tuple-element.28), kind=kOutput, calls=%fused_computation.17 | convolution fusion | flops 1025507328 | bytes 48249856 | tf_op jit(solution)/shard_map/leab,slac->secb/dot_general | solution.py:95
  35.9 71.7 %fusion.39 = (bf16[1,512,32,128]{3,2,0,1:T(8,128)(2,1)S(1)}, s32[1,512,32,128]{3,2,0,1:T(8,128)S(1)}) fusion(s32[32,128]{1,0:T(8,128)S(1)} %copy-done.8, s32[32,128]{1,0:T(8,128)S(1)} %copy-done.10, s32[32,128]{1,0:T(8,128)S(1)} %copy-done.12, f32[5,512,32,128]{3,2,0,1:T(8,128)} %convolution_bitcast_fusion), kind=kLoop, calls=%fused_computation.93 | loop fusion | flops 306184192 | bytes 54575104 | tf_op jit(solution)/shard_map/convert_element_type | solution.py:91
  107.6 12.9 %fusion.41 = (bf16[1,512,32,128]{3,2,0,1:T(8,128)(2,1)S(1)}, bf16[1,512,32,128]{3,2,0,1:T(8,128)(2,1)S(1)}) fusion(s32[1,512,32,128]{3,2,0,1:T(8,128)S(1)} %get-tuple-element.10), kind=kLoop, calls=%fused_computation.95 | loop fusion | flops 79691776 | bytes 16777216 | tf_op jit(solution)/shard_map/convert_element_type | solution.py:91
  120.5 5.6 maximum_bitcast_fusion.2
  126.1 29.1 %convolution_bitcast_fusion.1 = f32[5,128,32,512]{1,3,0,2:T(8,128)} fusion(bf16[5,3,128,128,1]{3,2,1,0,4:T(8,128)(2,1)S(1)} %copy-done.1, bf16[3,512,32,128,1]{3,2,0,1,4:T(8,128)(2,1)} %maximum_bitcast_fusion.2), kind=kOutput, calls=%fused_computation.26 | convolution fusion | flops 8053063680 | bytes 55017472 | tf_op jit(solution)/shard_map/lecb,slbd->sdce/dot_general | solution.py:95
  155.1 8.6 fusion.57
  163.7 24.4 %slice_convert_fusion.3 = (s32[1,128,32,512]{1,3,0,2:T(8,128)}, s32[1,128,32,512]{1,3,0,2:T(8,128)}, s32[1,128,32,512]{1,3,0,2:T(8,128)}, s32[1,128,32,512]{1,3,0,2:T(8,128)}) fusion(f32[5,128,32,512]{1,3,0,2:T(8,128)} %convolution_bitcast_fusion.1), kind=kLoop, calls=%fused_computation.114 | loop fusion | flops 8388608 | bytes 67108864 | tf_op jit(solution)/shard_map/convert_element_type | solution.py:101
  188.1 19.8 %copy.141 = s32[1,128,32,512]{2,1,3,0:T(8,128)} copy(s32[1,128,32,512]{1,3,0,2:T(8,128)} %get-tuple-element.11) | data formatting | bytes 16777216 | tf_op jit(solution)/shard_map/convert_element_type | solution.py:101
  207.8 24.7 %convert_element_type.500 = s32[4096,64,8]{0,2,1:T(8,128)} reshape(s32[1,128,32,512]{2,1,3,0:T(8,128)} %copy.141) | data formatting | bytes 16777216 | tf_op jit(solution)/shard_map/convert_element_type | solution.py:101
  232.5 19.7 %copy.140 = s32[1,128,32,512]{2,1,3,0:T(8,128)} copy(s32[1,128,32,512]{1,3,0,2:T(8,128)} %fusion.57) | data formatting | bytes 16777216 | tf_op jit(solution)/shard_map/jit(remainder)/rem | solution.py:70
  252.3 24.5 %rem.1099 = s32[4096,64,8]{0,2,1:T(8,128)} reshape(s32[1,128,32,512]{2,1,3,0:T(8,128)} %copy.140) | data formatting | bytes 16777216 | tf_op jit(solution)/shard_map/jit(remainder)/rem | solution.py:70
  276.8 19.7 %copy.144 = s32[1,128,32,512]{2,1,3,0:T(8,128)} copy(s32[1,128,32,512]{1,3,0,2:T(8,128)} %get-tuple-element.12) | data formatting | bytes 16777216 | tf_op jit(solution)/shard_map/convert_element_type | solution.py:101
  296.6 24.5 %convert_element_type.506 = s32[4096,64,8]{0,2,1:T(8,128)} reshape(s32[1,128,32,512]{2,1,3,0:T(8,128)} %copy.144) | data formatting | bytes 16777216 | tf_op jit(solution)/shard_map/convert_element_type | solution.py:101
  321.1 19.7 %copy.143 = s32[1,128,32,512]{2,1,3,0:T(8,128)} copy(s32[1,128,32,512]{1,3,0,2:T(8,128)} %get-tuple-element.13) | data formatting | bytes 16777216 | tf_op jit(solution)/shard_map/convert_element_type | solution.py:101
  340.8 24.5 %convert_element_type.504 = s32[4096,64,8]{0,2,1:T(8,128)} reshape(s32[1,128,32,512]{2,1,3,0:T(8,128)} %copy.143) | data formatting | bytes 16777216 | tf_op jit(solution)/shard_map/convert_element_type | solution.py:101
  365.3 19.7 %copy.142 = s32[1,128,32,512]{2,1,3,0:T(8,128)} copy(s32[1,128,32,512]{1,3,0,2:T(8,128)} %get-tuple-element.14) | data formatting | bytes 16777216 | tf_op jit(solution)/shard_map/convert_element_type | solution.py:101
  385.1 24.5 %convert_element_type.502 = s32[4096,64,8]{0,2,1:T(8,128)} reshape(s32[1,128,32,512]{2,1,3,0:T(8,128)} %copy.142) | data formatting | bytes 16777216 | tf_op jit(solution)/shard_map/convert_element_type | solution.py:101
  409.6 23.2 %fusion.56 = f32[4096,64,8]{0,2,1:T(8,128)} fusion(s32[4096,64,8]{0,2,1:T(8,128)} %convert_element_type.506, s32[4096,64,8]{0,2,1:T(8,128)} %convert_element_type.504, s32[4096,64,8]{0,2,1:T(8,128)} %convert_element_type.502, s32[4096,64,8]{0,2,1:T(8,128)} %convert_element_type.500, s32[4096,64,8]{0,2,1:T(8,128)} %rem.1099), kind=kLoop, calls=%fused_computation.110 | loop fusion | flops 79691776 | bytes 50331648 | tf_op jit(solution)/shard_map/convert_element_type | solution.py:151
  432.8 13.4 %copy.145 = f32[4096,64,8]{1,2,0:T(8,128)} copy(f32[4096,64,8]{0,2,1:T(8,128)} %fusion.56) | data formatting | bytes 16777216 | tf_op jit(solution)/shard_map/convert_element_type | solution.py:151
  446.1 18.5 %reshape.789 = f32[16,1,131072]{2,1,0:T(1,128)} reshape(f32[4096,8,64]{2,1,0:T(8,128)} %bitcast.355) | data formatting | bytes 16777216
  464.6 190.4 %all_to_all.36 = f32[16,1,131072]{2,1,0:T(1,128)} all-to-all(f32[16,1,131072]{2,1,0:T(1,128)} %reshape.789), channel_id=1, replica_groups=mesh['grp'=2,'pt'=16] {'pt'}, dimensions={0} | all-to-all | bytes 16777216 | tf_op jit(solution)/shard_map/all_to_all | solution.py:154
  655.5 25.2 %reduce = f32[16,131072]{1,0:T(8,128)} reduce(f32[16,1,131072]{2,1,0:T(1,128)} %all_to_all.36, f32[]{:T(128)} %broadcast.1876), dimensions={1}, to_apply=%all_to_all.12.reduce_sub_computation | reduce | bytes 16777220 | tf_op jit(solution)/shard_map/all_to_all | solution.py:154
  680.7 17.4 %reshape.790 = f32[4096,8,64]{2,1,0:T(8,128)} reshape(f32[16,131072]{1,0:T(8,128)} %reduce) | data formatting | bytes 16777216
  698.1 13.8 %copy.147 = f32[256,64,16,8]{0,3,2,1:T(8,128)} copy(f32[256,64,16,8]{1,3,0,2:T(8,128)} %bitcast.356) | data formatting | bytes 16777216 | tf_op jit(solution)/shard_map/all_to_all | solution.py:154
  711.9 8.7 copy.148
  723.7 9.1 fusion.121
  743.5 3.7 convert_element_type.526
  751.7 3.5 rem.1201
  757.8 3.5 convert_element_type.532
  761.3 3.6 copy.154
  764.9 4.3 convert_element_type.530
  769.2 3.6 copy.153
  772.8 4.3 convert_element_type.528
  777.1 5.1 fusion.138
  782.2 9.5 copy.156
  791.7 12.1 %reshape.791 = f32[16,1,16384]{2,1,0:T(1,128)S(1)} reshape(f32[4096,8,8]{2,1,0:T(8,128)} %copy.156) | data formatting | bytes 2097152
  803.9 30.5 %all_to_all.37 = f32[16,1,16384]{2,1,0:T(1,128)S(1)} all-to-all(f32[16,1,16384]{2,1,0:T(1,128)S(1)} %reshape.791), channel_id=1, replica_groups=mesh['grp'=2,'pt'=16] {'pt'}, dimensions={0} | all-to-all | bytes 2097152 | tf_op jit(solution)/shard_map/all_to_all | solution.py:153
  834.3 3.1 reduce.1
  837.5 15.6 %reshape.792 = f32[4096,8,8]{2,1,0:T(8,128)} reshape(f32[16,16384]{1,0:T(8,128)S(1)} %reduce.1) | data formatting | bytes 2097152
  853.1 9.6 copy.157
  866.0 53.8 %all-gather.2.cloned.1.call-done = f32[256,128,128]{2,1,0:T(8,128)} async-done(((f32[256,64,128]{2,1,0:T(8,128)}), f32[256,128,128]{2,1,0:T(8,128)}) %all-gather.2.cloned.1.call-update) | async-done | bytes 16777232 | tf_op jit(solution)/shard_map/all_gather | solution.py:156
  919.8 36.0 %fusion.63 = (bf16[1,256,128,128]{3,2,0,1:T(8,128)(2,1)}, bf16[1,256,128,128]{3,2,0,1:T(8,128)(2,1)}, bf16[1,256,128,128]{3,2,0,1:T(8,128)(2,1)}) fusion(f32[256,128,128]{2,1,0:T(8,128)} %all-gather.2.cloned.1.call-done), kind=kLoop, calls=%fused_computation.130 | loop fusion | flops 184549376 | bytes 41943040 | tf_op jit(solution)/shard_map/stack | solution.py:91
  955.7 17.0 %fusion.80 = f32[3,3,256,8,128]{4,3,0,1,2:T(8,128)} fusion(bf16[1,256,128,128]{3,2,0,1:T(8,128)(2,1)} %get-tuple-element.16, bf16[1,256,128,128]{3,2,0,1:T(8,128)(2,1)} %get-tuple-element.17, bf16[1,256,128,128]{3,2,0,1:T(8,128)(2,1)} %get-tuple-element.15, bf16[1,256,8,128]{3,2,0,1:T(8,128)(2,1)S(1)} %get-tuple-element.37, ...), kind=kOutput, calls=%fused_computation.162 | convolution fusion | flops 684195840 | bytes 36175872 | tf_op jit(solution)/shard_map/xpik,ypjk->xypij/dot_general | solution.py:125
  972.7 6.2 fusion.156
  979.5 31.4 %all_to_all.38 = f32[256,8,128]{0,1,2:T(8,128)S(1)} all-to-all(f32[256,8,128]{0,1,2:T(8,128)S(1)} %copy.171), channel_id=1, replica_groups=mesh['grp'=2,'pt'=16] {'pt'}, dimensions={2} | all-to-all | bytes 2097152 | tf_op jit(solution)/shard_map/all_to_all | solution.py:158
  1020.6 8.9 fusion.188
  1041.8 4.9 fusion.206
  (72 shorter events, 50.5 us)
Async XLA Ops:
  6.5 913.2 %all-gather.2.cloned.1.call-start = ((), (), s32[]{:S(2)}) async-start(), calls=%async_computation.3 | async-start | bytes 25165824 | tf_op jit(solution)/shard_map/all_gather | solution.py:156
  9.2 9.3 copy-start.5
  18.5 17.5 %copy-start.8 = (s32[32,128]{1,0:T(8,128)S(1)}, s32[32,128]{1,0:T(8,128)}, u32[]{:S(2)}) copy-start(s32[32,128]{1,0:T(8,128)} %constant.633) | copy-start | bytes 49156
  18.5 17.5 %copy-start.10 = (s32[32,128]{1,0:T(8,128)S(1)}, s32[32,128]{1,0:T(8,128)}, u32[]{:S(2)}) copy-start(s32[32,128]{1,0:T(8,128)} %constant.629) | copy-start | bytes 49156
  18.5 17.5 %copy-start.12 = (s32[32,128]{1,0:T(8,128)S(1)}, s32[32,128]{1,0:T(8,128)}, u32[]{:S(2)}) copy-start(s32[32,128]{1,0:T(8,128)} %constant.608) | copy-start | bytes 49156
  120.5 5.6 copy-start.1
  720.7 1.0 copy-start.3
  720.7 2.1 copy-start.6
  720.7 3.0 copy-start.9
  720.7 3.0 copy-start.11
  720.7 3.0 copy-start.13
  721.8 12.6 %copy-start.2 = (bf16[5,3,128,128,1]{3,2,1,0,4:T(8,128)(2,1)S(1)}, bf16[5,3,128,128,1]{3,2,1,0,4:T(8,128)(2,1)}, u32[]{:S(2)}) copy-start(bf16[5,3,128,128,1]{3,2,1,0,4:T(8,128)(2,1)} %constant.675) | copy-start | bytes 1474564
  736.1 2.5 copy-start
  1010.9 8.1 copy-start.4
  1014.0 6.7 copy-start.14
  1014.0 6.7 copy-start.15
  1014.0 6.7 copy-start.16
  1018.9 12.5 %copy-start.7 = (bf16[5,3,32,32,1]{2,3,1,0,4:T(8,128)(2,1)S(1)}, bf16[5,3,32,32,1]{2,3,1,0,4:T(8,128)(2,1)}, u32[]{:S(2)}) copy-start(bf16[5,3,32,32,1]{2,3,1,0,4:T(8,128)(2,1)} %constant.677) | copy-start | bytes 92164
Sparse Core Ops, SparseCore 0:
  720.8 198.8 all-gather.1
where the time goes:
time: 1070 us; the launch traced here: 1050 us
  local copies, waits for them, and re-layouts  394 us (37%)
  other arithmetic  270 us (25%)
  blocking collectives  252 us (24%)
  matrix products  69.1 us (6%)
  waiting for transfers between devices  53.8 us (5%)
  between operations  14 us (1%)
    convert_element_type x20, local copies, waits for them, and re-layouts, contract(): planes[limb_level].astype(jnp.int32)  212 us
    all_to_all x1, blocking collectives, body(): lax.all_to_all(right_send, 'pt', split_axis=0, concat_axis=2, tiled=True)  190 us
    convert_element_type x10, other arithmetic, limb_stack(): piece.astype(jnp.bfloat16)  119 us
    unnamed x41, local copies, waits for them, and re-layouts  68.6 us
    all_gather x1, waiting for transfers between devices, body(): right_whole = lax.all_gather(right_owned, 'grp', axis=1, tiled=True)  53.8 us
    dot_general x6, matrix products, contract(): jnp.einsum(form, limb_stack(values), jnp.asarray(stacked_table(table_np),...  52.1 us
    rem x5, local copies, waits for them, and re-layouts, fold_sums(): result = level_sums[4] % modulus  50.7 us
    another operation x3, other arithmetic, limb_stack(): jnp.stack([piece.astype(jnp.bfloat16) for piece in limb_split(values)])  41.7 us
  transfers between devices with their start and end apart: 1, of which 1 were waited for; matrix products, arithmetic and copies ran while one was open for 11% of the time, Pallas kernels for 0%

commit v1 on v0

v1 whole, which is shorter than its diff:
```python
import jax
import jax.numpy as jnp
import numpy as np
from jax import lax
from jax.sharding import PartitionSpec as P

FIRST = 32
SECOND = 128
HALF_FIRST = FIRST // 2
LENGTH = FIRST * SECOND

modulus = 7340033
INV_P = float(np.float32(1.0 / modulus))


def root_powers(length_all):
    for generator in range(2, 64):
        candidate = pow(generator, (modulus - 1) // length_all, modulus)
        if pow(candidate, length_all // 2, modulus) == modulus - 1:
            break
    powers = [1]
    for counter in range(length_all - 1):
        powers.append(powers[-1] * candidate % modulus)
    return np.array(powers, dtype=np.int64)


def balanced_limbs(values):
    v = np.asarray(values, dtype=np.int64)
    l0 = (v + 128) % 256 - 128
    v = (v - l0) // 256
    l1 = (v + 128) % 256 - 128
    l2 = (v - l1) // 256
    return [l0, l1, l2]


def scaled_stack(table):
    n, k = table.shape
    out = np.zeros((3, n, 3, k), dtype=np.float32)
    for level in range(3):
        scaled = table * pow(256, level, modulus) % modulus
        for limb, piece in enumerate(balanced_limbs(scaled)):
            out[limb, :, level, :] = piece
    return out.reshape(3 * n, 3 * k)


def twist_stack(table):
    out = np.zeros((3, 3) + table.shape, dtype=np.float32)
    for level in range(3):
        scaled = table * pow(256, level, modulus) % modulus
        for limb, piece in enumerate(balanced_limbs(scaled)):
            out[level, limb] = piece
    return out


def build_tables():
    powers = root_powers(LENGTH)

    def pw(e):
        return powers[np.asarray(e) % LENGTH]

    a16 = np.arange(HALF_FIRST)
    c32 = np.arange(FIRST)
    b128 = np.arange(SECOND)
    scale_inv = pow(LENGTH, modulus - 2, modulus)
    fwd1 = pw(SECOND * np.outer(c32, a16))
    fwd_twist = pw(np.outer(c32, b128))
    fwd2 = pw(FIRST * np.outer(b128, b128))
    inv1 = pw(-FIRST * np.outer(b128, b128))
    inv_twist = pw(-np.outer(c32, b128))
    inv2 = pw(-SECOND * np.outer(c32, c32)) * scale_inv % modulus
    return dict(
        fwd1=scaled_stack(fwd1),
        fwd_twist=twist_stack(fwd_twist),
        fwd2=scaled_stack(fwd2).T.copy(),
        inv1=scaled_stack(inv1).T.copy(),
        inv_twist=twist_stack(inv_twist),
        inv2=scaled_stack(inv2),
    )


def split3(x):
    h = jnp.floor(x * (1.0 / 256.0))
    x0 = x - 256.0 * h
    x2 = jnp.floor(h * (1.0 / 256.0))
    x1 = h - 256.0 * x2
    return x0, x1, x2


def fold3(s0, s1, s2):
    f = s2 * 65536.0 + s1 * 256.0 + s0
    q = jnp.round(f * INV_P)
    d = s2 - 112.0 * q
    e = s1 + 256.0 * d
    r = s0 + 256.0 * e - q
    return jnp.where(r < 0, r + float(modulus), r)


def twist(z, tw):
    zl = split3(z)
    s = [zl[0] * tw[0, u] + zl[1] * tw[1, u] + zl[2] * tw[2, u] for u in range(3)]
    return fold3(*s)


def limbs_bf16(x, axis):
    return jnp.concatenate([piece.astype(jnp.bfloat16) for piece in split3(x)], axis=axis)


def forward(x, tables):
    entries = x.shape[0]
    x = x.reshape(entries, HALF_FIRST, SECOND)
    xl = limbs_bf16(x, 1)
    y = jnp.einsum(
        "eLb,NL->eNb", xl, jnp.asarray(tables["fwd1"], jnp.bfloat16), preferred_element_type=jnp.float32
    )
    z = fold3(y[:, 0:FIRST], y[:, FIRST : 2 * FIRST], y[:, 2 * FIRST :])
    z = twist(z, jnp.asarray(tables["fwd_twist"]))
    zl = limbs_bf16(z, 2)
    y2 = jnp.einsum(
        "ecK,KN->ecN", zl, jnp.asarray(tables["fwd2"], jnp.bfloat16), preferred_element_type=jnp.float32
    )
    return fold3(y2[..., 0:SECOND], y2[..., SECOND : 2 * SECOND], y2[..., 2 * SECOND :])


def inverse(pv, tables):
    entries = pv.shape[0]
    pl_ = limbs_bf16(pv, 2)
    y = jnp.einsum(
        "ecK,KN->ecN", pl_, jnp.asarray(tables["inv1"], jnp.bfloat16), preferred_element_type=jnp.float32
    )
    z = fold3(y[..., 0:SECOND], y[..., SECOND : 2 * SECOND], y[..., 2 * SECOND :])
    z = twist(z, jnp.asarray(tables["inv_twist"]))
    zl = limbs_bf16(z, 1)
    y2 = jnp.einsum(
        "eLb,NL->eNb", zl, jnp.asarray(tables["inv2"], jnp.bfloat16), preferred_element_type=jnp.float32
    )
    out = fold3(y2[:, 0:FIRST], y2[:, FIRST : 2 * FIRST], y2[:, 2 * FIRST :])
    return out.reshape(entries, LENGTH)


def multiply_points(left, right):
    ll = jnp.stack([v.astype(jnp.bfloat16) for v in split3(left)])
    rl = jnp.stack([v.astype(jnp.bfloat16) for v in split3(right)])
    planes = jnp.einsum("xpik,ypjk->xypij", ll, rl, preferred_element_type=jnp.float32)
    lv0 = planes[0, 0]
    lv1 = planes[0, 1] + planes[1, 0]
    lv2 = planes[0, 2] + planes[1, 1] + planes[2, 0]
    lv3 = planes[1, 2] + planes[2, 1]
    lv4 = planes[2, 2]
    high = fold3(lv2, lv3, lv4)
    return fold3(lv0, lv1, high)


def make_body(n_grp, n_pt):
    tables = build_tables()
    d_local = SECOND // n_pt
    half = n_pt // n_grp

    def body(left_factor, right_factor):
        il, kl, _ = left_factor.shape
        jl = right_factor.shape[0]
        left_eval = forward(left_factor.reshape(il * kl, -1), tables)
        right_eval = forward(right_factor.reshape(jl * kl, -1), tables)

        def to_points(ev, rows):
            ev = ev.reshape(rows, kl, FIRST, n_pt, d_local)
            ev = jnp.transpose(ev, (3, 2, 4, 0, 1))
            ev = lax.all_to_all(ev, "pt", split_axis=0, concat_axis=4, tiled=True)
            return ev.reshape(FIRST * d_local, rows, n_pt * kl)

        left_pts = to_points(left_eval, il)
        left_pts = lax.all_gather(left_pts, "grp", axis=1, tiled=True)
        right_pts = to_points(right_eval, jl)
        prod = multiply_points(left_pts, right_pts)
        n_i = prod.shape[1]
        ib = n_i // n_grp
        jb = jl // half
        prod = prod.reshape(FIRST, d_local, n_grp, ib, half, jb)
        prod = jnp.transpose(prod, (2, 4, 0, 1, 3, 5))
        prod = prod.reshape(n_pt, FIRST, d_local, ib, jb)
        prod = lax.all_to_all(prod, "pt", split_axis=0, concat_axis=0, tiled=False)
        perm = []
        for h in range(n_grp):
            for q in range(n_pt):
                g_o, r = q // half, q % half
                perm.append((h * n_pt + q, g_o * n_pt + h * half + r))
        prod = lax.ppermute(prod, ("grp", "pt"), perm)
        pv = jnp.transpose(prod, (3, 4, 1, 0, 2)).reshape(ib * jb, FIRST, SECOND)
        coeffs = inverse(pv, tables)
        return (coeffs / float(modulus)).reshape(ib, jb, LENGTH)

    return body


def solution(mesh):
    n_grp = mesh.shape["grp"]
    n_pt = mesh.shape["pt"]
    return jax.shard_map(
        make_body(n_grp, n_pt),
        mesh=mesh,
        in_specs=(P("grp", "pt", None), P("grp", "pt", None)),
        out_specs=P("grp", "pt", None),
        check_vma=False,
    )
```

time: 1070 us -> 827 us (0.77)
  the two profiles are of different devices: /device:TPU:1 before, /device:TPU:3 now
where the time goes in v1:
time: 827 us; the launch traced here: 818 us
  waiting for transfers between devices  292 us (35%)
  local copies, waits for them, and re-layouts  257 us (31%)
  other arithmetic  133 us (16%)
  blocking collectives  61.5 us (7%)
  matrix products  43.7 us (5%)
  starting transfers between devices  16.2 us (2%)
  between operations  14.2 us (2%)
    ppermute x1, waiting for transfers between devices, body(): prod = lax.ppermute(prod, ('grp', 'pt'), perm)  183 us
    all_to_all x2, waiting for transfers between devices, to_points(): ev = lax.all_to_all(ev, 'pt', split_axis=0, concat_axis=4, tiled=True)  76.2 us
    all_to_all x1, blocking collectives, body(): prod = lax.all_to_all(prod, 'pt', split_axis=0, concat_axis=0, tiled=False)  61.5 us
    unnamed x58, local copies, waits for them, and re-layouts  54.4 us
    transpose x1, other arithmetic, body(): prod = jnp.transpose(prod, (2, 4, 0, 1, 3, 5))  35.7 us
    transpose x2, local copies, waits for them, and re-layouts, to_points(): ev = jnp.transpose(ev, (3, 2, 4, 0, 1))  34 us
    all_to_all x5, local copies, waits for them, and re-layouts, to_points(): ev = lax.all_to_all(ev, 'pt', split_axis=0, concat_axis=4, tiled=True)  33 us
    all_gather x1, waiting for transfers between devices, body(): left_pts = lax.all_gather(left_pts, 'grp', axis=1, tiled=True)  33 us
  transfers between devices with their start and end apart: 4, of which 3 were waited for; matrix products, arithmetic and copies ran while one was open for 21% of the time, Pallas kernels for 0%

profile of v1, /device:TPU:3, one launch (start us, length us, event | category | flops | bytes accessed | tf_op | source)
XLA Modules:
  0.0 817.6 jit_solution(14543807361729395650)
XLA Ops:
  9.2 3.0 subtract_convert_fusion.12
  14.2 2.7 copy.69
  16.9 4.8 copy.92
  21.7 4.7 reshape.125
  26.4 6.8 all-to-all-start.1
  33.2 3.1 copy.89
  38.3 10.1 %convolution_bitcast_fusion = f32[512,96,128]{2,1,0:T(8,128)} fusion(bf16[96,48,1]{0,1,2:T(8,128)(2,1)S(1)} %copy-done.12, bf16[512,16,128]{2,1,0:T(8,128)(2,1)S(1)} %get-tuple-element.23, bf16[512,16,128]{2,1,0:T(8,128)(2,1)S(1)} %get-tuple-element.22, bf16[512,16,128]{2,1,0:T(8,128)(2,1)S(1)} %get-tuple-element.21), kind=kOutput, calls=%fused_computation.18 | convolution fusion | flops 622854144 | bytes 31466496 | tf_op jit(solution)/shard_map/eLb,NL->eNb/dot_general | solution.py:112
  48.5 18.6 %subtract_convert_fusion.3 = (bf16[512,32,128]{2,1,0:T(8,128)(2,1)S(1)}, f32[512,32,128]{2,1,0:T(8,128)S(1)}) fusion(f32[32,128]{1,0:T(8,128)S(1)} %copy-done.3, f32[32,128]{1,0:T(8,128)S(1)} %copy-done.4, f32[32,128]{1,0:T(8,128)S(1)} %copy-done.5, f32[32,128]{1,0:T(8,128)S(1)} %copy-done.6, f32[32,128]{1,0:T(8,128)S(1)} %copy-done.7, ...), kind=kLoop, calls=%fused_computation.28 | loop fusion | flops 125829120 | bytes 37896192 | tf_op jit(solution)/shard_map/convert_element_type | solution.py:105
  67.1 3.6 subtract_convert_fusion.2
  70.7 14.3 %fusion.1 = f32[512,32,384]{2,1,0:T(8,128)} fusion(bf16[384,384,1]{1,0,2:T(8,128)(2,1)S(1)} %copy-done.24, bf16[512,32,128]{2,1,0:T(8,128)(2,1)} %get-tuple-element.20, bf16[512,32,128]{2,1,0:T(8,128)(2,1)S(1)} %get-tuple-element.19, bf16[512,32,128]{2,1,0:T(8,128)(2,1)S(1)} %get-tuple-element.9), kind=kOutput, calls=%fused_computation.6 | convolution fusion | flops 4869586944 | bytes 38043648 | tf_op jit(solution)/shard_map/ecK,KN->ecN/dot_general | solution.py:118
  85.0 13.7 %compare_select_fusion.2 = f32[512,32,128]{2,1,0:T(8,128)} fusion(f32[512,32,384]{2,1,0:T(8,128)} %fusion.1), kind=kLoop, calls=%fused_computation.2 | loop fusion | flops 33554432 | bytes 33554432 | tf_op jit(solution)/shard_map/jit(_where)/select_n | solution.py:95
  98.6 18.9 %copy.64 = f32[512,32,128]{1,2,0:T(8,128)} copy(f32[512,32,128]{2,1,0:T(8,128)} %compare_select_fusion.2) | data formatting | bytes 16777216 | tf_op jit(solution)/shard_map/jit(_where)/select_n | solution.py:95
  117.6 29.2 %copy.65 = f32[16,32,8,64,8]{3,4,2,1,0:T(8,128)} copy(f32[16,32,8,64,8]{1,2,0,4,3:T(8,128)} %bitcast.125) | data formatting | bytes 16777216 | tf_op jit(solution)/shard_map/transpose | solution.py:166
  146.8 18.4 %reshape.123 = f32[16,1,131072]{2,1,0:T(1,128)} reshape(f32[16,32,8,8,64]{4,3,2,1,0:T(8,128)} %bitcast.126) | data formatting | bytes 16777216
  165.2 6.0 all-to-all-start
  171.8 3.1 reduce.1
  174.9 2.8 reshape.126
  177.7 4.8 bitcast_bitcast_fusion.1
  182.5 14.7 %copy.71 = f32[1,32,8,8,16,8]{5,4,3,2,1,0:T(8,128)} copy(f32[1,32,8,8,16,8]{1,2,5,3,4,0:T(8,128)} %bitcast_bitcast_fusion.1) | data formatting | bytes 2097152 | tf_op jit(solution)/shard_map/all_to_all | solution.py:167
  197.2 12.6 %reshape.114 = f32[256,8,128]{2,1,0:T(8,128)} reshape(f32[1,32,8,8,16,8]{5,4,3,2,1,0:T(8,128)} %copy.71) | data formatting | bytes 2097152 | tf_op jit(solution)/shard_map/reshape | solution.py:168
  209.9 33.0 %all-gather.2.cloned.1.call-done = f32[256,16,128]{2,1,0:T(8,128)} async-done(((f32[256,8,128]{2,1,0:T(8,128)}), f32[256,16,128]{2,1,0:T(8,128)}) %all-gather.2.cloned.1.call-update) | async-done | bytes 2097168 | tf_op jit(solution)/shard_map/all_gather | solution.py:171
  242.8 3.3 fusion.45
  246.1 76.2 %all-to-all-done = f32[16,1,131072]{2,1,0:T(1,128)} async-done(((f32[16,1,131072]{2,1,0:T(1,128)}), f32[16,1,131072]{2,1,0:T(1,128)}, u32[]{:S(2)}, u32[]{:S(2)}) %all-to-all-start) | async-done | bytes 8388640 | tf_op jit(solution)/shard_map/all_to_all | solution.py:167
  322.3 25.1 %reduce = f32[16,131072]{1,0:T(8,128)} reduce(f32[16,1,131072]{2,1,0:T(1,128)} %all-to-all-done, f32[]{:T(128)} %broadcast.278), dimensions={1}, to_apply=%all_to_all.25.reduce_sub_computation | reduce | bytes 16777220 | tf_op jit(solution)/shard_map/all_to_all | solution.py:167
  347.4 17.5 %reshape.124 = f32[16,32,8,8,64]{4,3,2,1,0:T(8,128)} reshape(f32[16,131072]{1,0:T(8,128)} %reduce) | data formatting | bytes 16777216
  364.9 6.5 bitcast_bitcast_fusion
  371.5 6.4 copy.66
  377.9 12.8 %copy.68 = f32[1,256,64,128]{3,2,0,1:T(8,128)} copy(f32[1,256,64,128]{2,3,1,0:T(8,128)} %bitcast.127) | data formatting | bytes 16777216 | tf_op jit(solution)/shard_map/reshape | solution.py:168
  390.7 7.4 subtract_convert_fusion.1
  398.1 15.2 %fusion.12 = f32[3,3,256,16,64]{4,3,0,1,2:T(8,128)} fusion(bf16[1,256,64,128]{3,2,0,1:T(8,128)(2,1)} %get-tuple-element.18, bf16[1,256,64,128]{3,2,0,1:T(8,128)(2,1)} %get-tuple-element.17, bf16[1,256,64,128]{3,2,0,1:T(8,128)(2,1)S(1)} %get-tuple-element.16, bf16[1,256,16,128]{3,2,0,1:T(8,128)(2,1)} %get-tuple-element.26, ...), kind=kOutput, calls=%fused_computation.19 | convolution fusion | flops 651165696 | bytes 25165824 | tf_op jit(solution)/shard_map/xpik,ypjk->xypij/dot_general | solution.py:143
  413.2 10.5 %fusion.67 = (f32[1,1,256,16,64]{4,3,0,1,2:T(8,128)}, f32[1,1,256,16,64]{4,3,0,1,2:T(8,128)}, f32[1,1,256,16,64]{4,3,0,1,2:T(8,128)}, f32[1,1,256,16,64]{4,3,0,1,2:T(8,128)}, f32[1,1,256,16,64]{4,3,0,1,2:T(8,128)S(1)}) fusion(f32[3,3,256,16,64]{4,3,0,1,2:T(8,128)} %fusion.12), kind=kLoop, calls=%fused_computation.119 | loop fusion | flops 1048576 | bytes 14680064 | tf_op jit(solution)/shard_map/slice | solution.py:148
  426.2 3.5 copy.77
  429.7 3.5 copy.75
  433.2 3.5 copy.76
  438.6 12.1 %squeeze.4 = f32[32,8,2,8,8,8]{1,0,5,4,3,2:T(8,128)} reshape(f32[1,1,256,16,64]{2,4,3,1,0:T(8,128)} %copy.74) | data formatting | bytes 2097152 | tf_op jit(solution)/shard_map/squeeze | solution.py:144
  450.8 11.4 %add.301 = f32[32,8,2,8,8,8]{1,0,5,4,3,2:T(8,128)} reshape(f32[1,1,256,16,64]{2,4,3,1,0:T(8,128)S(1)} %copy-done.2) | data formatting | bytes 2097152 | tf_op jit(solution)/shard_map/add | solution.py:146
  462.2 11.1 %add.298 = f32[32,8,2,8,8,8]{1,0,5,4,3,2:T(8,128)} reshape(f32[1,1,256,16,64]{2,4,3,1,0:T(8,128)S(1)} %copy-done.1) | data formatting | bytes 2097152 | tf_op jit(solution)/shard_map/add | solution.py:145
  473.3 11.1 %add.303 = f32[32,8,2,8,8,8]{1,0,5,4,3,2:T(8,128)} reshape(f32[1,1,256,16,64]{2,4,3,1,0:T(8,128)S(1)} %copy-done) | data formatting | bytes 2097152 | tf_op jit(solution)/shard_map/add | solution.py:147
  484.4 11.2 %squeeze.5 = f32[32,8,2,8,8,8]{1,0,5,4,3,2:T(8,128)} reshape(f32[1,1,256,16,64]{2,4,3,1,0:T(8,128)S(1)} %copy.78) | data formatting | bytes 2097152 | tf_op jit(solution)/shard_map/squeeze | solution.py:148
  495.6 35.7 %fusion = f32[2,8,32,8,8,8]{3,2,5,1,4,0:T(8,128)} fusion(f32[32,8,2,8,8,8]{1,0,5,4,3,2:T(8,128)} %squeeze.4, f32[32,8,2,8,8,8]{1,0,5,4,3,2:T(8,128)} %add.298, f32[32,8,2,8,8,8]{1,0,5,4,3,2:T(8,128)} %add.301, f32[32,8,2,8,8,8]{1,0,5,4,3,2:T(8,128)} %add.303, f32[32,8,2,8,8,8]{1,0,5,4,3,2:T(8,128)} %squeeze.5), kind=kLoop, calls=%fused_computation.5 | loop fusion | flops 8388608 | bytes 6291456 | tf_op jit(solution)/shard_map/transpose | solution.py:178
  531.2 11.5 %copy.79 = f32[2,8,32,8,8,8]{2,5,4,3,1,0:T(8,128)} copy(f32[2,8,32,8,8,8]{3,2,5,1,4,0:T(8,128)} %fusion) | data formatting | bytes 2097152 | tf_op jit(solution)/shard_map/transpose | solution.py:178
  542.7 3.9 reshape.127
  546.6 61.5 %all_to_all.35 = f32[16,1,16384]{2,1,0:T(1,128)S(1)} all-to-all(f32[16,1,16384]{2,1,0:T(1,128)S(1)} %reshape.127), channel_id=1, replica_groups=mesh['grp'=2,'pt'=16] {'pt'}, dimensions={0} | all-to-all | bytes 2097152 | tf_op jit(solution)/shard_map/all_to_all | solution.py:180
  608.2 3.1 reduce.2
  611.4 2.7 reshape.128
  614.1 3.4 collective-permute-start
  617.5 182.9 %collective-permute-done = f32[16,32,8,8,8]{1,4,3,2,0:T(8,128)} collective-permute-done((f32[16,32,8,8,8]{1,4,3,2,0:T(8,128)}, f32[16,32,8,8,8]{1,4,3,2,0:T(8,128)}, u32[]{:S(2)}, u32[]{:S(2)}) %collective-permute-start) | collective-permute-done | bytes 1048608 | tf_op jit(solution)/shard_map/ppermute | solution.py:186
  800.4 3.7 copy.82
  (70 shorter events, 17.9 us)
Async XLA Ops:
  6.5 6.0 copy-start.24
  26.4 138.8 %all-to-all-start.1 = ((f32[16,1,16384]{2,1,0:T(1,128)}), f32[16,1,16384]{2,1,0:T(1,128)S(1)}, u32[]{:S(2)}, u32[]{:S(2)}) async-start(f32[16,1,16384]{2,1,0:T(1,128)} %reshape.125), calls=%async_computation.1 | async-start | bytes 2097152 | tf_op jit(solution)/shard_map/all_to_all | solution.py:167
  33.2 5.0 copy-start.12
  38.1 10.2 %copy-start.3 = (f32[32,128]{1,0:T(8,128)S(1)}, f32[32,128]{1,0:T(8,128)}, u32[]{:S(2)}) copy-start(f32[32,128]{1,0:T(8,128)} %constant.74) | copy-start | bytes 49156
  38.2 10.2 %copy-start.4 = (f32[32,128]{1,0:T(8,128)S(1)}, f32[32,128]{1,0:T(8,128)}, u32[]{:S(2)}) copy-start(f32[32,128]{1,0:T(8,128)} %constant.72) | copy-start | bytes 49156
  38.2 10.2 %copy-start.5 = (f32[32,128]{1,0:T(8,128)S(1)}, f32[32,128]{1,0:T(8,128)}, u32[]{:S(2)}) copy-start(f32[32,128]{1,0:T(8,128)} %constant.70) | copy-start | bytes 49156
  38.2 10.2 %copy-start.6 = (f32[32,128]{1,0:T(8,128)S(1)}, f32[32,128]{1,0:T(8,128)}, u32[]{:S(2)}) copy-start(f32[32,128]{1,0:T(8,128)} %constant.33) | copy-start | bytes 49156
  38.2 10.2 %copy-start.7 = (f32[32,128]{1,0:T(8,128)S(1)}, f32[32,128]{1,0:T(8,128)}, u32[]{:S(2)}) copy-start(f32[32,128]{1,0:T(8,128)} %constant.31) | copy-start | bytes 49156
  38.2 10.2 %copy-start.8 = (f32[32,128]{1,0:T(8,128)S(1)}, f32[32,128]{1,0:T(8,128)}, u32[]{:S(2)}) copy-start(f32[32,128]{1,0:T(8,128)} %constant.29) | copy-start | bytes 49156
  38.2 10.2 %copy-start.9 = (f32[32,128]{1,0:T(8,128)S(1)}, f32[32,128]{1,0:T(8,128)}, u32[]{:S(2)}) copy-start(f32[32,128]{1,0:T(8,128)} %constant.27) | copy-start | bytes 49156
  38.2 10.2 %copy-start.10 = (f32[32,128]{1,0:T(8,128)S(1)}, f32[32,128]{1,0:T(8,128)}, u32[]{:S(2)}) copy-start(f32[32,128]{1,0:T(8,128)} %constant.12) | copy-start | bytes 49156
  38.2 10.2 %copy-start.11 = (f32[32,128]{1,0:T(8,128)S(1)}, f32[32,128]{1,0:T(8,128)}, u32[]{:S(2)}) copy-start(f32[32,128]{1,0:T(8,128)} %constant.10) | copy-start | bytes 49156
  165.2 157.1 %all-to-all-start = ((f32[16,1,131072]{2,1,0:T(1,128)}), f32[16,1,131072]{2,1,0:T(1,128)}, u32[]{:S(2)}, u32[]{:S(2)}) async-start(f32[16,1,131072]{2,1,0:T(1,128)} %reshape.123), calls=%async_computation | async-start | bytes 16777216 | tf_op jit(solution)/shard_map/all_to_all | solution.py:167
  171.2 71.6 %all-gather.2.cloned.1.call-start = ((), (), s32[]{:S(2)}) async-start(), calls=%async_computation.3 | async-start | bytes 3145728 | tf_op jit(solution)/shard_map/all_gather | solution.py:171
  438.6 12.2 %copy-start.2 = (f32[1,1,256,16,64]{2,4,3,1,0:T(8,128)S(1)}, f32[1,1,256,16,64]{2,4,3,1,0:T(8,128)}, u32[]{:S(2)}) copy-start(f32[1,1,256,16,64]{2,4,3,1,0:T(8,128)} %copy.76) | copy-start | bytes 3145732
  450.8 11.4 %copy-start.1 = (f32[1,1,256,16,64]{2,4,3,1,0:T(8,128)S(1)}, f32[1,1,256,16,64]{2,4,3,1,0:T(8,128)}, u32[]{:S(2)}) copy-start(f32[1,1,256,16,64]{2,4,3,1,0:T(8,128)} %copy.75) | copy-start | bytes 3145732
  462.2 11.1 %copy-start = (f32[1,1,256,16,64]{2,4,3,1,0:T(8,128)S(1)}, f32[1,1,256,16,64]{2,4,3,1,0:T(8,128)}, u32[]{:S(2)}) copy-start(f32[1,1,256,16,64]{2,4,3,1,0:T(8,128)} %copy.77) | copy-start | bytes 3145732
  546.6 257.9 %copy-start.23 = (bf16[384,384,1]{1,0,2:T(8,128)(2,1)S(1)}, bf16[384,384,1]{1,0,2:T(8,128)(2,1)}, u32[]{:S(2)}) copy-start(bf16[384,384,1]{1,0,2:T(8,128)(2,1)} %constant.95) | copy-start | bytes 884740
  611.3 194.4 %copy-start.14 = (f32[32,128]{1,0:T(8,128)S(1)}, f32[32,128]{1,0:T(8,128)}, u32[]{:S(2)}) copy-start(f32[32,128]{1,0:T(8,128)} %constant.92) | copy-start | bytes 49156
  611.3 194.4 %copy-start.15 = (f32[32,128]{1,0:T(8,128)S(1)}, f32[32,128]{1,0:T(8,128)}, u32[]{:S(2)}) copy-start(f32[32,128]{1,0:T(8,128)} %constant.90) | copy-start | bytes 49156
  611.3 194.4 %copy-start.16 = (f32[32,128]{1,0:T(8,128)S(1)}, f32[32,128]{1,0:T(8,128)}, u32[]{:S(2)}) copy-start(f32[32,128]{1,0:T(8,128)} %constant.88) | copy-start | bytes 49156
  611.3 194.4 %copy-start.17 = (f32[32,128]{1,0:T(8,128)S(1)}, f32[32,128]{1,0:T(8,128)}, u32[]{:S(2)}) copy-start(f32[32,128]{1,0:T(8,128)} %constant.86) | copy-start | bytes 49156
  611.3 194.4 %copy-start.18 = (f32[32,128]{1,0:T(8,128)S(1)}, f32[32,128]{1,0:T(8,128)}, u32[]{:S(2)}) copy-start(f32[32,128]{1,0:T(8,128)} %constant.84) | copy-start | bytes 49156
  611.4 194.4 %copy-start.19 = (f32[32,128]{1,0:T(8,128)S(1)}, f32[32,128]{1,0:T(8,128)}, u32[]{:S(2)}) copy-start(f32[32,128]{1,0:T(8,128)} %constant.82) | copy-start | bytes 49156
  611.4 194.4 %copy-start.20 = (f32[32,128]{1,0:T(8,128)S(1)}, f32[32,128]{1,0:T(8,128)}, u32[]{:S(2)}) copy-start(f32[32,128]{1,0:T(8,128)} %constant.80) | copy-start | bytes 49156
  611.4 194.4 %copy-start.21 = (f32[32,128]{1,0:T(8,128)S(1)}, f32[32,128]{1,0:T(8,128)}, u32[]{:S(2)}) copy-start(f32[32,128]{1,0:T(8,128)} %constant.78) | copy-start | bytes 49156
  611.4 194.4 %copy-start.22 = (f32[32,128]{1,0:T(8,128)S(1)}, f32[32,128]{1,0:T(8,128)}, u32[]{:S(2)}) copy-start(f32[32,128]{1,0:T(8,128)} %constant.76) | copy-start | bytes 49156
  614.1 186.3 %collective-permute-start = (f32[16,32,8,8,8]{1,4,3,2,0:T(8,128)}, f32[16,32,8,8,8]{1,4,3,2,0:T(8,128)}, u32[]{:S(2)}, u32[]{:S(2)}) collective-permute-start(f32[16,32,8,8,8]{1,4,3,2,0:T(8,128)} %bitcast.131), channel_id=1, source_target_pairs={{0,0},{1,1},{2,2},{3,3},{4,4},{5,5},{6,6},{7,7},{8,16},{9,17},{10,... | collective-permute-start | bytes 3145736 | tf_op jit(solution)/shard_map/ppermute | solution.py:186
  804.1 4.0 copy-start.13
Sparse Core Ops, SparseCore 0:
  210.0 32.8 all-gather.1

commit v2 on v1

--- a/solution.py
+++ b/solution.py
@@ -138,22 +138,24 @@
 
 
 def multiply_points(left, right):
-    ll = jnp.stack([v.astype(jnp.bfloat16) for v in split3(left)])
-    rl = jnp.stack([v.astype(jnp.bfloat16) for v in split3(right)])
-    planes = jnp.einsum("xpik,ypjk->xypij", ll, rl, preferred_element_type=jnp.float32)
-    lv0 = planes[0, 0]
-    lv1 = planes[0, 1] + planes[1, 0]
-    lv2 = planes[0, 2] + planes[1, 1] + planes[2, 0]
-    lv3 = planes[1, 2] + planes[2, 1]
-    lv4 = planes[2, 2]
-    high = fold3(lv2, lv3, lv4)
-    return fold3(lv0, lv1, high)
+    left_limbs = [v.astype(jnp.bfloat16) for v in split3(left)]
+    zero = jnp.zeros_like(left_limbs[0])
+    rows = []
+    for level in range(5):
+        pieces = [left_limbs[level - y] if 0 <= level - y < 3 else zero for y in range(3)]
+        rows.append(jnp.concatenate(pieces, axis=2))
+    toeplitz = jnp.concatenate(rows, axis=1)
+    right_limbs = limbs_bf16(right, 2)
+    levels = jnp.einsum("pak,pjk->paj", toeplitz, right_limbs, preferred_element_type=jnp.float32)
+    n_i = left.shape[1]
+    lv = [levels[:, n * n_i : (n + 1) * n_i] for n in range(5)]
+    high = fold3(lv[2], lv[3], lv[4])
+    return fold3(lv[0], lv[1], high)
 
 
 def make_body(n_grp, n_pt):
     tables = build_tables()
     d_local = SECOND // n_pt
-    half = n_pt // n_grp
 
     def body(left_factor, right_factor):
         il, kl, _ = left_factor.shape
@@ -168,22 +170,19 @@
             return ev.reshape(FIRST * d_local, rows, n_pt * kl)
 
         left_pts = to_points(left_eval, il)
-        left_pts = lax.all_gather(left_pts, "grp", axis=1, tiled=True)
+        left_pts = jnp.broadcast_to(left_pts[None], (n_grp,) + left_pts.shape)
+        left_pts = lax.all_to_all(left_pts, "grp", split_axis=0, concat_axis=0, tiled=True)
+        left_pts = jnp.transpose(left_pts, (1, 0, 2, 3)).reshape(FIRST * d_local, n_grp * il, n_pt * kl)
         right_pts = to_points(right_eval, jl)
         prod = multiply_points(left_pts, right_pts)
         n_i = prod.shape[1]
         ib = n_i // n_grp
-        jb = jl // half
-        prod = prod.reshape(FIRST, d_local, n_grp, ib, half, jb)
-        prod = jnp.transpose(prod, (2, 4, 0, 1, 3, 5))
-        prod = prod.reshape(n_pt, FIRST, d_local, ib, jb)
+        jb = n_grp * jl // n_pt
+        prod = prod.reshape(FIRST * d_local, n_grp, ib, jl)
+        prod = lax.all_to_all(prod, "grp", split_axis=1, concat_axis=1, tiled=True)
+        prod = jnp.transpose(prod, (0, 2, 1, 3)).reshape(FIRST, d_local, ib, n_pt, jb)
+        prod = jnp.transpose(prod, (3, 0, 1, 2, 4))
         prod = lax.all_to_all(prod, "pt", split_axis=0, concat_axis=0, tiled=False)
-        perm = []
-        for h in range(n_grp):
-            for q in range(n_pt):
-                g_o, r = q // half, q % half
-                perm.append((h * n_pt + q, g_o * n_pt + h * half + r))
-        prod = lax.ppermute(prod, ("grp", "pt"), perm)
         pv = jnp.transpose(prod, (3, 4, 1, 0, 2)).reshape(ib * jb, FIRST, SECOND)
         coeffs = inverse(pv, tables)
         return (coeffs / float(modulus)).reshape(ib, jb, LENGTH)

time: 827 us -> 649 us (0.78)
  the two profiles are of different devices: /device:TPU:3 before, /device:TPU:1 now
where the time goes in v2:
time: 649 us; the launch traced here: 641 us
  local copies, waits for them, and re-layouts  271 us (42%)
  waiting for transfers between devices  139 us (21%)
  other arithmetic  92.8 us (14%)
  blocking collectives  78.6 us (12%)
  matrix products  41.5 us (6%)
  starting transfers between devices  17.7 us (3%)
    all_to_all x2, waiting for transfers between devices, to_points(): ev = lax.all_to_all(ev, 'pt', split_axis=0, concat_axis=4, tiled=True)  139 us
    unnamed x58, local copies, waits for them, and re-layouts  91.4 us
    all_to_all x1, blocking collectives, body(): prod = lax.all_to_all(prod, 'pt', split_axis=0, concat_axis=0, tiled=False)  61.9 us
    convert_element_type x10, other arithmetic, limbs_bf16(): piece.astype(jnp.bfloat16)  36.3 us
    slice x1, local copies, waits for them, and re-layouts, multiply_points(): lv = [levels[:, n * n_i:(n + 1) * n_i] for n in range(5)]  35.3 us
    transpose x2, local copies, waits for them, and re-layouts, to_points(): ev = jnp.transpose(ev, (3, 2, 4, 0, 1))  34 us
    all_to_all x5, local copies, waits for them, and re-layouts, to_points(): ev = lax.all_to_all(ev, 'pt', split_axis=0, concat_axis=4, tiled=True)  33 us
    all_to_all x2, other arithmetic, to_points(): ev = lax.all_to_all(ev, 'pt', split_axis=0, concat_axis=4, tiled=True)  28.3 us
  transfers between devices with their start and end apart: 3, of which 1 were waited for; matrix products, arithmetic and copies ran while one was open for 22% of the time, Pallas kernels for 0%

profile of v2, /device:TPU:1, one launch (start us, length us, event | category | flops | bytes accessed | tf_op | source)
XLA Modules:
  0.0 641.2 jit_solution(2827214090076393326)
XLA Ops:
  2.7 3.0 subtract_convert_fusion.11
  7.7 2.7 copy.50
  10.3 4.8 copy.93
  15.1 4.7 reshape.58
  19.8 7.6 %all-to-all-start = ((f32[16,1,16384]{2,1,0:T(1,128)}), f32[16,1,16384]{2,1,0:T(1,128)S(1)}, u32[]{:S(2)}, u32[]{:S(2)}) async-start(f32[16,1,16384]{2,1,0:T(1,128)} %reshape.58), calls=%async_computation | async-start | bytes 2097152 | tf_op jit(solution)/shard_map/all_to_all | solution.py:169
  27.5 3.1 copy.83
  32.6 10.1 %convolution_bitcast_fusion = f32[512,96,128]{2,1,0:T(8,128)} fusion(bf16[96,48,1]{0,1,2:T(8,128)(2,1)S(1)} %copy-done.9, bf16[512,16,128]{2,1,0:T(8,128)(2,1)S(1)} %get-tuple-element.23, bf16[512,16,128]{2,1,0:T(8,128)(2,1)S(1)} %get-tuple-element.22, bf16[512,16,128]{2,1,0:T(8,128)(2,1)S(1)} %get-tuple-element.21), kind=kOutput, calls=%fused_computation.15 | convolution fusion | flops 622854144 | bytes 31466496 | tf_op jit(solution)/shard_map/eLb,NL->eNb/dot_general | solution.py:112
  42.8 18.6 %subtract_convert_fusion.3 = (bf16[512,32,128]{2,1,0:T(8,128)(2,1)S(1)}, f32[512,32,128]{2,1,0:T(8,128)S(1)}) fusion(f32[32,128]{1,0:T(8,128)S(1)} %copy-done, f32[32,128]{1,0:T(8,128)S(1)} %copy-done.1, f32[32,128]{1,0:T(8,128)S(1)} %copy-done.2, f32[32,128]{1,0:T(8,128)S(1)} %copy-done.3, f32[32,128]{1,0:T(8,128)S(1)} %copy-done.4, ...), kind=kLoop, calls=%fused_computation.24 | loop fusion | flops 125829120 | bytes 37896192 | tf_op jit(solution)/shard_map/convert_element_type | solution.py:105
  61.4 3.6 subtract_convert_fusion.2
  65.0 14.5 %fusion = f32[512,32,384]{2,1,0:T(8,128)} fusion(bf16[384,384,1]{1,0,2:T(8,128)(2,1)S(1)} %copy-done.21, bf16[512,32,128]{2,1,0:T(8,128)(2,1)} %get-tuple-element.20, bf16[512,32,128]{2,1,0:T(8,128)(2,1)S(1)} %get-tuple-element.19, bf16[512,32,128]{2,1,0:T(8,128)(2,1)S(1)} %get-tuple-element.7), kind=kOutput, calls=%fused_computation.3 | convolution fusion | flops 4869586944 | bytes 38043648 | tf_op jit(solution)/shard_map/ecK,KN->ecN/dot_general | solution.py:118
  80.1 3.1 reduce
  83.3 2.7 reshape.59
  86.0 4.7 bitcast_bitcast_fusion.1
  90.7 14.8 %copy.52 = f32[1,32,8,8,16,8]{5,4,3,2,1,0:T(8,128)} copy(f32[1,32,8,8,16,8]{1,2,5,3,4,0:T(8,128)} %bitcast_bitcast_fusion.1) | data formatting | bytes 2097152 | tf_op jit(solution)/shard_map/all_to_all | solution.py:169
  105.5 11.8 %broadcast_in_dim.10 = f32[256,8,128]{2,1,0:T(8,128)S(1)} reshape(f32[1,32,8,8,16,8]{5,4,3,2,1,0:T(8,128)} %copy.52) | data formatting | bytes 2097152 | tf_op jit(solution)/shard_map/broadcast_in_dim | solution.py:173
  118.7 3.8 all-to-all-start.1
  122.4 13.7 %compare_select_fusion = f32[512,32,128]{2,1,0:T(8,128)} fusion(f32[512,32,384]{2,1,0:T(8,128)} %fusion), kind=kLoop, calls=%fused_computation | loop fusion | flops 33554432 | bytes 33554432 | tf_op jit(solution)/shard_map/jit(_where)/select_n | solution.py:95
  136.1 18.6 %copy.58 = f32[512,32,128]{1,2,0:T(8,128)} copy(f32[512,32,128]{2,1,0:T(8,128)} %compare_select_fusion) | data formatting | bytes 16777216 | tf_op jit(solution)/shard_map/jit(_where)/select_n | solution.py:95
  154.7 29.2 %copy.59 = f32[16,32,8,64,8]{3,4,2,1,0:T(8,128)} copy(f32[16,32,8,64,8]{1,2,0,4,3:T(8,128)} %bitcast.102) | data formatting | bytes 16777216 | tf_op jit(solution)/shard_map/transpose | solution.py:168
  183.9 18.5 %reshape.60 = f32[16,1,131072]{2,1,0:T(1,128)} reshape(f32[16,32,8,8,64]{4,3,2,1,0:T(8,128)} %bitcast.103) | data formatting | bytes 16777216
  202.4 6.3 all-to-all-start.2
  209.5 2.2 pad_dynamic-update-slice_fusion.1
  211.8 2.2 maximum_dynamic-update-slice_fusion.2
  214.0 2.2 maximum_dynamic-update-slice_fusion.1
  216.2 2.4 maximum_dynamic-update-slice_fusion
  220.8 138.9 %all-to-all-done.2 = f32[16,1,131072]{2,1,0:T(1,128)} async-done(((f32[16,1,131072]{2,1,0:T(1,128)}), f32[16,1,131072]{2,1,0:T(1,128)}, u32[]{:S(2)}, u32[]{:S(2)}) %all-to-all-start.2) | async-done | bytes 8388640 | tf_op jit(solution)/shard_map/all_to_all | solution.py:169
  359.6 25.1 %reduce.1 = f32[16,131072]{1,0:T(8,128)} reduce(f32[16,1,131072]{2,1,0:T(1,128)} %all-to-all-done.2, f32[]{:T(128)} %broadcast.227), dimensions={1}, to_apply=%all_to_all.35.reduce_sub_computation | reduce | bytes 16777220 | tf_op jit(solution)/shard_map/all_to_all | solution.py:169
  384.8 17.4 %reshape.61 = f32[16,32,8,8,64]{4,3,2,1,0:T(8,128)} reshape(f32[16,131072]{1,0:T(8,128)} %reduce.1) | data formatting | bytes 16777216
  402.2 6.5 %bitcast_bitcast_fusion = f32[1,32,8,64,16,8]{3,5,2,1,4,0:T(8,128)S(1)} fusion(f32[16,32,8,8,64]{4,3,2,1,0:T(8,128)} %reshape.61), kind=kLoop, calls=%fused_computation.113 | loop fusion | bytes 16777216 | tf_op jit(solution)/shard_map/all_to_all | solution.py:169
  408.8 6.4 copy.60
  415.1 12.7 %copy.62 = f32[256,64,128]{2,1,0:T(8,128)} copy(f32[256,64,128]{1,2,0:T(8,128)} %bitcast.105) | data formatting | bytes 16777216 | tf_op jit(solution)/shard_map/reshape | solution.py:170
  427.8 6.1 subtract_convert_fusion.1
  433.9 12.8 %fusion.6 = f32[256,80,64]{1,2,0:T(8,128)} fusion(bf16[256,80,384]{2,1,0:T(8,128)(2,1)} %pad_dynamic-update-slice_fusion, bf16[256,64,128]{2,1,0:T(8,128)(2,1)S(1)} %get-tuple-element.18, bf16[256,64,128]{2,1,0:T(8,128)(2,1)S(1)} %get-tuple-element.17, bf16[256,64,128]{2,1,0:T(8,128)(2,1)S(1)} %get-tuple-element.16), kind=kOutput, calls=%fused_computation.9 | convolution fusion | flops 1044381696 | bytes 33554432 | tf_op jit(solution)/shard_map/pak,pjk->paj/dot_general | solution.py:149
  446.7 35.3 %fusion.61 = (f32[256,16,64]{1,2,0:T(8,128)}, f32[256,16,64]{1,2,0:T(8,128)}, f32[256,16,64]{1,2,0:T(8,128)}, f32[256,16,64]{1,2,0:T(8,128)}, f32[256,16,64]{1,2,0:T(8,128)}) fusion(f32[256,80,64]{1,2,0:T(8,128)} %fusion.6), kind=kLoop, calls=%fused_computation.112 | loop fusion | bytes 10485760 | tf_op jit(solution)/shard_map/slice | solution.py:151
  481.9 6.6 %copy.81 = f32[256,16,64]{0,2,1:T(8,128)S(1)} copy(f32[256,16,64]{1,2,0:T(8,128)} %get-tuple-element.11) | data formatting | bytes 2097152
  488.6 6.6 %copy.80 = f32[256,16,64]{0,2,1:T(8,128)S(1)} copy(f32[256,16,64]{1,2,0:T(8,128)} %get-tuple-element.12) | data formatting | bytes 2097152
  495.2 6.6 %copy.79 = f32[256,16,64]{0,2,1:T(8,128)S(1)} copy(f32[256,16,64]{1,2,0:T(8,128)} %get-tuple-element.13) | data formatting | bytes 2097152
  501.8 7.5 %copy.78 = f32[256,16,64]{0,2,1:T(8,128)} copy(f32[256,16,64]{1,2,0:T(8,128)} %get-tuple-element.14) | data formatting | bytes 2097152
  509.3 7.4 %copy.77 = f32[256,16,64]{0,2,1:T(8,128)} copy(f32[256,16,64]{1,2,0:T(8,128)} %get-tuple-element.15) | data formatting | bytes 2097152
  516.8 2.6 compare_select_fusion.6
  519.4 16.8 %all_to_all.45 = f32[256,2,8,64]{0,3,2,1:T(8,128)S(1)} all-to-all(f32[256,2,8,64]{0,3,2,1:T(8,128)S(1)} %bitcast.112), channel_id=1, replica_groups=mesh['grp'=2,'pt'=16] {'grp'}, dimensions={1} | all-to-all | bytes 2097152 | tf_op jit(solution)/shard_map/all_to_all | solution.py:182
  536.3 11.2 %reshape.52 = f32[32,8,8,16,8]{1,0,4,3,2:T(8,128)} reshape(f32[256,8,2,64]{0,3,2,1:T(8,128)S(1)} %copy.68) | data formatting | bytes 2097152 | tf_op jit(solution)/shard_map/reshape | solution.py:183
  547.4 11.5 %copy.69 = f32[16,32,8,8,8]{1,4,3,2,0:T(8,128)} copy(f32[16,32,8,8,8]{2,1,4,0,3:T(8,128)} %bitcast.104) | data formatting | bytes 2097152 | tf_op jit(solution)/shard_map/transpose | solution.py:184
  558.9 3.9 reshape.62
  562.8 61.9 %all_to_all.46 = f32[16,1,16384]{2,1,0:T(1,128)S(1)} all-to-all(f32[16,1,16384]{2,1,0:T(1,128)S(1)} %reshape.62), channel_id=1, replica_groups=mesh['grp'=2,'pt'=16] {'pt'}, dimensions={0} | all-to-all | bytes 2097152 | tf_op jit(solution)/shard_map/all_to_all | solution.py:185
  624.7 3.1 reduce.2
  628.0 2.7 reshape.63
  630.7 3.7 copy.72
  (66 shorter events, 17.9 us)
Async XLA Ops:
  0.0 6.0 copy-start.21
  19.8 59.7 %all-to-all-start = ((f32[16,1,16384]{2,1,0:T(1,128)}), f32[16,1,16384]{2,1,0:T(1,128)S(1)}, u32[]{:S(2)}, u32[]{:S(2)}) async-start(f32[16,1,16384]{2,1,0:T(1,128)} %reshape.58), calls=%async_computation | async-start | bytes 2097152 | tf_op jit(solution)/shard_map/all_to_all | solution.py:169
  27.5 5.0 copy-start.9
  32.5 10.2 %copy-start = (f32[32,128]{1,0:T(8,128)S(1)}, f32[32,128]{1,0:T(8,128)}, u32[]{:S(2)}) copy-start(f32[32,128]{1,0:T(8,128)} %constant.81) | copy-start | bytes 49156
  32.5 10.2 %copy-start.1 = (f32[32,128]{1,0:T(8,128)S(1)}, f32[32,128]{1,0:T(8,128)}, u32[]{:S(2)}) copy-start(f32[32,128]{1,0:T(8,128)} %constant.79) | copy-start | bytes 49156
  32.5 10.2 %copy-start.2 = (f32[32,128]{1,0:T(8,128)S(1)}, f32[32,128]{1,0:T(8,128)}, u32[]{:S(2)}) copy-start(f32[32,128]{1,0:T(8,128)} %constant.77) | copy-start | bytes 49156
  32.5 10.2 %copy-start.3 = (f32[32,128]{1,0:T(8,128)S(1)}, f32[32,128]{1,0:T(8,128)}, u32[]{:S(2)}) copy-start(f32[32,128]{1,0:T(8,128)} %constant.75) | copy-start | bytes 49156
  32.5 10.2 %copy-start.4 = (f32[32,128]{1,0:T(8,128)S(1)}, f32[32,128]{1,0:T(8,128)}, u32[]{:S(2)}) copy-start(f32[32,128]{1,0:T(8,128)} %constant.36) | copy-start | bytes 49156
  32.5 10.2 %copy-start.5 = (f32[32,128]{1,0:T(8,128)S(1)}, f32[32,128]{1,0:T(8,128)}, u32[]{:S(2)}) copy-start(f32[32,128]{1,0:T(8,128)} %constant.34) | copy-start | bytes 49156
  32.5 10.2 %copy-start.6 = (f32[32,128]{1,0:T(8,128)S(1)}, f32[32,128]{1,0:T(8,128)}, u32[]{:S(2)}) copy-start(f32[32,128]{1,0:T(8,128)} %constant.32) | copy-start | bytes 49156
  32.6 10.2 %copy-start.7 = (f32[32,128]{1,0:T(8,128)S(1)}, f32[32,128]{1,0:T(8,128)}, u32[]{:S(2)}) copy-start(f32[32,128]{1,0:T(8,128)} %constant.30) | copy-start | bytes 49156
  32.6 10.2 %copy-start.8 = (f32[32,128]{1,0:T(8,128)S(1)}, f32[32,128]{1,0:T(8,128)}, u32[]{:S(2)}) copy-start(f32[32,128]{1,0:T(8,128)} %constant.28) | copy-start | bytes 49156
  118.7 83.7 %all-to-all-start.1 = ((f32[2,256,8,128]{3,2,1,0:T(8,128)}), f32[2,256,8,128]{3,2,1,0:T(8,128)S(1)}, u32[]{:S(2)}, u32[]{:S(2)}) async-start(f32[2,256,8,128]{3,2,1,0:T(8,128)} %broadcast_in_dim.11), calls=%async_computation.1 | async-start | bytes 4194304 | tf_op jit(solution)/shard_map/all_to_all | solution.py:174
  202.4 157.3 %all-to-all-start.2 = ((f32[16,1,131072]{2,1,0:T(1,128)}), f32[16,1,131072]{2,1,0:T(1,128)}, u32[]{:S(2)}, u32[]{:S(2)}) async-start(f32[16,1,131072]{2,1,0:T(1,128)} %reshape.60), calls=%async_computation.2 | async-start | bytes 16777216 | tf_op jit(solution)/shard_map/all_to_all | solution.py:169
  562.8 72.0 %copy-start.20 = (bf16[384,384,1]{1,0,2:T(8,128)(2,1)S(1)}, bf16[384,384,1]{1,0,2:T(8,128)(2,1)}, u32[]{:S(2)}) copy-start(bf16[384,384,1]{1,0,2:T(8,128)(2,1)} %constant.102) | copy-start | bytes 884740
  627.8 8.1 %copy-start.11 = (f32[32,128]{1,0:T(8,128)S(1)}, f32[32,128]{1,0:T(8,128)}, u32[]{:S(2)}) copy-start(f32[32,128]{1,0:T(8,128)} %constant.99) | copy-start | bytes 49156
  627.9 8.1 %copy-start.12 = (f32[32,128]{1,0:T(8,128)S(1)}, f32[32,128]{1,0:T(8,128)}, u32[]{:S(2)}) copy-start(f32[32,128]{1,0:T(8,128)} %constant.97) | copy-start | bytes 49156
  627.9 8.1 %copy-start.13 = (f32[32,128]{1,0:T(8,128)S(1)}, f32[32,128]{1,0:T(8,128)}, u32[]{:S(2)}) copy-start(f32[32,128]{1,0:T(8,128)} %constant.95) | copy-start | bytes 49156
  627.9 8.1 %copy-start.14 = (f32[32,128]{1,0:T(8,128)S(1)}, f32[32,128]{1,0:T(8,128)}, u32[]{:S(2)}) copy-start(f32[32,128]{1,0:T(8,128)} %constant.93) | copy-start | bytes 49156
  627.9 8.1 %copy-start.15 = (f32[32,128]{1,0:T(8,128)S(1)}, f32[32,128]{1,0:T(8,128)}, u32[]{:S(2)}) copy-start(f32[32,128]{1,0:T(8,128)} %constant.91) | copy-start | bytes 49156
  627.9 8.1 %copy-start.16 = (f32[32,128]{1,0:T(8,128)S(1)}, f32[32,128]{1,0:T(8,128)}, u32[]{:S(2)}) copy-start(f32[32,128]{1,0:T(8,128)} %constant.89) | copy-start | bytes 49156
  627.9 8.1 %copy-start.17 = (f32[32,128]{1,0:T(8,128)S(1)}, f32[32,128]{1,0:T(8,128)}, u32[]{:S(2)}) copy-start(f32[32,128]{1,0:T(8,128)} %constant.87) | copy-start | bytes 49156
  627.9 8.1 %copy-start.18 = (f32[32,128]{1,0:T(8,128)S(1)}, f32[32,128]{1,0:T(8,128)}, u32[]{:S(2)}) copy-start(f32[32,128]{1,0:T(8,128)} %constant.85) | copy-start | bytes 49156
  627.9 8.1 %copy-start.19 = (f32[32,128]{1,0:T(8,128)S(1)}, f32[32,128]{1,0:T(8,128)}, u32[]{:S(2)}) copy-start(f32[32,128]{1,0:T(8,128)} %constant.83) | copy-start | bytes 49156
  634.4 4.0 copy-start.10

commit v3 on v2

--- a/solution.py
+++ b/solution.py
@@ -116,9 +116,9 @@
     z = twist(z, jnp.asarray(tables["fwd_twist"]))
     zl = limbs_bf16(z, 2)
     y2 = jnp.einsum(
-        "ecK,KN->ecN", zl, jnp.asarray(tables["fwd2"], jnp.bfloat16), preferred_element_type=jnp.float32
-    )
-    return fold3(y2[..., 0:SECOND], y2[..., SECOND : 2 * SECOND], y2[..., 2 * SECOND :])
+        "ecK,KN->Nec", zl, jnp.asarray(tables["fwd2"], jnp.bfloat16), preferred_element_type=jnp.float32
+    )
+    return fold3(y2[0:SECOND], y2[SECOND : 2 * SECOND], y2[2 * SECOND :])
 
 
 def inverse(pv, tables):
@@ -153,37 +153,41 @@
     return fold3(lv[0], lv[1], high)
 
 
-def make_body(n_grp, n_pt):
+def make_body(n_grp, n_pt, n_chunks):
     tables = build_tables()
     d_local = SECOND // n_pt
 
     def body(left_factor, right_factor):
         il, kl, _ = left_factor.shape
         jl = right_factor.shape[0]
-        left_eval = forward(left_factor.reshape(il * kl, -1), tables)
-        right_eval = forward(right_factor.reshape(jl * kl, -1), tables)
-
-        def to_points(ev, rows):
-            ev = ev.reshape(rows, kl, FIRST, n_pt, d_local)
-            ev = jnp.transpose(ev, (3, 2, 4, 0, 1))
-            ev = lax.all_to_all(ev, "pt", split_axis=0, concat_axis=4, tiled=True)
-            return ev.reshape(FIRST * d_local, rows, n_pt * kl)
-
-        left_pts = to_points(left_eval, il)
+
+        def to_points(x, rows):
+            ev = forward(x.reshape(rows * kl, -1), tables)
+            ev = ev.reshape(n_pt, d_local, rows, kl, FIRST)
+            ev = lax.all_to_all(ev, "pt", split_axis=0, concat_axis=0, tiled=False)
+            return ev
+
+        left_pts = to_points(left_factor, il)
         left_pts = jnp.broadcast_to(left_pts[None], (n_grp,) + left_pts.shape)
         left_pts = lax.all_to_all(left_pts, "grp", split_axis=0, concat_axis=0, tiled=True)
-        left_pts = jnp.transpose(left_pts, (1, 0, 2, 3)).reshape(FIRST * d_local, n_grp * il, n_pt * kl)
-        right_pts = to_points(right_eval, jl)
-        prod = multiply_points(left_pts, right_pts)
+        left_pts = jnp.transpose(left_pts, (2, 5, 0, 3, 1, 4))
+        left_pts = left_pts.reshape(d_local * FIRST, n_grp * il, n_pt * kl)
+        jc = jl // n_chunks
+        prods = []
+        for chunk in range(n_chunks):
+            right_pts = to_points(right_factor[chunk * jc : (chunk + 1) * jc], jc)
+            right_pts = jnp.transpose(right_pts, (1, 4, 2, 0, 3)).reshape(d_local * FIRST, jc, n_pt * kl)
+            prods.append(multiply_points(left_pts, right_pts))
+        prod = jnp.concatenate(prods, axis=2) if n_chunks > 1 else prods[0]
         n_i = prod.shape[1]
         ib = n_i // n_grp
         jb = n_grp * jl // n_pt
-        prod = prod.reshape(FIRST * d_local, n_grp, ib, jl)
+        prod = prod.reshape(d_local * FIRST, n_grp, ib, jl)
         prod = lax.all_to_all(prod, "grp", split_axis=1, concat_axis=1, tiled=True)
-        prod = jnp.transpose(prod, (0, 2, 1, 3)).reshape(FIRST, d_local, ib, n_pt, jb)
+        prod = jnp.transpose(prod, (0, 2, 1, 3)).reshape(d_local, FIRST, ib, n_pt, jb)
         prod = jnp.transpose(prod, (3, 0, 1, 2, 4))
         prod = lax.all_to_all(prod, "pt", split_axis=0, concat_axis=0, tiled=False)
-        pv = jnp.transpose(prod, (3, 4, 1, 0, 2)).reshape(ib * jb, FIRST, SECOND)
+        pv = jnp.transpose(prod, (3, 4, 2, 0, 1)).reshape(ib * jb, FIRST, SECOND)
         coeffs = inverse(pv, tables)
         return (coeffs / float(modulus)).reshape(ib, jb, LENGTH)
 
@@ -194,7 +198,7 @@
     n_grp = mesh.shape["grp"]
     n_pt = mesh.shape["pt"]
     return jax.shard_map(
-        make_body(n_grp, n_pt),
+        make_body(n_grp, n_pt, 4),
         mesh=mesh,
         in_specs=(P("grp", "pt", None), P("grp", "pt", None)),
         out_specs=P("grp", "pt", None),

time: 649 us -> 612 us (0.943)
  waiting for transfers between devices: 139 us -> 21.4 us
  local copies, waits for them, and re-layouts: 271 us -> 323 us
  blocking collectives: 78.6 us -> 47.9 us
  starting transfers between devices: 17.7 us -> 42.3 us
  matrix products: 41.5 us -> 61.5 us
  other arithmetic: 92.8 us -> 105 us
    all_to_all x2 -> x5, waiting for transfers between devices: 139 us -> 5.18 us  [to_points(): ev = lax.all_to_all(ev, 'pt', split_axis=0, concat_axis=0, tiled=False)]
    unnamed x58 -> x119, local copies, waits for them, and re-layouts: 91.4 us -> 162 us
    all_to_all x1, blocking collectives: 61.9 us -> 31.9 us  [body(): prod = lax.all_to_all(prod, 'pt', split_axis=0, concat_axis=0, tiled=False)]
    all_to_all x5 -> x2, local copies, waits for them, and re-layouts: 33 us -> 5.1 us  [to_points(): ev = lax.all_to_all(ev, 'pt', split_axis=0, concat_axis=0, tiled=False)]
    all_to_all x2 -> x5, starting transfers between devices: 14 us -> 37.9 us  [to_points(): ev = lax.all_to_all(ev, 'pt', split_axis=0, concat_axis=0, tiled=False)]
    dot_general x1 -> x4, matrix products: 12.8 us -> 36.6 us  [multiply_points(): jnp.einsum('pak,pjk->paj', toeplitz, right_limbs, preferred_element_type=...]
    reshape x3 -> x12, local copies, waits for them, and re-layouts: 27.6 us -> 44.4 us  [the longest x8 31.3 us: body(): jnp.transpose(right_pts, (1, 4, 2, 0, 3))]
    all_to_all x1, waiting for transfers between devices: 0.01 us -> 16.3 us  [body(): lax.all_to_all(left_pts, 'grp', split_axis=0, concat_axis=0, tiled=True)]
  transfers between devices with their start and end apart: 3 -> 6, of which waited for: 1 -> 2; matrix products, arithmetic and copies ran while one was open for 22% -> 58% of each run, Pallas kernels for 0% -> 0%
where the time goes in v3:
time: 612 us; the launch traced here: 603 us
  local copies, waits for them, and re-layouts  323 us (53%)
  other arithmetic  105 us (17%)
  matrix products  61.5 us (10%)
  blocking collectives  47.9 us (8%)
  starting transfers between devices  42.3 us (7%)
  waiting for transfers between devices  21.4 us (3%)
    unnamed x119, local copies, waits for them, and re-layouts  162 us
    transpose x4, local copies, waits for them, and re-layouts, body(): jnp.transpose(right_pts, (1, 4, 2, 0, 3))  45.8 us
    convert_element_type x20, other arithmetic, limbs_bf16(): piece.astype(jnp.bfloat16)  39.4 us
    all_to_all x5, starting transfers between devices, to_points(): ev = lax.all_to_all(ev, 'pt', split_axis=0, concat_axis=0, tiled=False)  37.9 us
    dot_general x4, matrix products, multiply_points(): jnp.einsum('pak,pjk->paj', toeplitz, right_limbs, preferred_element_type=...  36.6 us
    all_to_all x1, blocking collectives, body(): prod = lax.all_to_all(prod, 'pt', split_axis=0, concat_axis=0, tiled=False)  31.9 us
    all_to_all x5, other arithmetic, to_points(): ev = lax.all_to_all(ev, 'pt', split_axis=0, concat_axis=0, tiled=False)  31.8 us
    reshape x8, local copies, waits for them, and re-layouts, body(): jnp.transpose(right_pts, (1, 4, 2, 0, 3))  31.3 us
  transfers between devices with their start and end apart: 6, of which 2 were waited for; matrix products, arithmetic and copies ran while one was open for 58% of the time, Pallas kernels for 0%

profile of v3, /device:TPU:1, one launch (start us, length us, event | category | flops | bytes accessed | tf_op | source)
XLA Modules:
  0.0 602.7 jit_solution(11652590626418822875)
XLA Ops:
  16.5 7.6 %all-to-all-start = ((f32[16,1,16384]{2,1,0:T(1,128)}), f32[16,1,16384]{2,1,0:T(1,128)S(1)}, u32[]{:S(2)}, u32[]{:S(2)}) async-start(f32[16,1,16384]{2,1,0:T(1,128)} %reshape.84), calls=%async_computation | async-start | bytes 2097152 | tf_op jit(solution)/shard_map/all_to_all | solution.py:167
  38.3 4.7 copy.143
  43.0 8.9 %reshape.88 = f32[16,1,32768]{2,1,0:T(1,128)} reshape(f32[16,8,16,8,32]{4,3,2,1,0:T(8,128)} %bitcast.166) | data formatting | bytes 4194304
  75.7 6.9 %reshape.86 = f32[2,1,262144]{2,1,0:T(1,128)} reshape(f32[2,8,16,8,8,32]{5,4,3,2,1,0:T(8,128)} %broadcast_bitcast_fusion) | data formatting | bytes 4194304
  95.7 16.3 %all-to-all-done.1 = f32[2,1,262144]{2,1,0:T(1,128)S(1)} async-done(((f32[2,1,262144]{2,1,0:T(1,128)}), f32[2,1,262144]{2,1,0:T(1,128)S(1)}, u32[]{:S(2)}, u32[]{:S(2)}) %all-to-all-start.1) | async-done | bytes 2097184 | tf_op jit(solution)/shard_map/all_to_all | solution.py:172
  113.3 6.4 %all-to-all-start.5 = ((f32[16,1,32768]{2,1,0:T(1,128)}), f32[16,1,32768]{2,1,0:T(1,128)}, u32[]{:S(2)}, u32[]{:S(2)}) async-start(f32[16,1,32768]{2,1,0:T(1,128)} %reshape.88), calls=%async_computation.5 | async-start | bytes 4194304 | tf_op jit(solution)/shard_map/all_to_all | solution.py:167
  119.7 15.8 %subtract_convert_fusion.15 = (bf16[128,32,128]{2,1,0:T(8,128)(2,1)}, f32[128,32,128]{2,1,0:T(8,128)}, bf16[128,32,128]{2,1,0:T(8,128)(2,1)}, f32[128,32,128]{2,...) fusion(f32[32,128]{1,0:T(8,128)S(1)} %copy-done.18, f32[32,128]{1,0:T(8,128)S(1)} %copy-done.19, ...), kind=kLoop, calls=%fused_computation.101 | loop fusion | flops 94371840 | bytes 28459008 | tf_op jit(solution)/shard_map/convert_element_type | solution.py:105
  141.2 6.3 %copy.132 = f32[128,128,32]{2,1,0:T(8,128)} copy(f32[128,128,32]{1,0,2:T(8,128)} %compare_select_fusion.3) | data formatting | bytes 4194304 | tf_op jit(solution)/shard_map/jit(_where)/select_n | solution.py:95
  147.5 8.6 %reshape.90 = f32[16,1,32768]{2,1,0:T(1,128)} reshape(f32[16,8,16,8,32]{4,3,2,1,0:T(8,128)} %bitcast.167) | data formatting | bytes 4194304
  156.1 5.2 all-to-all-done.5
  161.3 11.2 %all-to-all-start.4 = ((f32[16,1,32768]{2,1,0:T(1,128)}), f32[16,1,32768]{2,1,0:T(1,128)}, u32[]{:S(2)}, u32[]{:S(2)}) async-start(f32[16,1,32768]{2,1,0:T(1,128)} %reshape.90), calls=%async_computation.4 | async-start | bytes 4194304 | tf_op jit(solution)/shard_map/all_to_all | solution.py:167
  181.8 6.3 %copy.121 = f32[128,128,32]{2,1,0:T(8,128)} copy(f32[128,128,32]{1,0,2:T(8,128)} %compare_select_fusion.6) | data formatting | bytes 4194304 | tf_op jit(solution)/shard_map/jit(_where)/select_n | solution.py:95
  188.2 8.5 %reshape.92 = f32[16,1,32768]{2,1,0:T(1,128)} reshape(f32[16,8,16,8,32]{4,3,2,1,0:T(8,128)} %bitcast.168) | data formatting | bytes 4194304
  200.2 4.7 copy.110
  204.9 8.5 %reshape.94 = f32[16,1,32768]{2,1,0:T(1,128)} reshape(f32[16,8,16,8,32]{4,3,2,1,0:T(8,128)} %bitcast.169) | data formatting | bytes 4194304
  213.4 8.0 %reduce.1 = f32[2,262144]{1,0:T(2,128)S(1)} reduce(f32[2,1,262144]{2,1,0:T(1,128)} %copy-done, f32[]{:T(128)} %broadcast.370), dimensions={1}, to_apply=%all_to_all.25.reduce_sub_computation | reduce | bytes 4194308 | tf_op jit(solution)/shard_map/all_to_all | solution.py:172
  221.5 6.5 %reshape.87 = f32[2,8,16,8,8,32]{5,4,3,2,1,0:T(8,128)} reshape(f32[2,262144]{1,0:T(2,128)S(1)} %reduce.1) | data formatting | bytes 4194304
  227.9 6.6 %all-to-all-start.3 = ((f32[16,1,32768]{2,1,0:T(1,128)}), f32[16,1,32768]{2,1,0:T(1,128)}, u32[]{:S(2)}, u32[]{:S(2)}) async-start(f32[16,1,32768]{2,1,0:T(1,128)} %reshape.92), calls=%async_computation.3 | async-start | bytes 4194304 | tf_op jit(solution)/shard_map/all_to_all | solution.py:167
  234.5 8.3 %bitcast_bitcast_fusion = f32[8,32,2,8,16,8]{1,0,5,4,3,2:T(8,128)} fusion(f32[2,8,16,8,8,32]{5,4,3,2,1,0:T(8,128)} %reshape.87), kind=kLoop, calls=%fused_computation.228 | loop fusion | bytes 4194304 | tf_op jit(solution)/shard_map/transpose | solution.py:173
  242.9 5.8 reshape.64
  264.1 7.2 %reduce.2 = f32[16,32768]{1,0:T(8,128)S(1)} reduce(f32[16,1,32768]{2,1,0:T(1,128)} %all-to-all-done.5, f32[]{:T(128)} %broadcast.370), dimensions={1}, to_apply=%all_to_all.29.reduce_sub_computation | reduce | bytes 4194308 | tf_op jit(solution)/shard_map/all_to_all | solution.py:167
  271.3 4.9 reshape.89
  276.2 11.5 %copy.144 = f32[8,32,16,16,8]{1,0,4,3,2:T(8,128)} copy(f32[8,32,16,16,8]{1,4,2,0,3:T(8,128)} %bitcast.170) | data formatting | bytes 4194304 | tf_op jit(solution)/shard_map/transpose | solution.py:179
  287.7 5.8 reshape.72
  297.8 9.1 %fusion.18 = f32[256,80,16]{1,2,0:T(8,128)S(1)} fusion(bf16[256,80,384]{2,1,0:T(8,128)(2,1)} %pad_dynamic-update-slice_fusion, bf16[256,16,128]{2,1,0:T(8,128)(2,1)S(1)} %get-tuple-element.58, bf16[256,16,128]{2,1,0:T(8,128)(2,1)S(1)} %get-tuple-element.57, bf16[256,16,128]{2,1,0:T(8,128)(2,1)S(1)} %get-tuple-element.56), kind=kOutput, calls=%fused_computation.37 | convolution fusion | flops 261095424 | bytes 20185088 | tf_op jit(solution)/shard_map/pak,pjk->paj/dot_general | solution.py:149
  306.9 5.4 fusion.112
  323.8 7.2 %reduce.3 = f32[16,32768]{1,0:T(8,128)S(1)} reduce(f32[16,1,32768]{2,1,0:T(1,128)} %all-to-all-done.4, f32[]{:T(128)} %broadcast.370), dimensions={1}, to_apply=%all_to_all.28.reduce_sub_computation | reduce | bytes 4194308 | tf_op jit(solution)/shard_map/all_to_all | solution.py:167
  331.0 5.1 reshape.91
  336.1 11.5 %copy.133 = f32[8,32,16,16,8]{1,0,4,3,2:T(8,128)} copy(f32[8,32,16,16,8]{1,4,2,0,3:T(8,128)} %bitcast.171) | data formatting | bytes 4194304 | tf_op jit(solution)/shard_map/transpose | solution.py:179
  347.6 5.8 reshape.70
  355.4 6.2 %all-to-all-start.2 = ((f32[16,1,32768]{2,1,0:T(1,128)}), f32[16,1,32768]{2,1,0:T(1,128)}, u32[]{:S(2)}, u32[]{:S(2)}) async-start(f32[16,1,32768]{2,1,0:T(1,128)} %reshape.94), calls=%async_computation.2 | async-start | bytes 4194304 | tf_op jit(solution)/shard_map/all_to_all | solution.py:167
  362.3 9.1 %fusion.12 = f32[256,80,16]{1,2,0:T(8,128)S(1)} fusion(bf16[256,80,384]{2,1,0:T(8,128)(2,1)} %pad_dynamic-update-slice_fusion, bf16[256,16,128]{2,1,0:T(8,128)(2,1)S(1)} %get-tuple-element.48, bf16[256,16,128]{2,1,0:T(8,128)(2,1)S(1)} %get-tuple-element.47, bf16[256,16,128]{2,1,0:T(8,128)(2,1)S(1)} %get-tuple-element.46), kind=kOutput, calls=%fused_computation.30 | convolution fusion | flops 261095424 | bytes 20185088 | tf_op jit(solution)/shard_map/pak,pjk->paj/dot_general | solution.py:149
  371.4 5.4 fusion.111
  391.6 7.2 %reduce.4 = f32[16,32768]{1,0:T(8,128)S(1)} reduce(f32[16,1,32768]{2,1,0:T(1,128)} %all-to-all-done.3, f32[]{:T(128)} %broadcast.370), dimensions={1}, to_apply=%all_to_all.27.reduce_sub_computation | reduce | bytes 4194308 | tf_op jit(solution)/shard_map/all_to_all | solution.py:167
  398.8 5.0 reshape.93
  403.8 11.5 %copy.122 = f32[8,32,16,16,8]{1,0,4,3,2:T(8,128)} copy(f32[8,32,16,16,8]{1,4,2,0,3:T(8,128)} %bitcast.172) | data formatting | bytes 4194304 | tf_op jit(solution)/shard_map/transpose | solution.py:179
  415.2 5.8 reshape.68
  425.4 9.3 %fusion.6 = f32[256,80,16]{1,2,0:T(8,128)S(1)} fusion(bf16[256,80,384]{2,1,0:T(8,128)(2,1)} %pad_dynamic-update-slice_fusion, bf16[256,16,128]{2,1,0:T(8,128)(2,1)S(1)} %get-tuple-element.38, bf16[256,16,128]{2,1,0:T(8,128)(2,1)S(1)} %get-tuple-element.37, bf16[256,16,128]{2,1,0:T(8,128)(2,1)S(1)} %get-tuple-element.36), kind=kOutput, calls=%fused_computation.23 | convolution fusion | flops 261095424 | bytes 20185088 | tf_op jit(solution)/shard_map/pak,pjk->paj/dot_general | solution.py:149
  434.7 5.6 fusion.110
  455.1 7.2 %reduce.5 = f32[16,32768]{1,0:T(8,128)S(1)} reduce(f32[16,1,32768]{2,1,0:T(1,128)} %all-to-all-done.2, f32[]{:T(128)} %broadcast.370), dimensions={1}, to_apply=%all_to_all.26.reduce_sub_computation | reduce | bytes 4194308 | tf_op jit(solution)/shard_map/all_to_all | solution.py:167
  462.3 4.9 reshape.95
  467.2 11.5 %copy.111 = f32[8,32,16,16,8]{1,0,4,3,2:T(8,128)} copy(f32[8,32,16,16,8]{1,4,2,0,3:T(8,128)} %bitcast.173) | data formatting | bytes 4194304 | tf_op jit(solution)/shard_map/transpose | solution.py:179
  478.6 5.8 reshape.66
  488.8 9.1 %fusion = f32[256,80,16]{1,2,0:T(8,128)S(1)} fusion(bf16[256,80,384]{2,1,0:T(8,128)(2,1)} %pad_dynamic-update-slice_fusion, bf16[256,16,128]{2,1,0:T(8,128)(2,1)S(1)} %get-tuple-element.28, bf16[256,16,128]{2,1,0:T(8,128)(2,1)S(1)} %get-tuple-element.27, bf16[256,16,128]{2,1,0:T(8,128)(2,1)S(1)} %get-tuple-element.26), kind=kOutput, calls=%fused_computation.16 | convolution fusion | flops 261095424 | bytes 20185088 | tf_op jit(solution)/shard_map/pak,pjk->paj/dot_general | solution.py:149
  497.9 5.5 fusion.109
  522.2 16.0 %all_to_all.40 = f32[256,2,8,64]{0,3,2,1:T(8,128)S(1)} all-to-all(f32[256,2,8,64]{0,3,2,1:T(8,128)S(1)} %bitcast.176), channel_id=1, replica_groups=mesh['grp'=2,'pt'=16] {'grp'}, dimensions={1} | all-to-all | bytes 2097152 | tf_op jit(solution)/shard_map/all_to_all | solution.py:186
  540.8 4.8 copy_bitcast_fusion
  549.5 31.9 %all_to_all.41 = f32[16,1,16384]{2,1,0:T(1,128)S(1)} all-to-all(f32[16,1,16384]{2,1,0:T(1,128)S(1)} %reshape.96), channel_id=1, replica_groups=mesh['grp'=2,'pt'=16] {'pt'}, dimensions={0} | all-to-all | bytes 2097152 | tf_op jit(solution)/shard_map/all_to_all | solution.py:189
  (180 shorter events, 205.4 us)
Async XLA Ops:
  0.0 1.5 copy-start.17
  1.4 0.7 copy-start.18
  1.4 0.7 copy-start.19
  1.4 0.7 copy-start.20
  1.4 0.7 copy-start.21
  1.4 0.7 copy-start.22
  1.4 0.7 copy-start.23
  1.4 0.7 copy-start.24
  1.4 0.8 copy-start.25
  1.5 0.8 copy-start.26
  4.6 1.0 copy-start.2
  16.5 43.6 %all-to-all-start = ((f32[16,1,16384]{2,1,0:T(1,128)}), f32[16,1,16384]{2,1,0:T(1,128)S(1)}, u32[]{:S(2)}, u32[]{:S(2)}) async-start(f32[16,1,16384]{2,1,0:T(1,128)} %reshape.84), calls=%async_computation | async-start | bytes 2097152 | tf_op jit(solution)/shard_map/all_to_all | solution.py:167
  43.0 8.9 %copy-start.8 = (f32[16,8,16,128]{3,1,2,0:T(8,128)S(1)}, f32[16,8,16,128]{3,1,2,0:T(8,128)}, u32[]{:S(2)}) copy-start(f32[16,8,16,128]{3,1,2,0:T(8,128)} %get-tuple-element.17) | copy-start | bytes 3145732
  51.9 1.2 copy-start.7
  51.9 1.5 copy-start.6
  82.6 4.4 copy-start.5
  82.6 29.3 %all-to-all-start.1 = ((f32[2,1,262144]{2,1,0:T(1,128)}), f32[2,1,262144]{2,1,0:T(1,128)S(1)}, u32[]{:S(2)}, u32[]{:S(2)}) async-start(f32[2,1,262144]{2,1,0:T(1,128)} %reshape.86), calls=%async_computation.1 | async-start | bytes 4194304 | tf_op jit(solution)/shard_map/all_to_all | solution.py:172
  87.0 1.0 copy-start.9
  87.0 1.2 copy-start.10
  87.0 1.3 copy-start.11
  111.9 1.4 copy-start
  113.3 48.0 %all-to-all-start.5 = ((f32[16,1,32768]{2,1,0:T(1,128)}), f32[16,1,32768]{2,1,0:T(1,128)}, u32[]{:S(2)}, u32[]{:S(2)}) async-start(f32[16,1,32768]{2,1,0:T(1,128)} %reshape.88), calls=%async_computation.5 | async-start | bytes 4194304 | tf_op jit(solution)/shard_map/all_to_all | solution.py:167
  161.3 66.7 %all-to-all-start.4 = ((f32[16,1,32768]{2,1,0:T(1,128)}), f32[16,1,32768]{2,1,0:T(1,128)}, u32[]{:S(2)}, u32[]{:S(2)}) async-start(f32[16,1,32768]{2,1,0:T(1,128)} %reshape.90), calls=%async_computation.4 | async-start | bytes 4194304 | tf_op jit(solution)/shard_map/all_to_all | solution.py:167
  174.6 1.2 copy-start.3
  174.6 1.5 copy-start.4
  227.9 127.4 %all-to-all-start.3 = ((f32[16,1,32768]{2,1,0:T(1,128)}), f32[16,1,32768]{2,1,0:T(1,128)}, u32[]{:S(2)}, u32[]{:S(2)}) async-start(f32[16,1,32768]{2,1,0:T(1,128)} %reshape.92), calls=%async_computation.3 | async-start | bytes 4194304 | tf_op jit(solution)/shard_map/all_to_all | solution.py:167
  355.4 6.2 %copy-start.1 = (f32[256,16,128]{2,1,0:T(8,128)S(1)}, f32[256,16,128]{2,1,0:T(8,128)}, u32[]{:S(2)}) copy-start(f32[256,16,128]{2,1,0:T(8,128)} %copy.135) | copy-start | bytes 6291460
  355.4 99.7 %all-to-all-start.2 = ((f32[16,1,32768]{2,1,0:T(1,128)}), f32[16,1,32768]{2,1,0:T(1,128)}, u32[]{:S(2)}, u32[]{:S(2)}) async-start(f32[16,1,32768]{2,1,0:T(1,128)} %reshape.94), calls=%async_computation.2 | async-start | bytes 4194304 | tf_op jit(solution)/shard_map/all_to_all | solution.py:167
  518.2 3.2 copy-start.12
  518.2 3.2 copy-start.13
  518.2 3.2 copy-start.14
  518.2 3.3 copy-start.15
  518.2 3.3 copy-start.16
  595.0 1.0 copy-start.37
  596.0 1.2 copy-start.28
  596.0 1.2 copy-start.29
  596.0 1.2 copy-start.30
  596.0 1.2 copy-start.31
  596.0 1.2 copy-start.32
  596.0 1.2 copy-start.33
  596.0 1.2 copy-start.34
  596.0 1.2 copy-start.35
  596.1 1.2 copy-start.36
  599.4 0.7 copy-start.27

commit v4 on v3

v4 whole, which is shorter than its diff:
```python
import jax
import jax.numpy as jnp
import numpy as np
from jax import lax
from jax.sharding import PartitionSpec as P

FIRST = 32
SECOND = 128
HALF_FIRST = FIRST // 2
LENGTH = FIRST * SECOND

modulus = 7340033
INV_P = float(np.float32(1.0 / modulus))


def root_powers(length_all):
    for generator in range(2, 64):
        candidate = pow(generator, (modulus - 1) // length_all, modulus)
        if pow(candidate, length_all // 2, modulus) == modulus - 1:
            break
    powers = [1]
    for counter in range(length_all - 1):
        powers.append(powers[-1] * candidate % modulus)
    return np.array(powers, dtype=np.int64)


def balanced_limbs(values):
    v = np.asarray(values, dtype=np.int64)
    l0 = (v + 128) % 256 - 128
    v = (v - l0) // 256
    l1 = (v + 128) % 256 - 128
    l2 = (v - l1) // 256
    return [l0, l1, l2]


def scaled_stack(table):
    n, k = table.shape
    out = np.zeros((3, n, 3, k), dtype=np.float32)
    for level in range(3):
        scaled = table * pow(256, level, modulus) % modulus
        for limb, piece in enumerate(balanced_limbs(scaled)):
            out[limb, :, level, :] = piece
    return out.reshape(3 * n, 3 * k)


def twist_stack(table):
    out = np.zeros((3, 3) + table.shape, dtype=np.float32)
    for level in range(3):
        scaled = table * pow(256, level, modulus) % modulus
        for limb, piece in enumerate(balanced_limbs(scaled)):
            out[level, limb] = piece
    return out


def build_tables():
    powers = root_powers(LENGTH)

    def pw(e):
        return powers[np.asarray(e) % LENGTH]

    a16 = np.arange(HALF_FIRST)
    c32 = np.arange(FIRST)
    b128 = np.arange(SECOND)
    scale_inv = pow(LENGTH, modulus - 2, modulus)
    fwd1 = pw(SECOND * np.outer(c32, a16))
    fwd_twist = pw(np.outer(c32, b128))
    fwd2 = pw(FIRST * np.outer(b128, b128))
    inv1 = pw(-FIRST * np.outer(b128, b128))
    inv_twist = pw(-np.outer(b128, c32))
    inv2 = pw(-SECOND * np.outer(c32, c32)) * scale_inv % modulus
    return dict(
        fwd1=scaled_stack(fwd1),
        fwd_twist=twist_stack(fwd_twist)[..., None],
        fwd2=scaled_stack(fwd2),
        inv1=scaled_stack(inv1),
        inv_twist=twist_stack(inv_twist)[..., None],
        inv2=scaled_stack(inv2),
    )


def split3(x):
    h = jnp.floor(x * (1.0 / 256.0))
    x0 = x - 256.0 * h
    x2 = jnp.floor(h * (1.0 / 256.0))
    x1 = h - 256.0 * x2
    return x0, x1, x2


def fold3(s0, s1, s2):
    f = s2 * 65536.0 + s1 * 256.0 + s0
    q = jnp.round(f * INV_P)
    d = s2 - 112.0 * q
    e = s1 + 256.0 * d
    r = s0 + 256.0 * e - q
    return jnp.where(r < 0, r + float(modulus), r)


def twist(z, tw):
    zl = split3(z)
    s = [zl[0] * tw[0, u] + zl[1] * tw[1, u] + zl[2] * tw[2, u] for u in range(3)]
    return fold3(*s)


def limbs_bf16(x, axis):
    return jnp.concatenate([piece.astype(jnp.bfloat16) for piece in split3(x)], axis=axis)


def bf16_table(tables, name):
    return jnp.asarray(tables[name], jnp.bfloat16)


def forward(xt, tables):
    entries = xt.shape[1]
    x = xt.reshape(HALF_FIRST, SECOND, entries)
    xl = limbs_bf16(x, 0)
    y = jnp.einsum("NK,Kbe->Nbe", bf16_table(tables, "fwd1"), xl, preferred_element_type=jnp.float32)
    z = fold3(y[0:FIRST], y[FIRST : 2 * FIRST], y[2 * FIRST :])
    z = twist(z, jnp.asarray(tables["fwd_twist"]))
    zl = limbs_bf16(z, 1)
    y2 = jnp.einsum("NK,cKe->cNe", bf16_table(tables, "fwd2"), zl, preferred_element_type=jnp.float32)
    return fold3(y2[:, 0:SECOND], y2[:, SECOND : 2 * SECOND], y2[:, 2 * SECOND :])


def inverse(pv, tables):
    pl_ = limbs_bf16(pv, 0)
    y = jnp.einsum("NK,Kce->Nce", bf16_table(tables, "inv1"), pl_, preferred_element_type=jnp.float32)
    z = fold3(y[0:SECOND], y[SECOND : 2 * SECOND], y[2 * SECOND :])
    z = twist(z, jnp.asarray(tables["inv_twist"]))
    zl = limbs_bf16(z, 1)
    y2 = jnp.einsum("NK,bKe->bNe", bf16_table(tables, "inv2"), zl, preferred_element_type=jnp.float32)
    return fold3(y2[:, 0:FIRST], y2[:, FIRST : 2 * FIRST], y2[:, 2 * FIRST :])


def multiply_points(left_t, right):
    left_limbs = [v.astype(jnp.bfloat16) for v in split3(left_t)]
    zero = jnp.zeros_like(left_limbs[0])
    cols = []
    for level in range(5):
        pieces = [left_limbs[level - y] if 0 <= level - y < 3 else zero for y in range(3)]
        cols.append(jnp.concatenate(pieces, axis=1))
    toeplitz = jnp.concatenate(cols, axis=2)
    right_limbs = limbs_bf16(right, 1)
    levels = jnp.einsum("pKa,pKj->paj", toeplitz, right_limbs, preferred_element_type=jnp.float32)
    n_i = left_t.shape[2]
    lv = [levels[:, n * n_i : (n + 1) * n_i] for n in range(5)]
    high = fold3(lv[2], lv[3], lv[4])
    return fold3(lv[0], lv[1], high)


def make_body(n_grp, n_pt, n_chunks):
    tables = build_tables()
    d_local = SECOND // n_pt

    def body(left_factor, right_factor):
        il, kl, _ = left_factor.shape
        jl = right_factor.shape[0]

        def to_points(x):
            rows = x.shape[0]
            xt = jnp.transpose(x, (2, 1, 0)).reshape(x.shape[2], kl * rows)
            ev = forward(xt, tables)
            ev = ev.reshape(FIRST, n_pt, d_local, kl, rows)
            ev = jnp.transpose(ev, (1, 0, 2, 3, 4))
            ev = lax.all_to_all(ev, "pt", split_axis=0, concat_axis=0, tiled=False)
            return ev

        left_pts = to_points(left_factor)
        left_pts = jnp.broadcast_to(left_pts[None], (n_grp,) + left_pts.shape)
        left_pts = lax.all_to_all(left_pts, "grp", split_axis=0, concat_axis=0, tiled=True)
        left_pts = jnp.transpose(left_pts, (2, 3, 1, 4, 0, 5))
        left_pts = left_pts.reshape(FIRST * d_local, n_pt * kl, n_grp * il)
        jc = jl // n_chunks
        prods = []
        for chunk in range(n_chunks):
            right_pts = to_points(right_factor[chunk * jc : (chunk + 1) * jc])
            right_pts = jnp.transpose(right_pts, (1, 2, 0, 3, 4)).reshape(FIRST * d_local, n_pt * kl, jc)
            prods.append(multiply_points(left_pts, right_pts))
        prod = jnp.concatenate(prods, axis=2) if n_chunks > 1 else prods[0]
        n_i = prod.shape[1]
        ib = n_i // n_grp
        jb = n_grp * jl // n_pt
        prod = prod.reshape(FIRST * d_local, n_grp, ib, jl)
        prod = lax.all_to_all(prod, "grp", split_axis=1, concat_axis=1, tiled=True)
        prod = jnp.transpose(prod, (0, 2, 1, 3)).reshape(FIRST, d_local, ib, n_pt, jb)
        prod = jnp.transpose(prod, (3, 0, 1, 2, 4))
        prod = lax.all_to_all(prod, "pt", split_axis=0, concat_axis=0, tiled=False)
        pv = jnp.transpose(prod, (0, 2, 1, 3, 4)).reshape(SECOND, FIRST, ib * jb)
        coeffs = inverse(pv, tables)
        coeffs = jnp.transpose(coeffs, (2, 1, 0)).reshape(ib, jb, LENGTH)
        return coeffs / float(modulus)

    return body


def solution(mesh):
    n_grp = mesh.shape["grp"]
    n_pt = mesh.shape["pt"]
    return jax.shard_map(
        make_body(n_grp, n_pt, 2),
        mesh=mesh,
        in_specs=(P("grp", "pt", None), P("grp", "pt", None)),
        out_specs=P("grp", "pt", None),
        check_vma=False,
    )
```

time: 612 us -> 673 us (1.100)
  local copies, waits for them, and re-layouts: 323 us -> 393 us
  waiting for transfers between devices: 21.4 us -> 0.01 us
  other arithmetic: 105 us -> 116 us
  matrix products: 61.5 us -> 71.2 us
  starting transfers between devices: 42.3 us -> 35.2 us
    reshape x12 -> x9, local copies, waits for them, and re-layouts: 44.4 us -> 107 us  [the longest x4 45.4 us: to_points(): ev = ev.reshape(FIRST, n_pt, d_local, kl, rows)]
    dot_general x0 -> x3, local copies, waits for them, and re-layouts: none -> 27.2 us  [the longest x2 25.4 us: forward(): jnp.einsum('NK,cKe->cNe', bf16_table(tables, 'fwd2'), zl, preferred_eleme...]
    select_n x5 -> x1, local copies, waits for them, and re-layouts: 26.6 us -> 4.46 us  [fold3(): return jnp.where(r < 0, r + float(modulus), r)]
    transpose x8 -> x10, local copies, waits for them, and re-layouts: 59.3 us -> 78.2 us  [the longest x2 35.2 us: body(): left_pts = jnp.transpose(left_pts, (2, 3, 1, 4, 0, 5))]
    all_to_all x1, waiting for transfers between devices: 16.3 us -> 0.01 us  [body(): lax.all_to_all(left_pts, 'grp', split_axis=0, concat_axis=0, tiled=True)]
    unnamed x119 -> x87, local copies, waits for them, and re-layouts: 162 us -> 148 us
    dot_general x16 -> x9, matrix products: 61.5 us -> 70.1 us  [the longest x3 44.3 us: forward(): jnp.einsum('NK,cKe->cNe', bf16_table(tables, 'fwd2'), zl, preferred_eleme...]
    all_to_all x5 -> x3, starting transfers between devices: 37.9 us -> 31.3 us  [to_points(): ev = lax.all_to_all(ev, 'pt', split_axis=0, concat_axis=0, tiled=False)]
  transfers between devices with their start and end apart: 6 -> 4, of which waited for: 2 -> 0; matrix products, arithmetic and copies ran while one was open for 58% -> 53% of each run, Pallas kernels for 0% -> 0%
where the time goes in v4:
time: 673 us; the launch traced here: 665 us
  local copies, waits for them, and re-layouts  393 us (58%)
  other arithmetic  116 us (17%)
  matrix products  71.2 us (11%)
  blocking collectives  48 us (7%)
  starting transfers between devices  35.2 us (5%)
    unnamed x87, local copies, waits for them, and re-layouts  148 us
    reshape x4, local copies, waits for them, and re-layouts, to_points(): ev = ev.reshape(FIRST, n_pt, d_local, kl, rows)  45.4 us
    dot_general x3, matrix products, forward(): jnp.einsum('NK,cKe->cNe', bf16_table(tables, 'fwd2'), zl, preferred_eleme...  44.3 us
    convert_element_type x13, other arithmetic, limbs_bf16(): piece.astype(jnp.bfloat16)  42.3 us
    transpose x2, local copies, waits for them, and re-layouts, body(): left_pts = jnp.transpose(left_pts, (2, 3, 1, 4, 0, 5))  35.2 us
    all_to_all x1, blocking collectives, body(): prod = lax.all_to_all(prod, 'pt', split_axis=0, concat_axis=0, tiled=False)  31.9 us
    all_to_all x3, other arithmetic, to_points(): ev = lax.all_to_all(ev, 'pt', split_axis=0, concat_axis=0, tiled=False)  31.5 us
    all_to_all x3, starting transfers between devices, to_points(): ev = lax.all_to_all(ev, 'pt', split_axis=0, concat_axis=0, tiled=False)  31.3 us
  transfers between devices with their start and end apart: 4, of which 0 were waited for; matrix products, arithmetic and copies ran while one was open for 53% of the time, Pallas kernels for 0%

profile of v4, /device:TPU:1, one launch (start us, length us, event | category | flops | bytes accessed | tf_op | source)
XLA Modules:
  0.0 664.5 jit_solution(975384397558764312)
XLA Ops:
  11.8 4.7 reshape.63
  16.5 7.8 %all-to-all-start = ((f32[16,1,16384]{2,1,0:T(1,128)}), f32[16,1,16384]{2,1,0:T(1,128)}, u32[]{:S(2)}, u32[]{:S(2)}) async-start(f32[16,1,16384]{2,1,0:T(1,128)} %reshape.63), calls=%async_computation | async-start | bytes 2097152 | tf_op jit(solution)/shard_map/all_to_all | solution.py:164
  45.2 20.4 %subtract_convert_fusion.7 = (bf16[32,128,256]{2,0,1:T(8,128)(2,1)S(1)}, f32[32,128,256]{2,0,1:T(8,128)}, bf16[32,128,256]{2,0,1:T(8,128)(2,1)}, f32[32,128,256]{2,0,1:T(8,128)S(1)}) fusion(f32[32,128]{0,1:T(8,128)S(1)} %copy-done.11, f32[32,128]{0,1:T(8,128)} %constant.116, f32[32,128]{0,1:T(8,128)} %constant.115, f32[32,128]{0,1:T(8,128)} %constant.114, ...), kind=kLoop, calls=%fused_computation.44 | loop fusion | flops 125829120 | bytes 37896192 | tf_op jit(solution)/shard_map/convert_element_type | solution.py:105
  70.4 5.3 pad_maximum_fusion
  83.4 6.9 %broadcast_bitcast_fusion = f32[2,16,8,8,8,32]{5,4,3,2,1,0:T(8,128)} fusion(f32[16,32,8,8,8]{1,4,3,2,0:T(8,128)} %bitcast.109), kind=kLoop, calls=%fused_computation.142 | loop fusion | bytes 3145728
  90.3 6.9 %reshape.65 = f32[2,1,262144]{2,1,0:T(1,128)} reshape(f32[2,16,8,8,8,32]{5,4,3,2,1,0:T(8,128)} %broadcast_bitcast_fusion) | data formatting | bytes 4194304
  101.1 21.8 %fusion.12 = f32[32,256,384]{2,1,0:T(8,128)} fusion(bf16[384,384,1]{1,0,2:T(8,128)(2,1)S(1)} %copy-done.8, bf16[32,384,256]{2,0,1:T(8,128)(2,1)} %get-tuple-element.57), kind=kOutput, calls=%fused_computation.22 | convolution fusion | flops 2415919104 | bytes 19169280 | tf_op jit(solution)/shard_map/NK,cKe->cNe/dot_general | solution.py:120
  122.9 12.7 %copy.145 = f32[32,256,384]{1,0,2:T(8,128)} copy(f32[32,256,384]{2,1,0:T(8,128)} %fusion.12) | data formatting | bytes 25165824 | tf_op jit(solution)/shard_map/NK,cKe->cNe/dot_general | solution.py:120
  135.6 7.1 %compare_select_fusion = f32[32,128,256]{2,0,1:T(8,128)} fusion(f32[32,384,256]{2,0,1:T(8,128)} %bitcast.107), kind=kLoop, calls=%fused_computation.2 | loop fusion | flops 16777216 | bytes 16777216 | tf_op jit(solution)/shard_map/jit(_where)/select_n | solution.py:95
  142.7 10.9 %reshape.53 = f32[32,16,8,8,32]{4,3,0,2,1:T(8,128)} reshape(f32[32,128,256]{2,0,1:T(8,128)} %compare_select_fusion) | data formatting | bytes 8388608 | tf_op jit(solution)/shard_map/reshape | solution.py:162
  153.7 11.8 %copy.187 = f32[32,16,8,8,32]{4,3,2,0,1:T(8,128)} copy(f32[32,16,8,8,32]{4,3,0,2,1:T(8,128)} %reshape.53) | data formatting | bytes 8388608 | tf_op jit(solution)/shard_map/reshape | solution.py:162
  165.4 16.0 %reshape.67 = f32[16,1,65536]{2,1,0:T(1,128)} reshape(f32[16,32,8,8,32]{4,3,2,1,0:T(8,128)} %bitcast.100) | data formatting | bytes 8388608
  182.8 6.0 all-to-all-start.3
  188.8 21.4 %fusion.14 = f32[32,256,384]{2,1,0:T(8,128)} fusion(bf16[384,384,1]{1,0,2:T(8,128)(2,1)S(1)} %copy-done.8, bf16[32,384,256]{2,0,1:T(8,128)(2,1)} %get-tuple-element.56), kind=kOutput, calls=%fused_computation.24 | convolution fusion | flops 2415919104 | bytes 19169280 | tf_op jit(solution)/shard_map/NK,cKe->cNe/dot_general | solution.py:120
  210.3 12.7 %copy.131 = f32[32,256,384]{1,0,2:T(8,128)} copy(f32[32,256,384]{2,1,0:T(8,128)} %fusion.14) | data formatting | bytes 25165824 | tf_op jit(solution)/shard_map/NK,cKe->cNe/dot_general | solution.py:120
  223.0 7.1 %compare_select_fusion.3 = f32[32,128,256]{2,0,1:T(8,128)} fusion(f32[32,384,256]{2,0,1:T(8,128)} %bitcast.108), kind=kLoop, calls=%fused_computation.5 | loop fusion | flops 16777216 | bytes 16777216 | tf_op jit(solution)/shard_map/jit(_where)/select_n | solution.py:95
  230.0 10.8 %reshape.51 = f32[32,16,8,8,32]{4,3,0,2,1:T(8,128)} reshape(f32[32,128,256]{2,0,1:T(8,128)} %compare_select_fusion.3) | data formatting | bytes 8388608 | tf_op jit(solution)/shard_map/reshape | solution.py:162
  240.9 11.8 %copy.188 = f32[32,16,8,8,32]{4,3,2,0,1:T(8,128)} copy(f32[32,16,8,8,32]{4,3,0,2,1:T(8,128)} %reshape.51) | data formatting | bytes 8388608 | tf_op jit(solution)/shard_map/reshape | solution.py:162
  252.7 16.0 %reshape.69 = f32[16,1,65536]{2,1,0:T(1,128)} reshape(f32[16,32,8,8,32]{4,3,2,1,0:T(8,128)} %bitcast.101) | data formatting | bytes 8388608
  268.7 17.5 %all-to-all-start.2 = ((f32[16,1,65536]{2,1,0:T(1,128)}), f32[16,1,65536]{2,1,0:T(1,128)}, u32[]{:S(2)}, u32[]{:S(2)}) async-start(f32[16,1,65536]{2,1,0:T(1,128)} %reshape.69), calls=%async_computation.2 | async-start | bytes 8388608 | tf_op jit(solution)/shard_map/all_to_all | solution.py:164
  286.2 8.0 %reduce.1 = f32[2,262144]{1,0:T(2,128)S(1)} reduce(f32[2,1,262144]{2,1,0:T(1,128)} %copy-done.1, f32[]{:T(128)} %broadcast.302), dimensions={1}, to_apply=%all_to_all.19.reduce_sub_computation | reduce | bytes 4194308 | tf_op jit(solution)/shard_map/all_to_all | solution.py:169
  294.2 6.5 reshape.66
  300.7 8.3 %bitcast_bitcast_fusion = f32[32,8,16,8,2,8]{0,5,3,1,2,4:T(8,128)} fusion(f32[2,16,8,8,8,32]{5,4,3,2,1,0:T(8,128)} %reshape.66), kind=kLoop, calls=%fused_computation.141 | loop fusion | bytes 4194304 | tf_op jit(solution)/shard_map/transpose | solution.py:170
  309.0 26.9 %copy.117 = f32[32,8,16,8,2,8]{3,2,5,4,1,0:T(8,128)} copy(f32[32,8,16,8,2,8]{0,5,3,1,2,4:T(8,128)} %bitcast_bitcast_fusion) | data formatting | bytes 4194304 | tf_op jit(solution)/shard_map/transpose | solution.py:170
  335.9 22.9 %reshape.50 = f32[256,128,16]{1,2,0:T(8,128)S(1)} reshape(f32[32,8,16,8,2,8]{3,2,5,4,1,0:T(8,128)} %copy.117) | data formatting | bytes 4194304 | tf_op jit(solution)/shard_map/reshape | solution.py:171
  370.8 13.6 %reduce.2 = f32[16,65536]{1,0:T(8,128)} reduce(f32[16,1,65536]{2,1,0:T(1,128)} %all-to-all-done.3, f32[]{:T(128)} %broadcast.302), dimensions={1}, to_apply=%all_to_all.21.reduce_sub_computation | reduce | bytes 8388612 | tf_op jit(solution)/shard_map/all_to_all | solution.py:164
  384.4 15.2 %reshape.68 = f32[16,32,8,8,32]{4,3,2,1,0:T(8,128)} reshape(f32[16,65536]{1,0:T(8,128)} %reduce.2) | data formatting | bytes 8388608
  399.6 11.8 %copy.147 = f32[32,8,16,8,32]{4,3,2,1,0:T(8,128)} copy(f32[32,8,16,8,32]{4,3,1,0,2:T(8,128)} %bitcast.102) | data formatting | bytes 8388608 | tf_op jit(solution)/shard_map/transpose | solution.py:176
  411.4 11.6 %copy.149 = f32[256,128,32]{1,2,0:T(8,128)} copy(f32[256,128,32]{2,1,0:T(8,128)} %bitcast.103) | data formatting | bytes 8388608 | tf_op jit(solution)/shard_map/reshape | solution.py:176
  427.4 13.6 %reduce.3 = f32[16,65536]{1,0:T(8,128)} reduce(f32[16,1,65536]{2,1,0:T(1,128)} %all-to-all-done.2, f32[]{:T(128)} %broadcast.302), dimensions={1}, to_apply=%all_to_all.20.reduce_sub_computation | reduce | bytes 8388612 | tf_op jit(solution)/shard_map/all_to_all | solution.py:164
  441.0 15.4 %reshape.70 = f32[16,32,8,8,32]{4,3,2,1,0:T(8,128)} reshape(f32[16,65536]{1,0:T(8,128)} %reduce.3) | data formatting | bytes 8388608
  456.4 11.8 %copy.133 = f32[32,8,16,8,32]{4,3,2,1,0:T(8,128)} copy(f32[32,8,16,8,32]{4,3,1,0,2:T(8,128)} %bitcast.104) | data formatting | bytes 8388608 | tf_op jit(solution)/shard_map/transpose | solution.py:176
  468.2 11.6 %copy.135 = f32[256,128,32]{1,2,0:T(8,128)} copy(f32[256,128,32]{2,1,0:T(8,128)} %bitcast.105) | data formatting | bytes 8388608 | tf_op jit(solution)/shard_map/reshape | solution.py:176
  479.8 4.8 subtract_convert_fusion.5
  484.5 10.1 %fusion = f32[256,80,32]{1,2,0:T(8,128)S(1)} fusion(bf16[256,384,80]{1,2,0:T(8,128)(2,1)} %pad_dynamic-update-slice_fusion, bf16[256,128,32]{1,2,0:T(8,128)(2,1)} %get-tuple-element.20, bf16[256,128,32]{1,2,0:T(8,128)(2,1)} %get-tuple-element.19, bf16[256,128,32]{1,2,0:T(8,128)(2,1)} %get-tuple-element.18), kind=kOutput, calls=%fused_computation.9 | convolution fusion | flops 522190848 | bytes 24641536 | tf_op jit(solution)/shard_map/pKa,pKj->paj/dot_general | solution.py:143
  494.6 9.4 %fusion.62 = (f32[256,16,32]{1,2,0:T(8,128)}, f32[256,16,32]{1,2,0:T(8,128)}, f32[256,16,32]{1,2,0:T(8,128)}, f32[256,16,32]{1,2,0:T(8,128)}, f32[256,16,32]{1,2,0:T(8,128)}) fusion(f32[256,80,32]{1,2,0:T(8,128)S(1)} %fusion), kind=kLoop, calls=%fused_computation.139 | loop fusion | bytes 5242880 | tf_op jit(solution)/shard_map/slice | solution.py:145
  511.6 4.5 copy.166
  516.1 4.7 copy.165
  520.8 4.5 copy.164
  525.3 9.5 %fusion.6 = f32[256,80,32]{1,2,0:T(8,128)S(1)} fusion(bf16[256,384,80]{1,2,0:T(8,128)(2,1)} %pad_dynamic-update-slice_fusion, bf16[256,128,32]{1,2,0:T(8,128)(2,1)} %get-tuple-element.32, bf16[256,128,32]{1,2,0:T(8,128)(2,1)} %get-tuple-element.31, bf16[256,128,32]{1,2,0:T(8,128)(2,1)S(1)} %get-tuple-element.30), kind=kOutput, calls=%fused_computation.16 | convolution fusion | flops 522190848 | bytes 24641536 | tf_op jit(solution)/shard_map/pKa,pKj->paj/dot_general | solution.py:143
  534.8 9.4 %fusion.63 = (f32[256,16,32]{1,2,0:T(8,128)}, f32[256,16,32]{1,2,0:T(8,128)}, f32[256,16,32]{1,2,0:T(8,128)}, f32[256,16,32]{1,2,0:T(8,128)}, f32[256,16,32]{1,2,0:T(8,128)}) fusion(f32[256,80,32]{1,2,0:T(8,128)S(1)} %fusion.6), kind=kLoop, calls=%fused_computation.140 | loop fusion | bytes 5242880 | tf_op jit(solution)/shard_map/slice | solution.py:145
  552.5 4.5 copy.171
  557.0 4.6 copy.170
  561.6 4.9 copy.169
  569.2 16.0 %all_to_all.30 = f32[256,2,8,64]{0,3,2,1:T(8,128)S(1)} all-to-all(f32[256,2,8,64]{0,3,2,1:T(8,128)S(1)} %bitcast.120), channel_id=1, replica_groups=mesh['grp'=2,'pt'=16] {'grp'}, dimensions={1} | all-to-all | bytes 2097152 | tf_op jit(solution)/shard_map/all_to_all | solution.py:183
  585.4 11.2 %reshape.56 = f32[32,8,8,16,8]{1,0,4,3,2:T(8,128)} reshape(f32[256,8,2,64]{0,3,2,1:T(8,128)S(1)} %copy.155) | data formatting | bytes 2097152 | tf_op jit(solution)/shard_map/reshape | solution.py:184
  596.6 11.5 %copy.156 = f32[16,32,8,8,8]{1,4,3,2,0:T(8,128)} copy(f32[16,32,8,8,8]{2,1,4,0,3:T(8,128)} %bitcast.106) | data formatting | bytes 2097152 | tf_op jit(solution)/shard_map/transpose | solution.py:185
  611.9 31.9 %all_to_all.31 = f32[16,1,16384]{2,1,0:T(1,128)S(1)} all-to-all(f32[16,1,16384]{2,1,0:T(1,128)S(1)} %reshape.71), channel_id=1, replica_groups=mesh['grp'=2,'pt'=16] {'pt'}, dimensions={0} | all-to-all | bytes 2097152 | tf_op jit(solution)/shard_map/all_to_all | solution.py:186
  (123 shorter events, 109.3 us)
Async XLA Ops:
  0.0 3.1 copy-start.22
  0.0 3.1 copy-start.23
  0.0 3.1 copy-start.24
  0.0 3.1 copy-start.25
  0.0 3.1 copy-start.26
  0.0 3.1 copy-start.27
  0.0 3.1 copy-start.28
  0.1 3.1 copy-start.29
  0.1 3.1 copy-start.30
  3.2 2.4 copy-start.8
  16.5 59.2 %all-to-all-start = ((f32[16,1,16384]{2,1,0:T(1,128)}), f32[16,1,16384]{2,1,0:T(1,128)}, u32[]{:S(2)}, u32[]{:S(2)}) async-start(f32[16,1,16384]{2,1,0:T(1,128)} %reshape.63), calls=%async_computation | async-start | bytes 2097152 | tf_op jit(solution)/shard_map/all_to_all | solution.py:164
  33.5 2.0 copy-start.2
  38.5 3.0 copy-start.10
  41.5 1.8 copy-start.3
  41.5 1.8 copy-start.4
  43.3 1.8 copy-start.11
  68.8 1.6 copy-start
  97.2 84.3 %all-to-all-start.1 = ((f32[2,1,262144]{2,1,0:T(1,128)}), f32[2,1,262144]{2,1,0:T(1,128)S(1)}, u32[]{:S(2)}, u32[]{:S(2)}) async-start(f32[2,1,262144]{2,1,0:T(1,128)} %reshape.65), calls=%async_computation.1 | async-start | bytes 4194304 | tf_op jit(solution)/shard_map/all_to_all | solution.py:169
  181.4 1.4 copy-start.1
  182.8 85.9 %all-to-all-start.3 = ((f32[16,1,65536]{2,1,0:T(1,128)}), f32[16,1,65536]{2,1,0:T(1,128)}, u32[]{:S(2)}, u32[]{:S(2)}) async-start(f32[16,1,65536]{2,1,0:T(1,128)} %reshape.67), calls=%async_computation.3 | async-start | bytes 8388608 | tf_op jit(solution)/shard_map/all_to_all | solution.py:164
  268.7 158.7 %all-to-all-start.2 = ((f32[16,1,65536]{2,1,0:T(1,128)}), f32[16,1,65536]{2,1,0:T(1,128)}, u32[]{:S(2)}, u32[]{:S(2)}) async-start(f32[16,1,65536]{2,1,0:T(1,128)} %reshape.69), calls=%async_computation.2 | async-start | bytes 8388608 | tf_op jit(solution)/shard_map/all_to_all | solution.py:164
  557.0 9.5 %copy-start.5 = (f32[256,16,32]{0,2,1:T(8,128)S(1)}, f32[256,16,32]{0,2,1:T(8,128)}, u32[]{:S(2)}) copy-start(f32[256,16,32]{0,2,1:T(8,128)} %copy.166) | copy-start | bytes 1572868
  557.0 9.5 %copy-start.6 = (f32[256,16,32]{0,2,1:T(8,128)S(1)}, f32[256,16,32]{0,2,1:T(8,128)}, u32[]{:S(2)}) copy-start(f32[256,16,32]{0,2,1:T(8,128)} %copy.165) | copy-start | bytes 1572868
  557.0 9.5 %copy-start.7 = (f32[256,16,32]{0,2,1:T(8,128)S(1)}, f32[256,16,32]{0,2,1:T(8,128)}, u32[]{:S(2)}) copy-start(f32[256,16,32]{0,2,1:T(8,128)} %copy.164) | copy-start | bytes 1572868
  653.8 1.0 copy-start.9
  654.3 1.6 copy-start.13
  654.4 1.6 copy-start.14
  654.4 1.6 copy-start.15
  654.4 1.6 copy-start.16
  654.4 1.6 copy-start.17
  654.4 1.6 copy-start.18
  654.4 1.6 copy-start.19
  654.4 1.6 copy-start.20
  654.4 1.6 copy-start.21
  656.0 2.8 copy-start.12

commit v5 on v3

--- a/solution.py
+++ b/solution.py
@@ -163,9 +163,9 @@
 
         def to_points(x, rows):
             ev = forward(x.reshape(rows * kl, -1), tables)
-            ev = ev.reshape(n_pt, d_local, rows, kl, FIRST)
+            ev = ev.reshape(n_pt, d_local * rows * kl * FIRST // 128, 128)
             ev = lax.all_to_all(ev, "pt", split_axis=0, concat_axis=0, tiled=False)
-            return ev
+            return ev.reshape(n_pt, d_local, rows, kl, FIRST)
 
         left_pts = to_points(left_factor, il)
         left_pts = jnp.broadcast_to(left_pts[None], (n_grp,) + left_pts.shape)

time: 612 us -> 585 us (0.956)
  other arithmetic: 105 us -> 76.5 us
    unnamed x119 -> x113, local copies, waits for them, and re-layouts: 162 us -> 105 us
    reshape x0 -> x9, local copies, waits for them, and re-layouts: none -> 53.3 us  [the longest x5 32.1 us: to_points(): ev = ev.reshape(n_pt, d_local * rows * kl * FIRST // 128, 128)]
    all_to_all x5 -> x0, other arithmetic: 31.8 us -> none  [to_points(): ev = lax.all_to_all(ev, 'pt', split_axis=0, concat_axis=0, tiled=False)]
    broadcast_in_dim x0 -> x2, local copies, waits for them, and re-layouts: none -> 7.52 us  [body(): left_pts = jnp.broadcast_to(left_pts[None], (n_grp,) + left_pts.shape)]
  transfers between devices with their start and end apart: 6 -> 6, of which waited for: 2 -> 2; matrix products, arithmetic and copies ran while one was open for 58% -> 57% of each run, Pallas kernels for 0% -> 0%
where the time goes in v5:
time: 585 us; the launch traced here: 577 us
  local copies, waits for them, and re-layouts  326 us (56%)
  other arithmetic  76.5 us (13%)
  matrix products  60.6 us (10%)
  blocking collectives  47.9 us (8%)
  starting transfers between devices  41.5 us (7%)
  waiting for transfers between devices  22.3 us (4%)
    unnamed x113, local copies, waits for them, and re-layouts  105 us
    transpose x4, local copies, waits for them, and re-layouts, body(): jnp.transpose(right_pts, (1, 4, 2, 0, 3))  45.9 us
    convert_element_type x20, other arithmetic, limbs_bf16(): piece.astype(jnp.bfloat16)  41.6 us
    all_to_all x5, starting transfers between devices, to_points(): ev = lax.all_to_all(ev, 'pt', split_axis=0, concat_axis=0, tiled=False)  37.6 us
    dot_general x4, matrix products, multiply_points(): jnp.einsum('pak,pjk->paj', toeplitz, right_limbs, preferred_element_type=...  35.8 us
    reshape x8, local copies, waits for them, and re-layouts, body(): jnp.transpose(right_pts, (1, 4, 2, 0, 3))  33.9 us
    reshape x5, local copies, waits for them, and re-layouts, to_points(): ev = ev.reshape(n_pt, d_local * rows * kl * FIRST // 128, 128)  32.1 us
    all_to_all x1, blocking collectives, body(): prod = lax.all_to_all(prod, 'pt', split_axis=0, concat_axis=0, tiled=False)  31.4 us
  transfers between devices with their start and end apart: 6, of which 2 were waited for; matrix products, arithmetic and copies ran while one was open for 57% of the time, Pallas kernels for 0%

profile of v5, /device:TPU:1, one launch (start us, length us, event | category | flops | bytes accessed | tf_op | source)
XLA Modules:
  0.0 576.6 jit_solution(4009304272780414944)
XLA Ops:
  7.3 4.5 copy.99
  15.9 7.7 %all-to-all-start = ((f32[16,128,128]{2,1,0:T(8,128)}), f32[16,128,128]{2,1,0:T(8,128)S(1)}, u32[]{:S(2)}, u32[]{:S(2)}) async-start(f32[16,128,128]{2,1,0:T(8,128)} %reshape.75), calls=%async_computation | async-start | bytes 2097152 | tf_op jit(solution)/shard_map/all_to_all | solution.py:167
  29.1 4.2 subtract_convert_fusion.3
  37.7 4.7 copy.138
  42.5 7.1 %reshape.86 = f32[16,256,128]{2,1,0:T(8,128)} reshape(f32[128,128,32]{2,1,0:T(8,128)} %copy.138) | data formatting | bytes 4194304 | tf_op jit(solution)/shard_map/reshape | solution.py:166
  60.6 4.6 copy.100
  65.3 4.7 broadcast_bitcast_fusion
  69.9 6.9 %reshape.100 = f32[2,1,262144]{2,1,0:T(1,128)} reshape(f32[2,8,16,8,8,32]{5,4,3,2,1,0:T(8,128)} %broadcast_bitcast_fusion) | data formatting | bytes 4194304
  89.4 16.4 %all-to-all-done.1 = f32[2,1,262144]{2,1,0:T(1,128)S(1)} async-done(((f32[2,1,262144]{2,1,0:T(1,128)}), f32[2,1,262144]{2,1,0:T(1,128)S(1)}, u32[]{:S(2)}, u32[]{:S(2)}) %all-to-all-start.1) | async-done | bytes 2097184 | tf_op jit(solution)/shard_map/all_to_all | solution.py:172
  107.1 6.4 %all-to-all-start.5 = ((f32[16,256,128]{2,1,0:T(8,128)}), f32[16,256,128]{2,1,0:T(8,128)S(1)}, u32[]{:S(2)}, u32[]{:S(2)}) async-start(f32[16,256,128]{2,1,0:T(8,128)} %reshape.86), calls=%async_computation.5 | async-start | bytes 4194304 | tf_op jit(solution)/shard_map/all_to_all | solution.py:167
  113.6 16.3 %subtract_convert_fusion.15 = (bf16[128,32,128]{2,1,0:T(8,128)(2,1)}, f32[128,32,128]{2,1,0:T(8,128)}, bf16[128,32,128]{2,1,0:T(8,128)(2,1)}, f32[128,32,128]{2,...) fusion(f32[32,128]{1,0:T(8,128)S(1)} %copy-done.20, f32[32,128]{1,0:T(8,128)S(1)} %copy-done.21, ...), kind=kLoop, calls=%fused_computation.101 | loop fusion | flops 94371840 | bytes 28459008 | tf_op jit(solution)/shard_map/convert_element_type | solution.py:105
  135.7 6.4 %copy.127 = f32[128,128,32]{2,1,0:T(8,128)} copy(f32[128,128,32]{1,0,2:T(8,128)} %compare_select_fusion.3) | data formatting | bytes 4194304 | tf_op jit(solution)/shard_map/jit(_where)/select_n | solution.py:95
  142.1 7.0 %reshape.83 = f32[16,256,128]{2,1,0:T(8,128)} reshape(f32[128,128,32]{2,1,0:T(8,128)} %copy.127) | data formatting | bytes 4194304 | tf_op jit(solution)/shard_map/reshape | solution.py:166
  149.0 6.0 %all-to-all-done.5 = f32[16,256,128]{2,1,0:T(8,128)S(1)} async-done(((f32[16,256,128]{2,1,0:T(8,128)}), f32[16,256,128]{2,1,0:T(8,128)S(1)}, u32[]{:S(2)}, u32[]{:S(2)}) %all-to-all-start.5) | async-done | bytes 2097184 | tf_op jit(solution)/shard_map/all_to_all | solution.py:167
  156.4 11.2 %all-to-all-start.4 = ((f32[16,256,128]{2,1,0:T(8,128)}), f32[16,256,128]{2,1,0:T(8,128)}, u32[]{:S(2)}, u32[]{:S(2)}) async-start(f32[16,256,128]{2,1,0:T(8,128)} %reshape.83), calls=%async_computation.4 | async-start | bytes 4194304 | tf_op jit(solution)/shard_map/all_to_all | solution.py:167
  177.0 6.4 %copy.116 = f32[128,128,32]{2,1,0:T(8,128)} copy(f32[128,128,32]{1,0,2:T(8,128)} %compare_select_fusion.6) | data formatting | bytes 4194304 | tf_op jit(solution)/shard_map/jit(_where)/select_n | solution.py:95
  183.4 7.0 %reshape.80 = f32[16,256,128]{2,1,0:T(8,128)} reshape(f32[128,128,32]{2,1,0:T(8,128)} %copy.116) | data formatting | bytes 4194304 | tf_op jit(solution)/shard_map/reshape | solution.py:166
  193.8 4.7 copy.105
  198.6 7.0 %reshape.77 = f32[16,256,128]{2,1,0:T(8,128)} reshape(f32[128,128,32]{2,1,0:T(8,128)} %copy.105) | data formatting | bytes 4194304 | tf_op jit(solution)/shard_map/reshape | solution.py:166
  206.1 8.5 %reduce = f32[2,262144]{1,0:T(2,128)S(1)} reduce(f32[2,1,262144]{2,1,0:T(1,128)} %copy-done.3, f32[]{:T(128)} %broadcast.369), dimensions={1}, to_apply=%all_to_all.25.reduce_sub_computation | reduce | bytes 4194308 | tf_op jit(solution)/shard_map/all_to_all | solution.py:172
  214.6 6.5 %reshape.101 = f32[2,8,16,8,8,32]{5,4,3,2,1,0:T(8,128)} reshape(f32[2,262144]{1,0:T(2,128)S(1)} %reduce) | data formatting | bytes 4194304
  221.1 6.0 %all-to-all-start.3 = ((f32[16,256,128]{2,1,0:T(8,128)}), f32[16,256,128]{2,1,0:T(8,128)}, u32[]{:S(2)}, u32[]{:S(2)}) async-start(f32[16,256,128]{2,1,0:T(8,128)} %reshape.80), calls=%async_computation.3 | async-start | bytes 4194304 | tf_op jit(solution)/shard_map/all_to_all | solution.py:167
  227.1 8.4 %bitcast_bitcast_fusion = f32[8,32,2,8,16,8]{1,0,5,4,3,2:T(8,128)} fusion(f32[2,8,16,8,8,32]{5,4,3,2,1,0:T(8,128)} %reshape.101), kind=kLoop, calls=%fused_computation.228 | loop fusion | bytes 4194304 | tf_op jit(solution)/shard_map/transpose | solution.py:173
  235.5 5.8 %reshape.76 = f32[256,16,128]{0,2,1:T(8,128)S(1)} reshape(f32[8,32,2,8,16,8]{1,0,5,4,3,2:T(8,128)} %bitcast_bitcast_fusion) | data formatting | bytes 4194304 | tf_op jit(solution)/shard_map/reshape | solution.py:174
  257.1 4.2 reshape.87
  261.4 11.5 %copy.139 = f32[8,32,16,16,8]{1,0,4,3,2:T(8,128)} copy(f32[8,32,16,16,8]{1,4,2,0,3:T(8,128)} %bitcast.161) | data formatting | bytes 4194304 | tf_op jit(solution)/shard_map/transpose | solution.py:179
  272.8 5.8 %reshape.88 = f32[256,16,128]{0,2,1:T(8,128)S(1)} reshape(f32[8,32,16,16,8]{1,0,4,3,2:T(8,128)} %copy.139) | data formatting | bytes 4194304 | tf_op jit(solution)/shard_map/reshape | solution.py:179
  283.2 8.9 %fusion.18 = f32[256,80,16]{1,2,0:T(8,128)S(1)} fusion(bf16[256,80,384]{2,1,0:T(8,128)(2,1)} %pad_dynamic-update-slice_fusion, bf16[256,16,128]{2,1,0:T(8,128)(2,1)S(1)} %get-tuple-element.58, bf16[256,16,128]{2,1,0:T(8,128)(2,1)S(1)} %get-tuple-element.57, bf16[256,16,128]{2,1,0:T(8,128)(2,1)S(1)} %get-tuple-element.56), kind=kOutput, calls=%fused_computation.37 | convolution fusion | flops 261095424 | bytes 20185088 | tf_op jit(solution)/shard_map/pak,pjk->paj/dot_general | solution.py:149
  292.1 5.5 fusion.112
  308.9 6.3 %reshape.84 = f32[16,8,16,8,32]{4,3,2,1,0:T(8,128)} reshape(f32[16,256,128]{2,1,0:T(8,128)} %all-to-all-done.4) | data formatting | bytes 4194304 | tf_op jit(solution)/shard_map/reshape | solution.py:168
  315.2 11.5 %copy.128 = f32[8,32,16,16,8]{1,0,4,3,2:T(8,128)} copy(f32[8,32,16,16,8]{1,4,2,0,3:T(8,128)} %bitcast.162) | data formatting | bytes 4194304 | tf_op jit(solution)/shard_map/transpose | solution.py:179
  326.7 5.8 %reshape.85 = f32[256,16,128]{0,2,1:T(8,128)S(1)} reshape(f32[8,32,16,16,8]{1,0,4,3,2:T(8,128)} %copy.128) | data formatting | bytes 4194304 | tf_op jit(solution)/shard_map/reshape | solution.py:179
  334.4 6.4 %all-to-all-start.2 = ((f32[16,256,128]{2,1,0:T(8,128)}), f32[16,256,128]{2,1,0:T(8,128)S(1)}, u32[]{:S(2)}, u32[]{:S(2)}) async-start(f32[16,256,128]{2,1,0:T(8,128)} %reshape.77), calls=%async_computation.2 | async-start | bytes 4194304 | tf_op jit(solution)/shard_map/all_to_all | solution.py:167
  343.1 8.9 %fusion.12 = f32[256,80,16]{1,2,0:T(8,128)S(1)} fusion(bf16[256,80,384]{2,1,0:T(8,128)(2,1)} %pad_dynamic-update-slice_fusion, bf16[256,16,128]{2,1,0:T(8,128)(2,1)S(1)} %get-tuple-element.48, bf16[256,16,128]{2,1,0:T(8,128)(2,1)S(1)} %get-tuple-element.47, bf16[256,16,128]{2,1,0:T(8,128)(2,1)S(1)} %get-tuple-element.46), kind=kOutput, calls=%fused_computation.30 | convolution fusion | flops 261095424 | bytes 20185088 | tf_op jit(solution)/shard_map/pak,pjk->paj/dot_general | solution.py:149
  352.0 6.2 %fusion.111 = (f32[256,16,16]{1,2,0:T(8,128)}, f32[256,16,16]{1,2,0:T(8,128)}, f32[256,16,16]{1,2,0:T(8,128)}, f32[256,16,16]{1,2,0:T(8,128)}, f32[256,16,16]{1,2,0:T(8,128)}) fusion(f32[256,80,16]{1,2,0:T(8,128)S(1)} %fusion.12), kind=kLoop, calls=%fused_computation.226 | loop fusion | bytes 2621440 | tf_op jit(solution)/shard_map/slice | solution.py:151
  374.6 6.5 %reshape.81 = f32[16,8,16,8,32]{4,3,2,1,0:T(8,128)} reshape(f32[16,256,128]{2,1,0:T(8,128)} %all-to-all-done.3) | data formatting | bytes 4194304 | tf_op jit(solution)/shard_map/reshape | solution.py:168
  381.1 11.5 %copy.117 = f32[8,32,16,16,8]{1,0,4,3,2:T(8,128)} copy(f32[8,32,16,16,8]{1,4,2,0,3:T(8,128)} %bitcast.163) | data formatting | bytes 4194304 | tf_op jit(solution)/shard_map/transpose | solution.py:179
  392.5 7.0 %reshape.82 = f32[256,16,128]{0,2,1:T(8,128)} reshape(f32[8,32,16,16,8]{1,0,4,3,2:T(8,128)} %copy.117) | data formatting | bytes 4194304 | tf_op jit(solution)/shard_map/reshape | solution.py:179
  405.0 9.1 %fusion.6 = f32[256,80,16]{1,2,0:T(8,128)S(1)} fusion(bf16[256,80,384]{2,1,0:T(8,128)(2,1)} %pad_dynamic-update-slice_fusion, bf16[256,16,128]{2,1,0:T(8,128)(2,1)S(1)} %get-tuple-element.38, bf16[256,16,128]{2,1,0:T(8,128)(2,1)S(1)} %get-tuple-element.37, bf16[256,16,128]{2,1,0:T(8,128)(2,1)S(1)} %get-tuple-element.36), kind=kOutput, calls=%fused_computation.23 | convolution fusion | flops 261095424 | bytes 20185088 | tf_op jit(solution)/shard_map/pak,pjk->paj/dot_general | solution.py:149
  414.0 6.2 %fusion.110 = (f32[256,16,16]{1,2,0:T(8,128)}, f32[256,16,16]{1,2,0:T(8,128)}, f32[256,16,16]{1,2,0:T(8,128)}, f32[256,16,16]{1,2,0:T(8,128)}, f32[256,16,16]{1,2,0:T(8,128)}) fusion(f32[256,80,16]{1,2,0:T(8,128)S(1)} %fusion.6), kind=kLoop, calls=%fused_computation.225 | loop fusion | bytes 2621440 | tf_op jit(solution)/shard_map/slice | solution.py:151
  436.5 4.2 reshape.78
  440.8 11.5 %copy.106 = f32[8,32,16,16,8]{1,0,4,3,2:T(8,128)} copy(f32[8,32,16,16,8]{1,4,2,0,3:T(8,128)} %bitcast.164) | data formatting | bytes 4194304 | tf_op jit(solution)/shard_map/transpose | solution.py:179
  452.3 6.0 %reshape.79 = f32[256,16,128]{0,2,1:T(8,128)S(1)} reshape(f32[8,32,16,16,8]{1,0,4,3,2:T(8,128)} %copy.106) | data formatting | bytes 4194304 | tf_op jit(solution)/shard_map/reshape | solution.py:179
  462.6 8.9 %fusion = f32[256,80,16]{1,2,0:T(8,128)S(1)} fusion(bf16[256,80,384]{2,1,0:T(8,128)(2,1)} %pad_dynamic-update-slice_fusion, bf16[256,16,128]{2,1,0:T(8,128)(2,1)S(1)} %get-tuple-element.28, bf16[256,16,128]{2,1,0:T(8,128)(2,1)S(1)} %get-tuple-element.27, bf16[256,16,128]{2,1,0:T(8,128)(2,1)S(1)} %get-tuple-element.26), kind=kOutput, calls=%fused_computation.16 | convolution fusion | flops 261095424 | bytes 20185088 | tf_op jit(solution)/shard_map/pak,pjk->paj/dot_general | solution.py:149
  471.5 5.5 fusion.109
  495.8 16.4 %all_to_all.40 = f32[256,2,8,64]{0,3,2,1:T(8,128)S(1)} all-to-all(f32[256,2,8,64]{0,3,2,1:T(8,128)S(1)} %bitcast.166), channel_id=1, replica_groups=mesh['grp'=2,'pt'=16] {'grp'}, dimensions={1} | all-to-all | bytes 2097152 | tf_op jit(solution)/shard_map/all_to_all | solution.py:186
  514.9 4.8 copy_bitcast_fusion
  523.6 31.4 %all_to_all.41 = f32[16,1,16384]{2,1,0:T(1,128)S(1)} all-to-all(f32[16,1,16384]{2,1,0:T(1,128)S(1)} %reshape.102), channel_id=1, replica_groups=mesh['grp'=2,'pt'=16] {'pt'}, dimensions={0} | all-to-all | bytes 2097152 | tf_op jit(solution)/shard_map/all_to_all | solution.py:189
  (179 shorter events, 191.2 us)
Async XLA Ops:
  0.0 1.5 copy-start.19
  1.4 0.7 copy-start.20
  1.4 0.7 copy-start.21
  1.4 0.7 copy-start.22
  1.4 0.7 copy-start.23
  1.4 0.7 copy-start.24
  1.4 0.7 copy-start.25
  1.4 0.7 copy-start.26
  1.4 0.8 copy-start.27
  1.5 0.8 copy-start.28
  4.6 1.0 copy-start.4
  15.9 41.8 %all-to-all-start = ((f32[16,128,128]{2,1,0:T(8,128)}), f32[16,128,128]{2,1,0:T(8,128)S(1)}, u32[]{:S(2)}, u32[]{:S(2)}) async-start(f32[16,128,128]{2,1,0:T(8,128)} %reshape.75), calls=%async_computation | async-start | bytes 2097152 | tf_op jit(solution)/shard_map/all_to_all | solution.py:167
  42.5 7.1 %copy-start.10 = (f32[16,8,16,128]{3,1,2,0:T(8,128)S(1)}, f32[16,8,16,128]{3,1,2,0:T(8,128)}, u32[]{:S(2)}) copy-start(f32[16,8,16,128]{3,1,2,0:T(8,128)} %get-tuple-element.17) | copy-start | bytes 3145732
  49.5 1.2 copy-start.9
  49.5 1.5 copy-start.8
  76.9 3.9 copy-start.7
  76.9 28.9 %all-to-all-start.1 = ((f32[2,1,262144]{2,1,0:T(1,128)}), f32[2,1,262144]{2,1,0:T(1,128)S(1)}, u32[]{:S(2)}, u32[]{:S(2)}) async-start(f32[2,1,262144]{2,1,0:T(1,128)} %reshape.100), calls=%async_computation.1 | async-start | bytes 4194304 | tf_op jit(solution)/shard_map/all_to_all | solution.py:172
  80.8 1.0 copy-start.11
  80.8 1.2 copy-start.12
  80.8 1.3 copy-start.13
  105.8 1.4 copy-start.3
  107.1 47.9 %all-to-all-start.5 = ((f32[16,256,128]{2,1,0:T(8,128)}), f32[16,256,128]{2,1,0:T(8,128)S(1)}, u32[]{:S(2)}, u32[]{:S(2)}) async-start(f32[16,256,128]{2,1,0:T(8,128)} %reshape.86), calls=%async_computation.5 | async-start | bytes 4194304 | tf_op jit(solution)/shard_map/all_to_all | solution.py:167
  155.0 1.3 copy-start
  156.4 64.7 %all-to-all-start.4 = ((f32[16,256,128]{2,1,0:T(8,128)}), f32[16,256,128]{2,1,0:T(8,128)}, u32[]{:S(2)}, u32[]{:S(2)}) async-start(f32[16,256,128]{2,1,0:T(8,128)} %reshape.83), calls=%async_computation.4 | async-start | bytes 4194304 | tf_op jit(solution)/shard_map/all_to_all | solution.py:167
  167.6 2.3 copy-start.2
  169.9 1.2 copy-start.5
  169.9 1.5 copy-start.6
  221.1 113.4 %all-to-all-start.3 = ((f32[16,256,128]{2,1,0:T(8,128)}), f32[16,256,128]{2,1,0:T(8,128)}, u32[]{:S(2)}, u32[]{:S(2)}) async-start(f32[16,256,128]{2,1,0:T(8,128)} %reshape.80), calls=%async_computation.3 | async-start | bytes 4194304 | tf_op jit(solution)/shard_map/all_to_all | solution.py:167
  254.8 2.3 copy-start.1
  334.4 102.1 %all-to-all-start.2 = ((f32[16,256,128]{2,1,0:T(8,128)}), f32[16,256,128]{2,1,0:T(8,128)S(1)}, u32[]{:S(2)}, u32[]{:S(2)}) async-start(f32[16,256,128]{2,1,0:T(8,128)} %reshape.77), calls=%async_computation.2 | async-start | bytes 4194304 | tf_op jit(solution)/shard_map/all_to_all | solution.py:167
  491.9 3.2 copy-start.14
  491.9 3.2 copy-start.15
  491.9 3.2 copy-start.16
  491.9 3.3 copy-start.17
  491.9 3.3 copy-start.18
  568.7 1.0 copy-start.39
  569.7 1.2 copy-start.30
  569.7 1.2 copy-start.31
  569.7 1.2 copy-start.32
  569.7 1.2 copy-start.33
  569.7 1.2 copy-start.34
  569.7 1.2 copy-start.35
  569.7 1.2 copy-start.36
  569.8 1.2 copy-start.37
  569.8 1.2 copy-start.38
  573.1 0.7 copy-start.29

commit v6 on v5

--- a/solution.py
+++ b/solution.py
@@ -114,9 +114,12 @@
     )
     z = fold3(y[:, 0:FIRST], y[:, FIRST : 2 * FIRST], y[:, 2 * FIRST :])
     z = twist(z, jnp.asarray(tables["fwd_twist"]))
-    zl = limbs_bf16(z, 2)
-    y2 = jnp.einsum(
-        "ecK,KN->Nec", zl, jnp.asarray(tables["fwd2"], jnp.bfloat16), preferred_element_type=jnp.float32
+    zl = limbs_bf16(z, 2).reshape(entries * FIRST, 3 * SECOND)
+    y2 = lax.dot_general(
+        jnp.asarray(tables["fwd2"].T, jnp.bfloat16),
+        zl,
+        (((1,), (1,)), ((), ())),
+        preferred_element_type=jnp.float32,
     )
     return fold3(y2[0:SECOND], y2[SECOND : 2 * SECOND], y2[2 * SECOND :])
 
@@ -137,20 +140,25 @@
     return out.reshape(entries, LENGTH)
 
 
+def balanced3(x):
+    h = jnp.floor((x + 128.0) * (1.0 / 256.0))
+    x0 = x - 256.0 * h
+    h2 = jnp.floor((h + 128.0) * (1.0 / 256.0))
+    x1 = h - 256.0 * h2
+    return x0, x1, h2
+
+
 def multiply_points(left, right):
-    left_limbs = [v.astype(jnp.bfloat16) for v in split3(left)]
-    zero = jnp.zeros_like(left_limbs[0])
-    rows = []
-    for level in range(5):
-        pieces = [left_limbs[level - y] if 0 <= level - y < 3 else zero for y in range(3)]
-        rows.append(jnp.concatenate(pieces, axis=2))
-    toeplitz = jnp.concatenate(rows, axis=1)
+    x0, x1, x2 = split3(left)
+    zero = jnp.zeros_like(left)
+    scaled = [left, fold3(zero, x0, x1 + 256.0 * x2), fold3(zero, zero, left)]
+    limbs = [balanced3(v) for v in scaled]
+    rows = [jnp.concatenate([limbs[y][u].astype(jnp.bfloat16) for y in range(3)], axis=2) for u in range(3)]
+    stacked = jnp.concatenate(rows, axis=1)
     right_limbs = limbs_bf16(right, 2)
-    levels = jnp.einsum("pak,pjk->paj", toeplitz, right_limbs, preferred_element_type=jnp.float32)
+    levels = jnp.einsum("pak,pjk->paj", stacked, right_limbs, preferred_element_type=jnp.float32)
     n_i = left.shape[1]
-    lv = [levels[:, n * n_i : (n + 1) * n_i] for n in range(5)]
-    high = fold3(lv[2], lv[3], lv[4])
-    return fold3(lv[0], lv[1], high)
+    return fold3(levels[:, 0:n_i], levels[:, n_i : 2 * n_i], levels[:, 2 * n_i :])
 
 
 def make_body(n_grp, n_pt, n_chunks):
@@ -163,7 +171,7 @@
 
         def to_points(x, rows):
             ev = forward(x.reshape(rows * kl, -1), tables)
-            ev = ev.reshape(n_pt, d_local * rows * kl * FIRST // 128, 128)
+            ev = ev.reshape(n_pt, d_local, rows * kl * FIRST)
             ev = lax.all_to_all(ev, "pt", split_axis=0, concat_axis=0, tiled=False)
             return ev.reshape(n_pt, d_local, rows, kl, FIRST)
 

time: 585 us -> 499 us (0.85)
  local copies, waits for them, and re-layouts: 326 us -> 229 us
  waiting for transfers between devices: 22.3 us -> 44.5 us
  matrix products: 60.6 us -> 41.8 us
  other arithmetic: 76.5 us -> 82.8 us
    unnamed x113 -> x96, local copies, waits for them, and re-layouts: 105 us -> 71.8 us
    reshape x5 -> x0, local copies, waits for them, and re-layouts: 32.1 us -> none  [to_points(): ev = ev.reshape(n_pt, d_local * rows * kl * FIRST // 128, 128)]
    select_n x5 -> x0, local copies, waits for them, and re-layouts: 26.7 us -> none  [fold3(): return jnp.where(r < 0, r + float(modulus), r)]
    all_to_all x5, waiting for transfers between devices: 6 us -> 25.6 us  [to_points(): ev = lax.all_to_all(ev, 'pt', split_axis=0, concat_axis=0, tiled=False)]
    reshape x0 -> x5, other arithmetic: none -> 11.2 us  [to_points(): ev = ev.reshape(n_pt, d_local, rows * kl * FIRST)]
    dot_general x9, matrix products: 46.4 us -> 35.5 us  [the longest x4 25.4 us: multiply_points(): jnp.einsum('pak,pjk->paj', stacked, right_limbs, preferred_element_type=j...]
    slice x4, local copies, waits for them, and re-layouts: 23.4 us -> 13.5 us  [multiply_points(): return fold3(levels[:, 0:n_i], levels[:, n_i:2 * n_i], levels[:, 2 * n_i:])]
    select_n x8 -> x3, other arithmetic: 11.4 us -> 1.62 us  [fold3(): return jnp.where(r < 0, r + float(modulus), r)]
  transfers between devices with their start and end apart: 6 -> 6, of which waited for: 2 -> 2; matrix products, arithmetic and copies ran while one was open for 57% -> 50% of each run, Pallas kernels for 0% -> 0%
where the time goes in v6:
time: 499 us; the launch traced here: 493 us
  local copies, waits for them, and re-layouts  229 us (46%)
  other arithmetic  82.8 us (17%)
  blocking collectives  47.9 us (10%)
  starting transfers between devices  46.1 us (9%)
  waiting for transfers between devices  44.5 us (9%)
  matrix products  41.8 us (8%)
    unnamed x96, local copies, waits for them, and re-layouts  71.8 us
    transpose x4, local copies, waits for them, and re-layouts, body(): jnp.transpose(right_pts, (1, 4, 2, 0, 3))  46.3 us
    all_to_all x5, starting transfers between devices, to_points(): ev = lax.all_to_all(ev, 'pt', split_axis=0, concat_axis=0, tiled=False)  41.3 us
    convert_element_type x20, other arithmetic, limbs_bf16(): piece.astype(jnp.bfloat16)  40.7 us
    reshape x8, local copies, waits for them, and re-layouts, body(): jnp.transpose(right_pts, (1, 4, 2, 0, 3))  33.9 us
    all_to_all x1, blocking collectives, body(): prod = lax.all_to_all(prod, 'pt', split_axis=0, concat_axis=0, tiled=False)  31.7 us
    all_to_all x5, waiting for transfers between devices, to_points(): ev = lax.all_to_all(ev, 'pt', split_axis=0, concat_axis=0, tiled=False)  25.6 us
    dot_general x4, matrix products, multiply_points(): jnp.einsum('pak,pjk->paj', stacked, right_limbs, preferred_element_type=j...  25.4 us
  transfers between devices with their start and end apart: 6, of which 2 were waited for; matrix products, arithmetic and copies ran while one was open for 50% of the time, Pallas kernels for 0%

profile of v6, /device:TPU:1, one launch (start us, length us, event | category | flops | bytes accessed | tf_op | source)
XLA Modules:
  0.0 493.2 jit_solution(9831114731182307869)
XLA Ops:
  8.1 7.7 %all-to-all-start = ((f32[16,8,2048]{2,1,0:T(8,128)}), f32[16,8,2048]{2,1,0:T(8,128)}, u32[]{:S(2)}, u32[]{:S(2)}) async-start(f32[16,8,2048]{2,1,0:T(8,128)} %fusion.70), calls=%async_computation | async-start | bytes 2097152 | tf_op jit(solution)/shard_map/all_to_all | solution.py:175
  15.8 3.6 slice_bitcast_fusion.3
  24.1 13.3 %subtract_convert_fusion.15 = (bf16[128,32,128]{2,1,0:T(8,128)(2,1)S(1)}, f32[128,32,128]{2,1,0:T(8,128)S(1)}, bf16[128,32,128]{2,1,0:T(8,128)(2,1)S(1)}, f32[12...) fusion(f32[32,128]{1,0:T(8,128)S(1)} %copy-done.23, f32[32,128]{1,0:T(8,128)S(1)} %copy-done.21, ...), kind=kLoop, calls=%fused_computation.96 | loop fusion | flops 94371840 | bytes 28459008 | tf_op jit(solution)/shard_map/convert_element_type | solution.py:105
  40.7 3.9 broadcast_in_dim.7
  44.5 4.6 copy.94
  49.1 4.7 broadcast_bitcast_fusion
  53.8 7.2 %reshape.115 = f32[2,1,262144]{2,1,0:T(1,128)} reshape(f32[2,8,16,8,8,32]{5,4,3,2,1,0:T(8,128)} %broadcast_bitcast_fusion) | data formatting | bytes 4194304
  61.0 4.8 all-to-all-start.1
  65.8 3.7 fusion.111
  72.0 18.9 %all-to-all-done.1 = f32[2,1,262144]{2,1,0:T(1,128)} async-done(((f32[2,1,262144]{2,1,0:T(1,128)}), f32[2,1,262144]{2,1,0:T(1,128)}, u32[]{:S(2)}, u32[]{:S(2)}) %all-to-all-start.1) | async-done | bytes 2097184 | tf_op jit(solution)/shard_map/all_to_all | solution.py:180
  90.9 6.4 %all-to-all-start.2 = ((f32[16,8,4096]{2,1,0:T(8,128)}), f32[16,8,4096]{2,1,0:T(8,128)}, u32[]{:S(2)}, u32[]{:S(2)}) async-start(f32[16,8,4096]{2,1,0:T(8,128)} %fusion.24), calls=%async_computation.2 | async-start | bytes 4194304 | tf_op jit(solution)/shard_map/all_to_all | solution.py:175
  102.2 4.9 subtract_convert_fusion.3
  113.3 25.6 %all-to-all-done.2 = f32[16,8,4096]{2,1,0:T(8,128)} async-done(((f32[16,8,4096]{2,1,0:T(8,128)}), f32[16,8,4096]{2,1,0:T(8,128)}, u32[]{:S(2)}, u32[]{:S(2)}) %all-to-all-start.2) | async-done | bytes 2097184 | tf_op jit(solution)/shard_map/all_to_all | solution.py:175
  138.9 11.1 %all-to-all-start.3 = ((f32[16,8,4096]{2,1,0:T(8,128)}), f32[16,8,4096]{2,1,0:T(8,128)S(1)}, u32[]{:S(2)}, u32[]{:S(2)}) async-start(f32[16,8,4096]{2,1,0:T(8,128)} %fusion.25), calls=%async_computation.3 | async-start | bytes 4194304 | tf_op jit(solution)/shard_map/all_to_all | solution.py:175
  162.0 9.4 %reduce = f32[2,262144]{1,0:T(2,128)} reduce(f32[2,1,262144]{2,1,0:T(1,128)} %all-to-all-done.1, f32[]{:T(128)} %broadcast.447), dimensions={1}, to_apply=%all_to_all.25.reduce_sub_computation | reduce | bytes 4194308 | tf_op jit(solution)/shard_map/all_to_all | solution.py:180
  171.4 8.1 %reshape.116 = f32[2,8,16,8,8,32]{5,4,3,2,1,0:T(8,128)} reshape(f32[2,262144]{1,0:T(2,128)} %reduce) | data formatting | bytes 4194304
  179.5 8.4 %bitcast_bitcast_fusion = f32[8,32,2,8,16,8]{1,0,5,4,3,2:T(8,128)} fusion(f32[2,8,16,8,8,32]{5,4,3,2,1,0:T(8,128)} %reshape.116), kind=kLoop, calls=%fused_computation.228 | loop fusion | bytes 4194304 | tf_op jit(solution)/shard_map/transpose | solution.py:181
  187.8 7.0 %reshape.92 = f32[256,16,128]{0,2,1:T(8,128)} reshape(f32[8,32,2,8,16,8]{1,0,5,4,3,2:T(8,128)} %bitcast_bitcast_fusion) | data formatting | bytes 4194304 | tf_op jit(solution)/shard_map/reshape | solution.py:182
  197.9 6.6 %all-to-all-start.4 = ((f32[16,8,4096]{2,1,0:T(8,128)}), f32[16,8,4096]{2,1,0:T(8,128)}, u32[]{:S(2)}, u32[]{:S(2)}) async-start(f32[16,8,4096]{2,1,0:T(8,128)} %fusion.26), calls=%async_computation.4 | async-start | bytes 4194304 | tf_op jit(solution)/shard_map/all_to_all | solution.py:175
  204.5 5.5 %subtract_convert_fusion.21 = (bf16[256,16,128]{2,1,0:T(8,128)(2,1)S(1)}, bf16[256,16,128]{2,1,0:T(8,128)(2,1)S(1)}, bf16[256,16,128]{2,1,0:T(8,128)(2,1)S(1)}, ...) fusion(f32[256,16,128]{2,1,0:T(8,128)} %copy.96), kind=kLoop, calls=%fused_computation.111 | loop fusion | flops 33554432 | bytes 11534336 | tf_op jit(solution)/shard_map/convert_element_type | solution.py:156
  210.7 5.2 %maximum_maximum_fusion = bf16[256,48,384]{2,1,0:T(8,128)(2,1)} fusion(bf16[256,16,128]{2,1,0:T(8,128)(2,1)S(1)} %get-tuple-element.59, bf16[256,16,128]{2,1,0:T(8,128)(2,1)S(1)} %get-tuple-element.64, bf16[256,16,128]{2,1,0:T(8,128)(2,1)S(1)} %get-tuple-element.62, bf16[256,16,128]{2,1,0:T(8,128)(2,1)S(1)} %get-tuple-element.57, ...), kind=kLoop, calls=%fused_computation | loop fusion | flops 84934656 | bytes 18874368 | tf_op jit(solution)/shard_map/concatenate | solution.py:157
  215.9 6.4 %reshape.95 = f32[16,8,16,8,32]{4,3,2,1,0:T(8,128)} reshape(f32[16,8,4096]{2,1,0:T(8,128)} %all-to-all-done.2) | data formatting | bytes 4194304 | tf_op jit(solution)/shard_map/reshape | solution.py:176
  222.3 11.6 %copy.101 = f32[8,32,16,16,8]{1,0,4,3,2:T(8,128)} copy(f32[8,32,16,16,8]{1,4,2,0,3:T(8,128)} %bitcast.176) | data formatting | bytes 4194304 | tf_op jit(solution)/shard_map/transpose | solution.py:187
  233.9 7.0 %reshape.96 = f32[256,16,128]{0,2,1:T(8,128)} reshape(f32[8,32,16,16,8]{1,0,4,3,2:T(8,128)} %copy.101) | data formatting | bytes 4194304 | tf_op jit(solution)/shard_map/reshape | solution.py:187
  244.0 3.7 subtract_convert_fusion.13
  247.6 9.4 %all-to-all-start.5 = ((f32[16,8,4096]{2,1,0:T(8,128)}), f32[16,8,4096]{2,1,0:T(8,128)}, u32[]{:S(2)}, u32[]{:S(2)}) async-start(f32[16,8,4096]{2,1,0:T(8,128)} %fusion.27), calls=%async_computation.5 | async-start | bytes 4194304 | tf_op jit(solution)/shard_map/all_to_all | solution.py:175
  257.1 7.6 %fusion = f32[256,48,16]{1,2,0:T(8,128)S(1)} fusion(bf16[256,48,384]{2,1,0:T(8,128)(2,1)} %maximum_maximum_fusion, bf16[256,16,128]{2,1,0:T(8,128)(2,1)} %get-tuple-element.28, bf16[256,16,128]{2,1,0:T(8,128)(2,1)} %get-tuple-element.27, bf16[256,16,128]{2,1,0:T(8,128)(2,1)S(1)} %get-tuple-element.26), kind=kOutput, calls=%fused_computation.16 | convolution fusion | flops 160432128 | bytes 13369344 | tf_op jit(solution)/shard_map/pak,pjk->paj/dot_general | solution.py:159
  264.7 3.7 fusion.106
  276.1 4.8 reshape.99
  280.9 11.6 %copy.107 = f32[8,32,16,16,8]{1,0,4,3,2:T(8,128)} copy(f32[8,32,16,16,8]{1,4,2,0,3:T(8,128)} %bitcast.177) | data formatting | bytes 4194304 | tf_op jit(solution)/shard_map/transpose | solution.py:187
  292.5 6.0 %reshape.100 = f32[256,16,128]{0,2,1:T(8,128)S(1)} reshape(f32[8,32,16,16,8]{1,0,4,3,2:T(8,128)} %copy.107) | data formatting | bytes 4194304 | tf_op jit(solution)/shard_map/reshape | solution.py:187
  302.9 5.9 %fusion.6 = f32[256,48,16]{1,2,0:T(8,128)S(1)} fusion(bf16[256,48,384]{2,1,0:T(8,128)(2,1)} %maximum_maximum_fusion, bf16[256,16,128]{2,1,0:T(8,128)(2,1)S(1)} %get-tuple-element.36, bf16[256,16,128]{2,1,0:T(8,128)(2,1)S(1)} %get-tuple-element.35, bf16[256,16,128]{2,1,0:T(8,128)(2,1)S(1)} %get-tuple-element.34), kind=kOutput, calls=%fused_computation.23 | convolution fusion | flops 160432128 | bytes 13369344 | tf_op jit(solution)/shard_map/pak,pjk->paj/dot_general | solution.py:159
  308.7 3.3 fusion.107
  318.9 6.8 %reshape.103 = f32[16,8,16,8,32]{4,3,2,1,0:T(8,128)} reshape(f32[16,8,4096]{2,1,0:T(8,128)} %all-to-all-done.4) | data formatting | bytes 4194304 | tf_op jit(solution)/shard_map/reshape | solution.py:176
  325.8 11.6 %copy.113 = f32[8,32,16,16,8]{1,0,4,3,2:T(8,128)} copy(f32[8,32,16,16,8]{1,4,2,0,3:T(8,128)} %bitcast.178) | data formatting | bytes 4194304 | tf_op jit(solution)/shard_map/transpose | solution.py:187
  337.3 5.8 %reshape.104 = f32[256,16,128]{0,2,1:T(8,128)S(1)} reshape(f32[8,32,16,16,8]{1,0,4,3,2:T(8,128)} %copy.113) | data formatting | bytes 4194304 | tf_op jit(solution)/shard_map/reshape | solution.py:187
  347.5 6.0 %fusion.12 = f32[256,48,16]{1,2,0:T(8,128)S(1)} fusion(bf16[256,48,384]{2,1,0:T(8,128)(2,1)} %maximum_maximum_fusion, bf16[256,16,128]{2,1,0:T(8,128)(2,1)S(1)} %get-tuple-element.44, bf16[256,16,128]{2,1,0:T(8,128)(2,1)S(1)} %get-tuple-element.43, bf16[256,16,128]{2,1,0:T(8,128)(2,1)S(1)} %get-tuple-element.42), kind=kOutput, calls=%fused_computation.30 | convolution fusion | flops 160432128 | bytes 13369344 | tf_op jit(solution)/shard_map/pak,pjk->paj/dot_general | solution.py:159
  353.5 3.3 fusion.108
  356.8 3.3 copy.136
  365.1 6.4 %reshape.107 = f32[16,8,16,8,32]{4,3,2,1,0:T(8,128)} reshape(f32[16,8,4096]{2,1,0:T(8,128)} %all-to-all-done.5) | data formatting | bytes 4194304 | tf_op jit(solution)/shard_map/reshape | solution.py:176
  371.5 11.6 %copy.119 = f32[8,32,16,16,8]{1,0,4,3,2:T(8,128)} copy(f32[8,32,16,16,8]{1,4,2,0,3:T(8,128)} %bitcast.179) | data formatting | bytes 4194304 | tf_op jit(solution)/shard_map/transpose | solution.py:187
  383.1 5.8 %reshape.108 = f32[256,16,128]{0,2,1:T(8,128)S(1)} reshape(f32[8,32,16,16,8]{1,0,4,3,2:T(8,128)} %copy.119) | data formatting | bytes 4194304 | tf_op jit(solution)/shard_map/reshape | solution.py:187
  393.5 5.9 %fusion.18 = f32[256,48,16]{1,2,0:T(8,128)S(1)} fusion(bf16[256,48,384]{2,1,0:T(8,128)(2,1)} %maximum_maximum_fusion, bf16[256,16,128]{2,1,0:T(8,128)(2,1)S(1)} %get-tuple-element.52, bf16[256,16,128]{2,1,0:T(8,128)(2,1)S(1)} %get-tuple-element.51, bf16[256,16,128]{2,1,0:T(8,128)(2,1)S(1)} %get-tuple-element.50), kind=kOutput, calls=%fused_computation.37 | convolution fusion | flops 160432128 | bytes 13369344 | tf_op jit(solution)/shard_map/pak,pjk->paj/dot_general | solution.py:159
  405.8 3.3 copy.140
  412.7 16.2 %all_to_all.40 = f32[256,2,8,64]{0,3,2,1:T(8,128)S(1)} all-to-all(f32[256,2,8,64]{0,3,2,1:T(8,128)S(1)} %bitcast.186), channel_id=1, replica_groups=mesh['grp'=2,'pt'=16] {'grp'}, dimensions={1} | all-to-all | bytes 2097152 | tf_op jit(solution)/shard_map/all_to_all | solution.py:194
  431.5 4.8 copy_bitcast_fusion
  436.3 3.9 reshape.117
  440.2 31.7 %all_to_all.41 = f32[16,1,16384]{2,1,0:T(1,128)S(1)} all-to-all(f32[16,1,16384]{2,1,0:T(1,128)S(1)} %reshape.117), channel_id=1, replica_groups=mesh['grp'=2,'pt'=16] {'pt'}, dimensions={0} | all-to-all | bytes 2097152 | tf_op jit(solution)/shard_map/all_to_all | solution.py:197
  (149 shorter events, 114.3 us)
Async XLA Ops:
  0.0 1.5 copy-start.12
  1.4 0.7 copy-start.13
  1.4 0.7 copy-start.14
  1.4 0.7 copy-start.15
  1.4 0.7 copy-start.16
  1.4 0.7 copy-start.17
  1.4 0.7 copy-start.18
  1.4 0.7 copy-start.19
  1.4 0.8 copy-start.21
  1.5 0.8 copy-start.23
  4.6 1.0 copy-start.1
  8.1 32.6 %all-to-all-start = ((f32[16,8,2048]{2,1,0:T(8,128)}), f32[16,8,2048]{2,1,0:T(8,128)}, u32[]{:S(2)}, u32[]{:S(2)}) async-start(f32[16,8,2048]{2,1,0:T(8,128)} %fusion.70), calls=%async_computation | async-start | bytes 2097152 | tf_op jit(solution)/shard_map/all_to_all | solution.py:175
  61.0 29.9 %all-to-all-start.1 = ((f32[2,1,262144]{2,1,0:T(1,128)}), f32[2,1,262144]{2,1,0:T(1,128)}, u32[]{:S(2)}, u32[]{:S(2)}) async-start(f32[2,1,262144]{2,1,0:T(1,128)} %reshape.115), calls=%async_computation.1 | async-start | bytes 4194304 | tf_op jit(solution)/shard_map/all_to_all | solution.py:180
  90.9 48.0 %all-to-all-start.2 = ((f32[16,8,4096]{2,1,0:T(8,128)}), f32[16,8,4096]{2,1,0:T(8,128)}, u32[]{:S(2)}, u32[]{:S(2)}) async-start(f32[16,8,4096]{2,1,0:T(8,128)} %fusion.24), calls=%async_computation.2 | async-start | bytes 4194304 | tf_op jit(solution)/shard_map/all_to_all | solution.py:175
  97.4 2.0 copy-start
  101.2 1.0 copy-start.20
  101.2 1.0 copy-start.22
  101.2 1.0 copy-start.24
  113.3 36.7 %copy-start.2 = (bf16[128,32,128]{2,1,0:T(8,128)(2,1)S(1)}, bf16[128,32,128]{2,1,0:T(8,128)(2,1)}, u32[]{:S(2)}) copy-start(bf16[128,32,128]{2,1,0:T(8,128)(2,1)} %get-tuple-element.89) | copy-start | bytes 3145732
  138.9 59.0 %all-to-all-start.3 = ((f32[16,8,4096]{2,1,0:T(8,128)}), f32[16,8,4096]{2,1,0:T(8,128)S(1)}, u32[]{:S(2)}, u32[]{:S(2)}) async-start(f32[16,8,4096]{2,1,0:T(8,128)} %fusion.25), calls=%async_computation.3 | async-start | bytes 4194304 | tf_op jit(solution)/shard_map/all_to_all | solution.py:175
  150.1 2.1 copy-start.3
  150.1 2.2 copy-start.4
  150.1 2.5 copy-start.5
  197.9 49.7 %all-to-all-start.4 = ((f32[16,8,4096]{2,1,0:T(8,128)}), f32[16,8,4096]{2,1,0:T(8,128)}, u32[]{:S(2)}, u32[]{:S(2)}) async-start(f32[16,8,4096]{2,1,0:T(8,128)} %fusion.26), calls=%async_computation.4 | async-start | bytes 4194304 | tf_op jit(solution)/shard_map/all_to_all | solution.py:175
  247.6 117.5 %all-to-all-start.5 = ((f32[16,8,4096]{2,1,0:T(8,128)}), f32[16,8,4096]{2,1,0:T(8,128)}, u32[]{:S(2)}, u32[]{:S(2)}) async-start(f32[16,8,4096]{2,1,0:T(8,128)} %fusion.27), calls=%async_computation.5 | async-start | bytes 4194304 | tf_op jit(solution)/shard_map/all_to_all | solution.py:175
  410.9 1.4 copy-start.6
  410.9 1.4 copy-start.7
  410.9 1.4 copy-start.8
  410.9 1.4 copy-start.9
  410.9 1.4 copy-start.10
  410.9 1.4 copy-start.11
  485.5 1.0 copy-start.35
  486.5 1.2 copy-start.26
  486.5 1.2 copy-start.27
  486.5 1.2 copy-start.28
  486.5 1.2 copy-start.29
  486.5 1.2 copy-start.30
  486.5 1.2 copy-start.31
  486.5 1.2 copy-start.32
  486.5 1.2 copy-start.33
  486.6 1.2 copy-start.34
  489.9 0.7 copy-start.25

commit v7 on v6

--- a/solution.py
+++ b/solution.py
@@ -176,8 +176,7 @@
             return ev.reshape(n_pt, d_local, rows, kl, FIRST)
 
         left_pts = to_points(left_factor, il)
-        left_pts = jnp.broadcast_to(left_pts[None], (n_grp,) + left_pts.shape)
-        left_pts = lax.all_to_all(left_pts, "grp", split_axis=0, concat_axis=0, tiled=True)
+        left_pts = lax.all_gather(left_pts, "grp", axis=0, tiled=False)
         left_pts = jnp.transpose(left_pts, (2, 5, 0, 3, 1, 4))
         left_pts = left_pts.reshape(d_local * FIRST, n_grp * il, n_pt * kl)
         jc = jl // n_chunks

time: 499 us -> 537 us (1.076)
  waiting for transfers between devices: 44.5 us -> 101 us
  local copies, waits for them, and re-layouts: 229 us -> 208 us
  other arithmetic: 82.8 us -> 69.1 us
  between operations: 1.11 us -> 14.5 us
    all_to_all x5, waiting for transfers between devices: 25.6 us -> 101 us  [to_points(): ev = lax.all_to_all(ev, 'pt', split_axis=0, concat_axis=0, tiled=False)]
    unnamed x96 -> x105, local copies, waits for them, and re-layouts: 71.8 us -> 52.8 us
    all_to_all x1 -> x0, waiting for transfers between devices: 18.9 us -> none  [body(): lax.all_to_all(left_pts, 'grp', split_axis=0, concat_axis=0, tiled=True)]
    all_to_all x1 -> x0, other arithmetic: 9.42 us -> none  [body(): lax.all_to_all(left_pts, 'grp', split_axis=0, concat_axis=0, tiled=True)]
    broadcast_in_dim x2 -> x0, local copies, waits for them, and re-layouts: 8.48 us -> none  [body(): left_pts = jnp.broadcast_to(left_pts[None], (n_grp,) + left_pts.shape)]
    all_to_all x5, starting transfers between devices: 41.3 us -> 46.9 us  [to_points(): ev = lax.all_to_all(ev, 'pt', split_axis=0, concat_axis=0, tiled=False)]
  transfers between devices with their start and end apart: 6 -> 6, of which waited for: 2 -> 3; matrix products, arithmetic and copies ran while one was open for 50% -> 32% of each run, Pallas kernels for 0% -> 0%
where the time goes in v7:
time: 537 us; the launch traced here: 532 us
  local copies, waits for them, and re-layouts  208 us (39%)
  waiting for transfers between devices  101 us (19%)
  other arithmetic  69.1 us (13%)
  blocking collectives  47.9 us (9%)
  starting transfers between devices  47.1 us (9%)
  matrix products  44.5 us (8%)
  between operations  14.5 us (3%)
    all_to_all x5, waiting for transfers between devices, to_points(): ev = lax.all_to_all(ev, 'pt', split_axis=0, concat_axis=0, tiled=False)  101 us
    unnamed x105, local copies, waits for them, and re-layouts  52.8 us
    transpose x4, local copies, waits for them, and re-layouts, body(): jnp.transpose(right_pts, (1, 4, 2, 0, 3))  47.9 us
    all_to_all x5, starting transfers between devices, to_points(): ev = lax.all_to_all(ev, 'pt', split_axis=0, concat_axis=0, tiled=False)  46.9 us
    convert_element_type x20, other arithmetic, limbs_bf16(): piece.astype(jnp.bfloat16)  38.8 us
    reshape x8, local copies, waits for them, and re-layouts, body(): jnp.transpose(right_pts, (1, 4, 2, 0, 3))  33.8 us
    all_to_all x1, blocking collectives, body(): prod = lax.all_to_all(prod, 'pt', split_axis=0, concat_axis=0, tiled=False)  31.8 us
    dot_general x4, matrix products, multiply_points(): jnp.einsum('pak,pjk->paj', stacked, right_limbs, preferred_element_type=j...  29.9 us
  transfers between devices with their start and end apart: 6, of which 3 were waited for; matrix products, arithmetic and copies ran while one was open for 32% of the time, Pallas kernels for 0%

profile of v7, /device:TPU:1, one launch (start us, length us, event | category | flops | bytes accessed | tf_op | source)
XLA Modules:
  0.0 531.6 jit_solution(17617784986404183975)
XLA Ops:
  14.6 7.7 %all-to-all-start = ((f32[16,8,2048]{2,1,0:T(8,128)}), f32[16,8,2048]{2,1,0:T(8,128)}, u32[]{:S(2)}, u32[]{:S(2)}) async-start(f32[16,8,2048]{2,1,0:T(8,128)} %fusion.70), calls=%async_computation | async-start | bytes 2097152 | tf_op jit(solution)/shard_map/all_to_all | solution.py:175
  22.4 3.6 slice_bitcast_fusion.3
  30.7 13.3 %subtract_convert_fusion.15 = (bf16[128,32,128]{2,1,0:T(8,128)(2,1)S(1)}, f32[128,32,128]{2,1,0:T(8,128)S(1)}, bf16[128,32,128]{2,1,0:T(8,128)(2,1)S(1)}, f32[12...) fusion(f32[32,128]{1,0:T(8,128)S(1)} %copy-done.29, f32[32,128]{1,0:T(8,128)S(1)} %copy-done.27, ...), kind=kLoop, calls=%fused_computation.96 | loop fusion | flops 94371840 | bytes 28459008 | tf_op jit(solution)/shard_map/convert_element_type | solution.py:105
  50.5 6.6 %all-to-all-start.1 = ((f32[16,8,4096]{2,1,0:T(8,128)}), f32[16,8,4096]{2,1,0:T(8,128)}, u32[]{:S(2)}, u32[]{:S(2)}) async-start(f32[16,8,4096]{2,1,0:T(8,128)} %fusion.24), calls=%async_computation.1 | async-start | bytes 4194304 | tf_op jit(solution)/shard_map/all_to_all | solution.py:175
  61.3 37.1 %all-to-all-done.1 = f32[16,8,4096]{2,1,0:T(8,128)} async-done(((f32[16,8,4096]{2,1,0:T(8,128)}), f32[16,8,4096]{2,1,0:T(8,128)}, u32[]{:S(2)}, u32[]{:S(2)}) %all-to-all-start.1) | async-done | bytes 2097184 | tf_op jit(solution)/shard_map/all_to_all | solution.py:175
  98.5 10.9 %all-to-all-start.2 = ((f32[16,8,4096]{2,1,0:T(8,128)}), f32[16,8,4096]{2,1,0:T(8,128)S(1)}, u32[]{:S(2)}, u32[]{:S(2)}) async-start(f32[16,8,4096]{2,1,0:T(8,128)} %fusion.25), calls=%async_computation.2 | async-start | bytes 4194304 | tf_op jit(solution)/shard_map/all_to_all | solution.py:175
  116.2 34.6 %all-to-all-done.2 = f32[16,8,4096]{2,1,0:T(8,128)S(1)} async-done(((f32[16,8,4096]{2,1,0:T(8,128)}), f32[16,8,4096]{2,1,0:T(8,128)S(1)}, u32[]{:S(2)}, u32[]{:S(2)}) %all-to-all-start.2) | async-done | bytes 2097184 | tf_op jit(solution)/shard_map/all_to_all | solution.py:175
  150.8 10.9 %all-to-all-start.3 = ((f32[16,8,4096]{2,1,0:T(8,128)}), f32[16,8,4096]{2,1,0:T(8,128)}, u32[]{:S(2)}, u32[]{:S(2)}) async-start(f32[16,8,4096]{2,1,0:T(8,128)} %fusion.26), calls=%async_computation.3 | async-start | bytes 4194304 | tf_op jit(solution)/shard_map/all_to_all | solution.py:175
  164.5 4.2 subtract_convert_fusion.3
  174.0 29.2 %all-to-all-done.3 = f32[16,8,4096]{2,1,0:T(8,128)} async-done(((f32[16,8,4096]{2,1,0:T(8,128)}), f32[16,8,4096]{2,1,0:T(8,128)}, u32[]{:S(2)}, u32[]{:S(2)}) %all-to-all-start.3) | async-done | bytes 2097184 | tf_op jit(solution)/shard_map/all_to_all | solution.py:175
  203.2 10.9 %all-to-all-start.4 = ((f32[16,8,4096]{2,1,0:T(8,128)}), f32[16,8,4096]{2,1,0:T(8,128)}, u32[]{:S(2)}, u32[]{:S(2)}) async-start(f32[16,8,4096]{2,1,0:T(8,128)} %fusion.27), calls=%async_computation.4 | async-start | bytes 4194304 | tf_op jit(solution)/shard_map/all_to_all | solution.py:175
  214.3 3.8 all_gather_reshape.3
  218.2 6.4 %reshape.94 = f32[16,8,16,8,32]{4,3,2,1,0:T(8,128)} reshape(f32[16,8,4096]{2,1,0:T(8,128)} %all-to-all-done.1) | data formatting | bytes 4194304 | tf_op jit(solution)/shard_map/reshape | solution.py:176
  224.6 13.2 %copy.100 = f32[8,32,16,16,8]{1,0,4,3,2:T(8,128)} copy(f32[8,32,16,16,8]{1,4,2,0,3:T(8,128)} %bitcast.171) | data formatting | bytes 4194304 | tf_op jit(solution)/shard_map/transpose | solution.py:186
  237.7 7.2 %reshape.95 = f32[256,16,128]{0,2,1:T(8,128)} reshape(f32[8,32,16,16,8]{1,0,4,3,2:T(8,128)} %copy.100) | data formatting | bytes 4194304 | tf_op jit(solution)/shard_map/reshape | solution.py:186
  248.0 5.0 reshape.98
  253.0 11.6 %copy.106 = f32[8,32,16,16,8]{1,0,4,3,2:T(8,128)} copy(f32[8,32,16,16,8]{1,4,2,0,3:T(8,128)} %bitcast.172) | data formatting | bytes 4194304 | tf_op jit(solution)/shard_map/transpose | solution.py:186
  264.6 5.8 %reshape.99 = f32[256,16,128]{0,2,1:T(8,128)S(1)} reshape(f32[8,32,16,16,8]{1,0,4,3,2:T(8,128)} %copy.106) | data formatting | bytes 4194304 | tf_op jit(solution)/shard_map/reshape | solution.py:186
  272.4 6.6 %reshape.102 = f32[16,8,16,8,32]{4,3,2,1,0:T(8,128)} reshape(f32[16,8,4096]{2,1,0:T(8,128)} %all-to-all-done.3) | data formatting | bytes 4194304 | tf_op jit(solution)/shard_map/reshape | solution.py:176
  279.0 11.6 %copy.112 = f32[8,32,16,16,8]{1,0,4,3,2:T(8,128)} copy(f32[8,32,16,16,8]{1,4,2,0,3:T(8,128)} %bitcast.173) | data formatting | bytes 4194304 | tf_op jit(solution)/shard_map/transpose | solution.py:186
  290.6 5.8 %reshape.103 = f32[256,16,128]{0,2,1:T(8,128)S(1)} reshape(f32[8,32,16,16,8]{1,0,4,3,2:T(8,128)} %copy.112) | data formatting | bytes 4194304 | tf_op jit(solution)/shard_map/reshape | solution.py:186
  298.4 6.8 %reshape.106 = f32[16,8,16,8,32]{4,3,2,1,0:T(8,128)} reshape(f32[16,8,4096]{2,1,0:T(8,128)} %all-to-all-done.4) | data formatting | bytes 4194304 | tf_op jit(solution)/shard_map/reshape | solution.py:176
  305.2 11.6 %copy.118 = f32[8,32,16,16,8]{1,0,4,3,2:T(8,128)} copy(f32[8,32,16,16,8]{1,4,2,0,3:T(8,128)} %bitcast.174) | data formatting | bytes 4194304 | tf_op jit(solution)/shard_map/transpose | solution.py:186
  316.8 5.8 %reshape.107 = f32[256,16,128]{0,2,1:T(8,128)S(1)} reshape(f32[8,32,16,16,8]{1,0,4,3,2:T(8,128)} %copy.118) | data formatting | bytes 4194304 | tf_op jit(solution)/shard_map/reshape | solution.py:186
  324.8 4.0 subtract_convert_fusion.13
  335.3 11.5 %copy.93 = f32[8,32,2,8,16,8]{1,0,5,4,3,2:T(8,128)} copy(f32[8,32,2,8,16,8]{1,5,3,0,4,2:T(8,128)} %bitcast.180) | data formatting | bytes 4194304 | tf_op jit(solution)/shard_map/transpose | solution.py:180
  346.9 5.8 %reshape.91 = f32[256,16,128]{0,2,1:T(8,128)S(1)} reshape(f32[8,32,2,8,16,8]{1,0,5,4,3,2:T(8,128)} %copy.93) | data formatting | bytes 4194304 | tf_op jit(solution)/shard_map/reshape | solution.py:181
  354.6 5.5 %subtract_convert_fusion.21 = (bf16[256,16,128]{2,1,0:T(8,128)(2,1)S(1)}, bf16[256,16,128]{2,1,0:T(8,128)(2,1)S(1)}, bf16[256,16,128]{2,1,0:T(8,128)(2,1)S(1)}, ...) fusion(f32[256,16,128]{2,1,0:T(8,128)} %copy.95), kind=kLoop, calls=%fused_computation.111 | loop fusion | flops 33554432 | bytes 11534336 | tf_op jit(solution)/shard_map/convert_element_type | solution.py:156
  360.9 5.2 maximum_maximum_fusion
  366.2 6.3 %fusion = f32[256,48,16]{1,2,0:T(8,128)S(1)} fusion(bf16[256,48,384]{2,1,0:T(8,128)(2,1)} %maximum_maximum_fusion, bf16[256,16,128]{2,1,0:T(8,128)(2,1)S(1)} %copy-done.7, bf16[256,16,128]{2,1,0:T(8,128)(2,1)S(1)} %copy-done.6, bf16[256,16,128]{2,1,0:T(8,128)(2,1)S(1)} %copy-done.5), kind=kOutput, calls=%fused_computation.16 | convolution fusion | flops 160432128 | bytes 13369344 | tf_op jit(solution)/shard_map/pak,pjk->paj/dot_general | solution.py:159
  372.4 3.3 fusion.106
  378.3 3.3 copy.130
  383.3 7.9 %fusion.6 = f32[256,48,16]{1,2,0:T(8,128)S(1)} fusion(bf16[256,48,384]{2,1,0:T(8,128)(2,1)} %maximum_maximum_fusion, bf16[256,16,128]{2,1,0:T(8,128)(2,1)} %get-tuple-element.36, bf16[256,16,128]{2,1,0:T(8,128)(2,1)} %get-tuple-element.35, bf16[256,16,128]{2,1,0:T(8,128)(2,1)} %get-tuple-element.34), kind=kOutput, calls=%fused_computation.23 | convolution fusion | flops 160432128 | bytes 13369344 | tf_op jit(solution)/shard_map/pak,pjk->paj/dot_general | solution.py:159
  391.3 3.3 fusion.107
  394.6 3.3 copy.132
  397.8 3.3 copy.133
  402.9 8.1 %fusion.12 = f32[256,48,16]{1,2,0:T(8,128)S(1)} fusion(bf16[256,48,384]{2,1,0:T(8,128)(2,1)} %maximum_maximum_fusion, bf16[256,16,128]{2,1,0:T(8,128)(2,1)} %get-tuple-element.44, bf16[256,16,128]{2,1,0:T(8,128)(2,1)} %get-tuple-element.43, bf16[256,16,128]{2,1,0:T(8,128)(2,1)} %get-tuple-element.42), kind=kOutput, calls=%fused_computation.30 | convolution fusion | flops 160432128 | bytes 13369344 | tf_op jit(solution)/shard_map/pak,pjk->paj/dot_general | solution.py:159
  411.0 3.3 fusion.108
  414.3 3.3 copy.135
  417.5 3.3 copy.136
  422.6 7.6 %fusion.18 = f32[256,48,16]{1,2,0:T(8,128)S(1)} fusion(bf16[256,48,384]{2,1,0:T(8,128)(2,1)} %maximum_maximum_fusion, bf16[256,16,128]{2,1,0:T(8,128)(2,1)} %get-tuple-element.52, bf16[256,16,128]{2,1,0:T(8,128)(2,1)} %get-tuple-element.51, bf16[256,16,128]{2,1,0:T(8,128)(2,1)S(1)} %get-tuple-element.50), kind=kOutput, calls=%fused_computation.37 | convolution fusion | flops 160432128 | bytes 13369344 | tf_op jit(solution)/shard_map/pak,pjk->paj/dot_general | solution.py:159
  430.2 3.2 fusion.109
  433.4 3.3 copy.138
  436.7 3.3 copy.139
  443.7 16.0 %all_to_all.35 = f32[256,2,8,64]{0,3,2,1:T(8,128)S(1)} all-to-all(f32[256,2,8,64]{0,3,2,1:T(8,128)S(1)} %bitcast.182), channel_id=1, replica_groups=mesh['grp'=2,'pt'=16] {'grp'}, dimensions={1} | all-to-all | bytes 2097152 | tf_op jit(solution)/shard_map/all_to_all | solution.py:193
  462.3 4.8 copy_bitcast_fusion
  467.1 3.9 reshape.114
  471.0 31.8 %all_to_all.36 = f32[16,1,16384]{2,1,0:T(1,128)S(1)} all-to-all(f32[16,1,16384]{2,1,0:T(1,128)S(1)} %reshape.114), channel_id=1, replica_groups=mesh['grp'=2,'pt'=16] {'pt'}, dimensions={0} | all-to-all | bytes 2097152 | tf_op jit(solution)/shard_map/all_to_all | solution.py:196
  (157 shorter events, 92.5 us)
Async XLA Ops:
  6.5 1.5 copy-start.18
  7.9 0.7 copy-start.19
  7.9 0.7 copy-start.20
  7.9 0.7 copy-start.21
  7.9 0.7 copy-start.22
  7.9 0.7 copy-start.23
  8.0 0.7 copy-start.24
  8.0 0.7 copy-start.25
  8.0 0.8 copy-start.27
  8.0 0.8 copy-start.29
  11.1 1.0 copy-start.3
  14.6 35.8 %all-to-all-start = ((f32[16,8,2048]{2,1,0:T(8,128)}), f32[16,8,2048]{2,1,0:T(8,128)}, u32[]{:S(2)}, u32[]{:S(2)}) async-start(f32[16,8,2048]{2,1,0:T(8,128)} %fusion.70), calls=%async_computation | async-start | bytes 2097152 | tf_op jit(solution)/shard_map/all_to_all | solution.py:175
  50.5 48.0 %all-to-all-start.1 = ((f32[16,8,4096]{2,1,0:T(8,128)}), f32[16,8,4096]{2,1,0:T(8,128)}, u32[]{:S(2)}, u32[]{:S(2)}) async-start(f32[16,8,4096]{2,1,0:T(8,128)} %fusion.24), calls=%async_computation.1 | async-start | bytes 4194304 | tf_op jit(solution)/shard_map/all_to_all | solution.py:175
  98.5 52.3 %all-to-all-start.2 = ((f32[16,8,4096]{2,1,0:T(8,128)}), f32[16,8,4096]{2,1,0:T(8,128)S(1)}, u32[]{:S(2)}, u32[]{:S(2)}) async-start(f32[16,8,4096]{2,1,0:T(8,128)} %fusion.25), calls=%async_computation.2 | async-start | bytes 4194304 | tf_op jit(solution)/shard_map/all_to_all | solution.py:175
  109.3 2.2 copy-start.4
  150.8 52.4 %all-to-all-start.3 = ((f32[16,8,4096]{2,1,0:T(8,128)}), f32[16,8,4096]{2,1,0:T(8,128)}, u32[]{:S(2)}, u32[]{:S(2)}) async-start(f32[16,8,4096]{2,1,0:T(8,128)} %fusion.26), calls=%async_computation.3 | async-start | bytes 4194304 | tf_op jit(solution)/shard_map/all_to_all | solution.py:175
  163.4 1.1 copy-start.26
  163.5 1.1 copy-start.28
  163.5 1.0 copy-start.30
  203.2 95.2 %all-to-all-start.4 = ((f32[16,8,4096]{2,1,0:T(8,128)}), f32[16,8,4096]{2,1,0:T(8,128)}, u32[]{:S(2)}, u32[]{:S(2)}) async-start(f32[16,8,4096]{2,1,0:T(8,128)} %fusion.27), calls=%async_computation.4 | async-start | bytes 4194304 | tf_op jit(solution)/shard_map/all_to_all | solution.py:175
  214.1 121.3 %all-gather.2.cloned.1.call-start = ((), (), s32[]{:S(2)}) async-start(), calls=%async_computation.7 | async-start | bytes 12582912 | tf_op jit(solution)/shard_map/all_gather | solution.py:179
  324.8 4.0 copy-start
  328.8 2.3 copy-start.1
  331.1 2.2 copy-start.2
  360.9 5.3 copy-start.5
  360.9 5.3 copy-start.6
  360.9 5.3 copy-start.7
  436.7 5.1 copy-start.8
  436.7 5.1 copy-start.9
  440.0 2.0 copy-start.10
  440.0 2.0 copy-start.11
  441.8 1.4 copy-start.12
  441.8 1.4 copy-start.13
  441.8 1.4 copy-start.14
  441.8 1.4 copy-start.15
  441.8 1.4 copy-start.16
  441.9 1.4 copy-start.17
  517.1 1.0 copy-start.41
  518.1 1.2 copy-start.32
  518.1 1.2 copy-start.33
  518.1 1.2 copy-start.34
  518.1 1.2 copy-start.35
  518.1 1.2 copy-start.36
  518.1 1.2 copy-start.37
  518.1 1.2 copy-start.38
  518.1 1.2 copy-start.39
  518.1 1.2 copy-start.40
  521.5 0.7 copy-start.31
Sparse Core Ops, SparseCore 0:
  218.3 104.7 all-gather.1

commit v8 on v6

--- a/solution.py
+++ b/solution.py
@@ -206,7 +206,7 @@
     n_grp = mesh.shape["grp"]
     n_pt = mesh.shape["pt"]
     return jax.shard_map(
-        make_body(n_grp, n_pt, 4),
+        make_body(n_grp, n_pt, 8),
         mesh=mesh,
         in_specs=(P("grp", "pt", None), P("grp", "pt", None)),
         out_specs=P("grp", "pt", None),

time: 499 us -> 639 us (1.28)
  waiting for transfers between devices: 44.5 us -> 131 us
  matrix products: 41.8 us -> 75 us
  starting transfers between devices: 46.1 us -> 65.7 us
    all_to_all x5 -> x9, waiting for transfers between devices: 25.6 us -> 129 us  [to_points(): ev = lax.all_to_all(ev, 'pt', split_axis=0, concat_axis=0, tiled=False)]
    dot_general x4 -> x8, matrix products: 25.4 us -> 54.3 us  [multiply_points(): jnp.einsum('pak,pjk->paj', stacked, right_limbs, preferred_element_type=j...]
    all_to_all x5 -> x9, starting transfers between devices: 41.3 us -> 62 us  [to_points(): ev = lax.all_to_all(ev, 'pt', split_axis=0, concat_axis=0, tiled=False)]
    all_to_all x1, waiting for transfers between devices: 18.9 us -> 2.46 us  [body(): lax.all_to_all(left_pts, 'grp', split_axis=0, concat_axis=0, tiled=True)]
    unnamed x96 -> x212, local copies, waits for them, and re-layouts: 71.8 us -> 62.7 us
    slice x4 -> x8, local copies, waits for them, and re-layouts: 13.5 us -> 5.97 us  [multiply_points(): return fold3(levels[:, 0:n_i], levels[:, n_i:2 * n_i], levels[:, 2 * n_i:])]
    transpose x4 -> x8, local copies, waits for them, and re-layouts: 46.3 us -> 53.4 us  [body(): jnp.transpose(right_pts, (1, 4, 2, 0, 3))]
    convert_element_type x20 -> x32, other arithmetic: 40.7 us -> 46.5 us  [limbs_bf16(): piece.astype(jnp.bfloat16)]
  transfers between devices with their start and end apart: 6 -> 10, of which waited for: 2 -> 9; matrix products, arithmetic and copies ran while one was open for 50% -> 33% of each run, Pallas kernels for 0% -> 0%
where the time goes in v8:
time: 639 us; the launch traced here: 632 us
  local copies, waits for them, and re-layouts  225 us (35%)
  waiting for transfers between devices  131 us (21%)
  other arithmetic  85.6 us (13%)
  matrix products  75 us (12%)
  starting transfers between devices  65.7 us (10%)
  blocking collectives  47.4 us (7%)
    all_to_all x9, waiting for transfers between devices, to_points(): ev = lax.all_to_all(ev, 'pt', split_axis=0, concat_axis=0, tiled=False)  129 us
    unnamed x212, local copies, waits for them, and re-layouts  62.7 us
    all_to_all x9, starting transfers between devices, to_points(): ev = lax.all_to_all(ev, 'pt', split_axis=0, concat_axis=0, tiled=False)  62 us
    dot_general x8, matrix products, multiply_points(): jnp.einsum('pak,pjk->paj', stacked, right_limbs, preferred_element_type=j...  54.3 us
    transpose x8, local copies, waits for them, and re-layouts, body(): jnp.transpose(right_pts, (1, 4, 2, 0, 3))  53.4 us
    convert_element_type x32, other arithmetic, limbs_bf16(): piece.astype(jnp.bfloat16)  46.5 us
    reshape x16, local copies, waits for them, and re-layouts, body(): jnp.transpose(right_pts, (1, 4, 2, 0, 3))  37.5 us
    all_to_all x1, blocking collectives, body(): prod = lax.all_to_all(prod, 'pt', split_axis=0, concat_axis=0, tiled=False)  32.3 us
  transfers between devices with their start and end apart: 10, of which 9 were waited for; matrix products, arithmetic and copies ran while one was open for 33% of the time, Pallas kernels for 0%

profile of v8, /device:TPU:1, one launch (start us, length us, event | category | flops | bytes accessed | tf_op | source)
XLA Modules:
  0.0 631.6 jit_solution(10099077238932760210)
XLA Ops:
  7.0 7.0 %subtract_convert_fusion.21 = (bf16[64,32,128]{2,1,0:T(8,128)(2,1)}, f32[64,32,128]{2,1,0:T(8,128)}, bf16[64,32,128]{2,1,0:T(8,128)(2,1)S(1)}, f32[64,32,128]{2,...) fusion(f32[32,128]{1,0:T(8,128)S(1)} %copy-done.63, f32[32,128]{1,0:T(8,128)S(1)} %copy-done.64, ...), kind=kLoop, calls=%fused_computation.175 | loop fusion | flops 47185920 | bytes 14303232 | tf_op jit(solution)/shard_map/convert_element_type | solution.py:105
  18.8 7.9 %all-to-all-start = ((f32[16,8,2048]{2,1,0:T(8,128)}), f32[16,8,2048]{2,1,0:T(8,128)S(1)}, u32[]{:S(2)}, u32[]{:S(2)}) async-start(f32[16,8,2048]{2,1,0:T(8,128)} %fusion.62), calls=%async_computation | async-start | bytes 2097152 | tf_op jit(solution)/shard_map/all_to_all | solution.py:175
  30.7 7.0 %subtract_convert_fusion.13 = (bf16[64,32,128]{2,1,0:T(8,128)(2,1)}, f32[64,32,128]{2,1,0:T(8,128)}, bf16[64,32,128]{2,1,0:T(8,128)(2,1)S(1)}, f32[64,32,128]{2,...) fusion(f32[32,128]{1,0:T(8,128)S(1)} %copy-done.63, f32[32,128]{1,0:T(8,128)S(1)} %copy-done.64, ...), kind=kLoop, calls=%fused_computation.155 | loop fusion | flops 47185920 | bytes 14303232 | tf_op jit(solution)/shard_map/convert_element_type | solution.py:105
  44.8 4.9 all-to-all-done
  49.7 6.7 %all-to-all-start.2 = ((f32[16,8,2048]{2,1,0:T(8,128)}), f32[16,8,2048]{2,1,0:T(8,128)}, u32[]{:S(2)}, u32[]{:S(2)}) async-start(f32[16,8,2048]{2,1,0:T(8,128)} %fusion.63), calls=%async_computation.2 | async-start | bytes 2097152 | tf_op jit(solution)/shard_map/all_to_all | solution.py:175
  65.6 14.1 %all-to-all-done.2 = f32[16,8,2048]{2,1,0:T(8,128)} async-done(((f32[16,8,2048]{2,1,0:T(8,128)}), f32[16,8,2048]{2,1,0:T(8,128)}, u32[]{:S(2)}, u32[]{:S(2)}) %all-to-all-start.2) | async-done | bytes 1048608 | tf_op jit(solution)/shard_map/all_to_all | solution.py:175
  79.6 7.0 %all-to-all-start.3 = ((f32[16,8,2048]{2,1,0:T(8,128)}), f32[16,8,2048]{2,1,0:T(8,128)}, u32[]{:S(2)}, u32[]{:S(2)}) async-start(f32[16,8,2048]{2,1,0:T(8,128)} %fusion.64), calls=%async_computation.3 | async-start | bytes 2097152 | tf_op jit(solution)/shard_map/all_to_all | solution.py:175
  86.6 8.5 %subtract_convert_fusion.17 = (bf16[64,32,128]{2,1,0:T(8,128)(2,1)}, f32[64,32,128]{2,1,0:T(8,128)}, bf16[64,32,128]{2,1,0:T(8,128)(2,1)S(1)}, f32[64,32,128]{2,...) fusion(f32[32,128]{1,0:T(8,128)S(1)} %copy-done.63, f32[32,128]{1,0:T(8,128)S(1)} %copy-done.64, ...), kind=kLoop, calls=%fused_computation.165 | loop fusion | flops 47185920 | bytes 14303232 | tf_op jit(solution)/shard_map/convert_element_type | solution.py:105
  98.7 11.0 %all-to-all-done.3 = f32[16,8,2048]{2,1,0:T(8,128)} async-done(((f32[16,8,2048]{2,1,0:T(8,128)}), f32[16,8,2048]{2,1,0:T(8,128)}, u32[]{:S(2)}, u32[]{:S(2)}) %all-to-all-start.3) | async-done | bytes 1048608 | tf_op jit(solution)/shard_map/all_to_all | solution.py:175
  109.7 6.7 %all-to-all-start.4 = ((f32[16,8,2048]{2,1,0:T(8,128)}), f32[16,8,2048]{2,1,0:T(8,128)S(1)}, u32[]{:S(2)}, u32[]{:S(2)}) async-start(f32[16,8,2048]{2,1,0:T(8,128)} %fusion.65), calls=%async_computation.4 | async-start | bytes 2097152 | tf_op jit(solution)/shard_map/all_to_all | solution.py:175
  118.9 20.6 %all-to-all-done.4 = f32[16,8,2048]{2,1,0:T(8,128)S(1)} async-done(((f32[16,8,2048]{2,1,0:T(8,128)}), f32[16,8,2048]{2,1,0:T(8,128)S(1)}, u32[]{:S(2)}, u32[]{:S(2)}) %all-to-all-start.4) | async-done | bytes 1048608 | tf_op jit(solution)/shard_map/all_to_all | solution.py:175
  139.5 6.7 %all-to-all-start.5 = ((f32[16,8,2048]{2,1,0:T(8,128)}), f32[16,8,2048]{2,1,0:T(8,128)}, u32[]{:S(2)}, u32[]{:S(2)}) async-start(f32[16,8,2048]{2,1,0:T(8,128)} %fusion.66), calls=%async_computation.5 | async-start | bytes 2097152 | tf_op jit(solution)/shard_map/all_to_all | solution.py:175
  148.8 20.7 %all-to-all-done.5 = f32[16,8,2048]{2,1,0:T(8,128)} async-done(((f32[16,8,2048]{2,1,0:T(8,128)}), f32[16,8,2048]{2,1,0:T(8,128)}, u32[]{:S(2)}, u32[]{:S(2)}) %all-to-all-start.5) | async-done | bytes 1048608 | tf_op jit(solution)/shard_map/all_to_all | solution.py:175
  169.5 6.7 %all-to-all-start.6 = ((f32[16,8,2048]{2,1,0:T(8,128)}), f32[16,8,2048]{2,1,0:T(8,128)S(1)}, u32[]{:S(2)}, u32[]{:S(2)}) async-start(f32[16,8,2048]{2,1,0:T(8,128)} %fusion.67), calls=%async_computation.6 | async-start | bytes 2097152 | tf_op jit(solution)/shard_map/all_to_all | solution.py:175
  180.4 18.9 %all-to-all-done.6 = f32[16,8,2048]{2,1,0:T(8,128)S(1)} async-done(((f32[16,8,2048]{2,1,0:T(8,128)}), f32[16,8,2048]{2,1,0:T(8,128)S(1)}, u32[]{:S(2)}, u32[]{:S(2)}) %all-to-all-start.6) | async-done | bytes 1048608 | tf_op jit(solution)/shard_map/all_to_all | solution.py:175
  199.3 6.7 %all-to-all-start.7 = ((f32[16,8,2048]{2,1,0:T(8,128)}), f32[16,8,2048]{2,1,0:T(8,128)}, u32[]{:S(2)}, u32[]{:S(2)}) async-start(f32[16,8,2048]{2,1,0:T(8,128)} %fusion.68), calls=%async_computation.7 | async-start | bytes 2097152 | tf_op jit(solution)/shard_map/all_to_all | solution.py:175
  210.3 18.9 %all-to-all-done.7 = f32[16,8,2048]{2,1,0:T(8,128)} async-done(((f32[16,8,2048]{2,1,0:T(8,128)}), f32[16,8,2048]{2,1,0:T(8,128)}, u32[]{:S(2)}, u32[]{:S(2)}) %all-to-all-start.7) | async-done | bytes 1048608 | tf_op jit(solution)/shard_map/all_to_all | solution.py:175
  229.2 7.0 %all-to-all-start.8 = ((f32[16,8,2048]{2,1,0:T(8,128)}), f32[16,8,2048]{2,1,0:T(8,128)}, u32[]{:S(2)}, u32[]{:S(2)}) async-start(f32[16,8,2048]{2,1,0:T(8,128)} %fusion.69), calls=%async_computation.8 | async-start | bytes 2097152 | tf_op jit(solution)/shard_map/all_to_all | solution.py:175
  239.3 20.0 %all-to-all-done.8 = f32[16,8,2048]{2,1,0:T(8,128)} async-done(((f32[16,8,2048]{2,1,0:T(8,128)}), f32[16,8,2048]{2,1,0:T(8,128)}, u32[]{:S(2)}, u32[]{:S(2)}) %all-to-all-start.8) | async-done | bytes 1048608 | tf_op jit(solution)/shard_map/all_to_all | solution.py:175
  259.3 6.7 %all-to-all-start.9 = ((f32[16,8,2048]{2,1,0:T(8,128)}), f32[16,8,2048]{2,1,0:T(8,128)}, u32[]{:S(2)}, u32[]{:S(2)}) async-start(f32[16,8,2048]{2,1,0:T(8,128)} %fusion.70), calls=%async_computation.9 | async-start | bytes 2097152 | tf_op jit(solution)/shard_map/all_to_all | solution.py:175
  268.8 4.6 copy.142
  273.4 4.7 broadcast_bitcast_fusion
  278.1 6.9 %reshape.179 = f32[2,1,262144]{2,1,0:T(1,128)} reshape(f32[2,8,16,8,8,32]{5,4,3,2,1,0:T(8,128)} %broadcast_bitcast_fusion) | data formatting | bytes 4194304
  288.8 6.7 %copy.149 = f32[8,32,8,16,8]{1,0,4,3,2:T(8,128)} copy(f32[8,32,8,16,8]{1,4,2,0,3:T(8,128)} %bitcast.296) | data formatting | bytes 2097152 | tf_op jit(solution)/shard_map/transpose | solution.py:187
  300.1 4.2 reshape.147
  304.4 6.7 %copy.155 = f32[8,32,8,16,8]{1,0,4,3,2:T(8,128)} copy(f32[8,32,8,16,8]{1,4,2,0,3:T(8,128)} %bitcast.297) | data formatting | bytes 2097152 | tf_op jit(solution)/shard_map/transpose | solution.py:187
  318.5 6.7 %copy.161 = f32[8,32,8,16,8]{1,0,4,3,2:T(8,128)} copy(f32[8,32,8,16,8]{1,4,2,0,3:T(8,128)} %bitcast.298) | data formatting | bytes 2097152 | tf_op jit(solution)/shard_map/transpose | solution.py:187
  333.6 6.7 %copy.167 = f32[8,32,8,16,8]{1,0,4,3,2:T(8,128)} copy(f32[8,32,8,16,8]{1,4,2,0,3:T(8,128)} %bitcast.299) | data formatting | bytes 2097152 | tf_op jit(solution)/shard_map/transpose | solution.py:187
  347.9 6.7 %copy.173 = f32[8,32,8,16,8]{1,0,4,3,2:T(8,128)} copy(f32[8,32,8,16,8]{1,4,2,0,3:T(8,128)} %bitcast.300) | data formatting | bytes 2097152 | tf_op jit(solution)/shard_map/transpose | solution.py:187
  363.1 6.7 %copy.179 = f32[8,32,8,16,8]{1,0,4,3,2:T(8,128)} copy(f32[8,32,8,16,8]{1,4,2,0,3:T(8,128)} %bitcast.301) | data formatting | bytes 2097152 | tf_op jit(solution)/shard_map/transpose | solution.py:187
  374.5 4.0 reshape.167
  378.5 6.7 %copy.185 = f32[8,32,8,16,8]{1,0,4,3,2:T(8,128)} copy(f32[8,32,8,16,8]{1,4,2,0,3:T(8,128)} %bitcast.302) | data formatting | bytes 2097152 | tf_op jit(solution)/shard_map/transpose | solution.py:187
  403.2 6.7 %copy.191 = f32[8,32,8,16,8]{1,0,4,3,2:T(8,128)} copy(f32[8,32,8,16,8]{1,4,2,0,3:T(8,128)} %bitcast.303) | data formatting | bytes 2097152 | tf_op jit(solution)/shard_map/transpose | solution.py:187
  426.1 8.6 %reduce = f32[2,262144]{1,0:T(2,128)S(1)} reduce(f32[2,1,262144]{2,1,0:T(1,128)} %copy-done.2, f32[]{:T(128)} %broadcast.584), dimensions={1}, to_apply=%all_to_all.37.reduce_sub_computation | reduce | bytes 4194308 | tf_op jit(solution)/shard_map/all_to_all | solution.py:180
  434.6 6.6 %reshape.180 = f32[2,8,16,8,8,32]{5,4,3,2,1,0:T(8,128)} reshape(f32[2,262144]{1,0:T(2,128)S(1)} %reduce) | data formatting | bytes 4194304
  441.2 8.5 %bitcast_bitcast_fusion = f32[8,32,2,8,16,8]{1,0,5,4,3,2:T(8,128)} fusion(f32[2,8,16,8,8,32]{5,4,3,2,1,0:T(8,128)} %reshape.180), kind=kLoop, calls=%fused_computation.391 | loop fusion | bytes 4194304 | tf_op jit(solution)/shard_map/transpose | solution.py:181
  449.7 5.8 reshape.140
  457.5 5.5 subtract_convert_fusion.5
  472.9 7.4 %fusion.9 = f32[256,48,8]{1,2,0:T(8,128)S(1)} fusion(bf16[256,48,384]{2,1,0:T(8,128)(2,1)} %copy-done.1, bf16[256,8,128]{2,1,0:T(8,128)(2,1)} %get-tuple-element.103, bf16[256,8,128]{2,1,0:T(8,128)(2,1)} %get-tuple-element.102, bf16[256,8,128]{2,1,0:T(8,128)(2,1)S(1)} %copy-done.37), kind=kOutput, calls=%fused_computation.68 | convolution fusion | flops 80216064 | bytes 11403264 | tf_op jit(solution)/shard_map/pak,pjk->paj/dot_general | solution.py:159
  484.0 7.2 %fusion.15 = f32[256,48,8]{1,2,0:T(8,128)S(1)} fusion(bf16[256,48,384]{2,1,0:T(8,128)(2,1)} %copy-done.1, bf16[256,8,128]{2,1,0:T(8,128)(2,1)} %get-tuple-element.95, bf16[256,8,128]{2,1,0:T(8,128)(2,1)S(1)} %copy-done.36, bf16[256,8,128]{2,1,0:T(8,128)(2,1)S(1)} %copy-done.35), kind=kOutput, calls=%fused_computation.75 | convolution fusion | flops 80216064 | bytes 11403264 | tf_op jit(solution)/shard_map/pak,pjk->paj/dot_general | solution.py:159
  495.0 7.2 %fusion.21 = f32[256,48,8]{1,2,0:T(8,128)S(1)} fusion(bf16[256,48,384]{2,1,0:T(8,128)(2,1)} %copy-done.1, bf16[256,8,128]{2,1,0:T(8,128)(2,1)} %get-tuple-element.87, bf16[256,8,128]{2,1,0:T(8,128)(2,1)S(1)} %copy-done.32, bf16[256,8,128]{2,1,0:T(8,128)(2,1)S(1)} %copy-done.31), kind=kOutput, calls=%fused_computation.82 | convolution fusion | flops 80216064 | bytes 11403264 | tf_op jit(solution)/shard_map/pak,pjk->paj/dot_general | solution.py:159
  505.9 7.4 %fusion.27 = f32[256,48,8]{1,2,0:T(8,128)S(1)} fusion(bf16[256,48,384]{2,1,0:T(8,128)(2,1)} %copy-done.1, bf16[256,8,128]{2,1,0:T(8,128)(2,1)} %get-tuple-element.79, bf16[256,8,128]{2,1,0:T(8,128)(2,1)S(1)} %copy-done.34, bf16[256,8,128]{2,1,0:T(8,128)(2,1)S(1)} %copy-done.33), kind=kOutput, calls=%fused_computation.89 | convolution fusion | flops 80216064 | bytes 11403264 | tf_op jit(solution)/shard_map/pak,pjk->paj/dot_general | solution.py:159
  517.0 7.3 %fusion.33 = f32[256,48,8]{1,2,0:T(8,128)S(1)} fusion(bf16[256,48,384]{2,1,0:T(8,128)(2,1)} %copy-done.1, bf16[256,8,128]{2,1,0:T(8,128)(2,1)} %get-tuple-element.71, bf16[256,8,128]{2,1,0:T(8,128)(2,1)S(1)} %copy-done.30, bf16[256,8,128]{2,1,0:T(8,128)(2,1)S(1)} %copy-done.29), kind=kOutput, calls=%fused_computation.96 | convolution fusion | flops 80216064 | bytes 11403264 | tf_op jit(solution)/shard_map/pak,pjk->paj/dot_general | solution.py:159
  528.0 7.2 %fusion.39 = f32[256,48,8]{1,2,0:T(8,128)S(1)} fusion(bf16[256,48,384]{2,1,0:T(8,128)(2,1)} %copy-done.1, bf16[256,8,128]{2,1,0:T(8,128)(2,1)} %get-tuple-element.63, bf16[256,8,128]{2,1,0:T(8,128)(2,1)S(1)} %copy-done.28, bf16[256,8,128]{2,1,0:T(8,128)(2,1)S(1)} %copy-done.27), kind=kOutput, calls=%fused_computation.103 | convolution fusion | flops 80216064 | bytes 11403264 | tf_op jit(solution)/shard_map/pak,pjk->paj/dot_general | solution.py:159
  538.9 7.2 %fusion.45 = f32[256,48,8]{1,2,0:T(8,128)S(1)} fusion(bf16[256,48,384]{2,1,0:T(8,128)(2,1)} %copy-done.1, bf16[256,8,128]{2,1,0:T(8,128)(2,1)} %get-tuple-element.55, bf16[256,8,128]{2,1,0:T(8,128)(2,1)S(1)} %copy-done.26, bf16[256,8,128]{2,1,0:T(8,128)(2,1)S(1)} %copy-done.25), kind=kOutput, calls=%fused_computation.110 | convolution fusion | flops 80216064 | bytes 11403264 | tf_op jit(solution)/shard_map/pak,pjk->paj/dot_general | solution.py:159
  551.1 15.1 %all_to_all.60 = f32[256,2,8,64]{0,3,2,1:T(8,128)S(1)} all-to-all(f32[256,2,8,64]{0,3,2,1:T(8,128)S(1)} %bitcast.315), channel_id=1, replica_groups=mesh['grp'=2,'pt'=16] {'grp'}, dimensions={1} | all-to-all | bytes 2097152 | tf_op jit(solution)/shard_map/all_to_all | solution.py:194
  568.9 4.8 copy_bitcast_fusion
  577.6 32.3 %all_to_all.61 = f32[16,1,16384]{2,1,0:T(1,128)S(1)} all-to-all(f32[16,1,16384]{2,1,0:T(1,128)S(1)} %reshape.181), channel_id=1, replica_groups=mesh['grp'=2,'pt'=16] {'pt'}, dimensions={0} | all-to-all | bytes 2097152 | tf_op jit(solution)/shard_map/all_to_all | solution.py:197
  (327 shorter events, 200.5 us)
Async XLA Ops:
  18.8 30.9 %all-to-all-start = ((f32[16,8,2048]{2,1,0:T(8,128)}), f32[16,8,2048]{2,1,0:T(8,128)S(1)}, u32[]{:S(2)}, u32[]{:S(2)}) async-start(f32[16,8,2048]{2,1,0:T(8,128)} %fusion.62), calls=%async_computation | async-start | bytes 2097152 | tf_op jit(solution)/shard_map/all_to_all | solution.py:175
  49.7 6.9 %copy-start.5 = (f32[16,8,2048]{2,1,0:T(8,128)}, f32[16,8,2048]{2,1,0:T(8,128)S(1)}, u32[]{:S(2)}) copy-start(f32[16,8,2048]{2,1,0:T(8,128)S(1)} %all-to-all-done) | copy-start | bytes 3145732
  49.7 29.9 %all-to-all-start.2 = ((f32[16,8,2048]{2,1,0:T(8,128)}), f32[16,8,2048]{2,1,0:T(8,128)}, u32[]{:S(2)}, u32[]{:S(2)}) async-start(f32[16,8,2048]{2,1,0:T(8,128)} %fusion.63), calls=%async_computation.2 | async-start | bytes 2097152 | tf_op jit(solution)/shard_map/all_to_all | solution.py:175
  60.7 2.3 copy-start.4
  79.6 30.1 %all-to-all-start.3 = ((f32[16,8,2048]{2,1,0:T(8,128)}), f32[16,8,2048]{2,1,0:T(8,128)}, u32[]{:S(2)}, u32[]{:S(2)}) async-start(f32[16,8,2048]{2,1,0:T(8,128)} %fusion.64), calls=%async_computation.3 | async-start | bytes 2097152 | tf_op jit(solution)/shard_map/all_to_all | solution.py:175
  109.7 29.8 %all-to-all-start.4 = ((f32[16,8,2048]{2,1,0:T(8,128)}), f32[16,8,2048]{2,1,0:T(8,128)S(1)}, u32[]{:S(2)}, u32[]{:S(2)}) async-start(f32[16,8,2048]{2,1,0:T(8,128)} %fusion.65), calls=%async_computation.4 | async-start | bytes 2097152 | tf_op jit(solution)/shard_map/all_to_all | solution.py:175
  118.9 27.3 %copy-start.3 = (bf16[64,32,384]{2,1,0:T(8,128)(2,1)S(1)}, bf16[64,32,384]{2,1,0:T(8,128)(2,1)}, u32[]{:S(2)}) copy-start(bf16[64,32,384]{2,1,0:T(8,128)(2,1)} %get-tuple-element.156) | copy-start | bytes 4718596
  139.5 29.9 %all-to-all-start.5 = ((f32[16,8,2048]{2,1,0:T(8,128)}), f32[16,8,2048]{2,1,0:T(8,128)}, u32[]{:S(2)}, u32[]{:S(2)}) async-start(f32[16,8,2048]{2,1,0:T(8,128)} %fusion.66), calls=%async_computation.5 | async-start | bytes 2097152 | tf_op jit(solution)/shard_map/all_to_all | solution.py:175
  148.8 28.9 %copy-start.18 = (bf16[64,32,128]{2,1,0:T(8,128)(2,1)S(1)}, bf16[64,32,128]{2,1,0:T(8,128)(2,1)}, u32[]{:S(2)}) copy-start(bf16[64,32,128]{2,1,0:T(8,128)(2,1)} %get-tuple-element.11) | copy-start | bytes 1572868
  169.5 29.8 %all-to-all-start.6 = ((f32[16,8,2048]{2,1,0:T(8,128)}), f32[16,8,2048]{2,1,0:T(8,128)S(1)}, u32[]{:S(2)}, u32[]{:S(2)}) async-start(f32[16,8,2048]{2,1,0:T(8,128)} %fusion.67), calls=%async_computation.6 | async-start | bytes 2097152 | tf_op jit(solution)/shard_map/all_to_all | solution.py:175
  180.4 27.1 %copy-start.20 = (bf16[64,32,128]{2,1,0:T(8,128)(2,1)S(1)}, bf16[64,32,128]{2,1,0:T(8,128)(2,1)}, u32[]{:S(2)}) copy-start(bf16[64,32,128]{2,1,0:T(8,128)(2,1)} %get-tuple-element.9) | copy-start | bytes 1572868
  199.3 8.2 %copy-start.7 = (f32[16,8,2048]{2,1,0:T(8,128)}, f32[16,8,2048]{2,1,0:T(8,128)S(1)}, u32[]{:S(2)}) copy-start(f32[16,8,2048]{2,1,0:T(8,128)S(1)} %all-to-all-done.6) | copy-start | bytes 3145732
  199.3 29.9 %all-to-all-start.7 = ((f32[16,8,2048]{2,1,0:T(8,128)}), f32[16,8,2048]{2,1,0:T(8,128)}, u32[]{:S(2)}, u32[]{:S(2)}) async-start(f32[16,8,2048]{2,1,0:T(8,128)} %fusion.68), calls=%async_computation.7 | async-start | bytes 2097152 | tf_op jit(solution)/shard_map/all_to_all | solution.py:175
  210.3 26.0 %copy-start.16 = (f32[64,32,128]{2,1,0:T(8,128)S(1)}, f32[64,32,128]{2,1,0:T(8,128)}, u32[]{:S(2)}) copy-start(f32[64,32,128]{2,1,0:T(8,128)} %get-tuple-element.8) | copy-start | bytes 3145732
  210.3 26.2 %copy-start.19 = (bf16[64,32,128]{2,1,0:T(8,128)(2,1)S(1)}, bf16[64,32,128]{2,1,0:T(8,128)(2,1)}, u32[]{:S(2)}) copy-start(bf16[64,32,128]{2,1,0:T(8,128)(2,1)} %get-tuple-element.7) | copy-start | bytes 1572868
  229.2 30.1 %all-to-all-start.8 = ((f32[16,8,2048]{2,1,0:T(8,128)}), f32[16,8,2048]{2,1,0:T(8,128)}, u32[]{:S(2)}, u32[]{:S(2)}) async-start(f32[16,8,2048]{2,1,0:T(8,128)} %fusion.69), calls=%async_computation.8 | async-start | bytes 2097152 | tf_op jit(solution)/shard_map/all_to_all | solution.py:175
  239.3 26.7 %copy-start.6 = (f32[16,8,2048]{2,1,0:T(8,128)S(1)}, f32[16,8,2048]{2,1,0:T(8,128)}, u32[]{:S(2)}) copy-start(f32[16,8,2048]{2,1,0:T(8,128)} %copy-done.5) | copy-start | bytes 3145732
  259.3 136.3 %all-to-all-start.9 = ((f32[16,8,2048]{2,1,0:T(8,128)}), f32[16,8,2048]{2,1,0:T(8,128)}, u32[]{:S(2)}, u32[]{:S(2)}) async-start(f32[16,8,2048]{2,1,0:T(8,128)} %fusion.70), calls=%async_computation.9 | async-start | bytes 2097152 | tf_op jit(solution)/shard_map/all_to_all | solution.py:175
  388.6 2.8 copy-start.12
  389.9 2.9 copy-start.13
  391.4 2.8 copy-start.14
  395.6 28.6 %all-to-all-start.1 = ((f32[2,1,262144]{2,1,0:T(1,128)}), f32[2,1,262144]{2,1,0:T(1,128)S(1)}, u32[]{:S(2)}, u32[]{:S(2)}) async-start(f32[2,1,262144]{2,1,0:T(1,128)} %reshape.179), calls=%async_computation.1 | async-start | bytes 4194304 | tf_op jit(solution)/shard_map/all_to_all | solution.py:180
  414.5 2.8 copy-start.9
  414.5 4.3 copy-start.11
  417.4 2.9 copy-start.15
  465.3 3.7 copy-start.1
  470.5 2.4 copy-start.37
  482.0 2.1 copy-start.35
  482.0 2.1 copy-start.36
  492.9 2.0 copy-start.31
  492.9 2.0 copy-start.32
  503.8 2.0 copy-start.33
  503.8 2.0 copy-start.34
  515.0 2.0 copy-start.29
  515.0 2.0 copy-start.30
  526.0 2.0 copy-start.27
  526.0 2.0 copy-start.28
  536.9 2.1 copy-start.25
  536.9 2.1 copy-start.26
  547.8 2.3 copy-start.42
  547.8 2.3 copy-start.43
  547.8 2.3 copy-start.44
  547.8 2.4 copy-start.45
  547.8 2.4 copy-start.46
  547.8 2.4 copy-start.47
  547.8 2.5 copy-start.48
  547.8 2.5 copy-start.49
  548.9 2.0 copy-start.57
  (48 other events, 57.7 us)

commit v9 on v8

--- a/solution.py
+++ b/solution.py
@@ -206,7 +206,7 @@
     n_grp = mesh.shape["grp"]
     n_pt = mesh.shape["pt"]
     return jax.shard_map(
-        make_body(n_grp, n_pt, 8),
+        make_body(n_grp, n_pt, 2),
         mesh=mesh,
         in_specs=(P("grp", "pt", None), P("grp", "pt", None)),
         out_specs=P("grp", "pt", None),

time: 639 us -> 490 us (0.77)
  waiting for transfers between devices: 131 us -> 86.8 us
  matrix products: 75 us -> 34.8 us
  starting transfers between devices: 65.7 us -> 37.7 us
  local copies, waits for them, and re-layouts: 225 us -> 205 us
  other arithmetic: 85.6 us -> 70.9 us
    all_to_all x9 -> x3, waiting for transfers between devices: 129 us -> 68.9 us  [to_points(): ev = lax.all_to_all(ev, 'pt', split_axis=0, concat_axis=0, tiled=False)]
    dot_general x8 -> x2, matrix products: 54.3 us -> 15.3 us  [multiply_points(): jnp.einsum('pak,pjk->paj', stacked, right_limbs, preferred_element_type=j...]
    all_to_all x9 -> x3, starting transfers between devices: 62 us -> 33.9 us  [to_points(): ev = lax.all_to_all(ev, 'pt', split_axis=0, concat_axis=0, tiled=False)]
    transpose x8 -> x2, local copies, waits for them, and re-layouts: 53.4 us -> 35.8 us  [body(): jnp.transpose(right_pts, (1, 4, 2, 0, 3))]
    all_to_all x1, waiting for transfers between devices: 2.46 us -> 17.9 us  [body(): lax.all_to_all(left_pts, 'grp', split_axis=0, concat_axis=0, tiled=True)]
    convert_element_type x32 -> x13, other arithmetic: 46.5 us -> 33.4 us  [limbs_bf16(): piece.astype(jnp.bfloat16)]
    slice x8 -> x2, local copies, waits for them, and re-layouts: 5.97 us -> 13.7 us  [multiply_points(): return fold3(levels[:, 0:n_i], levels[:, n_i:2 * n_i], levels[:, 2 * n_i:])]
    reshape x8 -> x2, local copies, waits for them, and re-layouts: 29.1 us -> 21.9 us  [to_points(): return ev.reshape(n_pt, d_local, rows, kl, FIRST)]
  transfers between devices with their start and end apart: 10 -> 4, of which waited for: 9 -> 2; matrix products, arithmetic and copies ran while one was open for 33% -> 35% of each run, Pallas kernels for 0% -> 0%
where the time goes in v9:
time: 490 us; the launch traced here: 485 us
  local copies, waits for them, and re-layouts  205 us (42%)
  waiting for transfers between devices  86.8 us (18%)
  other arithmetic  70.9 us (14%)
  blocking collectives  47.9 us (10%)
  starting transfers between devices  37.7 us (8%)
  matrix products  34.8 us (7%)
    all_to_all x3, waiting for transfers between devices, to_points(): ev = lax.all_to_all(ev, 'pt', split_axis=0, concat_axis=0, tiled=False)  68.9 us
    unnamed x102, local copies, waits for them, and re-layouts  62.6 us
    transpose x2, local copies, waits for them, and re-layouts, body(): jnp.transpose(right_pts, (1, 4, 2, 0, 3))  35.8 us
    reshape x4, local copies, waits for them, and re-layouts, body(): jnp.transpose(right_pts, (1, 4, 2, 0, 3))  35.5 us
    all_to_all x3, starting transfers between devices, to_points(): ev = lax.all_to_all(ev, 'pt', split_axis=0, concat_axis=0, tiled=False)  33.9 us
    convert_element_type x13, other arithmetic, limbs_bf16(): piece.astype(jnp.bfloat16)  33.4 us
    all_to_all x1, blocking collectives, body(): prod = lax.all_to_all(prod, 'pt', split_axis=0, concat_axis=0, tiled=False)  31.5 us
    reshape x2, local copies, waits for them, and re-layouts, to_points(): return ev.reshape(n_pt, d_local, rows, kl, FIRST)  21.9 us
  transfers between devices with their start and end apart: 4, of which 2 were waited for; matrix products, arithmetic and copies ran while one was open for 35% of the time, Pallas kernels for 0%

profile of v9, /device:TPU:1, one launch (start us, length us, event | category | flops | bytes accessed | tf_op | source)
XLA Modules:
  0.0 484.6 jit_solution(1323994074509837375)
XLA Ops:
  8.1 7.6 %all-to-all-start = ((f32[16,8,2048]{2,1,0:T(8,128)}), f32[16,8,2048]{2,1,0:T(8,128)S(1)}, u32[]{:S(2)}, u32[]{:S(2)}) async-start(f32[16,8,2048]{2,1,0:T(8,128)} %fusion.48), calls=%async_computation | async-start | bytes 2097152 | tf_op jit(solution)/shard_map/all_to_all | solution.py:175
  24.2 17.8 %subtract_convert_fusion.7 = (bf16[256,32,128]{2,1,0:T(8,128)(2,1)}, f32[256,32,128]{2,1,0:T(8,128)S(1)}, bf16[256,32,128]{2,1,0:T(8,128)(2,1)}, f32[256,32,128]{2,1,0:T(8,128)S(1)}) fusion(f32[32,128]{1,0:T(8,128)S(1)} %copy-done.31, f32[32,128]{1,0:T(8,128)S(1)} %copy-done.30, f32[32,128]{1,0:T(8,128)S(1)} %copy-done.29, f32[32,128]{1,0:T(8,128)S(1)} %copy-done.28, ...), kind=kLoop, calls=%fused_computation.45 | loop fusion | flops 125829120 | bytes 37896192 | tf_op jit(solution)/shard_map/convert_element_type | solution.py:105
  45.3 3.8 pad_maximum_fusion
  49.2 6.3 %fusion.71 = f32[384,8192]{1,0:T(8,128)} fusion(bf16[384,384]{1,0:T(8,128)(2,1)S(1)} %copy-done.3, bf16[8192,384]{1,0:T(8,128)(2,1)S(1)} %bitcast.117), kind=kOutput, calls=%fused_computation.155 | convolution fusion | flops 2415919104 | bytes 19169280 | tf_op jit(solution)/shard_map/dot_general | solution.py:118
  55.5 2.9 broadcast_in_dim.7
  58.4 4.6 copy.52
  63.0 4.6 broadcast_bitcast_fusion
  67.6 6.9 %reshape.83 = f32[2,1,262144]{2,1,0:T(1,128)} reshape(f32[2,8,16,8,8,32]{5,4,3,2,1,0:T(8,128)} %broadcast_bitcast_fusion) | data formatting | bytes 4194304
  74.5 3.8 all-to-all-start.1
  78.3 7.1 %fusion.12 = f32[16,8,8192]{2,1,0:T(8,128)} fusion(f32[384,8192]{1,0:T(8,128)} %fusion.71), kind=kLoop, calls=%fused_computation.25 | loop fusion | flops 16777216 | bytes 16777216 | tf_op jit(solution)/shard_map/reshape | solution.py:174
  85.3 17.9 %all-to-all-done.1 = f32[2,1,262144]{2,1,0:T(1,128)S(1)} async-done(((f32[2,1,262144]{2,1,0:T(1,128)}), f32[2,1,262144]{2,1,0:T(1,128)S(1)}, u32[]{:S(2)}, u32[]{:S(2)}) %all-to-all-start.1) | async-done | bytes 2097184 | tf_op jit(solution)/shard_map/all_to_all | solution.py:180
  104.7 6.4 %all-to-all-start.2 = ((f32[16,8,8192]{2,1,0:T(8,128)}), f32[16,8,8192]{2,1,0:T(8,128)}, u32[]{:S(2)}, u32[]{:S(2)}) async-start(f32[16,8,8192]{2,1,0:T(8,128)} %fusion.12), calls=%async_computation.2 | async-start | bytes 8388608 | tf_op jit(solution)/shard_map/all_to_all | solution.py:175
  111.1 5.6 %fusion.72 = f32[384,8192]{1,0:T(8,128)S(1)} fusion(bf16[384,384]{1,0:T(8,128)(2,1)S(1)} %copy-done.3, bf16[8192,384]{1,0:T(8,128)(2,1)} %bitcast.116), kind=kOutput, calls=%fused_computation.156 | convolution fusion | flops 2415919104 | bytes 19169280 | tf_op jit(solution)/shard_map/dot_general | solution.py:118
  116.7 3.6 fusion.13
  120.3 68.9 %all-to-all-done.2 = f32[16,8,8192]{2,1,0:T(8,128)} async-done(((f32[16,8,8192]{2,1,0:T(8,128)}), f32[16,8,8192]{2,1,0:T(8,128)}, u32[]{:S(2)}, u32[]{:S(2)}) %all-to-all-start.2) | async-done | bytes 4194336 | tf_op jit(solution)/shard_map/all_to_all | solution.py:175
  189.2 19.8 %all-to-all-start.3 = ((f32[16,8,8192]{2,1,0:T(8,128)}), f32[16,8,8192]{2,1,0:T(8,128)}, u32[]{:S(2)}, u32[]{:S(2)}) async-start(f32[16,8,8192]{2,1,0:T(8,128)} %fusion.13), calls=%async_computation.3 | async-start | bytes 8388608 | tf_op jit(solution)/shard_map/all_to_all | solution.py:175
  209.5 8.0 %reduce = f32[2,262144]{1,0:T(2,128)S(1)} reduce(f32[2,1,262144]{2,1,0:T(1,128)} %copy-done.2, f32[]{:T(128)} %broadcast.357), dimensions={1}, to_apply=%all_to_all.19.reduce_sub_computation | reduce | bytes 4194308 | tf_op jit(solution)/shard_map/all_to_all | solution.py:180
  217.6 6.5 %reshape.84 = f32[2,8,16,8,8,32]{5,4,3,2,1,0:T(8,128)} reshape(f32[2,262144]{1,0:T(2,128)S(1)} %reduce) | data formatting | bytes 4194304
  224.1 8.4 %bitcast_bitcast_fusion = f32[8,32,2,8,16,8]{1,0,5,4,3,2:T(8,128)} fusion(f32[2,8,16,8,8,32]{5,4,3,2,1,0:T(8,128)} %reshape.84), kind=kLoop, calls=%fused_computation.150 | loop fusion | bytes 4194304 | tf_op jit(solution)/shard_map/transpose | solution.py:181
  232.4 5.8 %reshape.68 = f32[256,16,128]{0,2,1:T(8,128)S(1)} reshape(f32[8,32,2,8,16,8]{1,0,5,4,3,2:T(8,128)} %bitcast_bitcast_fusion) | data formatting | bytes 4194304 | tf_op jit(solution)/shard_map/reshape | solution.py:182
  240.2 7.1 %subtract_convert_fusion.15 = (bf16[256,16,128]{2,1,0:T(8,128)(2,1)}, bf16[256,16,128]{2,1,0:T(8,128)(2,1)}, bf16[256,16,128]{2,1,0:T(8,128)(2,1)}, bf16[256,16,...) fusion(f32[256,16,128]{2,1,0:T(8,128)} %copy.54), kind=kLoop, calls=%fused_computation.93 | loop fusion | flops 33554432 | bytes 11534336 | tf_op jit(solution)/shard_map/convert_element_type | solution.py:156
  248.1 11.2 %reshape.71 = f32[16,8,32,8,32]{4,3,2,1,0:T(8,128)} reshape(f32[16,8,8192]{2,1,0:T(8,128)} %all-to-all-done.2) | data formatting | bytes 8388608 | tf_op jit(solution)/shard_map/reshape | solution.py:176
  259.3 17.9 %copy.59 = f32[8,32,32,16,8]{1,0,4,3,2:T(8,128)} copy(f32[8,32,32,16,8]{1,4,2,0,3:T(8,128)} %bitcast.114) | data formatting | bytes 8388608 | tf_op jit(solution)/shard_map/transpose | solution.py:187
  277.1 12.2 %reshape.72 = f32[256,32,128]{0,2,1:T(8,128)} reshape(f32[8,32,32,16,8]{1,0,4,3,2:T(8,128)} %copy.59) | data formatting | bytes 8388608 | tf_op jit(solution)/shard_map/reshape | solution.py:187
  289.4 5.5 %copy.61 = f32[256,32,128]{2,1,0:T(8,128)} copy(f32[256,32,128]{0,2,1:T(8,128)} %reshape.72) | data formatting | bytes 8388608 | tf_op jit(solution)/shard_map/reshape | solution.py:187
  294.9 3.3 subtract_convert_fusion.5
  299.3 7.6 %fusion = f32[256,48,32]{1,2,0:T(8,128)S(1)} fusion(bf16[256,32,128]{2,1,0:T(8,128)(2,1)S(1)} %get-tuple-element.20, bf16[256,32,128]{2,1,0:T(8,128)(2,1)S(1)} %get-tuple-element.19, bf16[256,32,128]{2,1,0:T(8,128)(2,1)S(1)} %get-tuple-element.18, bf16[256,16,128]{2,1,0:T(8,128)(2,1)S(1)} %copy-done.16, bf16[256,16,128]{2,1,0:T(8,128)(2,1)S(1)} %get-tuple-element.45, ...), kind=kOutput, calls=%fused_computation.8 | convolution fusion | flops 405798912 | bytes 17301504 | tf_op jit(solution)/shard_map/pak,pjk->paj/dot_general | solution.py:159
  306.9 6.8 %fusion.68 = (f32[256,16,32]{1,2,0:T(8,128)}, f32[256,16,32]{1,2,0:T(8,128)}, f32[256,16,32]{1,2,0:T(8,128)}) fusion(f32[256,48,32]{1,2,0:T(8,128)S(1)} %fusion), kind=kLoop, calls=%fused_computation.148 | loop fusion | bytes 3145728 | tf_op jit(solution)/shard_map/slice | solution.py:161
  313.7 3.8 copy.76
  317.5 3.8 copy.77
  321.3 3.8 copy.78
  325.1 10.8 %reshape.75 = f32[16,8,32,8,32]{4,3,2,1,0:T(8,128)} reshape(f32[16,8,8192]{2,1,0:T(8,128)} %all-to-all-done.3) | data formatting | bytes 8388608 | tf_op jit(solution)/shard_map/reshape | solution.py:176
  335.9 17.9 %copy.65 = f32[8,32,32,16,8]{1,0,4,3,2:T(8,128)} copy(f32[8,32,32,16,8]{1,4,2,0,3:T(8,128)} %bitcast.115) | data formatting | bytes 8388608 | tf_op jit(solution)/shard_map/transpose | solution.py:187
  353.8 12.2 %reshape.76 = f32[256,32,128]{0,2,1:T(8,128)} reshape(f32[8,32,32,16,8]{1,0,4,3,2:T(8,128)} %copy.65) | data formatting | bytes 8388608 | tf_op jit(solution)/shard_map/reshape | solution.py:187
  366.0 5.5 %copy.67 = f32[256,32,128]{2,1,0:T(8,128)} copy(f32[256,32,128]{0,2,1:T(8,128)} %reshape.76) | data formatting | bytes 8388608 | tf_op jit(solution)/shard_map/reshape | solution.py:187
  371.6 3.3 subtract_convert_fusion.1
  376.5 7.7 %fusion.6 = f32[256,48,32]{1,2,0:T(8,128)S(1)} fusion(bf16[256,32,128]{2,1,0:T(8,128)(2,1)S(1)} %get-tuple-element.30, bf16[256,32,128]{2,1,0:T(8,128)(2,1)S(1)} %get-tuple-element.29, bf16[256,32,128]{2,1,0:T(8,128)(2,1)S(1)} %get-tuple-element.28, bf16[256,16,128]{2,1,0:T(8,128)(2,1)S(1)} %copy-done.17, bf16[256,16,128]{2,1,0:T(8,128)(2,1)S(1)} %copy-done.7, ...), kind=kOutput, calls=%fused_computation.15 | convolution fusion | flops 405798912 | bytes 17301504 | tf_op jit(solution)/shard_map/pak,pjk->paj/dot_general | solution.py:159
  384.2 6.8 %fusion.69 = (f32[256,16,32]{1,2,0:T(8,128)}, f32[256,16,32]{1,2,0:T(8,128)}, f32[256,16,32]{1,2,0:T(8,128)}) fusion(f32[256,48,32]{1,2,0:T(8,128)S(1)} %fusion.6), kind=kLoop, calls=%fused_computation.149 | loop fusion | bytes 3145728 | tf_op jit(solution)/shard_map/slice | solution.py:161
  391.0 3.8 copy.79
  394.8 3.8 copy.80
  398.6 4.5 copy.81
  404.8 16.4 %all_to_all.30 = f32[256,2,8,64]{0,3,2,1:T(8,128)S(1)} all-to-all(f32[256,2,8,64]{0,3,2,1:T(8,128)S(1)} %bitcast.120), channel_id=1, replica_groups=mesh['grp'=2,'pt'=16] {'grp'}, dimensions={1} | all-to-all | bytes 2097152 | tf_op jit(solution)/shard_map/all_to_all | solution.py:194
  423.8 4.8 copy_bitcast_fusion
  428.6 3.9 reshape.85
  432.5 31.5 %all_to_all.31 = f32[16,1,16384]{2,1,0:T(1,128)S(1)} all-to-all(f32[16,1,16384]{2,1,0:T(1,128)S(1)} %reshape.85), channel_id=1, replica_groups=mesh['grp'=2,'pt'=16] {'pt'}, dimensions={0} | all-to-all | bytes 2097152 | tf_op jit(solution)/shard_map/all_to_all | solution.py:197
  464.0 3.1 reduce.1
  467.0 2.8 reshape.86
  474.9 2.8 copy.75
  (122 shorter events, 42.5 us)
Async XLA Ops:
  0.0 2.8 copy-start.23
  0.0 2.8 copy-start.24
  0.0 2.8 copy-start.25
  0.0 2.8 copy-start.26
  0.0 2.8 copy-start.27
  0.0 2.8 copy-start.28
  0.0 2.8 copy-start.29
  0.1 2.8 copy-start.30
  0.1 2.8 copy-start.31
  2.9 2.6 copy-start.3
  8.1 47.4 %all-to-all-start = ((f32[16,8,2048]{2,1,0:T(8,128)}), f32[16,8,2048]{2,1,0:T(8,128)S(1)}, u32[]{:S(2)}, u32[]{:S(2)}) async-start(f32[16,8,2048]{2,1,0:T(8,128)} %fusion.48), calls=%async_computation | async-start | bytes 2097152 | tf_op jit(solution)/shard_map/all_to_all | solution.py:175
  19.3 1.2 copy-start.22
  43.1 1.6 copy-start
  43.1 2.2 copy-start.1
  74.5 28.7 %all-to-all-start.1 = ((f32[2,1,262144]{2,1,0:T(1,128)}), f32[2,1,262144]{2,1,0:T(1,128)S(1)}, u32[]{:S(2)}, u32[]{:S(2)}) async-start(f32[2,1,262144]{2,1,0:T(1,128)} %reshape.83), calls=%async_computation.1 | async-start | bytes 4194304 | tf_op jit(solution)/shard_map/all_to_all | solution.py:180
  103.2 1.4 copy-start.2
  104.7 84.5 %all-to-all-start.2 = ((f32[16,8,8192]{2,1,0:T(8,128)}), f32[16,8,8192]{2,1,0:T(8,128)}, u32[]{:S(2)}, u32[]{:S(2)}) async-start(f32[16,8,8192]{2,1,0:T(8,128)} %fusion.12), calls=%async_computation.2 | async-start | bytes 8388608 | tf_op jit(solution)/shard_map/all_to_all | solution.py:175
  189.2 135.9 %all-to-all-start.3 = ((f32[16,8,8192]{2,1,0:T(8,128)}), f32[16,8,8192]{2,1,0:T(8,128)}, u32[]{:S(2)}, u32[]{:S(2)}) async-start(f32[16,8,8192]{2,1,0:T(8,128)} %fusion.13), calls=%async_computation.3 | async-start | bytes 8388608 | tf_op jit(solution)/shard_map/all_to_all | solution.py:175
  248.1 50.1 %copy-start.4 = (bf16[256,16,128]{2,1,0:T(8,128)(2,1)}, bf16[256,16,128]{2,1,0:T(8,128)(2,1)S(1)}, u32[]{:S(2)}) copy-start(bf16[256,16,128]{2,1,0:T(8,128)(2,1)S(1)} %get-tuple-element.44) | copy-start | bytes 3145732
  248.1 50.1 %copy-start.6 = (bf16[256,16,128]{2,1,0:T(8,128)(2,1)}, bf16[256,16,128]{2,1,0:T(8,128)(2,1)S(1)}, u32[]{:S(2)}) copy-start(bf16[256,16,128]{2,1,0:T(8,128)(2,1)S(1)} %get-tuple-element.45) | copy-start | bytes 3145732
  294.9 3.3 copy-start.8
  294.9 3.4 copy-start.10
  294.9 3.4 copy-start.12
  294.9 3.4 copy-start.14
  294.9 3.7 copy-start.16
  294.9 4.0 copy-start.18
  294.9 4.3 copy-start.20
  371.5 3.3 copy-start.5
  371.5 3.4 copy-start.7
  371.5 3.4 copy-start.9
  371.5 3.4 copy-start.11
  371.5 3.7 copy-start.13
  371.6 4.0 copy-start.15
  371.6 4.3 copy-start.17
  371.6 4.6 copy-start.19
  371.6 4.9 %copy-start.21 = (bf16[256,16,128]{2,1,0:T(8,128)(2,1)S(1)}, bf16[256,16,128]{2,1,0:T(8,128)(2,1)}, u32[]{:S(2)}) copy-start(bf16[256,16,128]{2,1,0:T(8,128)(2,1)} %get-tuple-element.43) | copy-start | bytes 3145732
  474.9 3.3 copy-start.42
  477.7 1.6 copy-start.33
  477.7 1.6 copy-start.34
  477.7 1.6 copy-start.35
  477.8 1.6 copy-start.36
  477.8 1.6 copy-start.37
  477.8 1.6 copy-start.38
  477.8 1.6 copy-start.39
  477.8 1.6 copy-start.40
  477.8 1.6 copy-start.41
  479.4 2.4 copy-start.32

commit v10 on v9

--- a/solution.py
+++ b/solution.py
@@ -175,19 +175,23 @@
             ev = lax.all_to_all(ev, "pt", split_axis=0, concat_axis=0, tiled=False)
             return ev.reshape(n_pt, d_local, rows, kl, FIRST)
 
-        left_pts = to_points(left_factor, il)
-        left_pts = jnp.broadcast_to(left_pts[None], (n_grp,) + left_pts.shape)
-        left_pts = lax.all_to_all(left_pts, "grp", split_axis=0, concat_axis=0, tiled=True)
-        left_pts = jnp.transpose(left_pts, (2, 5, 0, 3, 1, 4))
-        left_pts = left_pts.reshape(d_local * FIRST, n_grp * il, n_pt * kl)
+        left_all = lax.all_gather(left_factor, "grp", axis=0, tiled=True)
+        n_i = left_all.shape[0]
         jc = jl // n_chunks
+        left_pts = None
         prods = []
         for chunk in range(n_chunks):
-            right_pts = to_points(right_factor[chunk * jc : (chunk + 1) * jc], jc)
+            right_part = right_factor[chunk * jc : (chunk + 1) * jc]
+            if chunk == 0:
+                both = to_points(jnp.concatenate([left_all, right_part], axis=0), n_i + jc)
+                left_pts = jnp.transpose(both[:, :, :n_i], (1, 4, 2, 0, 3))
+                left_pts = left_pts.reshape(d_local * FIRST, n_i, n_pt * kl)
+                right_pts = both[:, :, n_i:]
+            else:
+                right_pts = to_points(right_part, jc)
             right_pts = jnp.transpose(right_pts, (1, 4, 2, 0, 3)).reshape(d_local * FIRST, jc, n_pt * kl)
             prods.append(multiply_points(left_pts, right_pts))
         prod = jnp.concatenate(prods, axis=2) if n_chunks > 1 else prods[0]
-        n_i = prod.shape[1]
         ib = n_i // n_grp
         jb = n_grp * jl // n_pt
         prod = prod.reshape(d_local * FIRST, n_grp, ib, jl)

time: 490 us -> 520 us (1.061)
  blocking collectives: 47.9 us -> 69.5 us
  waiting for transfers between devices: 86.8 us -> 102 us
  between operations: 1.28 us -> 14.4 us
  starting transfers between devices: 37.7 us -> 27.6 us
  local copies, waits for them, and re-layouts: 205 us -> 198 us
  other arithmetic: 70.9 us -> 65.2 us
    all_to_all x3 -> x2, waiting for transfers between devices: 68.9 us -> 101 us  [to_points(): ev = lax.all_to_all(ev, 'pt', split_axis=0, concat_axis=0, tiled=False)]
    all_to_all x1, blocking collectives: 31.5 us -> 53.2 us  [body(): prod = lax.all_to_all(prod, 'pt', split_axis=0, concat_axis=0, tiled=False)]
    unnamed x102 -> x97, local copies, waits for them, and re-layouts: 62.6 us -> 42.9 us
    all_to_all x1 -> x0, waiting for transfers between devices: 17.9 us -> none  [body(): lax.all_to_all(left_pts, 'grp', split_axis=0, concat_axis=0, tiled=True)]
    transpose x2 -> x3, local copies, waits for them, and re-layouts: 35.8 us -> 47.3 us  [body(): jnp.transpose(right_pts, (1, 4, 2, 0, 3))]
    all_to_all x1 -> x0, other arithmetic: 8.02 us -> none  [body(): lax.all_to_all(left_pts, 'grp', split_axis=0, concat_axis=0, tiled=True)]
    broadcast_in_dim x2 -> x0, local copies, waits for them, and re-layouts: 7.5 us -> none  [body(): left_pts = jnp.broadcast_to(left_pts[None], (n_grp,) + left_pts.shape)]
    all_to_all x3 -> x2, starting transfers between devices: 33.9 us -> 27.6 us  [to_points(): ev = lax.all_to_all(ev, 'pt', split_axis=0, concat_axis=0, tiled=False)]
  transfers between devices with their start and end apart: 4 -> 3, of which waited for: 2 -> 2; matrix products, arithmetic and copies ran while one was open for 35% -> 22% of each run, Pallas kernels for 0% -> 0%
where the time goes in v10:
time: 520 us; the launch traced here: 511 us
  local copies, waits for them, and re-layouts  198 us (38%)
  waiting for transfers between devices  102 us (20%)
  blocking collectives  69.5 us (13%)
  other arithmetic  65.2 us (13%)
  matrix products  34.2 us (7%)
  starting transfers between devices  27.6 us (5%)
  between operations  14.4 us (3%)
    all_to_all x2, waiting for transfers between devices, to_points(): ev = lax.all_to_all(ev, 'pt', split_axis=0, concat_axis=0, tiled=False)  101 us
    all_to_all x1, blocking collectives, body(): prod = lax.all_to_all(prod, 'pt', split_axis=0, concat_axis=0, tiled=False)  53.2 us
    transpose x3, local copies, waits for them, and re-layouts, body(): jnp.transpose(right_pts, (1, 4, 2, 0, 3))  47.3 us
    unnamed x97, local copies, waits for them, and re-layouts  42.9 us
    convert_element_type x11, other arithmetic, limbs_bf16(): piece.astype(jnp.bfloat16)  36.4 us
    reshape x4, local copies, waits for them, and re-layouts, body(): jnp.transpose(right_pts, (1, 4, 2, 0, 3))  35.4 us
    all_to_all x2, starting transfers between devices, to_points(): ev = lax.all_to_all(ev, 'pt', split_axis=0, concat_axis=0, tiled=False)  27.6 us
    reshape x2, local copies, waits for them, and re-layouts, to_points(): return ev.reshape(n_pt, d_local, rows, kl, FIRST)  24.6 us
  transfers between devices with their start and end apart: 3, of which 2 were waited for; matrix products, arithmetic and copies ran while one was open for 22% of the time, Pallas kernels for 0%

profile of v10, /device:TPU:1, one launch (start us, length us, event | category | flops | bytes accessed | tf_op | source)
XLA Modules:
  0.0 510.7 jit_solution(12267703839987951568)
XLA Ops:
  7.3 2.5 fusion.59
  13.0 8.4 %subtract_convert_fusion.5 = (bf16[256,32,128]{2,1,0:T(8,128)(2,1)S(1)}, f32[256,32,128]{2,1,0:T(8,128)S(1)}) fusion(f32[32,128]{1,0:T(8,128)S(1)} %copy-done.22, f32[32,128]{1,0:T(8,128)S(1)} %copy-done.23, f32[32,128]{1,0:T(8,128)S(1)} %copy-done.24, f32[32,128]{1,0:T(8,128)S(1)} %copy-done.25, f32[32,128]{1,0:T(8,128)S(1)} %copy-done.26, ...), kind=kLoop, calls=%fused_computation.47 | loop fusion | flops 62914560 | bytes 19021824 | tf_op jit(solution)/shard_map/convert_element_type | solution.py:105
  23.4 3.4 fusion.61
  26.9 3.6 fusion.19
  30.4 8.0 %all-to-all-start.1 = ((f32[16,8,8192]{2,1,0:T(8,128)}), f32[16,8,8192]{2,1,0:T(8,128)}, u32[]{:S(2)}, u32[]{:S(2)}) async-start(f32[16,8,8192]{2,1,0:T(8,128)} %fusion.19), calls=%async_computation.1 | async-start | bytes 8388608 | tf_op jit(solution)/shard_map/all_to_all | solution.py:175
  41.7 2.9 convolution_bitcast_fusion
  44.5 12.5 %subtract_convert_fusion.1 = (bf16[384,32,128]{2,1,0:T(8,128)(2,1)S(1)}, f32[384,32,128]{2,1,0:T(8,128)S(1)}) fusion(f32[32,128]{1,0:T(8,128)S(1)} %copy-done.22, f32[32,128]{1,0:T(8,128)S(1)} %copy-done.23, f32[32,128]{1,0:T(8,128)S(1)} %copy-done.24, f32[32,128]{1,0:T(8,128)S(1)} %copy-done.25, f32[32,128]{1,0:T(8,128)S(1)} %copy-done.26, ...), kind=kLoop, calls=%fused_computation.28 | loop fusion | flops 94371840 | bytes 28459008 | tf_op jit(solution)/shard_map/convert_element_type | solution.py:105
  60.1 9.1 %fusion.60 = f32[384,12288]{1,0:T(8,128)} fusion(bf16[384,384]{1,0:T(8,128)(2,1)S(1)} %copy-done.3, bf16[12288,384]{1,0:T(8,128)(2,1)S(1)} %bitcast.89), kind=kOutput, calls=%fused_computation.131 | convolution fusion | flops 3623878656 | bytes 28606464 | tf_op jit(solution)/shard_map/dot_general | solution.py:118
  69.2 9.8 %fusion = f32[16,8,12288]{2,1,0:T(8,128)} fusion(f32[384,12288]{1,0:T(8,128)} %fusion.60), kind=kLoop, calls=%fused_computation.11 | loop fusion | flops 25165824 | bytes 25165824 | tf_op jit(solution)/shard_map/reshape | solution.py:174
  79.0 37.4 %all-to-all-done.1 = f32[16,8,8192]{2,1,0:T(8,128)} async-done(((f32[16,8,8192]{2,1,0:T(8,128)}), f32[16,8,8192]{2,1,0:T(8,128)}, u32[]{:S(2)}, u32[]{:S(2)}) %all-to-all-start.1) | async-done | bytes 4194336 | tf_op jit(solution)/shard_map/all_to_all | solution.py:175
  116.3 19.6 %all-to-all-start = ((f32[16,8,12288]{2,1,0:T(8,128)}), f32[16,8,12288]{2,1,0:T(8,128)}, u32[]{:S(2)}, u32[]{:S(2)}) async-start(f32[16,8,12288]{2,1,0:T(8,128)} %fusion), calls=%async_computation | async-start | bytes 12582912 | tf_op jit(solution)/shard_map/all_to_all | solution.py:175
  135.9 10.8 %reshape.66 = f32[16,8,32,8,32]{4,3,2,1,0:T(8,128)} reshape(f32[16,8,8192]{2,1,0:T(8,128)} %all-to-all-done.1) | data formatting | bytes 8388608 | tf_op jit(solution)/shard_map/reshape | solution.py:176
  146.7 17.7 %copy.64 = f32[8,32,32,16,8]{1,0,4,3,2:T(8,128)} copy(f32[8,32,32,16,8]{1,4,2,0,3:T(8,128)} %bitcast.88) | data formatting | bytes 8388608 | tf_op jit(solution)/shard_map/transpose | solution.py:192
  164.4 12.2 %reshape.67 = f32[256,32,128]{0,2,1:T(8,128)} reshape(f32[8,32,32,16,8]{1,0,4,3,2:T(8,128)} %copy.64) | data formatting | bytes 8388608 | tf_op jit(solution)/shard_map/reshape | solution.py:192
  176.6 5.5 %copy.66 = f32[256,32,128]{2,1,0:T(8,128)} copy(f32[256,32,128]{0,2,1:T(8,128)} %reshape.67) | data formatting | bytes 8388608 | tf_op jit(solution)/shard_map/reshape | solution.py:192
  182.1 4.8 subtract_convert_fusion.3
  186.9 63.4 %all-to-all-done = f32[16,8,12288]{2,1,0:T(8,128)} async-done(((f32[16,8,12288]{2,1,0:T(8,128)}), f32[16,8,12288]{2,1,0:T(8,128)}, u32[]{:S(2)}, u32[]{:S(2)}) %all-to-all-start) | async-done | bytes 6291488 | tf_op jit(solution)/shard_map/all_to_all | solution.py:175
  250.4 13.8 %reshape.61 = f32[16,8,48,8,32]{4,3,2,1,0:T(8,128)} reshape(f32[16,8,12288]{2,1,0:T(8,128)} %all-to-all-done) | data formatting | bytes 12582912 | tf_op jit(solution)/shard_map/reshape | solution.py:176
  264.2 4.0 slice_bitcast_fusion.1
  268.2 11.8 %slice_bitcast_fusion = f32[8,32,32,16,8]{1,4,2,0,3:T(8,128)} fusion(f32[16,8,48,8,32]{4,3,2,1,0:T(8,128)} %reshape.61), kind=kLoop, calls=%fused_computation.3 | loop fusion | bytes 8388608 | tf_op jit(solution)/shard_map/transpose | solution.py:192
  280.0 8.2 %copy.51 = f32[8,32,16,16,8]{1,0,4,3,2:T(8,128)} copy(f32[8,32,16,16,8]{1,4,2,0,3:T(8,128)S(1)} %slice_bitcast_fusion.1) | data formatting | bytes 4194304 | tf_op jit(solution)/shard_map/transpose | solution.py:187
  288.2 5.8 %reshape.62 = f32[256,16,128]{0,2,1:T(8,128)S(1)} reshape(f32[8,32,16,16,8]{1,0,4,3,2:T(8,128)} %copy.51) | data formatting | bytes 4194304 | tf_op jit(solution)/shard_map/reshape | solution.py:188
  296.0 5.6 %subtract_convert_fusion.15 = (bf16[256,16,128]{2,1,0:T(8,128)(2,1)S(1)}, bf16[256,16,128]{2,1,0:T(8,128)(2,1)S(1)}, bf16[256,16,128]{2,1,0:T(8,128)(2,1)S(1)}, ...) fusion(f32[256,16,128]{2,1,0:T(8,128)} %copy.53), kind=kLoop, calls=%fused_computation.92 | loop fusion | flops 33554432 | bytes 11534336 | tf_op jit(solution)/shard_map/convert_element_type | solution.py:156
  307.0 7.7 %fusion.7 = f32[256,48,32]{1,2,0:T(8,128)S(1)} fusion(bf16[256,32,128]{2,1,0:T(8,128)(2,1)S(1)} %copy-done.2, bf16[256,32,128]{2,1,0:T(8,128)(2,1)S(1)} %copy-done.1, bf16[256,32,128]{2,1,0:T(8,128)(2,1)S(1)} %copy-done, bf16[256,16,128]{2,1,0:T(8,128)(2,1)S(1)} %get-tuple-element.38, bf16[256,16,128]{2,1,0:T(8,128)(2,1)S(1)} %get-tuple-element.43, ...), kind=kOutput, calls=%fused_computation.19 | convolution fusion | flops 405798912 | bytes 17301504 | tf_op jit(solution)/shard_map/pak,pjk->paj/dot_general | solution.py:159
  314.7 6.8 %fusion.58 = (f32[256,16,32]{1,2,0:T(8,128)}, f32[256,16,32]{1,2,0:T(8,128)}, f32[256,16,32]{1,2,0:T(8,128)}) fusion(f32[256,48,32]{1,2,0:T(8,128)S(1)} %fusion.7), kind=kLoop, calls=%fused_computation.127 | loop fusion | bytes 3145728 | tf_op jit(solution)/shard_map/slice | solution.py:161
  321.5 3.8 copy.78
  325.3 4.3 copy.79
  329.5 3.8 copy.80
  333.3 17.7 %copy.58 = f32[8,32,32,16,8]{1,0,4,3,2:T(8,128)} copy(f32[8,32,32,16,8]{1,4,2,0,3:T(8,128)} %slice_bitcast_fusion) | data formatting | bytes 8388608 | tf_op jit(solution)/shard_map/transpose | solution.py:192
  351.1 12.2 %reshape.63 = f32[256,32,128]{0,2,1:T(8,128)} reshape(f32[8,32,32,16,8]{1,0,4,3,2:T(8,128)} %copy.58) | data formatting | bytes 8388608 | tf_op jit(solution)/shard_map/reshape | solution.py:192
  363.3 5.5 %copy.60 = f32[256,32,128]{2,1,0:T(8,128)} copy(f32[256,32,128]{0,2,1:T(8,128)} %reshape.63) | data formatting | bytes 8388608 | tf_op jit(solution)/shard_map/reshape | solution.py:192
  368.8 3.3 subtract_convert_fusion.7
  373.7 7.7 %fusion.1 = f32[256,48,32]{1,2,0:T(8,128)S(1)} fusion(bf16[256,32,128]{2,1,0:T(8,128)(2,1)S(1)} %get-tuple-element.20, bf16[256,32,128]{2,1,0:T(8,128)(2,1)S(1)} %get-tuple-element.19, bf16[256,32,128]{2,1,0:T(8,128)(2,1)S(1)} %get-tuple-element.18, bf16[256,16,128]{2,1,0:T(8,128)(2,1)S(1)} %copy-done.17, bf16[256,16,128]{2,1,0:T(8,128)(2,1)S(1)} %copy-done.7, ...), kind=kOutput, calls=%fused_computation.12 | convolution fusion | flops 405798912 | bytes 17301504 | tf_op jit(solution)/shard_map/pak,pjk->paj/dot_general | solution.py:159
  381.4 6.8 %fusion.57 = (f32[256,16,32]{1,2,0:T(8,128)}, f32[256,16,32]{1,2,0:T(8,128)}, f32[256,16,32]{1,2,0:T(8,128)}) fusion(f32[256,48,32]{1,2,0:T(8,128)S(1)} %fusion.1), kind=kLoop, calls=%fused_computation.126 | loop fusion | bytes 3145728 | tf_op jit(solution)/shard_map/slice | solution.py:161
  388.2 3.8 copy.75
  392.0 4.0 copy.76
  396.0 4.5 copy.77
  402.1 16.3 %all_to_all.20 = f32[256,2,8,64]{0,3,2,1:T(8,128)S(1)} all-to-all(f32[256,2,8,64]{0,3,2,1:T(8,128)S(1)} %bitcast.92), channel_id=1, replica_groups=mesh['grp'=2,'pt'=16] {'grp'}, dimensions={1} | all-to-all | bytes 2097152 | tf_op jit(solution)/shard_map/all_to_all | solution.py:198
  418.5 2.5 reshape.69
  421.0 4.8 copy_bitcast_fusion
  425.8 3.9 reshape.74
  429.7 53.2 %all_to_all.21 = f32[16,1,16384]{2,1,0:T(1,128)S(1)} all-to-all(f32[16,1,16384]{2,1,0:T(1,128)S(1)} %reshape.74), channel_id=1, replica_groups=mesh['grp'=2,'pt'=16] {'pt'}, dimensions={0} | all-to-all | bytes 2097152 | tf_op jit(solution)/shard_map/all_to_all | solution.py:201
  483.4 3.1 reduce
  486.6 2.8 reshape.75
  489.3 2.5 bitcast_bitcast_fusion
  491.8 2.6 copy.72
  494.4 2.8 copy.74
  499.0 2.1 subtract_convert_fusion.17
  (111 shorter events, 27.3 us)
Async XLA Ops:
  6.5 31.9 %all-gather.2.cloned.1.call-start = ((), (), s32[]{:S(2)}) async-start(), calls=%async_computation.4 | async-start | bytes 1572864 | tf_op jit(solution)/shard_map/all_gather | solution.py:178
  9.8 1.2 copy-start.31
  10.9 1.9 copy-start.22
  10.9 1.9 copy-start.23
  10.9 1.9 copy-start.24
  11.0 1.9 copy-start.25
  11.0 1.9 copy-start.26
  11.0 1.9 copy-start.27
  11.0 1.9 copy-start.28
  11.0 1.9 copy-start.29
  11.0 1.9 copy-start.30
  22.5 1.0 copy-start.3
  30.4 85.9 %all-to-all-start.1 = ((f32[16,8,8192]{2,1,0:T(8,128)}), f32[16,8,8192]{2,1,0:T(8,128)}, u32[]{:S(2)}, u32[]{:S(2)}) async-start(f32[16,8,8192]{2,1,0:T(8,128)} %fusion.19), calls=%async_computation.1 | async-start | bytes 8388608 | tf_op jit(solution)/shard_map/all_to_all | solution.py:175
  116.3 134.1 %all-to-all-start = ((f32[16,8,12288]{2,1,0:T(8,128)}), f32[16,8,12288]{2,1,0:T(8,128)}, u32[]{:S(2)}, u32[]{:S(2)}) async-start(f32[16,8,12288]{2,1,0:T(8,128)} %fusion), calls=%async_computation | async-start | bytes 12582912 | tf_op jit(solution)/shard_map/all_to_all | solution.py:175
  296.0 10.2 %copy-start.2 = (bf16[256,32,128]{2,1,0:T(8,128)(2,1)S(1)}, bf16[256,32,128]{2,1,0:T(8,128)(2,1)}, u32[]{:S(2)}) copy-start(bf16[256,32,128]{2,1,0:T(8,128)(2,1)} %get-tuple-element.28) | copy-start | bytes 6291460
  301.7 1.0 copy-start.8
  301.7 1.4 copy-start.10
  301.7 1.7 copy-start.12
  301.7 2.1 copy-start.14
  301.7 2.6 copy-start.16
  301.7 3.1 copy-start.18
  301.7 3.5 copy-start.20
  301.7 4.5 copy-start
  301.7 5.3 %copy-start.1 = (bf16[256,32,128]{2,1,0:T(8,128)(2,1)S(1)}, bf16[256,32,128]{2,1,0:T(8,128)(2,1)}, u32[]{:S(2)}) copy-start(bf16[256,32,128]{2,1,0:T(8,128)(2,1)} %get-tuple-element.27) | copy-start | bytes 6291460
  302.5 3.3 copy-start.4
  302.5 3.7 copy-start.6
  368.7 3.3 copy-start.5
  368.7 3.4 copy-start.7
  368.7 3.4 copy-start.9
  368.7 3.4 copy-start.11
  368.7 3.7 copy-start.13
  368.8 4.0 copy-start.15
  368.8 4.3 copy-start.17
  368.8 4.6 copy-start.19
  368.8 4.9 copy-start.21
  494.4 3.3 copy-start.42
  497.2 1.6 copy-start.33
  497.2 1.6 copy-start.34
  497.3 1.6 copy-start.35
  497.3 1.6 copy-start.36
  497.3 1.6 copy-start.37
  497.3 1.6 copy-start.38
  497.3 1.6 copy-start.39
  497.3 1.6 copy-start.40
  497.3 1.6 copy-start.41
  499.0 2.4 copy-start.32
Sparse Core Ops, SparseCore 0:
  8.9 23.3 all-gather.1

commit v11 on v10

--- a/solution.py
+++ b/solution.py
@@ -169,28 +169,41 @@
         il, kl, _ = left_factor.shape
         jl = right_factor.shape[0]
 
-        def to_points(x, rows):
+        def send_points(x, rows):
             ev = forward(x.reshape(rows * kl, -1), tables)
-            ev = ev.reshape(n_pt, d_local, rows * kl * FIRST)
-            ev = lax.all_to_all(ev, "pt", split_axis=0, concat_axis=0, tiled=False)
-            return ev.reshape(n_pt, d_local, rows, kl, FIRST)
+            return ev.reshape(n_pt, d_local, rows * kl * FIRST)
+
+        def exchange(ev):
+            return lax.all_to_all(ev, "pt", split_axis=0, concat_axis=0, tiled=False)
 
         left_all = lax.all_gather(left_factor, "grp", axis=0, tiled=True)
         n_i = left_all.shape[0]
         jc = jl // n_chunks
+        sends = []
+        for chunk in range(n_chunks):
+            right_part = right_factor[chunk * jc : (chunk + 1) * jc]
+            if chunk == 0:
+                right_part = jnp.concatenate([left_all, right_part], axis=0)
+            sends.append(send_points(right_part, right_part.shape[0]))
+        received = exchange(sends[0])
         left_pts = None
         prods = []
         for chunk in range(n_chunks):
-            right_part = right_factor[chunk * jc : (chunk + 1) * jc]
+            if chunk + 1 < n_chunks:
+                received, sends[chunk + 1] = lax.optimization_barrier((received, sends[chunk + 1]))
+                nxt = exchange(sends[chunk + 1])
+            rows = received.shape[2] // (kl * FIRST)
+            both = received.reshape(n_pt, d_local, rows, kl, FIRST)
             if chunk == 0:
-                both = to_points(jnp.concatenate([left_all, right_part], axis=0), n_i + jc)
                 left_pts = jnp.transpose(both[:, :, :n_i], (1, 4, 2, 0, 3))
                 left_pts = left_pts.reshape(d_local * FIRST, n_i, n_pt * kl)
                 right_pts = both[:, :, n_i:]
             else:
-                right_pts = to_points(right_part, jc)
+                right_pts = both
             right_pts = jnp.transpose(right_pts, (1, 4, 2, 0, 3)).reshape(d_local * FIRST, jc, n_pt * kl)
             prods.append(multiply_points(left_pts, right_pts))
+            if chunk + 1 < n_chunks:
+                received = nxt
         prod = jnp.concatenate(prods, axis=2) if n_chunks > 1 else prods[0]
         ib = n_i // n_grp
         jb = n_grp * jl // n_pt

time: 520 us -> 505 us (0.971)
  blocking collectives: 69.5 us -> 47.9 us
  waiting for transfers between devices: 102 us -> 116 us
  local copies, waits for them, and re-layouts: 198 us -> 188 us
  starting transfers between devices: 27.6 us -> 34.9 us
    all_to_all x1, blocking collectives: 53.2 us -> 31.4 us  [body(): prod = lax.all_to_all(prod, 'pt', split_axis=0, concat_axis=0, tiled=False)]
    all_gather x1, waiting for transfers between devices: 0.02 us -> 21.2 us  [body(): left_all = lax.all_gather(left_factor, 'grp', axis=0, tiled=True)]
    transpose x3, local copies, waits for them, and re-layouts: 47.3 us -> 36.1 us  [body(): jnp.transpose(right_pts, (1, 4, 2, 0, 3))]
    all_to_all x2, starting transfers between devices: 27.6 us -> 34.9 us  [exchange(): return lax.all_to_all(ev, 'pt', split_axis=0, concat_axis=0, tiled=False)]
    all_to_all x2, waiting for transfers between devices: 101 us -> 94 us  [exchange(): return lax.all_to_all(ev, 'pt', split_axis=0, concat_axis=0, tiled=False)]
    unnamed x97 -> x98, local copies, waits for them, and re-layouts: 42.9 us -> 45.6 us
  transfers between devices with their start and end apart: 3 -> 3, of which waited for: 2 -> 2; matrix products, arithmetic and copies ran while one was open for 22% -> 26% of each run, Pallas kernels for 0% -> 0%
where the time goes in v11:
time: 505 us; the launch traced here: 496 us
  local copies, waits for them, and re-layouts  188 us (37%)
  waiting for transfers between devices  116 us (23%)
  other arithmetic  60.7 us (12%)
  blocking collectives  47.9 us (9%)
  starting transfers between devices  34.9 us (7%)
  matrix products  34.3 us (7%)
  between operations  14.7 us (3%)
    all_to_all x2, waiting for transfers between devices, exchange(): return lax.all_to_all(ev, 'pt', split_axis=0, concat_axis=0, tiled=False)  94 us
    unnamed x98, local copies, waits for them, and re-layouts  45.6 us
    transpose x3, local copies, waits for them, and re-layouts, body(): jnp.transpose(right_pts, (1, 4, 2, 0, 3))  36.1 us
    reshape x4, local copies, waits for them, and re-layouts, body(): jnp.transpose(right_pts, (1, 4, 2, 0, 3))  35.7 us
    all_to_all x2, starting transfers between devices, exchange(): return lax.all_to_all(ev, 'pt', split_axis=0, concat_axis=0, tiled=False)  34.9 us
    convert_element_type x11, other arithmetic, limbs_bf16(): piece.astype(jnp.bfloat16)  33.1 us
    all_to_all x1, blocking collectives, body(): prod = lax.all_to_all(prod, 'pt', split_axis=0, concat_axis=0, tiled=False)  31.4 us
    reshape x2, local copies, waits for them, and re-layouts, body(): both = received.reshape(n_pt, d_local, rows, kl, FIRST)  24.6 us
  transfers between devices with their start and end apart: 3, of which 2 were waited for; matrix products, arithmetic and copies ran while one was open for 26% of the time, Pallas kernels for 0%

profile of v11, /device:TPU:1, one launch (start us, length us, event | category | flops | bytes accessed | tf_op | source)
XLA Modules:
  0.0 496.2 jit_solution(622756394389184521)
XLA Ops:
  7.3 3.9 slice_bitcast_fusion.2
  11.2 21.2 %all-gather.2.cloned.1.call-done = f32[16,8,2048]{2,1,0:T(8,128)} async-done(((f32[8,8,2048]{2,1,0:T(8,128)}), f32[16,8,2048]{2,1,0:T(8,128)}) %all-gather.2.cloned.1.call-update) | async-done | bytes 1048592 | tf_op jit(solution)/shard_map/all_gather | solution.py:179
  35.7 2.9 convolution_bitcast_fusion
  38.7 12.5 %subtract_convert_fusion.1 = (bf16[384,32,128]{2,1,0:T(8,128)(2,1)S(1)}, f32[384,32,128]{2,1,0:T(8,128)S(1)}) fusion(f32[32,128]{1,0:T(8,128)S(1)} %copy-done.22, f32[32,128]{1,0:T(8,128)S(1)} %copy-done.23, f32[32,128]{1,0:T(8,128)S(1)} %copy-done.24, f32[32,128]{1,0:T(8,128)S(1)} %copy-done.25, f32[32,128]{1,0:T(8,128)S(1)} %copy-done.26, ...), kind=kLoop, calls=%fused_computation.28 | loop fusion | flops 94371840 | bytes 28459008 | tf_op jit(solution)/shard_map/convert_element_type | solution.py:105
  54.2 9.1 %fusion.59 = f32[384,12288]{1,0:T(8,128)} fusion(bf16[384,384]{1,0:T(8,128)(2,1)S(1)} %copy-done.3, bf16[12288,384]{1,0:T(8,128)(2,1)S(1)} %bitcast.89), kind=kOutput, calls=%fused_computation.130 | convolution fusion | flops 3623878656 | bytes 28606464 | tf_op jit(solution)/shard_map/dot_general | solution.py:118
  63.3 9.8 %fusion = f32[16,8,12288]{2,1,0:T(8,128)} fusion(f32[384,12288]{1,0:T(8,128)} %fusion.59), kind=kLoop, calls=%fused_computation.11 | loop fusion | flops 25165824 | bytes 25165824 | tf_op jit(solution)/shard_map/reshape | solution.py:174
  73.1 6.7 %all-to-all-start = ((f32[16,8,12288]{2,1,0:T(8,128)}), f32[16,8,12288]{2,1,0:T(8,128)}, u32[]{:S(2)}, u32[]{:S(2)}) async-start(f32[16,8,12288]{2,1,0:T(8,128)} %fusion), calls=%async_computation | async-start | bytes 12582912 | tf_op jit(solution)/shard_map/all_to_all | solution.py:177
  82.8 8.4 %subtract_convert_fusion.7 = (bf16[256,32,128]{2,1,0:T(8,128)(2,1)S(1)}, f32[256,32,128]{2,1,0:T(8,128)S(1)}) fusion(f32[32,128]{1,0:T(8,128)S(1)} %copy-done.22, f32[32,128]{1,0:T(8,128)S(1)} %copy-done.23, f32[32,128]{1,0:T(8,128)S(1)} %copy-done.24, f32[32,128]{1,0:T(8,128)S(1)} %copy-done.25, f32[32,128]{1,0:T(8,128)S(1)} %copy-done.26, ...), kind=kLoop, calls=%fused_computation.52 | loop fusion | flops 62914560 | bytes 19021824 | tf_op jit(solution)/shard_map/convert_element_type | solution.py:105
  93.2 3.5 fusion.60
  96.7 3.6 fusion.19
  100.3 94.0 %all-to-all-done = f32[16,8,12288]{2,1,0:T(8,128)} async-done(((f32[16,8,12288]{2,1,0:T(8,128)}), f32[16,8,12288]{2,1,0:T(8,128)}, u32[]{:S(2)}, u32[]{:S(2)}) %all-to-all-start) | async-done | bytes 6291488 | tf_op jit(solution)/shard_map/all_to_all | solution.py:177
  194.3 28.3 %all-to-all-start.1 = ((f32[16,8,8192]{2,1,0:T(8,128)}), f32[16,8,8192]{2,1,0:T(8,128)}, u32[]{:S(2)}, u32[]{:S(2)}) async-start(f32[16,8,8192]{2,1,0:T(8,128)} %fusion.19), calls=%async_computation.1 | async-start | bytes 8388608 | tf_op jit(solution)/shard_map/all_to_all | solution.py:177
  222.6 13.8 %reshape.63 = f32[16,8,48,8,32]{4,3,2,1,0:T(8,128)} reshape(f32[16,8,12288]{2,1,0:T(8,128)} %all-to-all-done) | data formatting | bytes 12582912 | tf_op jit(solution)/shard_map/reshape | solution.py:196
  236.4 4.0 slice_bitcast_fusion.1
  240.4 8.1 %copy.51 = f32[8,32,16,16,8]{1,0,4,3,2:T(8,128)} copy(f32[8,32,16,16,8]{1,4,2,0,3:T(8,128)S(1)} %slice_bitcast_fusion.1) | data formatting | bytes 4194304 | tf_op jit(solution)/shard_map/transpose | solution.py:198
  248.5 5.8 %reshape.64 = f32[256,16,128]{0,2,1:T(8,128)S(1)} reshape(f32[8,32,16,16,8]{1,0,4,3,2:T(8,128)} %copy.51) | data formatting | bytes 4194304 | tf_op jit(solution)/shard_map/reshape | solution.py:199
  256.3 6.6 %slice_bitcast_fusion = f32[8,32,32,16,8]{1,4,2,0,3:T(8,128)S(1)} fusion(f32[16,8,48,8,32]{4,3,2,1,0:T(8,128)} %reshape.63), kind=kLoop, calls=%fused_computation.3 | loop fusion | bytes 8388608 | tf_op jit(solution)/shard_map/transpose | solution.py:203
  262.9 11.6 %copy.58 = f32[8,32,32,16,8]{1,0,4,3,2:T(8,128)} copy(f32[8,32,32,16,8]{1,4,2,0,3:T(8,128)S(1)} %slice_bitcast_fusion) | data formatting | bytes 8388608 | tf_op jit(solution)/shard_map/transpose | solution.py:203
  274.5 12.4 %reshape.65 = f32[256,32,128]{0,2,1:T(8,128)} reshape(f32[8,32,32,16,8]{1,0,4,3,2:T(8,128)} %copy.58) | data formatting | bytes 8388608 | tf_op jit(solution)/shard_map/reshape | solution.py:203
  286.8 5.6 %copy.60 = f32[256,32,128]{2,1,0:T(8,128)} copy(f32[256,32,128]{0,2,1:T(8,128)} %reshape.65) | data formatting | bytes 8388608 | tf_op jit(solution)/shard_map/reshape | solution.py:203
  292.4 4.4 subtract_convert_fusion.14
  297.7 4.0 copy-done
  303.3 7.7 %fusion.1 = f32[256,48,32]{1,2,0:T(8,128)S(1)} fusion(bf16[256,32,128]{2,1,0:T(8,128)(2,1)S(1)} %get-tuple-element.24, bf16[256,32,128]{2,1,0:T(8,128)(2,1)S(1)} %get-tuple-element.23, bf16[256,32,128]{2,1,0:T(8,128)(2,1)S(1)} %get-tuple-element.22, bf16[256,16,128]{2,1,0:T(8,128)(2,1)S(1)} %get-tuple-element.42, ...), kind=kOutput, calls=%fused_computation.13 | convolution fusion | flops 405798912 | bytes 17301504 | tf_op jit(solution)/shard_map/pak,pjk->paj/dot_general | solution.py:159
  311.0 6.8 %fusion.57 = (f32[256,16,32]{1,2,0:T(8,128)}, f32[256,16,32]{1,2,0:T(8,128)}, f32[256,16,32]{1,2,0:T(8,128)}) fusion(f32[256,48,32]{1,2,0:T(8,128)S(1)} %fusion.1), kind=kLoop, calls=%fused_computation.126 | loop fusion | bytes 3145728 | tf_op jit(solution)/shard_map/slice | solution.py:161
  317.9 3.8 copy.75
  321.6 3.8 copy.76
  325.4 3.8 copy.77
  329.2 10.8 %reshape.66 = f32[16,8,32,8,32]{4,3,2,1,0:T(8,128)} reshape(f32[16,8,8192]{2,1,0:T(8,128)} %all-to-all-done.1) | data formatting | bytes 8388608 | tf_op jit(solution)/shard_map/reshape | solution.py:196
  340.0 17.9 %copy.64 = f32[8,32,32,16,8]{1,0,4,3,2:T(8,128)} copy(f32[8,32,32,16,8]{1,4,2,0,3:T(8,128)} %bitcast.88) | data formatting | bytes 8388608 | tf_op jit(solution)/shard_map/transpose | solution.py:203
  357.9 12.2 %reshape.67 = f32[256,32,128]{0,2,1:T(8,128)} reshape(f32[8,32,32,16,8]{1,0,4,3,2:T(8,128)} %copy.64) | data formatting | bytes 8388608 | tf_op jit(solution)/shard_map/reshape | solution.py:203
  370.2 5.5 %copy.66 = f32[256,32,128]{2,1,0:T(8,128)} copy(f32[256,32,128]{0,2,1:T(8,128)} %reshape.67) | data formatting | bytes 8388608 | tf_op jit(solution)/shard_map/reshape | solution.py:203
  375.7 3.3 subtract_convert_fusion.3
  380.7 7.7 %fusion.7 = f32[256,48,32]{1,2,0:T(8,128)S(1)} fusion(bf16[256,32,128]{2,1,0:T(8,128)(2,1)S(1)} %get-tuple-element.30, bf16[256,32,128]{2,1,0:T(8,128)(2,1)S(1)} %get-tuple-element.29, bf16[256,32,128]{2,1,0:T(8,128)(2,1)S(1)} %get-tuple-element.28, bf16[256,16,128]{2,1,0:T(8,128)(2,1)S(1)} %copy-done.17, bf16[256,16,128]{2,1,0:T(8,128)(2,1)S(1)} %copy-done.7, ...), kind=kOutput, calls=%fused_computation.19 | convolution fusion | flops 405798912 | bytes 17301504 | tf_op jit(solution)/shard_map/pak,pjk->paj/dot_general | solution.py:159
  388.3 6.8 %fusion.58 = (f32[256,16,32]{1,2,0:T(8,128)}, f32[256,16,32]{1,2,0:T(8,128)}, f32[256,16,32]{1,2,0:T(8,128)}) fusion(f32[256,48,32]{1,2,0:T(8,128)S(1)} %fusion.7), kind=kLoop, calls=%fused_computation.127 | loop fusion | bytes 3145728 | tf_op jit(solution)/shard_map/slice | solution.py:161
  395.2 3.8 copy.78
  398.9 3.8 copy.79
  402.7 4.5 copy.80
  408.9 16.4 %all_to_all.20 = f32[256,2,8,64]{0,3,2,1:T(8,128)S(1)} all-to-all(f32[256,2,8,64]{0,3,2,1:T(8,128)S(1)} %bitcast.92), channel_id=1, replica_groups=mesh['grp'=2,'pt'=16] {'grp'}, dimensions={1} | all-to-all | bytes 2097152 | tf_op jit(solution)/shard_map/all_to_all | solution.py:211
  425.5 2.5 reshape.69
  428.0 4.8 copy_bitcast_fusion
  432.7 3.9 reshape.74
  436.6 31.4 %all_to_all.21 = f32[16,1,16384]{2,1,0:T(1,128)S(1)} all-to-all(f32[16,1,16384]{2,1,0:T(1,128)S(1)} %reshape.74), channel_id=1, replica_groups=mesh['grp'=2,'pt'=16] {'pt'}, dimensions={0} | all-to-all | bytes 2097152 | tf_op jit(solution)/shard_map/all_to_all | solution.py:214
  468.6 3.1 reduce
  471.7 2.8 reshape.75
  474.5 2.5 bitcast_bitcast_fusion
  477.0 2.6 copy.72
  479.6 2.8 copy.74
  484.1 2.1 subtract_convert_fusion.17
  (111 shorter events, 24.3 us)
Async XLA Ops:
  6.5 25.8 %all-gather.2.cloned.1.call-start = ((), (), s32[]{:S(2)}) async-start(), calls=%async_computation.4 | async-start | bytes 1572864 | tf_op jit(solution)/shard_map/all_gather | solution.py:179
  34.4 1.1 copy-start.31
  35.6 3.0 copy-start.22
  35.6 3.0 copy-start.23
  35.6 3.0 copy-start.24
  35.6 3.0 copy-start.25
  35.6 3.0 copy-start.26
  35.7 3.0 copy-start.27
  35.7 3.0 copy-start.28
  35.7 3.0 copy-start.29
  35.7 3.0 copy-start.30
  52.8 1.4 copy-start.3
  73.1 6.7 %copy-start.1 = (f32[32,8,16,128]{3,1,2,0:T(8,128)S(1)}, f32[32,8,16,128]{3,1,2,0:T(8,128)}, u32[]{:S(2)}) copy-start(f32[32,8,16,128]{3,1,2,0:T(8,128)} %get-tuple-element.33) | copy-start | bytes 6291460
  73.1 121.1 %all-to-all-start = ((f32[16,8,12288]{2,1,0:T(8,128)}), f32[16,8,12288]{2,1,0:T(8,128)}, u32[]{:S(2)}, u32[]{:S(2)}) async-start(f32[16,8,12288]{2,1,0:T(8,128)} %fusion), calls=%async_computation | async-start | bytes 12582912 | tf_op jit(solution)/shard_map/all_to_all | solution.py:177
  194.3 134.9 %all-to-all-start.1 = ((f32[16,8,8192]{2,1,0:T(8,128)}), f32[16,8,8192]{2,1,0:T(8,128)}, u32[]{:S(2)}, u32[]{:S(2)}) async-start(f32[16,8,8192]{2,1,0:T(8,128)} %fusion.19), calls=%async_computation.1 | async-start | bytes 8388608 | tf_op jit(solution)/shard_map/all_to_all | solution.py:177
  286.8 5.6 %copy-start.2 = (f32[256,16,128]{2,1,0:T(8,128)S(1)}, f32[256,16,128]{2,1,0:T(8,128)}, u32[]{:S(2)}) copy-start(f32[256,16,128]{2,1,0:T(8,128)} %copy.53) | copy-start | bytes 6291460
  296.9 6.3 %copy-start.8 = (bf16[256,16,128]{2,1,0:T(8,128)(2,1)}, bf16[256,16,128]{2,1,0:T(8,128)(2,1)S(1)}, u32[]{:S(2)}) copy-start(bf16[256,16,128]{2,1,0:T(8,128)(2,1)S(1)} %get-tuple-element.38) | copy-start | bytes 3145732
  296.9 6.3 %copy-start.10 = (bf16[256,16,128]{2,1,0:T(8,128)(2,1)}, bf16[256,16,128]{2,1,0:T(8,128)(2,1)S(1)}, u32[]{:S(2)}) copy-start(bf16[256,16,128]{2,1,0:T(8,128)(2,1)S(1)} %get-tuple-element.39) | copy-start | bytes 3145732
  296.9 6.3 %copy-start.12 = (bf16[256,16,128]{2,1,0:T(8,128)(2,1)}, bf16[256,16,128]{2,1,0:T(8,128)(2,1)S(1)}, u32[]{:S(2)}) copy-start(bf16[256,16,128]{2,1,0:T(8,128)(2,1)S(1)} %get-tuple-element.40) | copy-start | bytes 3145732
  296.9 6.3 %copy-start.14 = (bf16[256,16,128]{2,1,0:T(8,128)(2,1)}, bf16[256,16,128]{2,1,0:T(8,128)(2,1)S(1)}, u32[]{:S(2)}) copy-start(bf16[256,16,128]{2,1,0:T(8,128)(2,1)S(1)} %get-tuple-element.41) | copy-start | bytes 3145732
  296.9 6.3 %copy-start.16 = (bf16[256,16,128]{2,1,0:T(8,128)(2,1)}, bf16[256,16,128]{2,1,0:T(8,128)(2,1)S(1)}, u32[]{:S(2)}) copy-start(bf16[256,16,128]{2,1,0:T(8,128)(2,1)S(1)} %get-tuple-element.42) | copy-start | bytes 3145732
  296.9 6.3 %copy-start.18 = (bf16[256,16,128]{2,1,0:T(8,128)(2,1)}, bf16[256,16,128]{2,1,0:T(8,128)(2,1)S(1)}, u32[]{:S(2)}) copy-start(bf16[256,16,128]{2,1,0:T(8,128)(2,1)S(1)} %get-tuple-element.43) | copy-start | bytes 3145732
  297.0 6.3 %copy-start.20 = (bf16[256,16,128]{2,1,0:T(8,128)(2,1)}, bf16[256,16,128]{2,1,0:T(8,128)(2,1)S(1)}, u32[]{:S(2)}) copy-start(bf16[256,16,128]{2,1,0:T(8,128)(2,1)S(1)} %get-tuple-element.45) | copy-start | bytes 3145732
  297.0 4.7 copy-start
  301.7 1.6 copy-start.4
  301.7 1.6 copy-start.6
  375.7 3.3 copy-start.5
  375.7 3.4 copy-start.7
  375.7 3.4 copy-start.9
  375.7 3.4 copy-start.11
  375.7 3.7 copy-start.13
  375.7 4.0 copy-start.15
  375.7 4.3 copy-start.17
  375.7 4.6 copy-start.19
  375.7 4.9 copy-start.21
  479.6 3.3 copy-start.42
  482.4 1.6 copy-start.33
  482.4 1.6 copy-start.34
  482.4 1.6 copy-start.35
  482.5 1.6 copy-start.36
  482.5 1.6 copy-start.37
  482.5 1.6 copy-start.38
  482.5 1.6 copy-start.39
  482.5 1.6 copy-start.40
  482.5 1.6 copy-start.41
  484.1 2.4 copy-start.32
Sparse Core Ops, SparseCore 0:
  8.9 23.3 all-gather.1

commit v12 on v11

--- a/solution.py
+++ b/solution.py
@@ -161,7 +161,7 @@
     return fold3(levels[:, 0:n_i], levels[:, n_i : 2 * n_i], levels[:, 2 * n_i :])
 
 
-def make_body(n_grp, n_pt, n_chunks):
+def make_body(n_grp, n_pt):
     tables = build_tables()
     d_local = SECOND // n_pt
 
@@ -178,10 +178,13 @@
 
         left_all = lax.all_gather(left_factor, "grp", axis=0, tiled=True)
         n_i = left_all.shape[0]
-        jc = jl // n_chunks
+        sizes = [jl // 2, 3 * jl // 8, jl - jl // 2 - 3 * jl // 8] if jl % 8 == 0 else [jl]
+        sizes = [size for size in sizes if size > 0]
+        n_chunks = len(sizes)
+        offsets = [sum(sizes[:chunk]) for chunk in range(n_chunks)]
         sends = []
         for chunk in range(n_chunks):
-            right_part = right_factor[chunk * jc : (chunk + 1) * jc]
+            right_part = right_factor[offsets[chunk] : offsets[chunk] + sizes[chunk]]
             if chunk == 0:
                 right_part = jnp.concatenate([left_all, right_part], axis=0)
             sends.append(send_points(right_part, right_part.shape[0]))
@@ -200,7 +203,7 @@
                 right_pts = both[:, :, n_i:]
             else:
                 right_pts = both
-            right_pts = jnp.transpose(right_pts, (1, 4, 2, 0, 3)).reshape(d_local * FIRST, jc, n_pt * kl)
+            right_pts = jnp.transpose(right_pts, (1, 4, 2, 0, 3)).reshape(d_local * FIRST, sizes[chunk], n_pt * kl)
             prods.append(multiply_points(left_pts, right_pts))
             if chunk + 1 < n_chunks:
                 received = nxt
@@ -223,7 +226,7 @@
     n_grp = mesh.shape["grp"]
     n_pt = mesh.shape["pt"]
     return jax.shard_map(
-        make_body(n_grp, n_pt, 2),
+        make_body(n_grp, n_pt),
         mesh=mesh,
         in_specs=(P("grp", "pt", None), P("grp", "pt", None)),
         out_specs=P("grp", "pt", None),

time: 505 us -> 551 us (1.091)
  other arithmetic: 60.7 us -> 77.4 us
  local copies, waits for them, and re-layouts: 188 us -> 200 us
  matrix products: 34.3 us -> 44.6 us
  starting transfers between devices: 34.9 us -> 41.2 us
    transpose x3 -> x4, local copies, waits for them, and re-layouts: 36.1 us -> 52.4 us  [body(): jnp.transpose(right_pts, (1, 4, 2, 0, 3))]
    dot_general x2 -> x3, matrix products: 15.4 us -> 25.3 us  [multiply_points(): jnp.einsum('pak,pjk->paj', stacked, right_limbs, preferred_element_type=j...]
    all_to_all x2 -> x3, starting transfers between devices: 34.9 us -> 41.2 us  [exchange(): return lax.all_to_all(ev, 'pt', split_axis=0, concat_axis=0, tiled=False)]
    concatenate x0 -> x1, other arithmetic: none -> 5.61 us  [multiply_points(): stacked = jnp.concatenate(rows, axis=1)]
    unnamed x98 -> x83, local copies, waits for them, and re-layouts: 45.6 us -> 40.2 us
    slice x2 -> x3, local copies, waits for them, and re-layouts: 13.7 us -> 17.5 us  [multiply_points(): return fold3(levels[:, 0:n_i], levels[:, n_i:2 * n_i], levels[:, 2 * n_i:])]
    all_to_all x2 -> x3, waiting for transfers between devices: 94 us -> 90.3 us  [exchange(): return lax.all_to_all(ev, 'pt', split_axis=0, concat_axis=0, tiled=False)]
    convert_element_type x11 -> x15, other arithmetic: 33.1 us -> 35.2 us  [limbs_bf16(): piece.astype(jnp.bfloat16)]
  transfers between devices with their start and end apart: 3 -> 4, of which waited for: 2 -> 2; matrix products, arithmetic and copies ran while one was open for 26% -> 26% of each run, Pallas kernels for 0% -> 0%
where the time goes in v12:
time: 551 us; the launch traced here: 542 us
  local copies, waits for them, and re-layouts  200 us (36%)
  waiting for transfers between devices  116 us (21%)
  other arithmetic  77.4 us (14%)
  blocking collectives  47.7 us (9%)
  matrix products  44.6 us (8%)
  starting transfers between devices  41.2 us (7%)
  between operations  14.6 us (3%)
    all_to_all x3, waiting for transfers between devices, exchange(): return lax.all_to_all(ev, 'pt', split_axis=0, concat_axis=0, tiled=False)  90.3 us
    transpose x4, local copies, waits for them, and re-layouts, body(): jnp.transpose(right_pts, (1, 4, 2, 0, 3))  52.4 us
    all_to_all x3, starting transfers between devices, exchange(): return lax.all_to_all(ev, 'pt', split_axis=0, concat_axis=0, tiled=False)  41.2 us
    unnamed x83, local copies, waits for them, and re-layouts  40.2 us
    convert_element_type x15, other arithmetic, limbs_bf16(): piece.astype(jnp.bfloat16)  35.2 us
    reshape x6, local copies, waits for them, and re-layouts, body(): jnp.transpose(right_pts, (1, 4, 2, 0, 3))  33.6 us
    all_to_all x1, blocking collectives, body(): prod = lax.all_to_all(prod, 'pt', split_axis=0, concat_axis=0, tiled=False)  31.4 us
    dot_general x3, matrix products, multiply_points(): jnp.einsum('pak,pjk->paj', stacked, right_limbs, preferred_element_type=j...  25.3 us
  transfers between devices with their start and end apart: 4, of which 2 were waited for; matrix products, arithmetic and copies ran while one was open for 26% of the time, Pallas kernels for 0%

profile of v12, /device:TPU:1, one launch (start us, length us, event | category | flops | bytes accessed | tf_op | source)
XLA Modules:
  0.0 541.8 jit_solution(16618948942113803303)
XLA Ops:
  7.3 25.1 %all-gather.2.cloned.1.call-done = f32[16,8,2048]{2,1,0:T(8,128)} async-done(((f32[8,8,2048]{2,1,0:T(8,128)}), f32[16,8,2048]{2,1,0:T(8,128)}) %all-gather.2.cloned.1.call-update) | async-done | bytes 1048592 | tf_op jit(solution)/shard_map/all_gather | solution.py:179
  35.7 2.9 convolution_bitcast_fusion
  38.7 12.5 %subtract_convert_fusion.1 = (bf16[384,32,128]{2,1,0:T(8,128)(2,1)S(1)}, f32[384,32,128]{2,1,0:T(8,128)S(1)}) fusion(f32[32,128]{1,0:T(8,128)S(1)} %copy-done.20, f32[32,128]{1,0:T(8,128)S(1)} %copy-done.19, f32[32,128]{1,0:T(8,128)S(1)} %copy-done.18, f32[32,128]{1,0:T(8,128)S(1)} %copy-done.17, f32[32,128]{1,0:T(8,128)S(1)} %copy-done.16, ...), kind=kLoop, calls=%fused_computation.21 | loop fusion | flops 94371840 | bytes 28459008 | tf_op jit(solution)/shard_map/convert_element_type | solution.py:105
  54.2 9.1 %fusion.79 = f32[384,12288]{1,0:T(8,128)} fusion(bf16[384,384]{1,0:T(8,128)(2,1)S(1)} %copy-done.10, bf16[12288,384]{1,0:T(8,128)(2,1)S(1)} %bitcast.121), kind=kOutput, calls=%fused_computation.169 | convolution fusion | flops 3623878656 | bytes 28606464 | tf_op jit(solution)/shard_map/dot_general | solution.py:118
  63.3 9.8 %fusion = f32[16,8,12288]{2,1,0:T(8,128)} fusion(f32[384,12288]{1,0:T(8,128)} %fusion.79), kind=kLoop, calls=%fused_computation.11 | loop fusion | flops 25165824 | bytes 25165824 | tf_op jit(solution)/shard_map/reshape | solution.py:174
  73.1 6.8 %all-to-all-start = ((f32[16,8,12288]{2,1,0:T(8,128)}), f32[16,8,12288]{2,1,0:T(8,128)}, u32[]{:S(2)}, u32[]{:S(2)}) async-start(f32[16,8,12288]{2,1,0:T(8,128)} %fusion), calls=%async_computation | async-start | bytes 12582912 | tf_op jit(solution)/shard_map/all_to_all | solution.py:177
  88.2 6.2 %subtract_convert_fusion.7 = (bf16[192,32,128]{2,1,0:T(8,128)(2,1)S(1)}, f32[192,32,128]{2,1,0:T(8,128)S(1)}) fusion(f32[32,128]{1,0:T(8,128)S(1)} %copy-done.20, f32[32,128]{1,0:T(8,128)S(1)} %copy-done.19, f32[32,128]{1,0:T(8,128)S(1)} %copy-done.18, f32[32,128]{1,0:T(8,128)S(1)} %copy-done.17, f32[32,128]{1,0:T(8,128)S(1)} %copy-done.16, ...), kind=kLoop, calls=%fused_computation.58 | loop fusion | flops 47185920 | bytes 14303232 | tf_op jit(solution)/shard_map/convert_element_type | solution.py:105
  98.6 2.7 fusion.80
  101.3 2.8 fusion.20
  104.1 90.3 %all-to-all-done = f32[16,8,12288]{2,1,0:T(8,128)} async-done(((f32[16,8,12288]{2,1,0:T(8,128)}), f32[16,8,12288]{2,1,0:T(8,128)}, u32[]{:S(2)}, u32[]{:S(2)}) %all-to-all-start) | async-done | bytes 6291488 | tf_op jit(solution)/shard_map/all_to_all | solution.py:177
  194.4 14.0 %reshape.75 = f32[16,8,48,8,32]{4,3,2,1,0:T(8,128)} reshape(f32[16,8,12288]{2,1,0:T(8,128)} %all-to-all-done) | data formatting | bytes 12582912 | tf_op jit(solution)/shard_map/reshape | solution.py:199
  208.3 4.0 slice_bitcast_fusion.1
  212.3 11.6 %slice_bitcast_fusion = f32[8,32,32,16,8]{1,4,2,0,3:T(8,128)} fusion(f32[16,8,48,8,32]{4,3,2,1,0:T(8,128)} %reshape.75), kind=kLoop, calls=%fused_computation.3 | loop fusion | bytes 8388608 | tf_op jit(solution)/shard_map/transpose | solution.py:206
  224.0 8.2 %copy.81 = f32[8,32,16,16,8]{1,0,4,3,2:T(8,128)} copy(f32[8,32,16,16,8]{1,4,2,0,3:T(8,128)S(1)} %slice_bitcast_fusion.1) | data formatting | bytes 4194304 | tf_op jit(solution)/shard_map/transpose | solution.py:201
  232.1 5.8 %reshape.76 = f32[256,16,128]{0,2,1:T(8,128)S(1)} reshape(f32[8,32,16,16,8]{1,0,4,3,2:T(8,128)} %copy.81) | data formatting | bytes 4194304 | tf_op jit(solution)/shard_map/reshape | solution.py:202
  239.9 28.0 %all-to-all-start.1 = ((f32[16,8,6144]{2,1,0:T(8,128)}), f32[16,8,6144]{2,1,0:T(8,128)S(1)}, u32[]{:S(2)}, u32[]{:S(2)}) async-start(f32[16,8,6144]{2,1,0:T(8,128)} %fusion.20), calls=%async_computation.1 | async-start | bytes 6291456 | tf_op jit(solution)/shard_map/all_to_all | solution.py:177
  267.9 7.4 %subtract_convert_fusion.14 = (bf16[256,16,128]{2,1,0:T(8,128)(2,1)}, bf16[256,16,128]{2,1,0:T(8,128)(2,1)}, bf16[256,16,128]{2,1,0:T(8,128)(2,1)}, bf16[256,16,...) fusion(f32[256,16,128]{2,1,0:T(8,128)} %copy.83), kind=kLoop, calls=%fused_computation.87 | loop fusion | flops 33554432 | bytes 11534336 | tf_op jit(solution)/shard_map/convert_element_type | solution.py:156
  275.3 17.7 %copy.88 = f32[8,32,32,16,8]{1,0,4,3,2:T(8,128)} copy(f32[8,32,32,16,8]{1,4,2,0,3:T(8,128)} %slice_bitcast_fusion) | data formatting | bytes 8388608 | tf_op jit(solution)/shard_map/transpose | solution.py:206
  293.0 12.2 %reshape.77 = f32[256,32,128]{0,2,1:T(8,128)} reshape(f32[8,32,32,16,8]{1,0,4,3,2:T(8,128)} %copy.88) | data formatting | bytes 8388608 | tf_op jit(solution)/shard_map/reshape | solution.py:206
  305.3 5.5 %copy.90 = f32[256,32,128]{2,1,0:T(8,128)} copy(f32[256,32,128]{0,2,1:T(8,128)} %reshape.77) | data formatting | bytes 8388608 | tf_op jit(solution)/shard_map/reshape | solution.py:206
  313.6 3.7 subtract_convert_fusion.3
  318.9 5.6 %maximum_maximum_fusion = bf16[256,48,384]{2,1,0:T(8,128)(2,1)} fusion(bf16[256,16,128]{2,1,0:T(8,128)(2,1)S(1)} %copy-done.7, bf16[256,16,128]{2,1,0:T(8,128)(2,1)S(1)} %get-tuple-element.51, bf16[256,16,128]{2,1,0:T(8,128)(2,1)S(1)} %copy-done.9, bf16[256,16,128]{2,1,0:T(8,128)(2,1)S(1)} %copy-done.5, bf16[256,16,128]{2,1,0:T(8,128)(2,1)S(1)} %get-tuple-element.50, ...), kind=kLoop, calls=%fused_computation.5 | loop fusion | flops 84934656 | bytes 18874368 | tf_op jit(solution)/shard_map/concatenate | solution.py:157
  324.5 10.9 %fusion.1 = f32[256,48,32]{1,2,0:T(8,128)} fusion(bf16[256,48,384]{2,1,0:T(8,128)(2,1)} %maximum_maximum_fusion, bf16[256,32,128]{2,1,0:T(8,128)(2,1)} %get-tuple-element.30, bf16[256,32,128]{2,1,0:T(8,128)(2,1)} %get-tuple-element.29, bf16[256,32,128]{2,1,0:T(8,128)(2,1)} %get-tuple-element.28), kind=kOutput, calls=%fused_computation.12 | convolution fusion | flops 320864256 | bytes 17301504 | tf_op jit(solution)/shard_map/pak,pjk->paj/dot_general | solution.py:159
  335.4 11.5 %fusion.76 = (f32[256,16,32]{1,2,0:T(8,128)}, f32[256,16,32]{1,2,0:T(8,128)}, f32[256,16,32]{1,2,0:T(8,128)}) fusion(f32[256,48,32]{1,2,0:T(8,128)} %fusion.1), kind=kLoop, calls=%fused_computation.164 | loop fusion | bytes 3145728 | tf_op jit(solution)/shard_map/slice | solution.py:161
  346.9 4.5 copy.111
  351.4 4.5 copy.112
  355.9 4.5 copy.113
  362.8 6.6 %reshape.80 = f32[16,8,24,8,32]{4,3,2,1,0:T(8,128)} reshape(f32[16,8,6144]{2,1,0:T(8,128)S(1)} %all-to-all-done.1) | data formatting | bytes 6291456 | tf_op jit(solution)/shard_map/reshape | solution.py:199
  369.4 16.4 %copy.94 = f32[8,32,24,16,8]{1,0,4,3,2:T(8,128)} copy(f32[8,32,24,16,8]{1,4,2,0,3:T(8,128)} %bitcast.120) | data formatting | bytes 6291456 | tf_op jit(solution)/shard_map/transpose | solution.py:206
  385.9 9.6 %reshape.81 = f32[256,24,128]{0,2,1:T(8,128)} reshape(f32[8,32,24,16,8]{1,0,4,3,2:T(8,128)} %copy.94) | data formatting | bytes 6291456 | tf_op jit(solution)/shard_map/reshape | solution.py:206
  398.0 6.4 %all-to-all-start.2 = ((f32[16,8,2048]{2,1,0:T(8,128)}), f32[16,8,2048]{2,1,0:T(8,128)}, u32[]{:S(2)}, u32[]{:S(2)}) async-start(f32[16,8,2048]{2,1,0:T(8,128)} %fusion.54), calls=%async_computation.2 | async-start | bytes 2097152 | tf_op jit(solution)/shard_map/all_to_all | solution.py:177
  404.4 2.9 subtract_convert_fusion.5
  407.4 8.4 %fusion.13 = f32[256,48,24]{1,2,0:T(8,128)S(1)} fusion(bf16[256,48,384]{2,1,0:T(8,128)(2,1)} %maximum_maximum_fusion, bf16[256,24,128]{2,1,0:T(8,128)(2,1)} %get-tuple-element.36, bf16[256,24,128]{2,1,0:T(8,128)(2,1)} %get-tuple-element.35, bf16[256,24,128]{2,1,0:T(8,128)(2,1)} %get-tuple-element.34), kind=kOutput, calls=%fused_computation.31 | convolution fusion | flops 240648192 | bytes 15335424 | tf_op jit(solution)/shard_map/pak,pjk->paj/dot_general | solution.py:159
  415.8 5.3 fusion.77
  421.0 3.2 copy.114
  424.2 3.0 copy.115
  430.5 3.9 reshape.82
  434.4 6.6 %copy.100 = f32[8,32,8,16,8]{1,0,4,3,2:T(8,128)} copy(f32[8,32,8,16,8]{1,4,2,0,3:T(8,128)} %bitcast.123) | data formatting | bytes 2097152 | tf_op jit(solution)/shard_map/transpose | solution.py:206
  441.0 3.3 reshape.83
  445.2 6.0 %fusion.36 = f32[256,48,8]{1,2,0:T(8,128)S(1)} fusion(bf16[256,48,384]{2,1,0:T(8,128)(2,1)} %maximum_maximum_fusion, bf16[256,8,128]{2,1,0:T(8,128)(2,1)S(1)} %get-tuple-element.65, bf16[256,8,128]{2,1,0:T(8,128)(2,1)S(1)} %get-tuple-element.64, bf16[256,8,128]{2,1,0:T(8,128)(2,1)S(1)} %get-tuple-element.63), kind=kOutput, calls=%fused_computation.96 | convolution fusion | flops 80216064 | bytes 11403264 | tf_op jit(solution)/shard_map/pak,pjk->paj/dot_general | solution.py:159
  454.7 16.2 %all_to_all.25 = f32[256,2,8,64]{0,3,2,1:T(8,128)S(1)} all-to-all(f32[256,2,8,64]{0,3,2,1:T(8,128)S(1)} %bitcast.126), channel_id=1, replica_groups=mesh['grp'=2,'pt'=16] {'grp'}, dimensions={1} | all-to-all | bytes 2097152 | tf_op jit(solution)/shard_map/all_to_all | solution.py:214
  473.6 4.8 copy_bitcast_fusion
  478.3 3.9 reshape.90
  482.2 31.4 %all_to_all.26 = f32[16,1,16384]{2,1,0:T(1,128)S(1)} all-to-all(f32[16,1,16384]{2,1,0:T(1,128)S(1)} %reshape.90), channel_id=1, replica_groups=mesh['grp'=2,'pt'=16] {'pt'}, dimensions={0} | all-to-all | bytes 2097152 | tf_op jit(solution)/shard_map/all_to_all | solution.py:217
  514.2 3.1 reduce
  517.3 2.8 reshape.91
  522.6 2.6 copy.108
  525.2 2.8 copy.110
  (117 shorter events, 50.1 us)
Async XLA Ops:
  6.5 25.8 %slice-start = ((f32[64,8,2048]{2,1,0:T(8,128)}), f32[32,8,2048]{2,1,0:T(8,128)S(1)}, s32[]{:S(2)}) async-start(f32[64,8,2048]{2,1,0:T(8,128)} %param.13), calls=%async_computation.6 | async-start | bytes 4194304 | tf_op jit(solution)/shard_map/slice | solution.py:187
  6.5 25.8 %all-gather.2.cloned.1.call-start = ((), (), s32[]{:S(2)}) async-start(), calls=%async_computation.5 | async-start | bytes 1572864 | tf_op jit(solution)/shard_map/all_gather | solution.py:179
  34.4 1.1 copy-start.21
  35.6 3.0 copy-start.12
  35.6 3.0 copy-start.13
  35.6 3.0 copy-start.14
  35.6 3.0 copy-start.15
  35.6 3.0 copy-start.16
  35.7 3.0 copy-start.17
  35.7 3.0 copy-start.18
  35.7 3.0 copy-start.19
  35.7 3.0 copy-start.20
  52.8 1.4 copy-start.10
  73.1 121.3 %all-to-all-start = ((f32[16,8,12288]{2,1,0:T(8,128)}), f32[16,8,12288]{2,1,0:T(8,128)}, u32[]{:S(2)}, u32[]{:S(2)}) async-start(f32[16,8,12288]{2,1,0:T(8,128)} %fusion), calls=%async_computation | async-start | bytes 12582912 | tf_op jit(solution)/shard_map/all_to_all | solution.py:177
  79.9 2.7 copy-start.2
  239.9 122.9 %all-to-all-start.1 = ((f32[16,8,6144]{2,1,0:T(8,128)}), f32[16,8,6144]{2,1,0:T(8,128)S(1)}, u32[]{:S(2)}, u32[]{:S(2)}) async-start(f32[16,8,6144]{2,1,0:T(8,128)} %fusion.20), calls=%async_computation.1 | async-start | bytes 6291456 | tf_op jit(solution)/shard_map/all_to_all | solution.py:177
  310.7 2.8 copy-start
  313.5 3.7 copy-start.3
  313.5 3.7 copy-start.4
  313.5 3.7 copy-start.5
  313.5 3.8 copy-start.6
  313.5 4.7 copy-start.7
  313.6 5.0 copy-start.8
  313.6 5.3 copy-start.9
  398.0 32.5 %all-to-all-start.2 = ((f32[16,8,2048]{2,1,0:T(8,128)}), f32[16,8,2048]{2,1,0:T(8,128)}, u32[]{:S(2)}, u32[]{:S(2)}) async-start(f32[16,8,2048]{2,1,0:T(8,128)} %fusion.54), calls=%async_computation.2 | async-start | bytes 2097152 | tf_op jit(solution)/shard_map/all_to_all | solution.py:177
  421.0 6.2 %copy-start.1 = (f32[256,16,24]{1,2,0:T(8,128)S(1)}, f32[256,16,24]{1,2,0:T(8,128)}, u32[]{:S(2)}) copy-start(f32[256,16,24]{1,2,0:T(8,128)} %get-tuple-element.31) | copy-start | bytes 1179652
  452.9 1.7 copy-start.11
  525.2 3.3 copy-start.32
  528.4 1.2 copy-start.23
  528.4 1.2 copy-start.24
  528.4 1.2 copy-start.25
  528.4 1.2 copy-start.26
  528.4 1.2 copy-start.27
  528.5 1.2 copy-start.28
  528.5 1.2 copy-start.29
  528.5 1.2 copy-start.30
  528.5 1.2 copy-start.31
  529.7 2.4 copy-start.22
Sparse Core Ops, SparseCore 0:
  8.9 23.3 all-gather.1

commit v13 on v9

--- a/solution.py
+++ b/solution.py
@@ -175,16 +175,23 @@
             ev = lax.all_to_all(ev, "pt", split_axis=0, concat_axis=0, tiled=False)
             return ev.reshape(n_pt, d_local, rows, kl, FIRST)
 
+        jc = jl // n_chunks
         left_pts = to_points(left_factor, il)
+        right_recv = [to_points(right_factor[0:jc], jc)]
+        left_pts, right_recv[0] = lax.optimization_barrier((left_pts, right_recv[0]))
         left_pts = jnp.broadcast_to(left_pts[None], (n_grp,) + left_pts.shape)
         left_pts = lax.all_to_all(left_pts, "grp", split_axis=0, concat_axis=0, tiled=True)
         left_pts = jnp.transpose(left_pts, (2, 5, 0, 3, 1, 4))
         left_pts = left_pts.reshape(d_local * FIRST, n_grp * il, n_pt * kl)
-        jc = jl // n_chunks
         prods = []
         for chunk in range(n_chunks):
-            right_pts = to_points(right_factor[chunk * jc : (chunk + 1) * jc], jc)
-            right_pts = jnp.transpose(right_pts, (1, 4, 2, 0, 3)).reshape(d_local * FIRST, jc, n_pt * kl)
+            if chunk + 1 < n_chunks:
+                ev = forward(right_factor[(chunk + 1) * jc : (chunk + 2) * jc].reshape(jc * kl, -1), tables)
+                ev = ev.reshape(n_pt, d_local, jc * kl * FIRST)
+                left_pts, ev = lax.optimization_barrier((left_pts, ev))
+                ev = lax.all_to_all(ev, "pt", split_axis=0, concat_axis=0, tiled=False)
+                right_recv.append(ev.reshape(n_pt, d_local, jc, kl, FIRST))
+            right_pts = jnp.transpose(right_recv[chunk], (1, 4, 2, 0, 3)).reshape(d_local * FIRST, jc, n_pt * kl)
             prods.append(multiply_points(left_pts, right_pts))
         prod = jnp.concatenate(prods, axis=2) if n_chunks > 1 else prods[0]
         n_i = prod.shape[1]

time: 490 us -> 501 us (1.022)
  blocking collectives: 47.9 us -> 59.3 us
    all_to_all x3 -> x2, starting transfers between devices: 33.9 us -> 13.6 us  [to_points(): ev = lax.all_to_all(ev, 'pt', split_axis=0, concat_axis=0, tiled=False)]
    all_to_all x0 -> x1, starting transfers between devices: none -> 20 us  [body(): ev = lax.all_to_all(ev, 'pt', split_axis=0, concat_axis=0, tiled=False)]
    all_to_all x1, blocking collectives: 31.5 us -> 43.1 us  [body(): prod = lax.all_to_all(prod, 'pt', split_axis=0, concat_axis=0, tiled=False)]
    reshape x4 -> x5, local copies, waits for them, and re-layouts: 35.5 us -> 46.2 us  [the longest x4 35.4 us: body(): jnp.transpose(right_recv[chunk], (1, 4, 2, 0, 3))]
    reshape x2, local copies, waits for them, and re-layouts: 21.9 us -> 13.5 us  [to_points(): return ev.reshape(n_pt, d_local, rows, kl, FIRST)]
    broadcast_in_dim x2 -> x0, local copies, waits for them, and re-layouts: 7.5 us -> none  [body(): left_pts = jnp.broadcast_to(left_pts[None], (n_grp,) + left_pts.shape)]
    reshape x0 -> x1, other arithmetic: none -> 7.12 us  [body(): ev = ev.reshape(n_pt, d_local, jc * kl * FIRST)]
    reshape x3 -> x2, other arithmetic: 12.2 us -> 5.07 us  [to_points(): ev = ev.reshape(n_pt, d_local, rows * kl * FIRST)]
  transfers between devices with their start and end apart: 4 -> 4, of which waited for: 2 -> 2; matrix products, arithmetic and copies ran while one was open for 35% -> 27% of each run, Pallas kernels for 0% -> 0%
where the time goes in v13:
time: 501 us; the launch traced here: 495 us
  local copies, waits for them, and re-layouts  207 us (41%)
  waiting for transfers between devices  83.2 us (17%)
  other arithmetic  70.3 us (14%)
  blocking collectives  59.3 us (12%)
  starting transfers between devices  37.8 us (8%)
  matrix products  36.5 us (7%)
    unnamed x104, local copies, waits for them, and re-layouts  65.5 us
    all_to_all x2, waiting for transfers between devices, to_points(): ev = lax.all_to_all(ev, 'pt', split_axis=0, concat_axis=0, tiled=False)  65.1 us
    all_to_all x1, blocking collectives, body(): prod = lax.all_to_all(prod, 'pt', split_axis=0, concat_axis=0, tiled=False)  43.1 us
    transpose x2, local copies, waits for them, and re-layouts, body(): jnp.transpose(right_recv[chunk], (1, 4, 2, 0, 3))  35.5 us
    reshape x4, local copies, waits for them, and re-layouts, body(): jnp.transpose(right_recv[chunk], (1, 4, 2, 0, 3))  35.4 us
    convert_element_type x13, other arithmetic, limbs_bf16(): piece.astype(jnp.bfloat16)  35.1 us
    all_to_all x1, starting transfers between devices, body(): ev = lax.all_to_all(ev, 'pt', split_axis=0, concat_axis=0, tiled=False)  20 us
    all_to_all x1, waiting for transfers between devices, body(): lax.all_to_all(left_pts, 'grp', split_axis=0, concat_axis=0, tiled=True)  18.1 us
  transfers between devices with their start and end apart: 4, of which 2 were waited for; matrix products, arithmetic and copies ran while one was open for 27% of the time, Pallas kernels for 0%

profile of v13, /device:TPU:1, one launch (start us, length us, event | category | flops | bytes accessed | tf_op | source)
XLA Modules:
  0.0 495.4 jit_solution(11512552903562389388)
XLA Ops:
  8.1 7.6 %all-to-all-start = ((f32[16,8,2048]{2,1,0:T(8,128)}), f32[16,8,2048]{2,1,0:T(8,128)S(1)}, u32[]{:S(2)}, u32[]{:S(2)}) async-start(f32[16,8,2048]{2,1,0:T(8,128)} %fusion.48), calls=%async_computation | async-start | bytes 2097152 | tf_op jit(solution)/shard_map/all_to_all | solution.py:175
  24.2 17.8 %subtract_convert_fusion.5 = (bf16[256,32,128]{2,1,0:T(8,128)(2,1)}, f32[256,32,128]{2,1,0:T(8,128)S(1)}, bf16[256,32,128]{2,1,0:T(8,128)(2,1)}, f32[256,32,128]{2,1,0:T(8,128)S(1)}) fusion(f32[32,128]{1,0:T(8,128)S(1)} %copy-done.24, f32[32,128]{1,0:T(8,128)S(1)} %copy-done.25, f32[32,128]{1,0:T(8,128)S(1)} %copy-done.26, f32[32,128]{1,0:T(8,128)S(1)} %copy-done.27, ...), kind=kLoop, calls=%fused_computation.40 | loop fusion | flops 125829120 | bytes 37896192 | tf_op jit(solution)/shard_map/convert_element_type | solution.py:105
  45.3 4.1 pad_maximum_fusion
  49.4 3.5 fusion.71
  52.8 3.5 fusion.12
  56.4 6.0 %all-to-all-start.1 = ((f32[16,8,8192]{2,1,0:T(8,128)}), f32[16,8,8192]{2,1,0:T(8,128)}, u32[]{:S(2)}, u32[]{:S(2)}) async-start(f32[16,8,8192]{2,1,0:T(8,128)} %fusion.12), calls=%async_computation.1 | async-start | bytes 8388608 | tf_op jit(solution)/shard_map/all_to_all | solution.py:175
  62.4 10.2 %fusion.72 = f32[384,8192]{1,0:T(8,128)} fusion(bf16[384,384]{1,0:T(8,128)(2,1)S(1)} %copy-done.3, bf16[8192,384]{1,0:T(8,128)(2,1)} %bitcast.116), kind=kOutput, calls=%fused_computation.156 | convolution fusion | flops 2415919104 | bytes 19169280 | tf_op jit(solution)/shard_map/dot_general | solution.py:118
  72.6 2.8 reshape.71
  75.3 65.1 %all-to-all-done.1 = f32[16,8,8192]{2,1,0:T(8,128)} async-done(((f32[16,8,8192]{2,1,0:T(8,128)}), f32[16,8,8192]{2,1,0:T(8,128)}, u32[]{:S(2)}, u32[]{:S(2)}) %all-to-all-start.1) | async-done | bytes 4194336 | tf_op jit(solution)/shard_map/all_to_all | solution.py:175
  140.5 10.8 %reshape.74 = f32[16,8,32,8,32]{4,3,2,1,0:T(8,128)} reshape(f32[16,8,8192]{2,1,0:T(8,128)} %all-to-all-done.1) | data formatting | bytes 8388608 | tf_op jit(solution)/shard_map/reshape | solution.py:176
  151.2 4.6 copy.52
  155.9 4.7 broadcast_bitcast_fusion
  160.6 6.9 %reshape.87 = f32[2,1,262144]{2,1,0:T(1,128)} reshape(f32[2,8,16,8,8,32]{5,4,3,2,1,0:T(8,128)} %broadcast_bitcast_fusion) | data formatting | bytes 4194304
  167.4 4.2 all-to-all-start.2
  171.6 7.1 %fusion.13 = f32[16,8,8192]{2,1,0:T(8,128)} fusion(f32[384,8192]{1,0:T(8,128)} %fusion.72), kind=kLoop, calls=%fused_computation.26 | loop fusion | flops 16777216 | bytes 16777216 | tf_op jit(solution)/shard_map/reshape | solution.py:190
  178.7 18.1 %all-to-all-done.2 = f32[2,1,262144]{2,1,0:T(1,128)S(1)} async-done(((f32[2,1,262144]{2,1,0:T(1,128)}), f32[2,1,262144]{2,1,0:T(1,128)S(1)}, u32[]{:S(2)}, u32[]{:S(2)}) %all-to-all-start.2) | async-done | bytes 2097184 | tf_op jit(solution)/shard_map/all_to_all | solution.py:183
  198.7 8.1 %reduce = f32[2,262144]{1,0:T(2,128)S(1)} reduce(f32[2,1,262144]{2,1,0:T(1,128)} %copy-done.2, f32[]{:T(128)} %broadcast.358), dimensions={1}, to_apply=%all_to_all.20.reduce_sub_computation | reduce | bytes 4194308 | tf_op jit(solution)/shard_map/all_to_all | solution.py:183
  206.8 6.5 %reshape.88 = f32[2,8,16,8,8,32]{5,4,3,2,1,0:T(8,128)} reshape(f32[2,262144]{1,0:T(2,128)S(1)} %reduce) | data formatting | bytes 4194304
  213.3 8.3 %bitcast_bitcast_fusion = f32[8,32,2,8,16,8]{1,0,5,4,3,2:T(8,128)} fusion(f32[2,8,16,8,8,32]{5,4,3,2,1,0:T(8,128)} %reshape.88), kind=kLoop, calls=%fused_computation.150 | loop fusion | bytes 4194304 | tf_op jit(solution)/shard_map/transpose | solution.py:184
  221.6 5.8 %reshape.75 = f32[256,16,128]{0,2,1:T(8,128)S(1)} reshape(f32[8,32,2,8,16,8]{1,0,5,4,3,2:T(8,128)} %bitcast_bitcast_fusion) | data formatting | bytes 4194304 | tf_op jit(solution)/shard_map/reshape | solution.py:185
  227.4 20.0 %all-to-all-start.3 = ((f32[16,8,8192]{2,1,0:T(8,128)}), f32[16,8,8192]{2,1,0:T(8,128)}, u32[]{:S(2)}, u32[]{:S(2)}) async-start(f32[16,8,8192]{2,1,0:T(8,128)} %fusion.13), calls=%async_computation.3 | async-start | bytes 8388608 | tf_op jit(solution)/shard_map/all_to_all | solution.py:192
  247.4 17.7 %copy.59 = f32[8,32,32,16,8]{1,0,4,3,2:T(8,128)} copy(f32[8,32,32,16,8]{1,4,2,0,3:T(8,128)} %bitcast.114) | data formatting | bytes 8388608 | tf_op jit(solution)/shard_map/transpose | solution.py:194
  265.2 12.2 %reshape.78 = f32[256,32,128]{0,2,1:T(8,128)} reshape(f32[8,32,32,16,8]{1,0,4,3,2:T(8,128)} %copy.59) | data formatting | bytes 8388608 | tf_op jit(solution)/shard_map/reshape | solution.py:194
  277.4 5.5 %copy.61 = f32[256,32,128]{2,1,0:T(8,128)} copy(f32[256,32,128]{0,2,1:T(8,128)} %reshape.78) | data formatting | bytes 8388608 | tf_op jit(solution)/shard_map/reshape | solution.py:194
  282.8 4.9 subtract_convert_fusion.3
  289.7 5.6 %subtract_convert_fusion.13 = (bf16[256,16,128]{2,1,0:T(8,128)(2,1)S(1)}, bf16[256,16,128]{2,1,0:T(8,128)(2,1)S(1)}, bf16[256,16,128]{2,1,0:T(8,128)(2,1)S(1)}, ...) fusion(f32[256,16,128]{2,1,0:T(8,128)} %copy.54), kind=kLoop, calls=%fused_computation.85 | loop fusion | flops 33554432 | bytes 11534336 | tf_op jit(solution)/shard_map/convert_element_type | solution.py:156
  300.5 7.6 %fusion = f32[256,48,32]{1,2,0:T(8,128)S(1)} fusion(bf16[256,32,128]{2,1,0:T(8,128)(2,1)S(1)} %copy-done.6, bf16[256,32,128]{2,1,0:T(8,128)(2,1)S(1)} %copy-done.5, bf16[256,32,128]{2,1,0:T(8,128)(2,1)S(1)} %copy-done.4, bf16[256,16,128]{2,1,0:T(8,128)(2,1)S(1)} %get-tuple-element.45, bf16[256,16,128]{2,1,0:T(8,128)(2,1)S(1)} %get-tuple-element.50, ...), kind=kOutput, calls=%fused_computation.9 | convolution fusion | flops 405798912 | bytes 17301504 | tf_op jit(solution)/shard_map/pak,pjk->paj/dot_general | solution.py:159
  308.2 6.8 %fusion.68 = (f32[256,16,32]{1,2,0:T(8,128)}, f32[256,16,32]{1,2,0:T(8,128)}, f32[256,16,32]{1,2,0:T(8,128)}) fusion(f32[256,48,32]{1,2,0:T(8,128)S(1)} %fusion), kind=kLoop, calls=%fused_computation.148 | loop fusion | bytes 3145728 | tf_op jit(solution)/shard_map/slice | solution.py:161
  315.0 3.8 copy.78
  318.8 4.2 copy.77
  323.0 3.8 copy.76
  327.1 10.8 %reshape.79 = f32[16,8,32,8,32]{4,3,2,1,0:T(8,128)} reshape(f32[16,8,8192]{2,1,0:T(8,128)} %all-to-all-done.3) | data formatting | bytes 8388608 | tf_op jit(solution)/shard_map/reshape | solution.py:193
  337.8 17.7 %copy.65 = f32[8,32,32,16,8]{1,0,4,3,2:T(8,128)} copy(f32[8,32,32,16,8]{1,4,2,0,3:T(8,128)} %bitcast.115) | data formatting | bytes 8388608 | tf_op jit(solution)/shard_map/transpose | solution.py:194
  355.6 12.2 %reshape.80 = f32[256,32,128]{0,2,1:T(8,128)} reshape(f32[8,32,32,16,8]{1,0,4,3,2:T(8,128)} %copy.65) | data formatting | bytes 8388608 | tf_op jit(solution)/shard_map/reshape | solution.py:194
  367.8 5.5 %copy.67 = f32[256,32,128]{2,1,0:T(8,128)} copy(f32[256,32,128]{0,2,1:T(8,128)} %reshape.80) | data formatting | bytes 8388608 | tf_op jit(solution)/shard_map/reshape | solution.py:194
  373.3 3.3 subtract_convert_fusion.1
  378.0 7.7 %fusion.6 = f32[256,48,32]{1,2,0:T(8,128)S(1)} fusion(bf16[256,32,128]{2,1,0:T(8,128)(2,1)S(1)} %get-tuple-element.34, bf16[256,32,128]{2,1,0:T(8,128)(2,1)S(1)} %get-tuple-element.33, bf16[256,32,128]{2,1,0:T(8,128)(2,1)S(1)} %get-tuple-element.32, bf16[256,16,128]{2,1,0:T(8,128)(2,1)S(1)} %copy-done.18, bf16[256,16,128]{2,1,0:T(8,128)(2,1)S(1)} %copy-done.8, ...), kind=kOutput, calls=%fused_computation.15 | convolution fusion | flops 405798912 | bytes 17301504 | tf_op jit(solution)/shard_map/pak,pjk->paj/dot_general | solution.py:159
  385.6 6.8 %fusion.69 = (f32[256,16,32]{1,2,0:T(8,128)}, f32[256,16,32]{1,2,0:T(8,128)}, f32[256,16,32]{1,2,0:T(8,128)}) fusion(f32[256,48,32]{1,2,0:T(8,128)S(1)} %fusion.6), kind=kLoop, calls=%fused_computation.149 | loop fusion | bytes 3145728 | tf_op jit(solution)/shard_map/slice | solution.py:161
  392.5 3.9 copy.81
  396.4 3.8 copy.80
  400.2 3.8 copy.79
  404.4 16.2 %all_to_all.30 = f32[256,2,8,64]{0,3,2,1:T(8,128)S(1)} all-to-all(f32[256,2,8,64]{0,3,2,1:T(8,128)S(1)} %bitcast.120), channel_id=1, replica_groups=mesh['grp'=2,'pt'=16] {'grp'}, dimensions={1} | all-to-all | bytes 2097152 | tf_op jit(solution)/shard_map/all_to_all | solution.py:201
  423.2 4.8 copy_bitcast_fusion
  428.0 3.9 reshape.89
  431.9 43.1 %all_to_all.31 = f32[16,1,16384]{2,1,0:T(1,128)S(1)} all-to-all(f32[16,1,16384]{2,1,0:T(1,128)S(1)} %reshape.89), channel_id=1, replica_groups=mesh['grp'=2,'pt'=16] {'pt'}, dimensions={0} | all-to-all | bytes 2097152 | tf_op jit(solution)/shard_map/all_to_all | solution.py:204
  475.0 3.1 reduce.1
  478.1 2.8 reshape.90
  486.0 2.8 copy.75
  (124 shorter events, 44.4 us)
Async XLA Ops:
  0.0 2.8 copy-start.24
  0.0 2.8 copy-start.25
  0.0 2.8 copy-start.26
  0.0 2.8 copy-start.27
  0.0 2.8 copy-start.28
  0.0 2.8 copy-start.29
  0.0 2.8 copy-start.30
  0.1 2.8 copy-start.31
  0.1 2.8 copy-start.32
  2.9 2.6 copy-start.3
  8.1 48.3 %all-to-all-start = ((f32[16,8,2048]{2,1,0:T(8,128)}), f32[16,8,2048]{2,1,0:T(8,128)S(1)}, u32[]{:S(2)}, u32[]{:S(2)}) async-start(f32[16,8,2048]{2,1,0:T(8,128)} %fusion.48), calls=%async_computation | async-start | bytes 2097152 | tf_op jit(solution)/shard_map/all_to_all | solution.py:175
  19.3 1.2 copy-start.23
  43.1 1.6 copy-start
  43.1 2.2 copy-start.1
  56.4 84.1 %all-to-all-start.1 = ((f32[16,8,8192]{2,1,0:T(8,128)}), f32[16,8,8192]{2,1,0:T(8,128)}, u32[]{:S(2)}, u32[]{:S(2)}) async-start(f32[16,8,8192]{2,1,0:T(8,128)} %fusion.12), calls=%async_computation.1 | async-start | bytes 8388608 | tf_op jit(solution)/shard_map/all_to_all | solution.py:175
  167.4 29.3 %all-to-all-start.2 = ((f32[2,1,262144]{2,1,0:T(1,128)}), f32[2,1,262144]{2,1,0:T(1,128)S(1)}, u32[]{:S(2)}, u32[]{:S(2)}) async-start(f32[2,1,262144]{2,1,0:T(1,128)} %reshape.87), calls=%async_computation.2 | async-start | bytes 4194304 | tf_op jit(solution)/shard_map/all_to_all | solution.py:183
  196.8 1.3 copy-start.2
  227.4 99.7 %all-to-all-start.3 = ((f32[16,8,8192]{2,1,0:T(8,128)}), f32[16,8,8192]{2,1,0:T(8,128)}, u32[]{:S(2)}, u32[]{:S(2)}) async-start(f32[16,8,8192]{2,1,0:T(8,128)} %fusion.13), calls=%async_computation.3 | async-start | bytes 8388608 | tf_op jit(solution)/shard_map/all_to_all | solution.py:192
  289.7 9.3 %copy-start.6 = (bf16[256,32,128]{2,1,0:T(8,128)(2,1)S(1)}, bf16[256,32,128]{2,1,0:T(8,128)(2,1)}, u32[]{:S(2)}) copy-start(bf16[256,32,128]{2,1,0:T(8,128)(2,1)} %get-tuple-element.28) | copy-start | bytes 6291460
  295.4 1.0 copy-start.9
  295.4 1.3 copy-start.11
  295.4 1.6 copy-start.13
  295.4 2.1 copy-start.15
  295.4 2.6 copy-start.17
  295.4 3.1 copy-start.19
  295.5 3.5 copy-start.21
  295.5 3.5 copy-start.4
  295.5 5.1 %copy-start.5 = (bf16[256,32,128]{2,1,0:T(8,128)(2,1)S(1)}, bf16[256,32,128]{2,1,0:T(8,128)(2,1)}, u32[]{:S(2)}) copy-start(bf16[256,32,128]{2,1,0:T(8,128)(2,1)} %get-tuple-element.27) | copy-start | bytes 6291460
  296.2 11.9 %copy-start.7 = (bf16[256,16,128]{2,1,0:T(8,128)(2,1)}, bf16[256,16,128]{2,1,0:T(8,128)(2,1)S(1)}, u32[]{:S(2)}) copy-start(bf16[256,16,128]{2,1,0:T(8,128)(2,1)S(1)} %get-tuple-element.50) | copy-start | bytes 3145732
  373.3 3.3 copy-start.8
  373.3 3.3 copy-start.10
  373.3 3.4 copy-start.12
  373.3 3.4 copy-start.14
  373.3 3.7 copy-start.16
  373.3 4.0 copy-start.18
  373.3 4.3 copy-start.20
  373.3 4.6 copy-start.22
  486.0 3.3 copy-start.43
  488.8 1.6 copy-start.34
  488.8 1.6 copy-start.35
  488.8 1.6 copy-start.36
  488.8 1.6 copy-start.37
  488.8 1.6 copy-start.38
  488.9 1.6 copy-start.39
  488.9 1.6 copy-start.40
  488.9 1.6 copy-start.41
  488.9 1.6 copy-start.42
  490.5 2.4 copy-start.33

commit v14 on v9

--- a/solution.py
+++ b/solution.py
@@ -176,8 +176,10 @@
             return ev.reshape(n_pt, d_local, rows, kl, FIRST)
 
         left_pts = to_points(left_factor, il)
-        left_pts = jnp.broadcast_to(left_pts[None], (n_grp,) + left_pts.shape)
-        left_pts = lax.all_to_all(left_pts, "grp", split_axis=0, concat_axis=0, tiled=True)
+        left_shape = left_pts.shape
+        left_pts = jnp.broadcast_to(left_pts.reshape(1, -1, 128), (n_grp, left_pts.size // 128, 128))
+        left_pts = lax.all_to_all(left_pts, "grp", split_axis=0, concat_axis=0, tiled=False)
+        left_pts = left_pts.reshape((n_grp,) + left_shape)
         left_pts = jnp.transpose(left_pts, (2, 5, 0, 3, 1, 4))
         left_pts = left_pts.reshape(d_local * FIRST, n_grp * il, n_pt * kl)
         jc = jl // n_chunks
@@ -190,11 +192,16 @@
         n_i = prod.shape[1]
         ib = n_i // n_grp
         jb = n_grp * jl // n_pt
-        prod = prod.reshape(d_local * FIRST, n_grp, ib, jl)
-        prod = lax.all_to_all(prod, "grp", split_axis=1, concat_axis=1, tiled=True)
-        prod = jnp.transpose(prod, (0, 2, 1, 3)).reshape(d_local, FIRST, ib, n_pt, jb)
+        n_pts = d_local * FIRST
+        prod = jnp.transpose(prod.reshape(n_pts, n_grp, ib, jl), (1, 0, 2, 3))
+        prod = prod.reshape(n_grp, n_pts * ib * jl // 128, 128)
+        prod = lax.all_to_all(prod, "grp", split_axis=0, concat_axis=0, tiled=False)
+        prod = prod.reshape(n_grp, d_local, FIRST, ib, jl)
+        prod = jnp.transpose(prod, (1, 2, 3, 0, 4)).reshape(d_local, FIRST, ib, n_pt, jb)
         prod = jnp.transpose(prod, (3, 0, 1, 2, 4))
+        prod = prod.reshape(n_pt, n_pts * ib * jb // 128, 128)
         prod = lax.all_to_all(prod, "pt", split_axis=0, concat_axis=0, tiled=False)
+        prod = prod.reshape(n_pt, d_local, FIRST, ib, jb)
         pv = jnp.transpose(prod, (3, 4, 2, 0, 1)).reshape(ib * jb, FIRST, SECOND)
         coeffs = inverse(pv, tables)
         return (coeffs / float(modulus)).reshape(ib, jb, LENGTH)

time: 490 us -> 475 us (0.969)
  other arithmetic: 70.9 us -> 59.8 us
    unnamed x102 -> x94, local copies, waits for them, and re-layouts: 62.6 us -> 32 us
    reshape x1 -> x5, local copies, waits for them, and re-layouts: 2.5 us -> 14.3 us  [the longest x1 5.22 us: body(): prod = prod.reshape(n_pt, n_pts * ib * jb // 128, 128)]
    all_to_all x2 -> x0, other arithmetic: 11.1 us -> none  [the longest x1 8.02 us: body(): lax.all_to_all(left_pts, 'grp', split_axis=0, concat_axis=0, tiled=True)]
    transpose x1 -> x2, local copies, waits for them, and re-layouts: 0.09 us -> 9.98 us  [the longest x1 9.21 us: body(): prod = jnp.transpose(prod, (3, 0, 1, 2, 4))]
    broadcast_in_dim x2, local copies, waits for them, and re-layouts: 7.5 us -> 1.64 us  [body(): jnp.broadcast_to(left_pts.reshape(1, -1, 128), (n_grp, left_pts.size // 1...]
where the time goes in v14:
time: 475 us; the launch traced here: 469 us
  local copies, waits for them, and re-layouts  201 us (42%)
  waiting for transfers between devices  86.8 us (18%)
  other arithmetic  59.8 us (13%)
  blocking collectives  48.4 us (10%)
  starting transfers between devices  37.6 us (8%)
  matrix products  34.8 us (7%)
    all_to_all x3, waiting for transfers between devices, to_points(): ev = lax.all_to_all(ev, 'pt', split_axis=0, concat_axis=0, tiled=False)  68.9 us
    transpose x2, local copies, waits for them, and re-layouts, body(): jnp.transpose(right_pts, (1, 4, 2, 0, 3))  35.8 us
    reshape x4, local copies, waits for them, and re-layouts, body(): jnp.transpose(right_pts, (1, 4, 2, 0, 3))  35.5 us
    convert_element_type x13, other arithmetic, limbs_bf16(): piece.astype(jnp.bfloat16)  33.4 us
    all_to_all x3, starting transfers between devices, to_points(): ev = lax.all_to_all(ev, 'pt', split_axis=0, concat_axis=0, tiled=False)  33.4 us
    unnamed x94, local copies, waits for them, and re-layouts  32 us
    all_to_all x1, blocking collectives, body(): prod = lax.all_to_all(prod, 'pt', split_axis=0, concat_axis=0, tiled=False)  31.6 us
    reshape x2, local copies, waits for them, and re-layouts, to_points(): return ev.reshape(n_pt, d_local, rows, kl, FIRST)  21.9 us
  transfers between devices with their start and end apart: 4, of which 2 were waited for; matrix products, arithmetic and copies ran while one was open for 35% of the time, Pallas kernels for 0%

profile of v14, /device:TPU:1, one launch (start us, length us, event | category | flops | bytes accessed | tf_op | source)
XLA Modules:
  0.0 469.3 jit_solution(2639959934611634143)
XLA Ops:
  2.9 2.1 subtract_convert_fusion.21
  8.1 7.7 %all-to-all-start = ((f32[16,8,2048]{2,1,0:T(8,128)}), f32[16,8,2048]{2,1,0:T(8,128)S(1)}, u32[]{:S(2)}, u32[]{:S(2)}) async-start(f32[16,8,2048]{2,1,0:T(8,128)} %fusion.48), calls=%async_computation | async-start | bytes 2097152 | tf_op jit(solution)/shard_map/all_to_all | solution.py:175
  15.7 2.5 slice_bitcast_fusion.1
  24.2 17.8 %subtract_convert_fusion.7 = (bf16[256,32,128]{2,1,0:T(8,128)(2,1)}, f32[256,32,128]{2,1,0:T(8,128)S(1)}, bf16[256,32,128]{2,1,0:T(8,128)(2,1)}, f32[256,32,128]{2,1,0:T(8,128)S(1)}) fusion(f32[32,128]{1,0:T(8,128)S(1)} %copy-done.30, f32[32,128]{1,0:T(8,128)S(1)} %copy-done.29, f32[32,128]{1,0:T(8,128)S(1)} %copy-done.28, f32[32,128]{1,0:T(8,128)S(1)} %copy-done.27, ...), kind=kLoop, calls=%fused_computation.45 | loop fusion | flops 125829120 | bytes 37896192 | tf_op jit(solution)/shard_map/convert_element_type | solution.py:105
  45.4 3.8 pad_maximum_fusion
  49.2 6.3 %fusion.71 = f32[384,8192]{1,0:T(8,128)} fusion(bf16[384,384]{1,0:T(8,128)(2,1)S(1)} %copy-done.2, bf16[8192,384]{1,0:T(8,128)(2,1)S(1)} %bitcast.114), kind=kOutput, calls=%fused_computation.151 | convolution fusion | flops 2415919104 | bytes 19169280 | tf_op jit(solution)/shard_map/dot_general | solution.py:118
  57.1 4.2 all-to-all-start.1
  61.4 7.1 %fusion.12 = f32[16,8,8192]{2,1,0:T(8,128)} fusion(f32[384,8192]{1,0:T(8,128)} %fusion.71), kind=kLoop, calls=%fused_computation.25 | loop fusion | flops 16777216 | bytes 16777216 | tf_op jit(solution)/shard_map/reshape | solution.py:174
  68.4 17.9 %all-to-all-done.1 = f32[2,2048,128]{2,1,0:T(8,128)S(1)} async-done(((f32[2,2048,128]{2,1,0:T(8,128)}), f32[2,2048,128]{2,1,0:T(8,128)S(1)}, u32[]{:S(2)}, u32[]{:S(2)}) %all-to-all-start.1) | async-done | bytes 2097184 | tf_op jit(solution)/shard_map/all_to_all | solution.py:181
  86.3 6.4 %all-to-all-start.2 = ((f32[16,8,8192]{2,1,0:T(8,128)}), f32[16,8,8192]{2,1,0:T(8,128)}, u32[]{:S(2)}, u32[]{:S(2)}) async-start(f32[16,8,8192]{2,1,0:T(8,128)} %fusion.12), calls=%async_computation.2 | async-start | bytes 8388608 | tf_op jit(solution)/shard_map/all_to_all | solution.py:175
  92.8 5.6 %fusion.72 = f32[384,8192]{1,0:T(8,128)S(1)} fusion(bf16[384,384]{1,0:T(8,128)(2,1)S(1)} %copy-done.2, bf16[8192,384]{1,0:T(8,128)(2,1)} %bitcast.113), kind=kOutput, calls=%fused_computation.152 | convolution fusion | flops 2415919104 | bytes 19169280 | tf_op jit(solution)/shard_map/dot_general | solution.py:118
  98.3 3.6 fusion.13
  101.9 68.9 %all-to-all-done.2 = f32[16,8,8192]{2,1,0:T(8,128)} async-done(((f32[16,8,8192]{2,1,0:T(8,128)}), f32[16,8,8192]{2,1,0:T(8,128)}, u32[]{:S(2)}, u32[]{:S(2)}) %all-to-all-start.2) | async-done | bytes 4194336 | tf_op jit(solution)/shard_map/all_to_all | solution.py:175
  170.8 19.3 %all-to-all-start.3 = ((f32[16,8,8192]{2,1,0:T(8,128)}), f32[16,8,8192]{2,1,0:T(8,128)}, u32[]{:S(2)}, u32[]{:S(2)}) async-start(f32[16,8,8192]{2,1,0:T(8,128)} %fusion.13), calls=%async_computation.3 | async-start | bytes 8388608 | tf_op jit(solution)/shard_map/all_to_all | solution.py:175
  190.1 4.3 reshape.83
  194.5 11.5 %copy.56 = f32[8,32,2,8,16,8]{1,0,5,4,3,2:T(8,128)} copy(f32[8,32,2,8,16,8]{1,5,3,0,4,2:T(8,128)} %bitcast.110) | data formatting | bytes 4194304 | tf_op jit(solution)/shard_map/transpose | solution.py:183
  206.0 5.8 %reshape.84 = f32[256,16,128]{0,2,1:T(8,128)S(1)} reshape(f32[8,32,2,8,16,8]{1,0,5,4,3,2:T(8,128)} %copy.56) | data formatting | bytes 4194304 | tf_op jit(solution)/shard_map/reshape | solution.py:184
  211.8 2.0 copy.58
  213.8 7.2 %subtract_convert_fusion.15 = (bf16[256,16,128]{2,1,0:T(8,128)(2,1)}, bf16[256,16,128]{2,1,0:T(8,128)(2,1)}, bf16[256,16,128]{2,1,0:T(8,128)(2,1)}, bf16[256,16,...) fusion(f32[256,16,128]{2,1,0:T(8,128)} %copy.58), kind=kLoop, calls=%fused_computation.93 | loop fusion | flops 33554432 | bytes 11534336 | tf_op jit(solution)/shard_map/convert_element_type | solution.py:156
  221.7 11.2 %reshape.87 = f32[16,8,32,8,32]{4,3,2,1,0:T(8,128)} reshape(f32[16,8,8192]{2,1,0:T(8,128)} %all-to-all-done.2) | data formatting | bytes 8388608 | tf_op jit(solution)/shard_map/reshape | solution.py:176
  232.9 17.9 %copy.63 = f32[8,32,32,16,8]{1,0,4,3,2:T(8,128)} copy(f32[8,32,32,16,8]{1,4,2,0,3:T(8,128)} %bitcast.108) | data formatting | bytes 8388608 | tf_op jit(solution)/shard_map/transpose | solution.py:189
  250.8 12.2 %reshape.88 = f32[256,32,128]{0,2,1:T(8,128)} reshape(f32[8,32,32,16,8]{1,0,4,3,2:T(8,128)} %copy.63) | data formatting | bytes 8388608 | tf_op jit(solution)/shard_map/reshape | solution.py:189
  263.0 5.5 %copy.65 = f32[256,32,128]{2,1,0:T(8,128)} copy(f32[256,32,128]{0,2,1:T(8,128)} %reshape.88) | data formatting | bytes 8388608 | tf_op jit(solution)/shard_map/reshape | solution.py:189
  268.5 3.3 subtract_convert_fusion.5
  272.9 7.6 %fusion = f32[256,48,32]{1,2,0:T(8,128)S(1)} fusion(bf16[256,32,128]{2,1,0:T(8,128)(2,1)S(1)} %get-tuple-element.20, bf16[256,32,128]{2,1,0:T(8,128)(2,1)S(1)} %get-tuple-element.19, bf16[256,32,128]{2,1,0:T(8,128)(2,1)S(1)} %get-tuple-element.18, bf16[256,16,128]{2,1,0:T(8,128)(2,1)S(1)} %copy-done.15, bf16[256,16,128]{2,1,0:T(8,128)(2,1)S(1)} %get-tuple-element.45, ...), kind=kOutput, calls=%fused_computation.8 | convolution fusion | flops 405798912 | bytes 17301504 | tf_op jit(solution)/shard_map/pak,pjk->paj/dot_general | solution.py:159
  280.5 6.8 %fusion.68 = (f32[256,16,32]{1,2,0:T(8,128)}, f32[256,16,32]{1,2,0:T(8,128)}, f32[256,16,32]{1,2,0:T(8,128)}) fusion(f32[256,48,32]{1,2,0:T(8,128)S(1)} %fusion), kind=kLoop, calls=%fused_computation.148 | loop fusion | bytes 3145728 | tf_op jit(solution)/shard_map/slice | solution.py:161
  287.3 3.8 copy.83
  291.1 3.8 copy.84
  294.9 3.8 copy.85
  298.7 10.8 %reshape.91 = f32[16,8,32,8,32]{4,3,2,1,0:T(8,128)} reshape(f32[16,8,8192]{2,1,0:T(8,128)} %all-to-all-done.3) | data formatting | bytes 8388608 | tf_op jit(solution)/shard_map/reshape | solution.py:176
  309.5 17.9 %copy.69 = f32[8,32,32,16,8]{1,0,4,3,2:T(8,128)} copy(f32[8,32,32,16,8]{1,4,2,0,3:T(8,128)} %bitcast.109) | data formatting | bytes 8388608 | tf_op jit(solution)/shard_map/transpose | solution.py:189
  327.4 12.2 %reshape.92 = f32[256,32,128]{0,2,1:T(8,128)} reshape(f32[8,32,32,16,8]{1,0,4,3,2:T(8,128)} %copy.69) | data formatting | bytes 8388608 | tf_op jit(solution)/shard_map/reshape | solution.py:189
  339.6 5.5 %copy.71 = f32[256,32,128]{2,1,0:T(8,128)} copy(f32[256,32,128]{0,2,1:T(8,128)} %reshape.92) | data formatting | bytes 8388608 | tf_op jit(solution)/shard_map/reshape | solution.py:189
  345.2 3.3 subtract_convert_fusion.1
  350.1 7.7 %fusion.6 = f32[256,48,32]{1,2,0:T(8,128)S(1)} fusion(bf16[256,32,128]{2,1,0:T(8,128)(2,1)S(1)} %get-tuple-element.30, bf16[256,32,128]{2,1,0:T(8,128)(2,1)S(1)} %get-tuple-element.29, bf16[256,32,128]{2,1,0:T(8,128)(2,1)S(1)} %get-tuple-element.28, bf16[256,16,128]{2,1,0:T(8,128)(2,1)S(1)} %copy-done.16, bf16[256,16,128]{2,1,0:T(8,128)(2,1)S(1)} %copy-done.6, ...), kind=kOutput, calls=%fused_computation.15 | convolution fusion | flops 405798912 | bytes 17301504 | tf_op jit(solution)/shard_map/pak,pjk->paj/dot_general | solution.py:159
  357.8 6.8 %fusion.69 = (f32[256,16,32]{1,2,0:T(8,128)}, f32[256,16,32]{1,2,0:T(8,128)}, f32[256,16,32]{1,2,0:T(8,128)}) fusion(f32[256,48,32]{1,2,0:T(8,128)S(1)} %fusion.6), kind=kLoop, calls=%fused_computation.149 | loop fusion | bytes 3145728 | tf_op jit(solution)/shard_map/slice | solution.py:161
  364.6 3.8 copy.86
  368.4 3.8 copy.87
  372.2 4.7 %copy.88 = f32[256,16,32]{0,2,1:T(8,128)} copy(f32[256,16,32]{1,2,0:T(8,128)} %get-tuple-element.25) | data formatting | bytes 1048576
  379.8 16.8 %all_to_all.30 = f32[2,1024,128]{2,1,0:T(8,128)} all-to-all(f32[2,1024,128]{2,1,0:T(8,128)S(1)} %reshape.94), channel_id=1, replica_groups=mesh['grp'=2,'pt'=16] {'grp'}, dimensions={0} | all-to-all | bytes 2097152 | tf_op jit(solution)/shard_map/all_to_all | solution.py:198
  398.2 2.9 copy.76
  401.0 9.2 %copy.77 = f32[16,8,32,8,8]{0,4,3,2,1:T(8,128)} copy(f32[16,8,32,8,8]{2,4,0,3,1:T(8,128)} %bitcast.116) | data formatting | bytes 2097152 | tf_op jit(solution)/shard_map/transpose | solution.py:201
  410.2 5.2 %copy.78 = f32[16,128,128]{2,1,0:T(8,128)S(1)} copy(f32[16,128,128]{0,2,1:T(8,128)} %bitcast.111) | data formatting | bytes 2097152 | tf_op jit(solution)/shard_map/reshape | solution.py:202
  415.5 31.6 %all_to_all.31 = f32[16,128,128]{2,1,0:T(8,128)S(1)} all-to-all(f32[16,128,128]{2,1,0:T(8,128)S(1)} %copy.78), channel_id=1, replica_groups=mesh['grp'=2,'pt'=16] {'pt'}, dimensions={0} | all-to-all | bytes 2097152 | tf_op jit(solution)/shard_map/all_to_all | solution.py:203
  447.1 4.6 copy.79
  451.7 7.9 %copy.80 = f32[8,8,32,16,8]{2,4,3,1,0:T(8,128)} copy(f32[8,8,32,16,8]{3,1,0,2,4:T(8,128)} %bitcast.112) | data formatting | bytes 2097152 | tf_op jit(solution)/shard_map/transpose | solution.py:205
  459.6 2.8 copy.82
  464.2 2.1 subtract_convert_fusion.17
  (116 shorter events, 28.5 us)
Async XLA Ops:
  0.0 2.8 copy-start.22
  0.0 2.8 copy-start.23
  0.0 2.8 copy-start.24
  0.0 2.8 copy-start.25
  0.0 2.8 copy-start.26
  0.0 2.8 copy-start.27
  0.0 2.8 copy-start.28
  0.1 2.8 copy-start.29
  0.1 2.8 copy-start.30
  2.9 2.6 copy-start.2
  8.1 47.4 %all-to-all-start = ((f32[16,8,2048]{2,1,0:T(8,128)}), f32[16,8,2048]{2,1,0:T(8,128)S(1)}, u32[]{:S(2)}, u32[]{:S(2)}) async-start(f32[16,8,2048]{2,1,0:T(8,128)} %fusion.48), calls=%async_computation | async-start | bytes 2097152 | tf_op jit(solution)/shard_map/all_to_all | solution.py:175
  19.4 1.2 copy-start.21
  43.1 1.6 copy-start
  43.1 2.2 copy-start.1
  57.1 29.2 %all-to-all-start.1 = ((f32[2,2048,128]{2,1,0:T(8,128)}), f32[2,2048,128]{2,1,0:T(8,128)S(1)}, u32[]{:S(2)}, u32[]{:S(2)}) async-start(f32[2,2048,128]{2,1,0:T(8,128)} %broadcast_in_dim.8), calls=%async_computation.1 | async-start | bytes 4194304 | tf_op jit(solution)/shard_map/all_to_all | solution.py:181
  86.3 84.5 %all-to-all-start.2 = ((f32[16,8,8192]{2,1,0:T(8,128)}), f32[16,8,8192]{2,1,0:T(8,128)}, u32[]{:S(2)}, u32[]{:S(2)}) async-start(f32[16,8,8192]{2,1,0:T(8,128)} %fusion.12), calls=%async_computation.2 | async-start | bytes 8388608 | tf_op jit(solution)/shard_map/all_to_all | solution.py:175
  170.8 127.9 %all-to-all-start.3 = ((f32[16,8,8192]{2,1,0:T(8,128)}), f32[16,8,8192]{2,1,0:T(8,128)}, u32[]{:S(2)}, u32[]{:S(2)}) async-start(f32[16,8,8192]{2,1,0:T(8,128)} %fusion.13), calls=%async_computation.3 | async-start | bytes 8388608 | tf_op jit(solution)/shard_map/all_to_all | solution.py:175
  221.7 50.1 %copy-start.3 = (bf16[256,16,128]{2,1,0:T(8,128)(2,1)}, bf16[256,16,128]{2,1,0:T(8,128)(2,1)S(1)}, u32[]{:S(2)}) copy-start(bf16[256,16,128]{2,1,0:T(8,128)(2,1)S(1)} %get-tuple-element.44) | copy-start | bytes 3145732
  221.7 50.1 %copy-start.5 = (bf16[256,16,128]{2,1,0:T(8,128)(2,1)}, bf16[256,16,128]{2,1,0:T(8,128)(2,1)S(1)}, u32[]{:S(2)}) copy-start(bf16[256,16,128]{2,1,0:T(8,128)(2,1)S(1)} %get-tuple-element.45) | copy-start | bytes 3145732
  268.5 3.3 copy-start.7
  268.5 3.4 copy-start.9
  268.5 3.4 copy-start.11
  268.5 3.4 copy-start.13
  268.5 3.7 copy-start.15
  268.5 4.0 copy-start.17
  268.5 4.3 copy-start.19
  345.1 3.3 copy-start.4
  345.1 3.4 copy-start.6
  345.1 3.4 copy-start.8
  345.1 3.4 copy-start.10
  345.1 3.7 copy-start.12
  345.2 4.0 copy-start.14
  345.2 4.3 copy-start.16
  345.2 4.6 copy-start.18
  345.2 4.9 %copy-start.20 = (bf16[256,16,128]{2,1,0:T(8,128)(2,1)S(1)}, bf16[256,16,128]{2,1,0:T(8,128)(2,1)}, u32[]{:S(2)}) copy-start(bf16[256,16,128]{2,1,0:T(8,128)(2,1)} %get-tuple-element.43) | copy-start | bytes 3145732
  459.6 3.3 copy-start.41
  462.4 1.6 copy-start.32
  462.5 1.6 copy-start.33
  462.5 1.6 copy-start.34
  462.5 1.6 copy-start.35
  462.5 1.6 copy-start.36
  462.5 1.6 copy-start.37
  462.5 1.6 copy-start.38
  462.5 1.6 copy-start.39
  462.5 1.6 copy-start.40
  464.2 2.4 copy-start.31

commit v15 on v14

--- a/solution.py
+++ b/solution.py
@@ -183,19 +183,20 @@
         left_pts = jnp.transpose(left_pts, (2, 5, 0, 3, 1, 4))
         left_pts = left_pts.reshape(d_local * FIRST, n_grp * il, n_pt * kl)
         jc = jl // n_chunks
+        n_i = n_grp * il
+        ib = n_i // n_grp
+        jb = n_grp * jl // n_pt
+        n_pts = d_local * FIRST
         prods = []
         for chunk in range(n_chunks):
             right_pts = to_points(right_factor[chunk * jc : (chunk + 1) * jc], jc)
             right_pts = jnp.transpose(right_pts, (1, 4, 2, 0, 3)).reshape(d_local * FIRST, jc, n_pt * kl)
-            prods.append(multiply_points(left_pts, right_pts))
-        prod = jnp.concatenate(prods, axis=2) if n_chunks > 1 else prods[0]
-        n_i = prod.shape[1]
-        ib = n_i // n_grp
-        jb = n_grp * jl // n_pt
-        n_pts = d_local * FIRST
-        prod = jnp.transpose(prod.reshape(n_pts, n_grp, ib, jl), (1, 0, 2, 3))
-        prod = prod.reshape(n_grp, n_pts * ib * jl // 128, 128)
-        prod = lax.all_to_all(prod, "grp", split_axis=0, concat_axis=0, tiled=False)
+            part = multiply_points(left_pts, right_pts)
+            part = jnp.transpose(part.reshape(n_pts, n_grp, ib, jc), (1, 0, 2, 3))
+            part = part.reshape(n_grp, n_pts * ib * jc // 128, 128)
+            part = lax.all_to_all(part, "grp", split_axis=0, concat_axis=0, tiled=False)
+            prods.append(part.reshape(n_grp, n_pts, ib, jc))
+        prod = jnp.concatenate(prods, axis=3) if n_chunks > 1 else prods[0]
         prod = prod.reshape(n_grp, d_local, FIRST, ib, jl)
         prod = jnp.transpose(prod, (1, 2, 3, 0, 4)).reshape(d_local, FIRST, ib, n_pt, jb)
         prod = jnp.transpose(prod, (3, 0, 1, 2, 4))

time: 475 us -> 477 us (level)
  blocking collectives: 48.4 us -> 31.6 us
  starting transfers between devices: 37.6 us -> 44.7 us
  waiting for transfers between devices: 86.8 us -> 92.5 us
    all_to_all x1 -> x0, blocking collectives: 16.8 us -> none  [body(): prod = lax.all_to_all(prod, 'grp', split_axis=0, concat_axis=0, tiled=False)]
    all_to_all x0 -> x2, starting transfers between devices: none -> 6.98 us  [body(): part = lax.all_to_all(part, 'grp', split_axis=0, concat_axis=0, tiled=False)]
    all_to_all x0 -> x2, waiting for transfers between devices: none -> 5.64 us  [body(): part = lax.all_to_all(part, 'grp', split_axis=0, concat_axis=0, tiled=False)]
    concatenate x1, other arithmetic: 0.09 us -> 5.03 us  [body(): prod = jnp.concatenate(prods, axis=3) if n_chunks > 1 else prods[0]]
  transfers between devices with their start and end apart: 4 -> 6, of which waited for: 2 -> 3; matrix products, arithmetic and copies ran while one was open for 35% -> 52% of each run, Pallas kernels for 0% -> 0%
where the time goes in v15:
time: 477 us; the launch traced here: 471 us
  local copies, waits for them, and re-layouts  203 us (43%)
  waiting for transfers between devices  92.5 us (19%)
  other arithmetic  63.6 us (13%)
  starting transfers between devices  44.7 us (9%)
  matrix products  34.8 us (7%)
  blocking collectives  31.6 us (7%)
    all_to_all x3, waiting for transfers between devices, to_points(): ev = lax.all_to_all(ev, 'pt', split_axis=0, concat_axis=0, tiled=False)  68.9 us
    transpose x2, local copies, waits for them, and re-layouts, body(): jnp.transpose(right_pts, (1, 4, 2, 0, 3))  35.6 us
    reshape x4, local copies, waits for them, and re-layouts, body(): jnp.transpose(right_pts, (1, 4, 2, 0, 3))  35.4 us
    all_to_all x3, starting transfers between devices, to_points(): ev = lax.all_to_all(ev, 'pt', split_axis=0, concat_axis=0, tiled=False)  33.4 us
    convert_element_type x13, other arithmetic, limbs_bf16(): piece.astype(jnp.bfloat16)  33.4 us
    all_to_all x1, blocking collectives, body(): prod = lax.all_to_all(prod, 'pt', split_axis=0, concat_axis=0, tiled=False)  31.6 us
    unnamed x94, local copies, waits for them, and re-layouts  31.5 us
    reshape x2, local copies, waits for them, and re-layouts, to_points(): return ev.reshape(n_pt, d_local, rows, kl, FIRST)  22.1 us
  transfers between devices with their start and end apart: 6, of which 3 were waited for; matrix products, arithmetic and copies ran while one was open for 52% of the time, Pallas kernels for 0%

profile of v15, /device:TPU:1, one launch (start us, length us, event | category | flops | bytes accessed | tf_op | source)
XLA Modules:
  0.0 471.4 jit_solution(7152166668731614780)
XLA Ops:
  2.9 2.1 subtract_convert_fusion.21
  8.1 7.7 %all-to-all-start = ((f32[16,8,2048]{2,1,0:T(8,128)}), f32[16,8,2048]{2,1,0:T(8,128)S(1)}, u32[]{:S(2)}, u32[]{:S(2)}) async-start(f32[16,8,2048]{2,1,0:T(8,128)} %fusion.48), calls=%async_computation | async-start | bytes 2097152 | tf_op jit(solution)/shard_map/all_to_all | solution.py:175
  15.8 2.5 slice_bitcast_fusion.1
  24.2 17.8 %subtract_convert_fusion.7 = (bf16[256,32,128]{2,1,0:T(8,128)(2,1)}, f32[256,32,128]{2,1,0:T(8,128)S(1)}, bf16[256,32,128]{2,1,0:T(8,128)(2,1)}, f32[256,32,128]{2,1,0:T(8,128)S(1)}) fusion(f32[32,128]{1,0:T(8,128)S(1)} %copy-done.30, f32[32,128]{1,0:T(8,128)S(1)} %copy-done.29, f32[32,128]{1,0:T(8,128)S(1)} %copy-done.28, f32[32,128]{1,0:T(8,128)S(1)} %copy-done.27, ...), kind=kLoop, calls=%fused_computation.46 | loop fusion | flops 125829120 | bytes 37896192 | tf_op jit(solution)/shard_map/convert_element_type | solution.py:105
  45.4 3.8 pad_maximum_fusion
  49.2 6.4 %fusion.71 = f32[384,8192]{1,0:T(8,128)} fusion(bf16[384,384]{1,0:T(8,128)(2,1)S(1)} %copy-done.2, bf16[8192,384]{1,0:T(8,128)(2,1)S(1)} %bitcast.119), kind=kOutput, calls=%fused_computation.151 | convolution fusion | flops 2415919104 | bytes 19169280 | tf_op jit(solution)/shard_map/dot_general | solution.py:118
  57.2 4.3 all-to-all-start.1
  61.5 7.1 %fusion.12 = f32[16,8,8192]{2,1,0:T(8,128)} fusion(f32[384,8192]{1,0:T(8,128)} %fusion.71), kind=kLoop, calls=%fused_computation.25 | loop fusion | flops 16777216 | bytes 16777216 | tf_op jit(solution)/shard_map/reshape | solution.py:174
  68.6 17.9 %all-to-all-done.1 = f32[2,2048,128]{2,1,0:T(8,128)S(1)} async-done(((f32[2,2048,128]{2,1,0:T(8,128)}), f32[2,2048,128]{2,1,0:T(8,128)S(1)}, u32[]{:S(2)}, u32[]{:S(2)}) %all-to-all-start.1) | async-done | bytes 2097184 | tf_op jit(solution)/shard_map/all_to_all | solution.py:181
  86.4 6.4 %all-to-all-start.2 = ((f32[16,8,8192]{2,1,0:T(8,128)}), f32[16,8,8192]{2,1,0:T(8,128)}, u32[]{:S(2)}, u32[]{:S(2)}) async-start(f32[16,8,8192]{2,1,0:T(8,128)} %fusion.12), calls=%async_computation.2 | async-start | bytes 8388608 | tf_op jit(solution)/shard_map/all_to_all | solution.py:175
  92.9 5.6 %fusion.72 = f32[384,8192]{1,0:T(8,128)S(1)} fusion(bf16[384,384]{1,0:T(8,128)(2,1)S(1)} %copy-done.2, bf16[8192,384]{1,0:T(8,128)(2,1)} %bitcast.118), kind=kOutput, calls=%fused_computation.152 | convolution fusion | flops 2415919104 | bytes 19169280 | tf_op jit(solution)/shard_map/dot_general | solution.py:118
  98.5 3.6 fusion.13
  102.0 68.9 %all-to-all-done.2 = f32[16,8,8192]{2,1,0:T(8,128)} async-done(((f32[16,8,8192]{2,1,0:T(8,128)}), f32[16,8,8192]{2,1,0:T(8,128)}, u32[]{:S(2)}, u32[]{:S(2)}) %all-to-all-start.2) | async-done | bytes 4194336 | tf_op jit(solution)/shard_map/all_to_all | solution.py:175
  171.0 19.3 %all-to-all-start.4 = ((f32[16,8,8192]{2,1,0:T(8,128)}), f32[16,8,8192]{2,1,0:T(8,128)}, u32[]{:S(2)}, u32[]{:S(2)}) async-start(f32[16,8,8192]{2,1,0:T(8,128)} %fusion.13), calls=%async_computation.4 | async-start | bytes 8388608 | tf_op jit(solution)/shard_map/all_to_all | solution.py:175
  190.3 4.3 reshape.93
  194.6 11.5 %copy.61 = f32[8,32,2,8,16,8]{1,0,5,4,3,2:T(8,128)} copy(f32[8,32,2,8,16,8]{1,5,3,0,4,2:T(8,128)} %bitcast.115) | data formatting | bytes 4194304 | tf_op jit(solution)/shard_map/transpose | solution.py:183
  206.1 5.8 %reshape.94 = f32[256,16,128]{0,2,1:T(8,128)S(1)} reshape(f32[8,32,2,8,16,8]{1,0,5,4,3,2:T(8,128)} %copy.61) | data formatting | bytes 4194304 | tf_op jit(solution)/shard_map/reshape | solution.py:184
  214.0 7.1 %subtract_convert_fusion.15 = (bf16[256,16,128]{2,1,0:T(8,128)(2,1)}, bf16[256,16,128]{2,1,0:T(8,128)(2,1)}, bf16[256,16,128]{2,1,0:T(8,128)(2,1)}, bf16[256,16,...) fusion(f32[256,16,128]{2,1,0:T(8,128)} %copy.63), kind=kLoop, calls=%fused_computation.94 | loop fusion | flops 33554432 | bytes 11534336 | tf_op jit(solution)/shard_map/convert_element_type | solution.py:156
  221.9 11.1 %reshape.97 = f32[16,8,32,8,32]{4,3,2,1,0:T(8,128)} reshape(f32[16,8,8192]{2,1,0:T(8,128)} %all-to-all-done.2) | data formatting | bytes 8388608 | tf_op jit(solution)/shard_map/reshape | solution.py:176
  233.0 17.9 %copy.68 = f32[8,32,32,16,8]{1,0,4,3,2:T(8,128)} copy(f32[8,32,32,16,8]{1,4,2,0,3:T(8,128)} %bitcast.113) | data formatting | bytes 8388608 | tf_op jit(solution)/shard_map/transpose | solution.py:193
  250.9 12.2 %reshape.98 = f32[256,32,128]{0,2,1:T(8,128)} reshape(f32[8,32,32,16,8]{1,0,4,3,2:T(8,128)} %copy.68) | data formatting | bytes 8388608 | tf_op jit(solution)/shard_map/reshape | solution.py:193
  263.1 5.5 %copy.70 = f32[256,32,128]{2,1,0:T(8,128)} copy(f32[256,32,128]{0,2,1:T(8,128)} %reshape.98) | data formatting | bytes 8388608 | tf_op jit(solution)/shard_map/reshape | solution.py:193
  268.6 3.3 subtract_convert_fusion.5
  273.0 7.6 %fusion = f32[256,48,32]{1,2,0:T(8,128)S(1)} fusion(bf16[256,32,128]{2,1,0:T(8,128)(2,1)S(1)} %get-tuple-element.20, bf16[256,32,128]{2,1,0:T(8,128)(2,1)S(1)} %get-tuple-element.19, bf16[256,32,128]{2,1,0:T(8,128)(2,1)S(1)} %get-tuple-element.18, bf16[256,16,128]{2,1,0:T(8,128)(2,1)S(1)} %copy-done.15, bf16[256,16,128]{2,1,0:T(8,128)(2,1)S(1)} %get-tuple-element.45, ...), kind=kOutput, calls=%fused_computation.8 | convolution fusion | flops 405798912 | bytes 17301504 | tf_op jit(solution)/shard_map/pak,pjk->paj/dot_general | solution.py:159
  280.6 6.8 %fusion.68 = (f32[256,16,32]{1,2,0:T(8,128)}, f32[256,16,32]{1,2,0:T(8,128)}, f32[256,16,32]{1,2,0:T(8,128)}) fusion(f32[256,48,32]{1,2,0:T(8,128)S(1)} %fusion), kind=kLoop, calls=%fused_computation.148 | loop fusion | bytes 3145728 | tf_op jit(solution)/shard_map/slice | solution.py:161
  287.4 3.8 copy.90
  291.2 3.8 copy.91
  295.0 3.8 copy.92
  301.1 3.5 all-to-all-start.3
  304.6 11.0 %reshape.103 = f32[16,8,32,8,32]{4,3,2,1,0:T(8,128)} reshape(f32[16,8,8192]{2,1,0:T(8,128)} %all-to-all-done.4) | data formatting | bytes 8388608 | tf_op jit(solution)/shard_map/reshape | solution.py:176
  315.6 17.7 %copy.75 = f32[8,32,32,16,8]{1,0,4,3,2:T(8,128)} copy(f32[8,32,32,16,8]{1,4,2,0,3:T(8,128)} %bitcast.114) | data formatting | bytes 8388608 | tf_op jit(solution)/shard_map/transpose | solution.py:193
  333.3 12.2 %reshape.104 = f32[256,32,128]{0,2,1:T(8,128)} reshape(f32[8,32,32,16,8]{1,0,4,3,2:T(8,128)} %copy.75) | data formatting | bytes 8388608 | tf_op jit(solution)/shard_map/reshape | solution.py:193
  345.5 5.5 %copy.77 = f32[256,32,128]{2,1,0:T(8,128)} copy(f32[256,32,128]{0,2,1:T(8,128)} %reshape.104) | data formatting | bytes 8388608 | tf_op jit(solution)/shard_map/reshape | solution.py:193
  351.1 3.3 subtract_convert_fusion.1
  356.0 7.6 %fusion.6 = f32[256,48,32]{1,2,0:T(8,128)S(1)} fusion(bf16[256,32,128]{2,1,0:T(8,128)(2,1)S(1)} %get-tuple-element.30, bf16[256,32,128]{2,1,0:T(8,128)(2,1)S(1)} %get-tuple-element.29, bf16[256,32,128]{2,1,0:T(8,128)(2,1)S(1)} %get-tuple-element.28, bf16[256,16,128]{2,1,0:T(8,128)(2,1)S(1)} %copy-done.16, bf16[256,16,128]{2,1,0:T(8,128)(2,1)S(1)} %copy-done.6, ...), kind=kOutput, calls=%fused_computation.15 | convolution fusion | flops 405798912 | bytes 17301504 | tf_op jit(solution)/shard_map/pak,pjk->paj/dot_general | solution.py:159
  363.6 6.8 %fusion.69 = (f32[256,16,32]{1,2,0:T(8,128)}, f32[256,16,32]{1,2,0:T(8,128)}, f32[256,16,32]{1,2,0:T(8,128)}) fusion(f32[256,48,32]{1,2,0:T(8,128)S(1)} %fusion.6), kind=kLoop, calls=%fused_computation.149 | loop fusion | bytes 3145728 | tf_op jit(solution)/shard_map/slice | solution.py:161
  370.5 3.8 copy.93
  374.2 3.8 copy.94
  378.0 4.2 copy.95
  384.6 3.5 all-to-all-start.5
  390.4 5.6 %all-to-all-done.5 = f32[2,512,128]{2,1,0:T(8,128)S(1)} async-done(((f32[2,512,128]{2,1,0:T(8,128)}), f32[2,512,128]{2,1,0:T(8,128)S(1)}, u32[]{:S(2)}, u32[]{:S(2)}) %all-to-all-start.5) | async-done | bytes 524320 | tf_op jit(solution)/shard_map/all_to_all | solution.py:197
  398.3 5.0 %pad_maximum_fusion.2 = f32[2,8,32,8,64]{2,4,0,3,1:T(8,128)} fusion(f32[2,8,32,8,32]{2,4,0,3,1:T(8,128)} %copy.83, f32[2,8,32,8,32]{2,4,0,3,1:T(8,128)} %copy.82), kind=kLoop, calls=%fused_computation.27 | loop fusion | flops 262144 | bytes 2097152 | tf_op jit(solution)/shard_map/concatenate | solution.py:199
  403.4 9.2 %copy.84 = f32[16,8,32,8,8]{0,4,3,2,1:T(8,128)} copy(f32[16,8,32,8,8]{2,4,0,3,1:T(8,128)} %bitcast.121) | data formatting | bytes 2097152 | tf_op jit(solution)/shard_map/transpose | solution.py:202
  412.6 5.2 %copy.85 = f32[16,128,128]{2,1,0:T(8,128)S(1)} copy(f32[16,128,128]{0,2,1:T(8,128)} %bitcast.116) | data formatting | bytes 2097152 | tf_op jit(solution)/shard_map/reshape | solution.py:203
  417.8 31.6 %all_to_all.35 = f32[16,128,128]{2,1,0:T(8,128)S(1)} all-to-all(f32[16,128,128]{2,1,0:T(8,128)S(1)} %copy.85), channel_id=1, replica_groups=mesh['grp'=2,'pt'=16] {'pt'}, dimensions={0} | all-to-all | bytes 2097152 | tf_op jit(solution)/shard_map/all_to_all | solution.py:204
  449.4 4.7 copy.86
  454.1 7.9 %copy.87 = f32[8,8,32,16,8]{2,4,3,1,0:T(8,128)} copy(f32[8,8,32,16,8]{3,1,0,2,4:T(8,128)} %bitcast.117) | data formatting | bytes 2097152 | tf_op jit(solution)/shard_map/transpose | solution.py:206
  462.0 2.8 copy.89
  (123 shorter events, 37.6 us)
Async XLA Ops:
  0.0 2.8 copy-start.22
  0.0 2.8 copy-start.23
  0.0 2.8 copy-start.24
  0.0 2.8 copy-start.25
  0.0 2.8 copy-start.26
  0.0 2.8 copy-start.27
  0.0 2.8 copy-start.28
  0.1 2.8 copy-start.29
  0.1 2.8 copy-start.30
  2.9 2.6 copy-start.2
  8.1 47.5 %all-to-all-start = ((f32[16,8,2048]{2,1,0:T(8,128)}), f32[16,8,2048]{2,1,0:T(8,128)S(1)}, u32[]{:S(2)}, u32[]{:S(2)}) async-start(f32[16,8,2048]{2,1,0:T(8,128)} %fusion.48), calls=%async_computation | async-start | bytes 2097152 | tf_op jit(solution)/shard_map/all_to_all | solution.py:175
  19.4 1.2 copy-start.21
  43.2 1.6 copy-start
  43.2 2.2 copy-start.1
  57.2 29.3 %all-to-all-start.1 = ((f32[2,2048,128]{2,1,0:T(8,128)}), f32[2,2048,128]{2,1,0:T(8,128)S(1)}, u32[]{:S(2)}, u32[]{:S(2)}) async-start(f32[2,2048,128]{2,1,0:T(8,128)} %broadcast_in_dim.8), calls=%async_computation.1 | async-start | bytes 4194304 | tf_op jit(solution)/shard_map/all_to_all | solution.py:181
  86.4 84.5 %all-to-all-start.2 = ((f32[16,8,8192]{2,1,0:T(8,128)}), f32[16,8,8192]{2,1,0:T(8,128)}, u32[]{:S(2)}, u32[]{:S(2)}) async-start(f32[16,8,8192]{2,1,0:T(8,128)} %fusion.12), calls=%async_computation.2 | async-start | bytes 8388608 | tf_op jit(solution)/shard_map/all_to_all | solution.py:175
  171.0 130.2 %all-to-all-start.4 = ((f32[16,8,8192]{2,1,0:T(8,128)}), f32[16,8,8192]{2,1,0:T(8,128)}, u32[]{:S(2)}, u32[]{:S(2)}) async-start(f32[16,8,8192]{2,1,0:T(8,128)} %fusion.13), calls=%async_computation.4 | async-start | bytes 8388608 | tf_op jit(solution)/shard_map/all_to_all | solution.py:175
  221.8 50.1 %copy-start.3 = (bf16[256,16,128]{2,1,0:T(8,128)(2,1)}, bf16[256,16,128]{2,1,0:T(8,128)(2,1)S(1)}, u32[]{:S(2)}) copy-start(bf16[256,16,128]{2,1,0:T(8,128)(2,1)S(1)} %get-tuple-element.44) | copy-start | bytes 3145732
  221.9 50.1 %copy-start.5 = (bf16[256,16,128]{2,1,0:T(8,128)(2,1)}, bf16[256,16,128]{2,1,0:T(8,128)(2,1)S(1)}, u32[]{:S(2)}) copy-start(bf16[256,16,128]{2,1,0:T(8,128)(2,1)S(1)} %get-tuple-element.45) | copy-start | bytes 3145732
  268.6 3.3 copy-start.7
  268.6 3.4 copy-start.9
  268.6 3.4 copy-start.11
  268.6 3.4 copy-start.13
  268.6 3.7 copy-start.15
  268.6 4.0 copy-start.17
  268.6 4.3 copy-start.19
  301.1 83.4 %all-to-all-start.3 = ((f32[2,512,128]{2,1,0:T(8,128)}), f32[2,512,128]{2,1,0:T(8,128)S(1)}, u32[]{:S(2)}, u32[]{:S(2)}) async-start(f32[2,512,128]{2,1,0:T(8,128)} %reshape.100), calls=%async_computation.3 | async-start | bytes 1048576 | tf_op jit(solution)/shard_map/all_to_all | solution.py:197
  351.0 3.3 copy-start.4
  351.0 3.4 copy-start.6
  351.0 3.4 copy-start.8
  351.0 3.4 copy-start.10
  351.0 3.7 copy-start.12
  351.0 4.0 copy-start.14
  351.0 4.3 copy-start.16
  351.0 4.6 copy-start.18
  351.1 4.9 %copy-start.20 = (bf16[256,16,128]{2,1,0:T(8,128)(2,1)S(1)}, bf16[256,16,128]{2,1,0:T(8,128)(2,1)}, u32[]{:S(2)}) copy-start(bf16[256,16,128]{2,1,0:T(8,128)(2,1)} %get-tuple-element.43) | copy-start | bytes 3145732
  384.6 11.5 %all-to-all-start.5 = ((f32[2,512,128]{2,1,0:T(8,128)}), f32[2,512,128]{2,1,0:T(8,128)S(1)}, u32[]{:S(2)}, u32[]{:S(2)}) async-start(f32[2,512,128]{2,1,0:T(8,128)} %reshape.106), calls=%async_computation.5 | async-start | bytes 1048576 | tf_op jit(solution)/shard_map/all_to_all | solution.py:197
  462.0 3.3 copy-start.41
  464.8 1.6 copy-start.32
  464.9 1.6 copy-start.33
  464.9 1.6 copy-start.34
  464.9 1.6 copy-start.35
  464.9 1.6 copy-start.36
  464.9 1.6 copy-start.37
  464.9 1.6 copy-start.38
  464.9 1.6 copy-start.39
  464.9 1.6 copy-start.40
  466.6 2.4 copy-start.31

commit v16 on v14

--- a/solution.py
+++ b/solution.py
@@ -175,12 +175,9 @@
             ev = lax.all_to_all(ev, "pt", split_axis=0, concat_axis=0, tiled=False)
             return ev.reshape(n_pt, d_local, rows, kl, FIRST)
 
-        left_pts = to_points(left_factor, il)
-        left_shape = left_pts.shape
-        left_pts = jnp.broadcast_to(left_pts.reshape(1, -1, 128), (n_grp, left_pts.size // 128, 128))
-        left_pts = lax.all_to_all(left_pts, "grp", split_axis=0, concat_axis=0, tiled=False)
-        left_pts = left_pts.reshape((n_grp,) + left_shape)
-        left_pts = jnp.transpose(left_pts, (2, 5, 0, 3, 1, 4))
+        left_all = lax.all_gather(left_factor, "grp", axis=0, tiled=True)
+        left_pts = to_points(left_all, n_grp * il)
+        left_pts = jnp.transpose(left_pts, (1, 4, 2, 0, 3))
         left_pts = left_pts.reshape(d_local * FIRST, n_grp * il, n_pt * kl)
         jc = jl // n_chunks
         prods = []

time: 475 us -> 502 us (1.057)
  between operations: 1.27 us -> 14.7 us
  waiting for transfers between devices: 86.8 us -> 96.1 us
    all_to_all x3, waiting for transfers between devices: 68.9 us -> 95.3 us  [to_points(): ev = lax.all_to_all(ev, 'pt', split_axis=0, concat_axis=0, tiled=False)]
    all_to_all x1 -> x0, waiting for transfers between devices: 17.9 us -> none  [body(): lax.all_to_all(left_pts, 'grp', split_axis=0, concat_axis=0, tiled=False)]
    convert_element_type x13, other arithmetic: 33.4 us -> 40.2 us  [limbs_bf16(): piece.astype(jnp.bfloat16)]
    reshape x2 -> x3, local copies, waits for them, and re-layouts: 21.9 us -> 28.4 us  [to_points(): return ev.reshape(n_pt, d_local, rows, kl, FIRST)]
    all_to_all x3, starting transfers between devices: 33.4 us -> 38.5 us  [to_points(): ev = lax.all_to_all(ev, 'pt', split_axis=0, concat_axis=0, tiled=False)]
    unnamed x94 -> x96, local copies, waits for them, and re-layouts: 32 us -> 32.3 us
  transfers between devices with their start and end apart: 4 -> 4, of which waited for: 2 -> 2; matrix products, arithmetic and copies ran while one was open for 35% -> 33% of each run, Pallas kernels for 0% -> 0%
where the time goes in v16:
time: 502 us; the launch traced here: 496 us
  local copies, waits for them, and re-layouts  201 us (40%)
  waiting for transfers between devices  96.1 us (19%)
  other arithmetic  64.1 us (13%)
  blocking collectives  48.4 us (10%)
  starting transfers between devices  38.5 us (8%)
  matrix products  32.4 us (6%)
  between operations  14.7 us (3%)
    all_to_all x3, waiting for transfers between devices, to_points(): ev = lax.all_to_all(ev, 'pt', split_axis=0, concat_axis=0, tiled=False)  95.3 us
    convert_element_type x13, other arithmetic, limbs_bf16(): piece.astype(jnp.bfloat16)  40.2 us
    all_to_all x3, starting transfers between devices, to_points(): ev = lax.all_to_all(ev, 'pt', split_axis=0, concat_axis=0, tiled=False)  38.5 us
    transpose x2, local copies, waits for them, and re-layouts, body(): jnp.transpose(right_pts, (1, 4, 2, 0, 3))  35.8 us
    reshape x4, local copies, waits for them, and re-layouts, body(): jnp.transpose(right_pts, (1, 4, 2, 0, 3))  35.4 us
    unnamed x96, local copies, waits for them, and re-layouts  32.3 us
    all_to_all x1, blocking collectives, body(): prod = lax.all_to_all(prod, 'pt', split_axis=0, concat_axis=0, tiled=False)  31.5 us
    reshape x3, local copies, waits for them, and re-layouts, to_points(): return ev.reshape(n_pt, d_local, rows, kl, FIRST)  28.4 us
  transfers between devices with their start and end apart: 4, of which 2 were waited for; matrix products, arithmetic and copies ran while one was open for 33% of the time, Pallas kernels for 0%

profile of v16, /device:TPU:1, one launch (start us, length us, event | category | flops | bytes accessed | tf_op | source)
XLA Modules:
  0.0 495.7 jit_solution(3532830085279939335)
XLA Ops:
  7.3 2.5 slice_bitcast_fusion.1
  15.9 17.7 %subtract_convert_fusion.7 = (bf16[256,32,128]{2,1,0:T(8,128)(2,1)S(1)}, f32[256,32,128]{2,1,0:T(8,128)S(1)}, bf16[256,32,128]{2,1,0:T(8,128)(2,1)}, f32[256,32,128]{2,1,0:T(8,128)}) fusion(f32[32,128]{1,0:T(8,128)S(1)} %copy-done.31, f32[32,128]{1,0:T(8,128)S(1)} %copy-done.30, f32[32,128]{1,0:T(8,128)S(1)} %copy-done.29, f32[32,128]{1,0:T(8,128)S(1)} %copy-done.28, ...), kind=kLoop, calls=%fused_computation.48 | loop fusion | flops 125829120 | bytes 37896192 | tf_op jit(solution)/shard_map/convert_element_type | solution.py:105
  33.7 3.1 subtract_convert_fusion.6
  39.6 4.2 subtract_convert_fusion.17
  47.1 2.4 fusion.28
  49.5 7.8 %all-to-all-start = ((f32[16,8,4096]{2,1,0:T(8,128)}), f32[16,8,4096]{2,1,0:T(8,128)}, u32[]{:S(2)}, u32[]{:S(2)}) async-start(f32[16,8,4096]{2,1,0:T(8,128)} %fusion.28), calls=%async_computation | async-start | bytes 4194304 | tf_op jit(solution)/shard_map/all_to_all | solution.py:175
  57.3 3.4 subtract_convert_fusion.2
  61.4 3.9 pad_maximum_fusion
  65.3 3.5 fusion.71
  68.8 3.5 fusion.12
  72.3 26.4 %all-to-all-done = f32[16,8,4096]{2,1,0:T(8,128)} async-done(((f32[16,8,4096]{2,1,0:T(8,128)}), f32[16,8,4096]{2,1,0:T(8,128)}, u32[]{:S(2)}, u32[]{:S(2)}) %all-to-all-start) | async-done | bytes 2097184 | tf_op jit(solution)/shard_map/all_to_all | solution.py:175
  98.7 10.9 %all-to-all-start.1 = ((f32[16,8,8192]{2,1,0:T(8,128)}), f32[16,8,8192]{2,1,0:T(8,128)}, u32[]{:S(2)}, u32[]{:S(2)}) async-start(f32[16,8,8192]{2,1,0:T(8,128)} %fusion.12), calls=%async_computation.1 | async-start | bytes 8388608 | tf_op jit(solution)/shard_map/all_to_all | solution.py:175
  109.6 5.6 %fusion.72 = f32[384,8192]{1,0:T(8,128)S(1)} fusion(bf16[384,384]{1,0:T(8,128)(2,1)S(1)} %copy-done.3, bf16[8192,384]{1,0:T(8,128)(2,1)} %bitcast.113), kind=kOutput, calls=%fused_computation.152 | convolution fusion | flops 2415919104 | bytes 19169280 | tf_op jit(solution)/shard_map/dot_general | solution.py:118
  115.1 3.6 fusion.13
  118.7 68.9 %all-to-all-done.1 = f32[16,8,8192]{2,1,0:T(8,128)} async-done(((f32[16,8,8192]{2,1,0:T(8,128)}), f32[16,8,8192]{2,1,0:T(8,128)}, u32[]{:S(2)}, u32[]{:S(2)}) %all-to-all-start.1) | async-done | bytes 4194336 | tf_op jit(solution)/shard_map/all_to_all | solution.py:175
  187.7 19.9 %all-to-all-start.2 = ((f32[16,8,8192]{2,1,0:T(8,128)}), f32[16,8,8192]{2,1,0:T(8,128)}, u32[]{:S(2)}, u32[]{:S(2)}) async-start(f32[16,8,8192]{2,1,0:T(8,128)} %fusion.13), calls=%async_computation.2 | async-start | bytes 8388608 | tf_op jit(solution)/shard_map/all_to_all | solution.py:175
  207.6 6.5 %reshape.82 = f32[16,8,16,8,32]{4,3,2,1,0:T(8,128)} reshape(f32[16,8,4096]{2,1,0:T(8,128)} %all-to-all-done) | data formatting | bytes 4194304 | tf_op jit(solution)/shard_map/reshape | solution.py:176
  214.0 11.5 %copy.76 = f32[8,32,16,16,8]{1,0,4,3,2:T(8,128)} copy(f32[8,32,16,16,8]{1,4,2,0,3:T(8,128)} %bitcast.110) | data formatting | bytes 4194304 | tf_op jit(solution)/shard_map/transpose | solution.py:180
  225.6 5.8 %reshape.83 = f32[256,16,128]{0,2,1:T(8,128)S(1)} reshape(f32[8,32,16,16,8]{1,0,4,3,2:T(8,128)} %copy.76) | data formatting | bytes 4194304 | tf_op jit(solution)/shard_map/reshape | solution.py:181
  233.4 7.1 %subtract_convert_fusion.15 = (bf16[256,16,128]{2,1,0:T(8,128)(2,1)}, bf16[256,16,128]{2,1,0:T(8,128)(2,1)}, bf16[256,16,128]{2,1,0:T(8,128)(2,1)}, bf16[256,16,...) fusion(f32[256,16,128]{2,1,0:T(8,128)} %copy.78), kind=kLoop, calls=%fused_computation.96 | loop fusion | flops 33554432 | bytes 11534336 | tf_op jit(solution)/shard_map/convert_element_type | solution.py:156
  241.2 11.2 %reshape.86 = f32[16,8,32,8,32]{4,3,2,1,0:T(8,128)} reshape(f32[16,8,8192]{2,1,0:T(8,128)} %all-to-all-done.1) | data formatting | bytes 8388608 | tf_op jit(solution)/shard_map/reshape | solution.py:176
  252.4 17.9 %copy.83 = f32[8,32,32,16,8]{1,0,4,3,2:T(8,128)} copy(f32[8,32,32,16,8]{1,4,2,0,3:T(8,128)} %bitcast.108) | data formatting | bytes 8388608 | tf_op jit(solution)/shard_map/transpose | solution.py:186
  270.3 12.2 %reshape.87 = f32[256,32,128]{0,2,1:T(8,128)} reshape(f32[8,32,32,16,8]{1,0,4,3,2:T(8,128)} %copy.83) | data formatting | bytes 8388608 | tf_op jit(solution)/shard_map/reshape | solution.py:186
  282.5 5.5 %copy.85 = f32[256,32,128]{2,1,0:T(8,128)} copy(f32[256,32,128]{0,2,1:T(8,128)} %reshape.87) | data formatting | bytes 8388608 | tf_op jit(solution)/shard_map/reshape | solution.py:186
  288.0 3.3 subtract_convert_fusion.5
  292.4 7.6 %fusion = f32[256,48,32]{1,2,0:T(8,128)S(1)} fusion(bf16[256,32,128]{2,1,0:T(8,128)(2,1)S(1)} %get-tuple-element.20, bf16[256,32,128]{2,1,0:T(8,128)(2,1)S(1)} %get-tuple-element.19, bf16[256,32,128]{2,1,0:T(8,128)(2,1)S(1)} %get-tuple-element.18, bf16[256,16,128]{2,1,0:T(8,128)(2,1)S(1)} %copy-done.16, bf16[256,16,128]{2,1,0:T(8,128)(2,1)S(1)} %get-tuple-element.45, ...), kind=kOutput, calls=%fused_computation.8 | convolution fusion | flops 405798912 | bytes 17301504 | tf_op jit(solution)/shard_map/pak,pjk->paj/dot_general | solution.py:159
  300.0 6.8 %fusion.68 = (f32[256,16,32]{1,2,0:T(8,128)}, f32[256,16,32]{1,2,0:T(8,128)}, f32[256,16,32]{1,2,0:T(8,128)}) fusion(f32[256,48,32]{1,2,0:T(8,128)S(1)} %fusion), kind=kLoop, calls=%fused_computation.148 | loop fusion | bytes 3145728 | tf_op jit(solution)/shard_map/slice | solution.py:161
  306.8 3.8 copy.103
  310.6 3.8 copy.104
  314.4 3.8 copy.105
  318.2 10.8 %reshape.90 = f32[16,8,32,8,32]{4,3,2,1,0:T(8,128)} reshape(f32[16,8,8192]{2,1,0:T(8,128)} %all-to-all-done.2) | data formatting | bytes 8388608 | tf_op jit(solution)/shard_map/reshape | solution.py:176
  329.0 17.9 %copy.89 = f32[8,32,32,16,8]{1,0,4,3,2:T(8,128)} copy(f32[8,32,32,16,8]{1,4,2,0,3:T(8,128)} %bitcast.109) | data formatting | bytes 8388608 | tf_op jit(solution)/shard_map/transpose | solution.py:186
  346.9 12.2 %reshape.91 = f32[256,32,128]{0,2,1:T(8,128)} reshape(f32[8,32,32,16,8]{1,0,4,3,2:T(8,128)} %copy.89) | data formatting | bytes 8388608 | tf_op jit(solution)/shard_map/reshape | solution.py:186
  359.1 5.5 %copy.91 = f32[256,32,128]{2,1,0:T(8,128)} copy(f32[256,32,128]{0,2,1:T(8,128)} %reshape.91) | data formatting | bytes 8388608 | tf_op jit(solution)/shard_map/reshape | solution.py:186
  364.6 3.3 subtract_convert_fusion.1
  369.6 7.7 %fusion.6 = f32[256,48,32]{1,2,0:T(8,128)S(1)} fusion(bf16[256,32,128]{2,1,0:T(8,128)(2,1)S(1)} %get-tuple-element.30, bf16[256,32,128]{2,1,0:T(8,128)(2,1)S(1)} %get-tuple-element.29, bf16[256,32,128]{2,1,0:T(8,128)(2,1)S(1)} %get-tuple-element.28, bf16[256,16,128]{2,1,0:T(8,128)(2,1)S(1)} %copy-done.17, bf16[256,16,128]{2,1,0:T(8,128)(2,1)S(1)} %copy-done.7, ...), kind=kOutput, calls=%fused_computation.15 | convolution fusion | flops 405798912 | bytes 17301504 | tf_op jit(solution)/shard_map/pak,pjk->paj/dot_general | solution.py:159
  377.2 6.8 %fusion.69 = (f32[256,16,32]{1,2,0:T(8,128)}, f32[256,16,32]{1,2,0:T(8,128)}, f32[256,16,32]{1,2,0:T(8,128)}) fusion(f32[256,48,32]{1,2,0:T(8,128)S(1)} %fusion.6), kind=kLoop, calls=%fused_computation.149 | loop fusion | bytes 3145728 | tf_op jit(solution)/shard_map/slice | solution.py:161
  384.0 3.8 copy.106
  387.8 3.8 copy.107
  391.6 4.7 copy.108
  399.2 17.0 %all_to_all.25 = f32[2,1024,128]{2,1,0:T(8,128)} all-to-all(f32[2,1024,128]{2,1,0:T(8,128)S(1)} %reshape.93), channel_id=1, replica_groups=mesh['grp'=2,'pt'=16] {'grp'}, dimensions={0} | all-to-all | bytes 2097152 | tf_op jit(solution)/shard_map/all_to_all | solution.py:195
  417.8 2.9 copy.96
  420.6 9.2 %copy.97 = f32[16,8,32,8,8]{0,4,3,2,1:T(8,128)} copy(f32[16,8,32,8,8]{2,4,0,3,1:T(8,128)} %bitcast.116) | data formatting | bytes 2097152 | tf_op jit(solution)/shard_map/transpose | solution.py:198
  429.8 5.2 %copy.98 = f32[16,128,128]{2,1,0:T(8,128)S(1)} copy(f32[16,128,128]{0,2,1:T(8,128)} %bitcast.111) | data formatting | bytes 2097152 | tf_op jit(solution)/shard_map/reshape | solution.py:199
  435.1 31.5 %all_to_all.26 = f32[16,128,128]{2,1,0:T(8,128)S(1)} all-to-all(f32[16,128,128]{2,1,0:T(8,128)S(1)} %copy.98), channel_id=1, replica_groups=mesh['grp'=2,'pt'=16] {'pt'}, dimensions={0} | all-to-all | bytes 2097152 | tf_op jit(solution)/shard_map/all_to_all | solution.py:200
  466.5 4.7 copy.99
  471.2 7.9 %copy.100 = f32[8,8,32,16,8]{2,4,3,1,0:T(8,128)} copy(f32[8,8,32,16,8]{3,1,0,2,4:T(8,128)} %bitcast.112) | data formatting | bytes 2097152 | tf_op jit(solution)/shard_map/transpose | solution.py:202
  479.1 2.8 copy.102
  (117 shorter events, 29.5 us)
Async XLA Ops:
  6.5 30.2 %all-gather.2.cloned.1.call-start = ((), (), s32[]{:S(2)}) async-start(), calls=%async_computation.5 | async-start | bytes 1572864 | tf_op jit(solution)/shard_map/all_gather | solution.py:178
  10.9 1.2 copy-start.22
  13.9 1.9 copy-start.23
  13.9 1.9 copy-start.24
  13.9 1.9 copy-start.25
  13.9 1.9 copy-start.26
  13.9 1.9 copy-start.27
  14.0 1.9 copy-start.28
  14.0 1.9 copy-start.29
  14.0 1.9 copy-start.30
  14.0 1.9 copy-start.31
  44.3 1.0 copy-start.3
  49.5 49.2 %all-to-all-start = ((f32[16,8,4096]{2,1,0:T(8,128)}), f32[16,8,4096]{2,1,0:T(8,128)}, u32[]{:S(2)}, u32[]{:S(2)}) async-start(f32[16,8,4096]{2,1,0:T(8,128)} %fusion.28), calls=%async_computation | async-start | bytes 4194304 | tf_op jit(solution)/shard_map/all_to_all | solution.py:175
  57.3 3.5 copy-start
  57.3 3.5 copy-start.1
  57.3 4.1 copy-start.2
  98.7 88.9 %all-to-all-start.1 = ((f32[16,8,8192]{2,1,0:T(8,128)}), f32[16,8,8192]{2,1,0:T(8,128)}, u32[]{:S(2)}, u32[]{:S(2)}) async-start(f32[16,8,8192]{2,1,0:T(8,128)} %fusion.12), calls=%async_computation.1 | async-start | bytes 8388608 | tf_op jit(solution)/shard_map/all_to_all | solution.py:175
  187.7 130.5 %all-to-all-start.2 = ((f32[16,8,8192]{2,1,0:T(8,128)}), f32[16,8,8192]{2,1,0:T(8,128)}, u32[]{:S(2)}, u32[]{:S(2)}) async-start(f32[16,8,8192]{2,1,0:T(8,128)} %fusion.13), calls=%async_computation.2 | async-start | bytes 8388608 | tf_op jit(solution)/shard_map/all_to_all | solution.py:175
  241.2 50.1 %copy-start.4 = (bf16[256,16,128]{2,1,0:T(8,128)(2,1)}, bf16[256,16,128]{2,1,0:T(8,128)(2,1)S(1)}, u32[]{:S(2)}) copy-start(bf16[256,16,128]{2,1,0:T(8,128)(2,1)S(1)} %get-tuple-element.44) | copy-start | bytes 3145732
  241.2 50.1 %copy-start.6 = (bf16[256,16,128]{2,1,0:T(8,128)(2,1)}, bf16[256,16,128]{2,1,0:T(8,128)(2,1)S(1)}, u32[]{:S(2)}) copy-start(bf16[256,16,128]{2,1,0:T(8,128)(2,1)S(1)} %get-tuple-element.45) | copy-start | bytes 3145732
  288.0 3.3 copy-start.8
  288.0 3.4 copy-start.10
  288.0 3.4 copy-start.12
  288.0 3.4 copy-start.14
  288.0 3.7 copy-start.16
  288.0 4.0 copy-start.18
  288.0 4.3 copy-start.20
  364.6 3.3 copy-start.5
  364.6 3.4 copy-start.7
  364.6 3.4 copy-start.9
  364.6 3.4 copy-start.11
  364.6 3.7 copy-start.13
  364.6 4.0 copy-start.15
  364.6 4.3 copy-start.17
  364.6 4.6 copy-start.19
  364.6 4.9 copy-start.21
  479.1 3.3 copy-start.42
  481.9 1.6 copy-start.33
  481.9 1.6 copy-start.34
  481.9 1.6 copy-start.35
  482.0 1.6 copy-start.36
  482.0 1.6 copy-start.37
  482.0 1.6 copy-start.38
  482.0 1.6 copy-start.39
  482.0 1.6 copy-start.40
  482.0 1.6 copy-start.41
  483.6 2.4 copy-start.32
Sparse Core Ops, SparseCore 0:
  8.9 23.3 all-gather.1

commit v17 on v14

--- a/solution.py
+++ b/solution.py
@@ -175,17 +175,22 @@
             ev = lax.all_to_all(ev, "pt", split_axis=0, concat_axis=0, tiled=False)
             return ev.reshape(n_pt, d_local, rows, kl, FIRST)
 
-        left_pts = to_points(left_factor, il)
+        jc = jl // n_chunks
+        both = to_points(jnp.concatenate([left_factor, right_factor[0:jc]], axis=0), il + jc)
+        left_pts = both[:, :, :il]
+        first_right = both[:, :, il:]
         left_shape = left_pts.shape
         left_pts = jnp.broadcast_to(left_pts.reshape(1, -1, 128), (n_grp, left_pts.size // 128, 128))
         left_pts = lax.all_to_all(left_pts, "grp", split_axis=0, concat_axis=0, tiled=False)
         left_pts = left_pts.reshape((n_grp,) + left_shape)
         left_pts = jnp.transpose(left_pts, (2, 5, 0, 3, 1, 4))
         left_pts = left_pts.reshape(d_local * FIRST, n_grp * il, n_pt * kl)
-        jc = jl // n_chunks
         prods = []
         for chunk in range(n_chunks):
-            right_pts = to_points(right_factor[chunk * jc : (chunk + 1) * jc], jc)
+            if chunk == 0:
+                right_pts = first_right
+            else:
+                right_pts = to_points(right_factor[chunk * jc : (chunk + 1) * jc], jc)
             right_pts = jnp.transpose(right_pts, (1, 4, 2, 0, 3)).reshape(d_local * FIRST, jc, n_pt * kl)
             prods.append(multiply_points(left_pts, right_pts))
         prod = jnp.concatenate(prods, axis=2) if n_chunks > 1 else prods[0]

time: 475 us -> 499 us (1.051)
  blocking collectives: 48.4 us -> 66.2 us
  local copies, waits for them, and re-layouts: 201 us -> 212 us
  starting transfers between devices: 37.6 us -> 31.8 us
  waiting for transfers between devices: 86.8 us -> 92.5 us
    all_to_all x3 -> x2, waiting for transfers between devices: 68.9 us -> 92.5 us  [to_points(): ev = lax.all_to_all(ev, 'pt', split_axis=0, concat_axis=0, tiled=False)]
    all_to_all x1, waiting for transfers between devices: 17.9 us -> 0.01 us  [body(): lax.all_to_all(left_pts, 'grp', split_axis=0, concat_axis=0, tiled=False)]
    all_to_all x1, blocking collectives: 31.6 us -> 49.1 us  [body(): prod = lax.all_to_all(prod, 'pt', split_axis=0, concat_axis=0, tiled=False)]
    slice x0 -> x2, local copies, waits for them, and re-layouts: none -> 7.29 us  [the longest x1 4.79 us: body(): left_pts = both[:, :, :il]]
    all_to_all x3 -> x2, starting transfers between devices: 33.4 us -> 27.9 us  [to_points(): ev = lax.all_to_all(ev, 'pt', split_axis=0, concat_axis=0, tiled=False)]
    reshape x3 -> x2, other arithmetic: 12.2 us -> 7.84 us  [to_points(): ev = ev.reshape(n_pt, d_local, rows * kl * FIRST)]
    dot_general x3 -> x2, matrix products: 12.9 us -> 10.1 us  [forward(): lax.dot_general(jnp.asarray(tables['fwd2'].T, jnp.bfloat16), zl, (((1,),...]
    convert_element_type x13 -> x11, other arithmetic: 33.4 us -> 35.3 us  [limbs_bf16(): piece.astype(jnp.bfloat16)]
  transfers between devices with their start and end apart: 4 -> 3, of which waited for: 2 -> 2; matrix products, arithmetic and copies ran while one was open for 35% -> 25% of each run, Pallas kernels for 0% -> 0%
where the time goes in v17:
time: 499 us; the launch traced here: 491 us
  local copies, waits for them, and re-layouts  212 us (42%)
  waiting for transfers between devices  92.5 us (19%)
  blocking collectives  66.2 us (13%)
  other arithmetic  55.6 us (11%)
  matrix products  31.8 us (6%)
  starting transfers between devices  31.8 us (6%)
    all_to_all x2, waiting for transfers between devices, to_points(): ev = lax.all_to_all(ev, 'pt', split_axis=0, concat_axis=0, tiled=False)  92.5 us
    all_to_all x1, blocking collectives, body(): prod = lax.all_to_all(prod, 'pt', split_axis=0, concat_axis=0, tiled=False)  49.1 us
    transpose x3, local copies, waits for them, and re-layouts, body(): jnp.transpose(right_pts, (1, 4, 2, 0, 3))  35.9 us
    reshape x4, local copies, waits for them, and re-layouts, body(): jnp.transpose(right_pts, (1, 4, 2, 0, 3))  35.4 us
    convert_element_type x11, other arithmetic, limbs_bf16(): piece.astype(jnp.bfloat16)  35.3 us
    unnamed x86, local copies, waits for them, and re-layouts  31.1 us
    all_to_all x2, starting transfers between devices, to_points(): ev = lax.all_to_all(ev, 'pt', split_axis=0, concat_axis=0, tiled=False)  27.9 us
    reshape x2, local copies, waits for them, and re-layouts, to_points(): return ev.reshape(n_pt, d_local, rows, kl, FIRST)  23.1 us
  transfers between devices with their start and end apart: 3, of which 2 were waited for; matrix products, arithmetic and copies ran while one was open for 25% of the time, Pallas kernels for 0%

profile of v17, /device:TPU:1, one launch (start us, length us, event | category | flops | bytes accessed | tf_op | source)
XLA Modules:
  0.0 490.5 jit_solution(12200609818027029536)
XLA Ops:
  0.0 2.5 fusion.59
  5.7 8.4 %subtract_convert_fusion.5 = (bf16[256,32,128]{2,1,0:T(8,128)(2,1)S(1)}, f32[256,32,128]{2,1,0:T(8,128)S(1)}) fusion(f32[32,128]{1,0:T(8,128)S(1)} %copy-done.18, f32[32,128]{1,0:T(8,128)S(1)} %copy-done.19, f32[32,128]{1,0:T(8,128)S(1)} %copy-done.20, f32[32,128]{1,0:T(8,128)S(1)} %copy-done.21, f32[32,128]{1,0:T(8,128)S(1)} %copy-done.22, ...), kind=kLoop, calls=%fused_computation.41 | loop fusion | flops 62914560 | bytes 19021824 | tf_op jit(solution)/shard_map/convert_element_type | solution.py:105
  16.2 3.5 fusion.61
  19.7 3.6 fusion.14
  23.2 7.9 %all-to-all-start.2 = ((f32[16,8,8192]{2,1,0:T(8,128)}), f32[16,8,8192]{2,1,0:T(8,128)}, u32[]{:S(2)}, u32[]{:S(2)}) async-start(f32[16,8,8192]{2,1,0:T(8,128)} %fusion.14), calls=%async_computation.2 | async-start | bytes 8388608 | tf_op jit(solution)/shard_map/all_to_all | solution.py:175
  35.3 10.4 %subtract_convert_fusion.1 = (bf16[320,32,128]{2,1,0:T(8,128)(2,1)S(1)}, f32[320,32,128]{2,1,0:T(8,128)S(1)}) fusion(f32[32,128]{1,0:T(8,128)S(1)} %copy-done.18, f32[32,128]{1,0:T(8,128)S(1)} %copy-done.19, f32[32,128]{1,0:T(8,128)S(1)} %copy-done.20, f32[32,128]{1,0:T(8,128)S(1)} %copy-done.21, f32[32,128]{1,0:T(8,128)S(1)} %copy-done.22, ...), kind=kLoop, calls=%fused_computation.29 | loop fusion | flops 78643200 | bytes 23740416 | tf_op jit(solution)/shard_map/convert_element_type | solution.py:105
  47.1 3.8 pad_maximum_fusion
  50.9 6.6 %fusion.60 = f32[384,10240]{1,0:T(8,128)S(1)} fusion(bf16[384,384]{1,0:T(8,128)(2,1)S(1)} %copy-done.7, bf16[10240,384]{1,0:T(8,128)(2,1)} %bitcast.92), kind=kOutput, calls=%fused_computation.128 | convolution fusion | flops 3019898880 | bytes 23887872 | tf_op jit(solution)/shard_map/dot_general | solution.py:118
  57.6 4.3 fusion.12
  61.8 47.2 %all-to-all-done.2 = f32[16,8,8192]{2,1,0:T(8,128)} async-done(((f32[16,8,8192]{2,1,0:T(8,128)}), f32[16,8,8192]{2,1,0:T(8,128)}, u32[]{:S(2)}, u32[]{:S(2)}) %all-to-all-start.2) | async-done | bytes 4194336 | tf_op jit(solution)/shard_map/all_to_all | solution.py:175
  109.1 19.9 %all-to-all-start = ((f32[16,8,10240]{2,1,0:T(8,128)}), f32[16,8,10240]{2,1,0:T(8,128)}, u32[]{:S(2)}, u32[]{:S(2)}) async-start(f32[16,8,10240]{2,1,0:T(8,128)} %fusion.12), calls=%async_computation | async-start | bytes 10485760 | tf_op jit(solution)/shard_map/all_to_all | solution.py:175
  129.0 10.8 %reshape.84 = f32[16,8,32,8,32]{4,3,2,1,0:T(8,128)} reshape(f32[16,8,8192]{2,1,0:T(8,128)} %all-to-all-done.2) | data formatting | bytes 8388608 | tf_op jit(solution)/shard_map/reshape | solution.py:176
  139.8 17.7 %copy.68 = f32[8,32,32,16,8]{1,0,4,3,2:T(8,128)} copy(f32[8,32,32,16,8]{1,4,2,0,3:T(8,128)} %bitcast.88) | data formatting | bytes 8388608 | tf_op jit(solution)/shard_map/transpose | solution.py:194
  157.5 12.2 %reshape.85 = f32[256,32,128]{0,2,1:T(8,128)} reshape(f32[8,32,32,16,8]{1,0,4,3,2:T(8,128)} %copy.68) | data formatting | bytes 8388608 | tf_op jit(solution)/shard_map/reshape | solution.py:194
  169.7 5.5 %copy.70 = f32[256,32,128]{2,1,0:T(8,128)} copy(f32[256,32,128]{0,2,1:T(8,128)} %reshape.85) | data formatting | bytes 8388608 | tf_op jit(solution)/shard_map/reshape | solution.py:194
  175.2 4.8 subtract_convert_fusion.3
  180.0 45.3 %all-to-all-done = f32[16,8,10240]{2,1,0:T(8,128)} async-done(((f32[16,8,10240]{2,1,0:T(8,128)}), f32[16,8,10240]{2,1,0:T(8,128)}, u32[]{:S(2)}, u32[]{:S(2)}) %all-to-all-start) | async-done | bytes 5242912 | tf_op jit(solution)/shard_map/all_to_all | solution.py:175
  225.2 12.4 %reshape.78 = f32[16,8,40,8,32]{4,3,2,1,0:T(8,128)} reshape(f32[16,8,10240]{2,1,0:T(8,128)} %all-to-all-done) | data formatting | bytes 10485760 | tf_op jit(solution)/shard_map/reshape | solution.py:176
  237.6 4.8 slice.199
  242.4 3.3 broadcast_in_dim.7
  247.2 3.9 all-to-all-start.1
  251.1 6.6 %slice_bitcast_fusion = f32[8,32,32,16,8]{1,4,2,0,3:T(8,128)S(1)} fusion(f32[16,8,40,8,32]{4,3,2,1,0:T(8,128)} %reshape.78), kind=kLoop, calls=%fused_computation | loop fusion | bytes 8388608 | tf_op jit(solution)/shard_map/transpose | solution.py:194
  257.7 11.6 %copy.62 = f32[8,32,32,16,8]{1,0,4,3,2:T(8,128)} copy(f32[8,32,32,16,8]{1,4,2,0,3:T(8,128)S(1)} %slice_bitcast_fusion) | data formatting | bytes 8388608 | tf_op jit(solution)/shard_map/transpose | solution.py:194
  269.3 12.2 %reshape.81 = f32[256,32,128]{0,2,1:T(8,128)} reshape(f32[8,32,32,16,8]{1,0,4,3,2:T(8,128)} %copy.62) | data formatting | bytes 8388608 | tf_op jit(solution)/shard_map/reshape | solution.py:194
  281.5 5.5 %copy.64 = f32[256,32,128]{2,1,0:T(8,128)} copy(f32[256,32,128]{0,2,1:T(8,128)} %reshape.81) | data formatting | bytes 8388608 | tf_op jit(solution)/shard_map/reshape | solution.py:194
  287.0 4.8 subtract_convert_fusion.7
  291.8 4.3 reshape.79
  296.2 11.5 %copy.55 = f32[8,32,2,8,16,8]{1,0,5,4,3,2:T(8,128)} copy(f32[8,32,2,8,16,8]{1,5,3,0,4,2:T(8,128)} %bitcast.89) | data formatting | bytes 4194304 | tf_op jit(solution)/shard_map/transpose | solution.py:186
  307.7 5.8 %reshape.80 = f32[256,16,128]{0,2,1:T(8,128)S(1)} reshape(f32[8,32,2,8,16,8]{1,0,5,4,3,2:T(8,128)} %copy.55) | data formatting | bytes 4194304 | tf_op jit(solution)/shard_map/reshape | solution.py:187
  315.8 5.6 %subtract_convert_fusion.15 = (bf16[256,16,128]{2,1,0:T(8,128)(2,1)S(1)}, bf16[256,16,128]{2,1,0:T(8,128)(2,1)S(1)}, bf16[256,16,128]{2,1,0:T(8,128)(2,1)S(1)}, ...) fusion(f32[256,16,128]{2,1,0:T(8,128)} %copy.57), kind=kLoop, calls=%fused_computation.91 | loop fusion | flops 33554432 | bytes 11534336 | tf_op jit(solution)/shard_map/convert_element_type | solution.py:156
  326.8 7.7 %fusion = f32[256,48,32]{1,2,0:T(8,128)S(1)} fusion(bf16[256,32,128]{2,1,0:T(8,128)(2,1)S(1)} %copy-done.3, bf16[256,32,128]{2,1,0:T(8,128)(2,1)S(1)} %copy-done.2, bf16[256,32,128]{2,1,0:T(8,128)(2,1)S(1)} %copy-done.1, bf16[256,16,128]{2,1,0:T(8,128)(2,1)S(1)} %get-tuple-element.38, bf16[256,16,128]{2,1,0:T(8,128)(2,1)S(1)} %get-tuple-element.43, ...), kind=kOutput, calls=%fused_computation.10 | convolution fusion | flops 405798912 | bytes 17301504 | tf_op jit(solution)/shard_map/pak,pjk->paj/dot_general | solution.py:159
  334.4 6.8 %fusion.57 = (f32[256,16,32]{1,2,0:T(8,128)}, f32[256,16,32]{1,2,0:T(8,128)}, f32[256,16,32]{1,2,0:T(8,128)}) fusion(f32[256,48,32]{1,2,0:T(8,128)S(1)} %fusion), kind=kLoop, calls=%fused_computation.125 | loop fusion | bytes 3145728 | tf_op jit(solution)/shard_map/slice | solution.py:161
  341.2 4.5 copy.84
  345.7 4.7 copy.83
  350.3 4.5 copy.82
  354.8 8.0 %fusion.6 = f32[256,48,32]{1,2,0:T(8,128)S(1)} fusion(bf16[256,32,128]{2,1,0:T(8,128)(2,1)} %get-tuple-element.28, bf16[256,32,128]{2,1,0:T(8,128)(2,1)} %get-tuple-element.27, bf16[256,32,128]{2,1,0:T(8,128)(2,1)S(1)} %copy-done, bf16[256,16,128]{2,1,0:T(8,128)(2,1)} %copy-done.14, bf16[256,16,128]{2,1,0:T(8,128)(2,1)} %copy-done.9, ...), kind=kOutput, calls=%fused_computation.17 | convolution fusion | flops 405798912 | bytes 17301504 | tf_op jit(solution)/shard_map/pak,pjk->paj/dot_general | solution.py:159
  362.9 6.8 %fusion.58 = (f32[256,16,32]{1,2,0:T(8,128)}, f32[256,16,32]{1,2,0:T(8,128)}, f32[256,16,32]{1,2,0:T(8,128)}) fusion(f32[256,48,32]{1,2,0:T(8,128)S(1)} %fusion.6), kind=kLoop, calls=%fused_computation.126 | loop fusion | bytes 3145728 | tf_op jit(solution)/shard_map/slice | solution.py:161
  369.7 3.8 copy.87
  373.5 4.2 copy.86
  377.8 3.8 copy.85
  383.4 17.2 %all_to_all.25 = f32[2,1024,128]{2,1,0:T(8,128)} all-to-all(f32[2,1024,128]{2,1,0:T(8,128)S(1)} %reshape.87), channel_id=1, replica_groups=mesh['grp'=2,'pt'=16] {'grp'}, dimensions={0} | all-to-all | bytes 2097152 | tf_op jit(solution)/shard_map/all_to_all | solution.py:203
  402.1 2.9 copy.75
  405.0 9.2 %copy.76 = f32[16,8,32,8,8]{0,4,3,2,1:T(8,128)} copy(f32[16,8,32,8,8]{2,4,0,3,1:T(8,128)} %bitcast.95) | data formatting | bytes 2097152 | tf_op jit(solution)/shard_map/transpose | solution.py:206
  414.2 5.2 %copy.77 = f32[16,128,128]{2,1,0:T(8,128)S(1)} copy(f32[16,128,128]{0,2,1:T(8,128)} %bitcast.90) | data formatting | bytes 2097152 | tf_op jit(solution)/shard_map/reshape | solution.py:207
  419.4 49.1 %all_to_all.26 = f32[16,128,128]{2,1,0:T(8,128)S(1)} all-to-all(f32[16,128,128]{2,1,0:T(8,128)S(1)} %copy.77), channel_id=1, replica_groups=mesh['grp'=2,'pt'=16] {'pt'}, dimensions={0} | all-to-all | bytes 2097152 | tf_op jit(solution)/shard_map/all_to_all | solution.py:208
  468.5 4.7 copy.78
  473.1 7.9 %copy.79 = f32[8,8,32,16,8]{2,4,3,1,0:T(8,128)} copy(f32[8,8,32,16,8]{3,1,0,2,4:T(8,128)} %bitcast.91) | data formatting | bytes 2097152 | tf_op jit(solution)/shard_map/transpose | solution.py:210
  481.0 2.8 copy.81
  (104 shorter events, 29.2 us)
Async XLA Ops:
  2.5 1.2 copy-start.27
  3.7 1.9 copy-start.18
  3.7 1.9 copy-start.19
  3.7 1.9 copy-start.20
  3.7 1.9 copy-start.21
  3.7 1.9 copy-start.22
  3.7 1.9 copy-start.23
  3.7 1.9 copy-start.24
  3.8 1.9 copy-start.25
  3.8 1.9 copy-start.26
  15.2 1.0 copy-start.7
  23.2 7.9 %copy-start.17 = (f32[8,8,2048]{2,1,0:T(8,128)S(1)}, f32[8,8,2048]{2,1,0:T(8,128)}, u32[]{:S(2)}) copy-start(f32[8,8,2048]{2,1,0:T(8,128)} %param.10) | copy-start | bytes 1572868
  23.2 85.8 %all-to-all-start.2 = ((f32[16,8,8192]{2,1,0:T(8,128)}), f32[16,8,8192]{2,1,0:T(8,128)}, u32[]{:S(2)}, u32[]{:S(2)}) async-start(f32[16,8,8192]{2,1,0:T(8,128)} %fusion.14), calls=%async_computation.2 | async-start | bytes 8388608 | tf_op jit(solution)/shard_map/all_to_all | solution.py:175
  109.1 116.1 %all-to-all-start = ((f32[16,8,10240]{2,1,0:T(8,128)}), f32[16,8,10240]{2,1,0:T(8,128)}, u32[]{:S(2)}, u32[]{:S(2)}) async-start(f32[16,8,10240]{2,1,0:T(8,128)} %fusion.12), calls=%async_computation | async-start | bytes 10485760 | tf_op jit(solution)/shard_map/all_to_all | solution.py:175
  247.2 44.6 %all-to-all-start.1 = ((f32[2,2048,128]{2,1,0:T(8,128)}), f32[2,2048,128]{2,1,0:T(8,128)S(1)}, u32[]{:S(2)}, u32[]{:S(2)}) async-start(f32[2,2048,128]{2,1,0:T(8,128)} %broadcast_in_dim.8), calls=%async_computation.1 | async-start | bytes 4194304 | tf_op jit(solution)/shard_map/all_to_all | solution.py:184
  315.8 10.2 %copy-start.3 = (bf16[256,32,128]{2,1,0:T(8,128)(2,1)S(1)}, bf16[256,32,128]{2,1,0:T(8,128)(2,1)}, u32[]{:S(2)}) copy-start(bf16[256,32,128]{2,1,0:T(8,128)(2,1)} %get-tuple-element.20) | copy-start | bytes 6291460
  321.4 1.0 copy-start.10
  321.4 1.4 copy-start.11
  321.4 1.7 copy-start.12
  321.5 2.1 copy-start.13
  321.5 2.6 copy-start.14
  321.5 3.1 copy-start.15
  321.5 3.5 copy-start.16
  321.5 4.5 copy-start.1
  321.5 5.3 %copy-start.2 = (bf16[256,32,128]{2,1,0:T(8,128)(2,1)S(1)}, bf16[256,32,128]{2,1,0:T(8,128)(2,1)}, u32[]{:S(2)}) copy-start(bf16[256,32,128]{2,1,0:T(8,128)(2,1)} %get-tuple-element.19) | copy-start | bytes 6291460
  322.2 3.3 copy-start.8
  322.3 3.7 copy-start.9
  345.7 9.2 %copy-start = (bf16[256,32,128]{2,1,0:T(8,128)(2,1)S(1)}, bf16[256,32,128]{2,1,0:T(8,128)(2,1)}, u32[]{:S(2)}) copy-start(bf16[256,32,128]{2,1,0:T(8,128)(2,1)} %get-tuple-element.26) | copy-start | bytes 6291460
  373.5 8.1 %copy-start.4 = (f32[256,16,32]{0,2,1:T(8,128)S(1)}, f32[256,16,32]{0,2,1:T(8,128)}, u32[]{:S(2)}) copy-start(f32[256,16,32]{0,2,1:T(8,128)} %copy.84) | copy-start | bytes 1572868
  373.5 8.1 %copy-start.5 = (f32[256,16,32]{0,2,1:T(8,128)S(1)}, f32[256,16,32]{0,2,1:T(8,128)}, u32[]{:S(2)}) copy-start(f32[256,16,32]{0,2,1:T(8,128)} %copy.83) | copy-start | bytes 1572868
  373.5 8.1 %copy-start.6 = (f32[256,16,32]{0,2,1:T(8,128)S(1)}, f32[256,16,32]{0,2,1:T(8,128)}, u32[]{:S(2)}) copy-start(f32[256,16,32]{0,2,1:T(8,128)} %copy.82) | copy-start | bytes 1572868
  481.0 3.3 copy-start.38
  483.9 1.6 copy-start.29
  483.9 1.6 copy-start.30
  483.9 1.6 copy-start.31
  483.9 1.6 copy-start.32
  483.9 1.6 copy-start.33
  483.9 1.6 copy-start.34
  484.0 1.6 copy-start.35
  484.0 1.6 copy-start.36
  484.0 1.6 copy-start.37
  485.6 2.4 copy-start.28
